TPU v7x, 128 devices: a whole 4x4x4 slice. The times are simulated.
128 devices in a mesh: px: 8 (over z, core), py: 16 (over x, y).
Axes of the slice: x: 4, y: 4, z: 4, core: 2. Of those that a mesh axis runs over, the one named last changes fastest.
Arguments:
- nodes: bfloat16 [8, 16, 2048, 256], P('px', 'py'), may hold values from -6 to 80
- tile_src: int32 [8, 16, 16, 4], P('px', 'py'), may hold values from 0 to 79
- tile_mask: int32 [8, 16, 16, 4, 128, 128], P('px', 'py'), may hold values 0 or 1
- tokens: bfloat16 [128, 2048, 256], P(('px', 'py')), may hold values from -6 to 16
- tok_count: int32 [128, 128], P(None, ('px', 'py')), may hold values from 1 to 16, as said below
- w_e1: bfloat16 [256, 256], replicated, may hold values from -0.375 to 0.375
- w_e2: bfloat16 [256, 256], replicated, may hold values from -0.375 to 0.375
- w_n1: bfloat16 [512, 256], replicated, may hold values from -0.25 to 0.25
- w_n2: bfloat16 [256, 256], replicated, may hold values from -0.375 to 0.375
- w_q: bfloat16 [256, 256], replicated
- w_kv: bfloat16 [256, 512], replicated
- w_o: bfloat16 [256, 256], replicated, may hold values from -0.375 to 0.375
- cotangent: bfloat16 [8, 16, 2048, 256], P('px', 'py'), may hold values from -6 to 6
Outputs:
- grad_nodes: bfloat16 [8, 16, 2048, 256], P('px', 'py')
- grad_tokens: bfloat16 [128, 2048, 256], P(('px', 'py'))
Inputs may be any that keep to these rules, and one draw needn't show every extreme that they name: tok_count[s, e] slots of the 16 that device s holds for partition e are live, the first ones; every device's own slots for its own partition are all live.
All inputs are finite; a program needn't handle non-finite values. No bound on the sum of `tile_mask` on one device may be relied on, other than what follows from the above.
Results may differ from a plain program's by a relative error of at most 0.025.
Values may be sent and summed in bfloat16 or wider, within the bound.
No kernel may reach another device: no remote copies, remote signals or barrier semaphores. Data moves between devices by JAX's collectives and lax.ppermute only.
A program may use at most 128 MiB of HBM per device.

v0:
```python
import math

import jax
import jax.numpy as jnp
from jax import lax
from jax.sharding import PartitionSpec as P


def with_halo(block, sides, width):
    for axis, dim in sides:
        count = lax.axis_size(axis)
        forward = [(i, i + 1) for i in range(count - 1)]
        backward = [(target, source) for source, target in forward]
        low = lax.ppermute(
            lax.slice_in_dim(block, block.shape[dim] - width, None, axis=dim), axis, forward
        )
        high = lax.ppermute(lax.slice_in_dim(block, 0, width, axis=dim), axis, backward)
        block = jnp.concatenate([low, block, high], axis=dim)
    return block


def passed_along(value, axis, steps):
    count = lax.axis_size(axis)
    leading, last = (max(0, -steps), min(count, count - steps))
    return lax.ppermute(value, axis, [(source, source + steps) for source in range(leading, last)])


def dense(left, right):
    return jnp.dot(left, right, preferred_element_type=jnp.float32)


def silu_slope(values):
    sigma = jax.nn.sigmoid(values)
    return sigma * (1.0 + values * (1.0 - sigma))


def on_device(
    nodes, tile_src, tile_mask, tokens, tok_count, w_e1, w_e2, w_n1, w_n2, w_q, w_kv, w_o, cotangent
):
    latent = nodes[0, 0]
    node_rows = latent.shape[0]
    latent_width = latent.shape[1]
    block_count = tile_src.shape[2]
    tile_count = tile_src.shape[3]
    blk_rows = tile_mask.shape[-1]
    rows_px = lax.axis_size("px")
    rows_py = lax.axis_size("py")
    devices = rows_px * rows_py
    score_scale = 1.0 / math.sqrt(latent_width)
    pre_act = dense(latent, w_e1)
    activation = jax.nn.silu(pre_act).astype(jnp.bfloat16)
    message = dense(activation, w_e2).astype(jnp.bfloat16)
    padded = with_halo(message[None, None], (("px", 0), ("py", 1)), 1)
    sources = jnp.stack([padded[1, 1], padded[0, 1], padded[2, 1], padded[1, 0], padded[1, 2]])
    picked_ids = tile_src[0, 0]
    tile_bf16 = tile_mask[0, 0].astype(jnp.bfloat16)
    picked = sources.reshape(5 * block_count, blk_rows, latent_width)[picked_ids]
    gathered = jnp.einsum("bkij,bkjl->bil", tile_bf16, picked, preferred_element_type=jnp.float32)
    gathered = gathered.reshape(node_rows, latent_width).astype(jnp.bfloat16)
    zvalue = dense(latent, w_n1[:latent_width]) + dense(gathered, w_n1[latent_width:])
    hidden = jax.nn.silu(zvalue).astype(jnp.bfloat16)
    updated = (latent.astype(jnp.float32) + dense(hidden, w_n2)).astype(jnp.bfloat16)
    queries = dense(updated, w_q).astype(jnp.bfloat16)
    own_tokens = tokens[0]
    slot_count = own_tokens.shape[0] // devices
    outgoing = dense(own_tokens, w_kv).astype(jnp.bfloat16)
    features = outgoing.shape[-1]
    arrived = lax.all_to_all(outgoing[None], ("px", "py"), split_axis=1, concat_axis=0, tiled=True)
    arrived = arrived.reshape(devices * slot_count, features)
    key_rows = arrived[:, :latent_width]
    value_rows = arrived[:, latent_width:]
    live_keys = (jnp.arange(slot_count)[None, :] < tok_count[:, 0][:, None]).reshape(-1)
    scores = (
        jnp.einsum("nl,kl->nk", queries, key_rows, preferred_element_type=jnp.float32) * score_scale
    )
    scores = jnp.where(live_keys[None, :], scores, -jnp.inf)
    highest = jnp.max(scores, axis=1, keepdims=True)
    expo_terms = jnp.exp(scores - highest)
    probability = expo_terms / jnp.sum(expo_terms, axis=1, keepdims=True)
    prob_low = probability.astype(jnp.bfloat16)
    grad_out = dense(cotangent[0, 0], w_o.T).astype(jnp.bfloat16)
    grad_prob = jnp.einsum("nl,kl->nk", grad_out, value_rows, preferred_element_type=jnp.float32)
    grad_vals = jnp.einsum("nk,nl->kl", prob_low, grad_out, preferred_element_type=jnp.float32)
    spread = jnp.sum(probability * grad_prob, axis=1, keepdims=True)
    grad_score = (probability * (grad_prob - spread) * score_scale).astype(jnp.bfloat16)
    grad_query = dense(grad_score, key_rows).astype(jnp.bfloat16)
    grad_keys = jnp.einsum("nk,nl->kl", grad_score, queries, preferred_element_type=jnp.float32)
    grad_kv = jnp.concatenate([grad_keys, grad_vals], axis=1).astype(jnp.bfloat16)
    back_width = grad_kv.shape[-1]
    returned = lax.all_to_all(
        grad_kv.reshape(devices, slot_count, back_width),
        ("px", "py"),
        split_axis=0,
        concat_axis=1,
        tiled=True,
    )
    returned = returned.reshape(devices * slot_count, back_width)
    grad_tokens = dense(returned, w_kv.T).astype(jnp.bfloat16)
    grad_update = cotangent[0, 0].astype(jnp.float32) + dense(grad_query, w_q.T)
    update_low = grad_update.astype(jnp.bfloat16)
    grad_z = (dense(update_low, w_n2.T) * silu_slope(zvalue)).astype(jnp.bfloat16)
    grad_agg = dense(grad_z, w_n1[latent_width:].T).astype(jnp.bfloat16)
    grad_node = grad_update + dense(grad_z, w_n1[:latent_width].T)
    grad_parts = jnp.einsum(
        "bkij,bil->bkjl",
        tile_bf16,
        grad_agg.reshape(block_count, blk_rows, latent_width),
        preferred_element_type=jnp.float32,
    )
    grad_src = jax.ops.segment_sum(
        grad_parts.reshape(block_count * tile_count, blk_rows, latent_width),
        picked_ids.reshape(-1),
        num_segments=5 * block_count,
    )
    grad_src = grad_src.reshape(5, node_rows, latent_width)
    outbound = grad_src[1:].astype(jnp.bfloat16)
    collected = grad_src[0]
    for member, offset in ((0, -1), (1, 1)):
        collected = collected + passed_along(outbound[member], "px", offset).astype(jnp.float32)
    for member, offset in ((2, -1), (3, 1)):
        collected = collected + passed_along(outbound[member], "py", offset).astype(jnp.float32)
    grad_msg = collected.astype(jnp.bfloat16)
    grad_pre = (dense(grad_msg, w_e2.T) * silu_slope(pre_act)).astype(jnp.bfloat16)
    grad_nodes = (grad_node + dense(grad_pre, w_e1.T)).astype(jnp.bfloat16)
    return (grad_nodes[None, None], grad_tokens[None])


def solution(mesh):
    return jax.shard_map(
        on_device,
        mesh=mesh,
        in_specs=(
            P("px", "py", None, None),
            P("px", "py", None, None),
            P("px", "py", None, None, None, None),
            P(("px", "py"), None, None),
            P(None, ("px", "py")),
            P(),
            P(),
            P(),
            P(),
            P(),
            P(),
            P(),
            P("px", "py", None, None),
        ),
        out_specs=(P("px", "py", None, None), P(("px", "py"), None, None)),
        check_vma=False,
    )
```

profile of v0, /device:TPU:1, one launch (start us, length us, event | category | flops | bytes accessed | tf_op | source)
XLA Modules:
  0.0 334.0 jit_solution(2361125768231765847)
XLA Ops:
  4.2 5.0 %collective-permute-start = (bf16[1,1,2048,256]{3,2,1,0:T(8,128)(2,1)S(1)}, bf16[1,1,2048,256]{3,2,1,0:T(8,128)(2,1)S(1)}, u32[]{:S(2)}, u32[]{:S(2)}) collective-permute-start(bf16[1,1,2048,256]{3,2,1,0:T(8,128)(2,1)S(1)} %bitcast.126), channel_id=1, source_target_pairs={{0,16},{16,32},{32,48},{48,64},{64,80},{80,96},{96,112},{1,17},{17... | collective-permute-start | bytes 3145736 | tf_op jit(solution)/shard_map/ppermute | solution.py:14
  11.1 9.8 %collective-permute-done = bf16[1,1,2048,256]{3,2,1,0:T(8,128)(2,1)S(1)} collective-permute-done((bf16[1,1,2048,256]{3,2,1,0:T(8,128)(2,1)S(1)}, bf16[1,1,2048,256]{3,2,1,0:T(8,128)(2,1)S(1)}, u32[]{:S(2)}, u32[]{:S(2)}) %collective-permute-start) | collective-permute-done | bytes 1048608 | tf_op jit(solution)/shard_map/ppermute | solution.py:14
  20.9 4.4 %collective-permute-done.1 = bf16[1,1,2048,256]{3,2,1,0:T(8,128)(2,1)S(1)} collective-permute-done((bf16[1,1,2048,256]{3,2,1,0:T(8,128)(2,1)S(1)}, bf16[1,1,2048,256]{3,2,1,0:T(8,128)(2,1)S(1)}, u32[]{:S(2)}, u32[]{:S(2)}) %collective-permute-start.1) | collective-permute-done | bytes 1048608 | tf_op jit(solution)/shard_map/ppermute | solution.py:17
  27.3 5.2 %collective-permute-start.2 = (bf16[3,1,2048,256]{3,2,1,0:T(8,128)(2,1)}, bf16[3,1,2048,256]{3,2,1,0:T(8,128)(2,1)}, u32[]{:S(2)}, u32[]{:S(2)}) collective-permute-start(bf16[3,1,2048,256]{3,2,1,0:T(8,128)(2,1)} %pad_maximum_fusion), channel_id=1, source_target_pairs={{0,1},{1,2},{2,3},{3,4},{4,5},{5,6},{6,7},{7,8},{8,9},{9,10},{10,1... | collective-permute-start | bytes 9437192 | tf_op jit(solution)/shard_map/ppermute | solution.py:14
  34.6 18.5 %copy.40 = bf16[1,2048,512]{2,0,1:T(2,128)(2,1)} copy(bf16[1,2048,512]{2,1,0:T(8,128)(2,1)S(1)} %fusion.5) | data formatting | bytes 4194304 | tf_op jit(solution)/shard_map/broadcast_in_dim | solution.py:68
  53.6 14.1 %reduce = bf16[2048,512]{1,0:T(8,128)(2,1)S(1)} reduce(bf16[2048,1,512]{2,1,0:T(2,128)(2,1)} %bitcast.116, bf16[]{:T(256)} %broadcast.44), dimensions={1}, to_apply=%bitcast.114.reduce_sub_computation | reduce | bytes 4194306
  70.5 9.6 %all-to-all-start = ((bf16[128,2,4096]{2,1,0:T(2,128)(2,1)}), bf16[128,2,4096]{2,1,0:T(2,128)(2,1)S(1)}, u32[]{:S(2)}, u32[]{:S(2)}) async-start(bf16[128,2,4096]{2,1,0:T(2,128)(2,1)} %reshape.118), calls=%async_computation | async-start | bytes 4194304 | tf_op jit(solution)/shard_map/all_to_all | solution.py:68
  90.9 50.0 %all-to-all-done = bf16[128,2,4096]{2,1,0:T(2,128)(2,1)S(1)} async-done(((bf16[128,2,4096]{2,1,0:T(2,128)(2,1)}), bf16[128,2,4096]{2,1,0:T(2,128)(2,1)S(1)}, u32[]{:S(2)}, u32[]{:S(2)}) %all-to-all-start) | async-done | bytes 2097184 | tf_op jit(solution)/shard_map/all_to_all | solution.py:68
  140.9 6.8 %reshape.119 = bf16[2048,1,512]{2,1,0:T(2,128)(2,1)} reshape(bf16[128,2,4096]{2,1,0:T(2,128)(2,1)S(1)} %all-to-all-done) | data formatting | bytes 4194304
  147.7 4.2 %copy.39 = bf16[1,2048,512]{2,1,0:T(8,128)(2,1)} copy(bf16[1,2048,512]{2,0,1:T(2,128)(2,1)} %bitcast.118) | data formatting | bytes 4194304
  156.5 5.3 %gather_fusion = bf16[64,128,256]{2,1,0:T(8,128)(2,1)} fusion(bf16[80,128,256]{2,1,0:T(8,128)(2,1)} %bitcast.9, s32[1024]{0:T(1024)S(1)} %pad_clamp_fusion), kind=kCustom, calls=%fused_computation | custom fusion | bytes 8388864 | tf_op jit(solution)/shard_map/gather | solution.py:57
  161.8 4.4 %bitcast_convert_fusion = bf16[16,256,128]{1,2,0:T(8,128)(2,1)S(1)} fusion(bf16[16,4,128,256]{3,2,1,0:T(8,128)(2,1)} %bitcast.117, s32[1,1,16,4,128,128]{5,4,3,2,1,0:T(8,128)} %param.15), kind=kOutput, calls=%fused_computation.42 | convolution fusion | flops 538443776 | bytes 9437184 | tf_op jit(solution)/shard_map/bkij,bkjl->bil/dot_general | solution.py:58
  170.0 4.1 %fusion = (f32[2048]{0:T(1024)S(1)}, f32[2048,2048]{0,1:T(8,128)S(1)}) fusion(pred[2048]{0:T(1024)(128)(4,1)S(1)} %copy-done.21, bf16[2048,256]{1,0:T(8,128)(2,1)} %convolution_convert_fusion.4, bf16[2048,512]{1,0:T(8,128)(2,1)} %bitcast.122), kind=kOutput, calls=%fused_computation.6 | convolution fusion | flops 2160064512 | bytes 18884608 | tf_op jit(solution)/shard_map/nl,kl->nk/dot_general | solution.py:74
  174.1 5.0 %fusion.2 = f32[2048]{0:T(1024)S(1)} fusion(f32[2048,2048]{0,1:T(8,128)S(1)} %get-tuple-element.9, f32[2048]{0:T(1024)S(1)} %get-tuple-element.8, pred[2048]{0:T(1024)(128)(4,1)S(1)} %copy-done.21), kind=kLoop, calls=%fused_computation.8 | loop fusion | flops 16775168 | bytes 16795648 | tf_op jit(solution)/shard_map/reduce_sum | solution.py:79
  179.2 5.7 %fusion.10 = bf16[2048,256]{1,0:T(8,128)(2,1)} fusion(bf16[2048,256]{1,0:T(8,128)(2,1)S(1)} %copy-done.14, f32[2048,2048]{0,1:T(8,128)S(1)} %get-tuple-element.9, f32[2048]{0:T(1024)S(1)} %fusion.2, f32[2048]{0:T(1024)S(1)} %get-tuple-element.8, pred[2048]{0:T(1024)(128)(4,1)S(1)} %copy-done.21), kind=kOutput, calls=%fused_computation.30 | convolution fusion | flops 2168979456 | bytes 18892800 | tf_op jit(solution)/shard_map/nk,nl->kl/dot_general | solution.py:83
  184.9 9.5 %multiply_reduce_fusion = (f32[2048]{0:T(1024)S(1)}, f32[2048,2048]{0,1:T(8,128)}) fusion(f32[2048]{0:T(1024)S(1)} %fusion.2, f32[2048]{0:T(1024)S(1)} %get-tuple-element.8, f32[2048,2048]{0,1:T(8,128)S(1)} %get-tuple-element.9, pred[2048]{0:T(1024)(128)(4,1)S(1)} %copy-done.21, bf16[2048,256]{1,0:T(8,128)(2,1)S(1)} %copy-done.14, ...), kind=kOutput, calls=%fused_computation.3 | convolution fusion | flops 2172647424 | bytes 35678208 | tf_op jit(solution)/shard_map/nl,kl->nk/dot_general | solution.py:82
  194.4 12.5 %multiply_convert_fusion = bf16[2048,2048]{0,1:T(8,128)(2,1)} fusion(f32[2048,2048]{0,1:T(8,128)} %get-tuple-element.11, f32[2048]{0:T(1024)S(1)} %get-tuple-element.10, f32[2048]{0:T(1024)S(1)} %fusion.2, f32[2048]{0:T(1024)S(1)} %get-tuple-element.8, f32[2048,2048]{0,1:T(8,128)S(1)} %get-tuple-element.9, pred[2048]{0:T(1024)(128)(4,1)S(1)} %copy-done.21), kind=kLoop, calls=%fused_computation.2 | loop fusion | flops 33554432 | bytes 41969664 | tf_op jit(solution)/shard_map/convert_element_type | solution.py:85
  206.8 6.4 %convolution_add_fusion.2 = f32[2048,256]{1,0:T(8,128)S(1)} fusion(bf16[256,256]{1,0:T(8,128)(2,1)S(1)} %copy-done.23, bf16[2048,2048]{0,1:T(8,128)(2,1)} %multiply_convert_fusion, bf16[1,1,2048,256]{3,2,1,0:T(8,128)(2,1)S(1)} %copy-done.13, bf16[2048,512]{1,0:T(8,128)(2,1)} %bitcast.124), kind=kOutput, calls=%fused_computation.18 | convolution fusion | flops 2417491968 | bytes 12713984 | tf_op jit(solution)/shard_map/dot_general | solution.py:29
  213.3 3.4 %fusion.7 = bf16[2048,256]{1,0:T(8,128)(2,1)S(1)} fusion(bf16[256,256]{1,0:T(8,128)(2,1)} %param.21, f32[2048,256]{1,0:T(8,128)} %copy-done.12, f32[2048,256]{1,0:T(8,128)S(1)} %convolution_add_fusion.2), kind=kOutput, calls=%fused_computation.23 | convolution fusion | flops 273678336 | bytes 5373952 | tf_op jit(solution)/shard_map/dot_general | solution.py:29
  217.2 4.6 %fusion.19 = f32[16,256,4,128]{3,1,2,0:T(8,128)} fusion(bf16[16,128,256,1]{2,1,3,0:T(8,128)(2,1)S(1)} %bitcast.121, s32[1,1,16,4,128,128]{5,4,3,2,1,0:T(8,128)S(1)} %copy-done.2), kind=kOutput, calls=%fused_computation.43 | convolution fusion | flops 537919488 | bytes 13631488 | tf_op jit(solution)/shard_map/bkij,bil->bkjl/dot_general | solution.py:104
  221.7 9.0 %copy.31 = f32[64,128,256]{2,1,0:T(8,128)} copy(f32[64,128,256]{1,2,0:T(8,128)} %bitcast.115) | data formatting | bytes 16777216 | tf_op jit(solution)/shard_map/reshape | solution.py:111
  230.7 5.3 %broadcast_in_dim.36 = f32[80,128,256]{2,1,0:T(8,128)} broadcast(f32[]{:T(128)} %constant.5.clone.1), dimensions={} | broadcast | bytes 10485764 | tf_op jit(solution)/shard_map/broadcast_in_dim | solution.py:110
  236.0 19.5 %scatter_fusion = f32[80,128,256]{2,1,0:T(8,128)} fusion(f32[80,128,256]{2,1,0:T(8,128)} %broadcast_in_dim.36, s32[64]{0:T(128)S(1)} %reshape.108, f32[64,128,256]{2,1,0:T(8,128)} %copy.31), kind=kCustom, calls=%fused_computation.1 | custom fusion | flops 2097152 | bytes 25166080 | tf_op jit(solution)/shard_map/scatter-add | solution.py:110
  255.6 4.8 %convert.11 = bf16[80,128,256]{2,1,0:T(8,128)(2,1)S(1)} convert(f32[80,128,256]{2,1,0:T(8,128)} %scatter_fusion) | non-fusion elementwise | flops 2621440 | bytes 15728640 | tf_op jit(solution)/shard_map/convert.4
  264.4 3.6 %collective-permute-start.5 = (bf16[2048,256]{1,0:T(8,128)(2,1)}, bf16[2048,256]{1,0:T(8,128)(2,1)}, u32[]{:S(2)}, u32[]{:S(2)}) collective-permute-start(bf16[2048,256]{1,0:T(8,128)(2,1)} %bitcast.25), channel_id=1, source_target_pairs={{0,16},{16,32},{32,48},{48,64},{64,80},{80,96},{96,112},{1,17},{17... | collective-permute-start | bytes 3145736 | tf_op jit(solution)/shard_map/ppermute | solution.py:25
  269.4 5.1 %collective-permute-start.7 = (bf16[2048,256]{1,0:T(8,128)(2,1)}, bf16[2048,256]{1,0:T(8,128)(2,1)}, u32[]{:S(2)}, u32[]{:S(2)}) collective-permute-start(bf16[2048,256]{1,0:T(8,128)(2,1)} %bitcast.27), channel_id=1, source_target_pairs={{0,1},{1,2},{2,3},{3,4},{4,5},{5,6},{6,7},{7,8},{8,9},{9,10},{10,1... | collective-permute-start | bytes 3145736 | tf_op jit(solution)/shard_map/ppermute | solution.py:25
  274.5 5.7 %convolution_convert_fusion.6 = bf16[2048,256]{1,0:T(8,128)(2,1)S(1)} fusion(bf16[2048,2048]{0,1:T(8,128)(2,1)} %multiply_convert_fusion, bf16[2048,256]{1,0:T(8,128)(2,1)S(1)} %copy-done.25), kind=kOutput, calls=%fused_computation.31 | convolution fusion | flops 2148007936 | bytes 10485760 | tf_op jit(solution)/shard_map/nk,nl->kl/dot_general | solution.py:87
  281.9 8.9 %all-to-all-start.1 = ((bf16[128,16,512]{2,1,0:T(8,128)(2,1)}), bf16[128,16,512]{2,1,0:T(8,128)(2,1)S(1)}, u32[]{:S(2)}, u32[]{:S(2)}) async-start(bf16[128,16,512]{2,1,0:T(8,128)(2,1)} %pad_maximum_fusion.1), calls=%async_computation.1 | async-start | bytes 4194304 | tf_op jit(solution)/shard_map/all_to_all | solution.py:90
  294.8 3.3 collective-permute-done.6
  298.5 3.8 %fusion.18 = bf16[2048,256]{1,0:T(8,128)(2,1)} fusion(f32[16,128,256]{2,1,0:T(8,128)S(1)} %slice.64, bf16[2048,256]{1,0:T(8,128)(2,1)} %collective-permute-done.7, bf16[2048,256]{1,0:T(8,128)(2,1)} %collective-permute-done.6, bf16[2048,256]{1,0:T(8,128)(2,1)} %collective-permute-done.5, bf16[2048,256]{1,0:T(8,128)(2,1)} %collective-permute-done.4), kind=kLoop, calls=%fused_computation.41 | loop fusion | flops 4718592 | bytes 7340032 | tf_op jit(solution)/shard_map/convert_element_type | solution.py:122
  302.4 4.7 %fusion.13 = bf16[1,1,2048,256]{3,2,1,0:T(8,128)(2,1)} fusion(f32[2048,256]{1,0:T(8,128)} %convolution_add_fusion.1, bf16[256,256]{1,0:T(8,128)(2,1)S(1)} %copy-done.20, bf16[2048,256]{1,0:T(8,128)(2,1)} %fusion.18, bf16[256,256]{1,0:T(8,128)(2,1)} %param.19, f32[2048,256]{1,0:T(8,128)} %copy-done.9), kind=kOutput, calls=%fused_computation.33 | convolution fusion | flops 542638080 | bytes 6553600 | tf_op jit(solution)/shard_map/dot_general | solution.py:29
  307.1 25.2 %all-to-all-done.1 = bf16[128,16,512]{2,1,0:T(8,128)(2,1)S(1)} async-done(((bf16[128,16,512]{2,1,0:T(8,128)(2,1)}), bf16[128,16,512]{2,1,0:T(8,128)(2,1)S(1)}, u32[]{:S(2)}, u32[]{:S(2)}) %all-to-all-start.1) | async-done | bytes 2097184 | tf_op jit(solution)/shard_map/all_to_all | solution.py:90
  (89 shorter events, 45.4 us)
Async XLA Ops:
  0.6 33.2 %copy-start = (bf16[1,2048,256]{2,1,0:T(8,128)(2,1)S(1)}, bf16[1,2048,256]{2,1,0:T(8,128)(2,1)}, u32[]{:S(2)}) copy-start(bf16[1,2048,256]{2,1,0:T(8,128)(2,1)} %param.16) | copy-start | bytes 3145732
  4.2 29.7 %copy-start.16 = (bf16[256,512]{1,0:T(8,128)(2,1)S(1)}, bf16[256,512]{1,0:T(8,128)(2,1)}, u32[]{:S(2)}) copy-start(bf16[256,512]{1,0:T(8,128)(2,1)} %param.23) | copy-start | bytes 786436
  4.2 16.8 %collective-permute-start = (bf16[1,1,2048,256]{3,2,1,0:T(8,128)(2,1)S(1)}, bf16[1,1,2048,256]{3,2,1,0:T(8,128)(2,1)S(1)}, u32[]{:S(2)}, u32[]{:S(2)}) collective-permute-start(bf16[1,1,2048,256]{3,2,1,0:T(8,128)(2,1)S(1)} %bitcast.126), channel_id=1, source_target_pairs={{0,16},{16,32},{32,48},{48,64},{64,80},{80,96},{96,112},{1,17},{17... | collective-permute-start | bytes 3145736 | tf_op jit(solution)/shard_map/ppermute | solution.py:14
  9.2 16.1 %collective-permute-start.1 = (bf16[1,1,2048,256]{3,2,1,0:T(8,128)(2,1)S(1)}, bf16[1,1,2048,256]{3,2,1,0:T(8,128)(2,1)S(1)}, u32[]{:S(2)}, u32[]{:S(2)}) collective-permute-start(bf16[1,1,2048,256]{3,2,1,0:T(8,128)(2,1)S(1)} %bitcast.127), channel_id=1, source_target_pairs={{16,0},{32,16},{48,32},{64,48},{80,64},{96,80},{112,96},{17,1},{33... | collective-permute-start | bytes 3145736 | tf_op jit(solution)/shard_map/ppermute | solution.py:17
  20.9 6.4 %copy-start.5 = (bf16[1,1,2048,256]{3,2,1,0:T(8,128)(2,1)}, bf16[1,1,2048,256]{3,2,1,0:T(8,128)(2,1)S(1)}, u32[]{:S(2)}) copy-start(bf16[1,1,2048,256]{3,2,1,0:T(8,128)(2,1)S(1)} %collective-permute-done) | copy-start | bytes 3145732
  27.3 124.6 %collective-permute-start.2 = (bf16[3,1,2048,256]{3,2,1,0:T(8,128)(2,1)}, bf16[3,1,2048,256]{3,2,1,0:T(8,128)(2,1)}, u32[]{:S(2)}, u32[]{:S(2)}) collective-permute-start(bf16[3,1,2048,256]{3,2,1,0:T(8,128)(2,1)} %pad_maximum_fusion), channel_id=1, source_target_pairs={{0,1},{1,2},{2,3},{3,4},{4,5},{5,6},{6,7},{7,8},{8,9},{9,10},{10,1... | collective-permute-start | bytes 9437192 | tf_op jit(solution)/shard_map/ppermute | solution.py:14
  32.6 121.6 %collective-permute-start.3 = (bf16[3,1,2048,256]{3,2,1,0:T(8,128)(2,1)}, bf16[3,1,2048,256]{3,2,1,0:T(8,128)(2,1)}, u32[]{:S(2)}, u32[]{:S(2)}) collective-permute-start(bf16[3,1,2048,256]{3,2,1,0:T(8,128)(2,1)} %pad_maximum_fusion), channel_id=1, source_target_pairs={{1,0},{2,1},{3,2},{4,3},{5,4},{6,5},{7,6},{8,7},{9,8},{10,9},{11,1... | collective-permute-start | bytes 9437192 | tf_op jit(solution)/shard_map/ppermute | solution.py:17
  70.5 9.6 %copy-start.22 = (s32[1,1,16,4]{2,3,1,0:T(4,128)S(1)}, s32[1,1,16,4]{2,3,1,0:T(4,128)}, u32[]{:S(2)}) copy-start(s32[1,1,16,4]{2,3,1,0:T(4,128)} %param.14) | copy-start | bytes 772
  70.5 14.0 %copy-start.19 = (bf16[256,256]{1,0:T(8,128)(2,1)S(1)}, bf16[256,256]{1,0:T(8,128)(2,1)}, u32[]{:S(2)}) copy-start(bf16[256,256]{1,0:T(8,128)(2,1)} %param.24) | copy-start | bytes 393220
  70.5 16.7 %copy-start.4 = (bf16[1,1,2048,256]{3,2,1,0:T(8,128)(2,1)S(1)}, bf16[1,1,2048,256]{3,2,1,0:T(8,128)(2,1)}, u32[]{:S(2)}) copy-start(bf16[1,1,2048,256]{3,2,1,0:T(8,128)(2,1)} %param.13) | copy-start | bytes 3145732
  70.5 16.7 %copy-start.18 = (bf16[512,256]{1,0:T(8,128)(2,1)S(1)}, bf16[512,256]{1,0:T(8,128)(2,1)}, u32[]{:S(2)}) copy-start(bf16[512,256]{1,0:T(8,128)(2,1)} %param.20) | copy-start | bytes 786436
  70.5 70.5 %all-to-all-start = ((bf16[128,2,4096]{2,1,0:T(2,128)(2,1)}), bf16[128,2,4096]{2,1,0:T(2,128)(2,1)S(1)}, u32[]{:S(2)}, u32[]{:S(2)}) async-start(bf16[128,2,4096]{2,1,0:T(2,128)(2,1)} %reshape.118), calls=%async_computation | async-start | bytes 4194304 | tf_op jit(solution)/shard_map/all_to_all | solution.py:68
  83.7 5.2 %copy-start.6 = (bf16[1,1,2048,256]{3,2,1,0:T(8,128)(2,1)S(1)}, bf16[1,1,2048,256]{3,2,1,0:T(8,128)(2,1)}, u32[]{:S(2)}) copy-start(bf16[1,1,2048,256]{3,2,1,0:T(8,128)(2,1)} %copy-done.5) | copy-start | bytes 3145732
  87.1 2.8 copy-start.8
  161.8 4.4 %copy-start.3 = (f32[2048,256]{1,0:T(8,128)S(1)}, f32[2048,256]{1,0:T(8,128)}, u32[]{:S(2)}) copy-start(f32[2048,256]{1,0:T(8,128)} %fusion.32) | copy-start | bytes 6291460
  167.2 2.9 copy-start.12
  167.2 2.9 copy-start.21
  174.1 5.1 %copy-start.14 = (bf16[2048,256]{1,0:T(8,128)(2,1)S(1)}, bf16[2048,256]{1,0:T(8,128)(2,1)}, u32[]{:S(2)}) copy-start(bf16[2048,256]{1,0:T(8,128)(2,1)} %convolution_convert_fusion.3) | copy-start | bytes 3145732
  194.4 12.5 %copy-start.13 = (bf16[1,1,2048,256]{3,2,1,0:T(8,128)(2,1)S(1)}, bf16[1,1,2048,256]{3,2,1,0:T(8,128)(2,1)}, u32[]{:S(2)}) copy-start(bf16[1,1,2048,256]{3,2,1,0:T(8,128)(2,1)} %param.25) | copy-start | bytes 3145732
  213.3 3.4 %copy-start.10 = (f32[2048,256]{1,0:T(8,128)}, f32[2048,256]{1,0:T(8,128)S(1)}, u32[]{:S(2)}) copy-start(f32[2048,256]{1,0:T(8,128)S(1)} %convolution_add_fusion.2) | copy-start | bytes 6291460
  213.3 3.9 %copy-start.2 = (s32[1,1,16,4,128,128]{5,4,3,2,1,0:T(8,128)S(1)}, s32[1,1,16,4,128,128]{5,4,3,2,1,0:T(8,128)}, u32[]{:S(2)}) copy-start(s32[1,1,16,4,128,128]{5,4,3,2,1,0:T(8,128)} %param.15) | copy-start | bytes 12582916
  260.3 14.2 %copy-start.25 = (bf16[2048,256]{1,0:T(8,128)(2,1)S(1)}, bf16[2048,256]{1,0:T(8,128)(2,1)}, u32[]{:S(2)}) copy-start(bf16[2048,256]{1,0:T(8,128)(2,1)} %convolution_convert_fusion.4) | copy-start | bytes 3145732
  262.5 32.3 %collective-permute-start.4 = (bf16[2048,256]{1,0:T(8,128)(2,1)}, bf16[2048,256]{1,0:T(8,128)(2,1)}, u32[]{:S(2)}, u32[]{:S(2)}) collective-permute-start(bf16[2048,256]{1,0:T(8,128)(2,1)} %bitcast.24), channel_id=1, source_target_pairs={{16,0},{32,16},{48,32},{64,48},{80,64},{96,80},{112,96},{17,1},{33... | collective-permute-start | bytes 3145736 | tf_op jit(solution)/shard_map/ppermute | solution.py:25
  264.4 30.4 %collective-permute-start.5 = (bf16[2048,256]{1,0:T(8,128)(2,1)}, bf16[2048,256]{1,0:T(8,128)(2,1)}, u32[]{:S(2)}, u32[]{:S(2)}) collective-permute-start(bf16[2048,256]{1,0:T(8,128)(2,1)} %bitcast.25), channel_id=1, source_target_pairs={{0,16},{16,32},{32,48},{48,64},{64,80},{80,96},{96,112},{1,17},{17... | collective-permute-start | bytes 3145736 | tf_op jit(solution)/shard_map/ppermute | solution.py:25
  268.1 30.1 %collective-permute-start.6 = (bf16[2048,256]{1,0:T(8,128)(2,1)}, bf16[2048,256]{1,0:T(8,128)(2,1)}, u32[]{:S(2)}, u32[]{:S(2)}) collective-permute-start(bf16[2048,256]{1,0:T(8,128)(2,1)} %bitcast.26), channel_id=1, source_target_pairs={{1,0},{2,1},{3,2},{4,3},{5,4},{6,5},{7,6},{8,7},{9,8},{10,9},{11,1... | collective-permute-start | bytes 3145736 | tf_op jit(solution)/shard_map/ppermute | solution.py:25
  269.4 10.9 %copy-start.15 = (bf16[2048,256]{1,0:T(8,128)(2,1)S(1)}, bf16[2048,256]{1,0:T(8,128)(2,1)}, u32[]{:S(2)}) copy-start(bf16[2048,256]{1,0:T(8,128)(2,1)} %fusion.10) | copy-start | bytes 3145732
  269.4 29.2 %collective-permute-start.7 = (bf16[2048,256]{1,0:T(8,128)(2,1)}, bf16[2048,256]{1,0:T(8,128)(2,1)}, u32[]{:S(2)}, u32[]{:S(2)}) collective-permute-start(bf16[2048,256]{1,0:T(8,128)(2,1)} %bitcast.27), channel_id=1, source_target_pairs={{0,1},{1,2},{2,3},{3,4},{4,5},{5,6},{6,7},{7,8},{8,9},{9,10},{10,1... | collective-permute-start | bytes 3145736 | tf_op jit(solution)/shard_map/ppermute | solution.py:25
  281.9 50.4 %all-to-all-start.1 = ((bf16[128,16,512]{2,1,0:T(8,128)(2,1)}), bf16[128,16,512]{2,1,0:T(8,128)(2,1)S(1)}, u32[]{:S(2)}, u32[]{:S(2)}) async-start(bf16[128,16,512]{2,1,0:T(8,128)(2,1)} %pad_maximum_fusion.1), calls=%async_computation.1 | async-start | bytes 4194304 | tf_op jit(solution)/shard_map/all_to_all | solution.py:90
  290.8 2.2 copy-start.11
  294.8 7.6 %copy-start.20 = (bf16[256,256]{1,0:T(8,128)(2,1)S(1)}, bf16[256,256]{1,0:T(8,128)(2,1)}, u32[]{:S(2)}) copy-start(bf16[256,256]{1,0:T(8,128)(2,1)} %param.18) | copy-start | bytes 393220
  302.4 29.9 %copy-start.17 = (bf16[256,512]{1,0:T(8,128)(2,1)S(1)}, bf16[256,512]{1,0:T(8,128)(2,1)}, u32[]{:S(2)}) copy-start(bf16[256,512]{1,0:T(8,128)(2,1)} %param.23) | copy-start | bytes 786436
  302.4 31.6 %copy-start.1 = (bf16[1,2048,256]{2,1,0:T(8,128)(2,1)S(1)}, bf16[1,2048,256]{2,1,0:T(8,128)(2,1)}, u32[]{:S(2)}) copy-start(bf16[1,2048,256]{2,1,0:T(8,128)(2,1)} %param.16) | copy-start | bytes 3145732
  (4 other events, 6.4 us)
where the time goes:
time: 336 us; the launch traced here: 334 us
  waiting for transfers between devices  93.2 us (28%)
  local copies, waits for them, and re-layouts  66.8 us (20%)
  other arithmetic  64.7 us (19%)
  matrix products  64.4 us (19%)
  starting transfers between devices  44 us (13%)
    all_to_all x1, waiting for transfers between devices, on_device(): lax.all_to_all(outgoing[None], ('px', 'py'), split_axis=1, concat_axis=0,...  50 us
    dot_general x13, matrix products, dense(): return jnp.dot(left, right, preferred_element_type=jnp.float32)  30.4 us
    all_to_all x1, waiting for transfers between devices, on_device(): lax.all_to_all(grad_kv.reshape(devices, slot_count, back_width), ('px', '...  25.2 us
    unnamed x60, local copies, waits for them, and re-layouts  20.1 us
    scatter-add x1, other arithmetic, on_device(): jax.ops.segment_sum(grad_parts.reshape(block_count * tile_count, blk_rows...  19.5 us
    broadcast_in_dim x1, local copies, waits for them, and re-layouts, on_device(): outgoing[None]  18.5 us
    unnamed x1, other arithmetic  14.1 us
    convert_element_type x1, other arithmetic, on_device(): (probability * (grad_prob - spread) * score_scale).astype(jnp.bfloat16)  12.5 us
  transfers between devices with their start and end apart: 10, of which 6 were waited for; matrix products, arithmetic and copies ran while one was open for 24% of the time, Pallas kernels for 0%

commit v1 on v0

--- a/solution.py
+++ b/solution.py
@@ -50,8 +50,15 @@
     pre_act = dense(latent, w_e1)
     activation = jax.nn.silu(pre_act).astype(jnp.bfloat16)
     message = dense(activation, w_e2).astype(jnp.bfloat16)
-    padded = with_halo(message[None, None], (("px", 0), ("py", 1)), 1)
-    sources = jnp.stack([padded[1, 1], padded[0, 1], padded[2, 1], padded[1, 0], padded[1, 2]])
+    sources = jnp.stack(
+        [
+            message,
+            passed_along(message, "px", 1),
+            passed_along(message, "px", -1),
+            passed_along(message, "py", 1),
+            passed_along(message, "py", -1),
+        ]
+    )
     picked_ids = tile_src[0, 0]
     tile_bf16 = tile_mask[0, 0].astype(jnp.bfloat16)
     picked = sources.reshape(5 * block_count, blk_rows, latent_width)[picked_ids]
@@ -63,10 +70,12 @@
     queries = dense(updated, w_q).astype(jnp.bfloat16)
     own_tokens = tokens[0]
     slot_count = own_tokens.shape[0] // devices
-    outgoing = dense(own_tokens, w_kv).astype(jnp.bfloat16)
-    features = outgoing.shape[-1]
-    arrived = lax.all_to_all(outgoing[None], ("px", "py"), split_axis=1, concat_axis=0, tiled=True)
-    arrived = arrived.reshape(devices * slot_count, features)
+    token_groups = own_tokens.reshape(devices, slot_count, latent_width)
+    arrived_tokens = lax.all_to_all(
+        token_groups, ("px", "py"), split_axis=0, concat_axis=0, tiled=True
+    )
+    arrived_tokens = arrived_tokens.reshape(devices * slot_count, latent_width)
+    arrived = dense(arrived_tokens, w_kv).astype(jnp.bfloat16)
     key_rows = arrived[:, :latent_width]
     value_rows = arrived[:, latent_width:]
     live_keys = (jnp.arange(slot_count)[None, :] < tok_count[:, 0][:, None]).reshape(-1)
@@ -86,16 +95,15 @@
     grad_query = dense(grad_score, key_rows).astype(jnp.bfloat16)
     grad_keys = jnp.einsum("nk,nl->kl", grad_score, queries, preferred_element_type=jnp.float32)
     grad_kv = jnp.concatenate([grad_keys, grad_vals], axis=1).astype(jnp.bfloat16)
-    back_width = grad_kv.shape[-1]
+    grad_slots = dense(grad_kv, w_kv.T).astype(jnp.bfloat16)
     returned = lax.all_to_all(
-        grad_kv.reshape(devices, slot_count, back_width),
+        grad_slots.reshape(devices, slot_count, latent_width),
         ("px", "py"),
         split_axis=0,
-        concat_axis=1,
+        concat_axis=0,
         tiled=True,
     )
-    returned = returned.reshape(devices * slot_count, back_width)
-    grad_tokens = dense(returned, w_kv.T).astype(jnp.bfloat16)
+    grad_tokens = returned.reshape(devices * slot_count, latent_width)
     grad_update = cotangent[0, 0].astype(jnp.float32) + dense(grad_query, w_q.T)
     update_low = grad_update.astype(jnp.bfloat16)
     grad_z = (dense(update_low, w_n2.T) * silu_slope(zvalue)).astype(jnp.bfloat16)

time: 336 us -> 261 us (0.78)
  waiting for transfers between devices: 93.2 us -> 61.3 us
  local copies, waits for them, and re-layouts: 66.8 us -> 38.4 us
  other arithmetic: 64.7 us -> 43.2 us
  matrix products: 64.4 us -> 70.2 us
    broadcast_in_dim x1 -> x0, local copies, waits for them, and re-layouts: 18.5 us -> none  [on_device(): outgoing[None]]
    ppermute x4 -> x0, waiting for transfers between devices: 14.2 us -> none  [the longest x2 9.8 us: with_halo(): lax.ppermute(lax.slice_in_dim(block, block.shape[dim] - width, None, axis...]
    unnamed x1 -> x0, other arithmetic: 14.1 us -> none
    all_to_all x2, waiting for transfers between devices: 75.2 us -> 61.3 us  [the longest x1 31.3 us: on_device(): lax.all_to_all(grad_slots.reshape(devices, slot_count, latent_width), ('p...]
    ppermute x4 -> x0, starting transfers between devices: 13.5 us -> none  [the longest x2 10.3 us: with_halo(): lax.ppermute(lax.slice_in_dim(block, block.shape[dim] - width, None, axis...]
    ppermute x4 -> x8, starting transfers between devices: 12 us -> 25.1 us  [passed_along(): lax.ppermute(value, axis, [(source, source + steps) for source in range(l...]
    unnamed x60 -> x45, local copies, waits for them, and re-layouts: 20.1 us -> 12.2 us
    dot_general x13, matrix products: 30.4 us -> 38 us  [dense(): return jnp.dot(left, right, preferred_element_type=jnp.float32)]
  transfers between devices with their start and end apart: 10 -> 10, of which waited for: 6 -> 2; matrix products, arithmetic and copies ran while one was open for 24% -> 8% of each run, Pallas kernels for 0% -> 0%
where the time goes in v1:
time: 261 us; the launch traced here: 260 us
  matrix products  70.2 us (27%)
  waiting for transfers between devices  61.3 us (23%)
  starting transfers between devices  45.6 us (17%)
  other arithmetic  43.2 us (17%)
  local copies, waits for them, and re-layouts  38.4 us (15%)
    dot_general x13, matrix products, dense(): return jnp.dot(left, right, preferred_element_type=jnp.float32)  38 us
    all_to_all x1, waiting for transfers between devices, on_device(): lax.all_to_all(grad_slots.reshape(devices, slot_count, latent_width), ('p...  31.3 us
    all_to_all x1, waiting for transfers between devices, on_device(): lax.all_to_all(token_groups, ('px', 'py'), split_axis=0, concat_axis=0, t...  30 us
    ppermute x8, starting transfers between devices, passed_along(): lax.ppermute(value, axis, [(source, source + steps) for source in range(l...  25.1 us
    scatter-add x1, other arithmetic, on_device(): jax.ops.segment_sum(grad_parts.reshape(block_count * tile_count, blk_rows...  19.5 us
    unnamed x45, local copies, waits for them, and re-layouts  12.2 us
    all_to_all x1, starting transfers between devices, on_device(): lax.all_to_all(token_groups, ('px', 'py'), split_axis=0, concat_axis=0, t...  11.6 us
    convert_element_type x1, other arithmetic, on_device(): (probability * (grad_prob - spread) * score_scale).astype(jnp.bfloat16)  9.98 us
  transfers between devices with their start and end apart: 10, of which 2 were waited for; matrix products, arithmetic and copies ran while one was open for 8% of the time, Pallas kernels for 0%

profile of v1, /device:TPU:1, one launch (start us, length us, event | category | flops | bytes accessed | tf_op | source)
XLA Modules:
  0.0 259.7 jit_solution(5944795980061732963)
XLA Ops:
  2.4 3.2 %bitcast_dynamic-update-slice_fusion.4 = (bf16[5,2048,256]{2,1,0:T(8,128)(2,1)}, bf16[2048,256]{1,0:T(8,128)(2,1)}) fusion(bf16[256,256]{1,0:T(8,128)(2,1)} %param.19, f32[2048,256]{1,0:T(8,128)S(1)} %fusion.28), kind=kOutput, calls=%fused_computation.55 | convolution fusion | flops 271581184 | bytes 4325376 | tf_op jit(solution)/shard_map/dot_general | solution.py:29
  5.6 5.0 %collective-permute-start = (bf16[2048,256]{1,0:T(8,128)(2,1)}, bf16[2048,256]{1,0:T(8,128)(2,1)}, u32[]{:S(2)}, u32[]{:S(2)}) collective-permute-start(bf16[2048,256]{1,0:T(8,128)(2,1)} %get-tuple-element.7), channel_id=1, source_target_pairs={{0,16},{16,32},{32,48},{48,64},{64,80},{80,96},{96,112},{1,17},{17... | collective-permute-start | bytes 3145736 | tf_op jit(solution)/shard_map/ppermute | solution.py:25
  12.6 4.2 %collective-permute-start.2 = (bf16[2048,256]{1,0:T(8,128)(2,1)}, bf16[2048,256]{1,0:T(8,128)(2,1)}, u32[]{:S(2)}, u32[]{:S(2)}) collective-permute-start(bf16[2048,256]{1,0:T(8,128)(2,1)} %get-tuple-element.7), channel_id=1, source_target_pairs={{0,1},{1,2},{2,3},{3,4},{4,5},{5,6},{6,7},{7,8},{8,9},{9,10},{10,1... | collective-permute-start | bytes 3145736 | tf_op jit(solution)/shard_map/ppermute | solution.py:25
  18.1 11.6 %all-to-all-start = ((bf16[128,16,256]{2,1,0:T(8,128)(2,1)}), bf16[128,16,256]{2,1,0:T(8,128)(2,1)}, u32[]{:S(2)}, u32[]{:S(2)}) async-start(bf16[128,16,256]{2,1,0:T(8,128)(2,1)} %bitcast.16), calls=%async_computation | async-start | bytes 2097152 | tf_op jit(solution)/shard_map/all_to_all | solution.py:74
  31.6 2.7 %convolution_convert_fusion.3 = bf16[2048,256]{1,0:T(8,128)(2,1)} fusion(bf16[256,256]{1,0:T(8,128)(2,1)S(1)} %copy-done.10, bf16[1,1,2048,256]{3,2,1,0:T(8,128)(2,1)} %param.25), kind=kOutput, calls=%fused_computation.25 | convolution fusion | flops 268959744 | bytes 2228224 | tf_op jit(solution)/shard_map/dot_general | solution.py:29
  34.3 30.0 %all-to-all-done = bf16[128,16,256]{2,1,0:T(8,128)(2,1)} async-done(((bf16[128,16,256]{2,1,0:T(8,128)(2,1)}), bf16[128,16,256]{2,1,0:T(8,128)(2,1)}, u32[]{:S(2)}, u32[]{:S(2)}) %all-to-all-start) | async-done | bytes 1048608 | tf_op jit(solution)/shard_map/all_to_all | solution.py:74
  64.3 3.2 %convolution_convert_fusion = bf16[2048,512]{1,0:T(8,128)(2,1)} fusion(bf16[2048,256]{1,0:T(8,128)(2,1)} %bitcast.17, bf16[256,512]{1,0:T(8,128)(2,1)S(1)} %copy-done), kind=kOutput, calls=%fused_computation.11 | convolution fusion | flops 537919488 | bytes 3407872 | tf_op jit(solution)/shard_map/dot_general | solution.py:29
  74.3 2.3 bitcast_dynamic-update-slice_fusion
  76.6 5.3 %gather_fusion = bf16[64,128,256]{2,1,0:T(8,128)(2,1)} fusion(bf16[80,128,256]{2,1,0:T(8,128)(2,1)} %bitcast.102, s32[1024]{0:T(1024)S(1)} %pad_clamp_fusion), kind=kCustom, calls=%fused_computation | custom fusion | bytes 8388864 | tf_op jit(solution)/shard_map/gather | solution.py:64
  82.0 4.3 %bitcast_convert_fusion = bf16[16,256,128]{1,2,0:T(8,128)(2,1)S(1)} fusion(bf16[16,4,128,256]{3,2,1,0:T(8,128)(2,1)} %bitcast.98, s32[1,1,16,4,128,128]{5,4,3,2,1,0:T(8,128)} %param.15), kind=kOutput, calls=%fused_computation.40 | convolution fusion | flops 538443776 | bytes 9437184 | tf_op jit(solution)/shard_map/bkij,bkjl->bil/dot_general | solution.py:65
  88.1 2.5 convolution_convert_fusion.4
  90.6 4.6 %fusion = (f32[2048]{0:T(1024)S(1)}, f32[2048,2048]{0,1:T(8,128)S(1)}) fusion(pred[2048]{0:T(1024)(128)(4,1)S(1)} %lt.39, bf16[2048,256]{1,0:T(8,128)(2,1)S(1)} %convolution_convert_fusion.4, bf16[2048,512]{1,0:T(8,128)(2,1)} %convolution_convert_fusion), kind=kOutput, calls=%fused_computation.6 | convolution fusion | flops 2160064512 | bytes 18884608 | tf_op jit(solution)/shard_map/nl,kl->nk/dot_general | solution.py:83
  95.2 5.0 %fusion.2 = f32[2048]{0:T(1024)S(1)} fusion(f32[2048,2048]{0,1:T(8,128)S(1)} %get-tuple-element.9, f32[2048]{0:T(1024)S(1)} %get-tuple-element.8, pred[2048]{0:T(1024)(128)(4,1)S(1)} %lt.39), kind=kLoop, calls=%fused_computation.8 | loop fusion | flops 16775168 | bytes 16795648 | tf_op jit(solution)/shard_map/reduce_sum | solution.py:88
  100.2 5.6 %fusion.9 = bf16[2048,256]{1,0:T(8,128)(2,1)} fusion(bf16[2048,256]{1,0:T(8,128)(2,1)S(1)} %copy-done.7, f32[2048,2048]{0,1:T(8,128)S(1)} %get-tuple-element.9, f32[2048]{0:T(1024)S(1)} %fusion.2, f32[2048]{0:T(1024)S(1)} %get-tuple-element.8, pred[2048]{0:T(1024)(128)(4,1)S(1)} %lt.39), kind=kOutput, calls=%fused_computation.28 | convolution fusion | flops 2168979456 | bytes 18892800 | tf_op jit(solution)/shard_map/nk,nl->kl/dot_general | solution.py:92
  105.8 9.6 %multiply_reduce_fusion = (f32[2048]{0:T(1024)S(1)}, f32[2048,2048]{0,1:T(8,128)}) fusion(f32[2048]{0:T(1024)S(1)} %fusion.2, f32[2048]{0:T(1024)S(1)} %get-tuple-element.8, f32[2048,2048]{0,1:T(8,128)S(1)} %get-tuple-element.9, pred[2048]{0:T(1024)(128)(4,1)S(1)} %lt.39, bf16[2048,256]{1,0:T(8,128)(2,1)} %convolution_convert_fusion.3, ...), kind=kOutput, calls=%fused_computation.3 | convolution fusion | flops 2172647424 | bytes 35678208 | tf_op jit(solution)/shard_map/nl,kl->nk/dot_general | solution.py:91
  115.4 10.0 %multiply_convert_fusion = bf16[2048,2048]{0,1:T(8,128)(2,1)S(1)} fusion(f32[2048,2048]{0,1:T(8,128)} %get-tuple-element.11, f32[2048]{0:T(1024)S(1)} %get-tuple-element.10, f32[2048]{0:T(1024)S(1)} %fusion.2, f32[2048]{0:T(1024)S(1)} %get-tuple-element.8, f32[2048,2048]{0,1:T(8,128)S(1)} %get-tuple-element.9, pred[2048]{0:T(1024)(128)(4,1)S(1)} %lt.39), kind=kLoop, calls=%fused_computation.2 | loop fusion | flops 33554432 | bytes 41969664 | tf_op jit(solution)/shard_map/convert_element_type | solution.py:94
  125.4 3.2 %copy-done.2 = bf16[2048,2048]{0,1:T(8,128)(2,1)} copy-done((bf16[2048,2048]{0,1:T(8,128)(2,1)}, bf16[2048,2048]{0,1:T(8,128)(2,1)S(1)}, u32[]{:S(2)}) %copy-start.2) | copy-done | bytes 8388632
  128.7 3.6 %convolution_convert_fusion.6 = bf16[2048,256]{1,0:T(8,128)(2,1)} fusion(bf16[2048,2048]{0,1:T(8,128)(2,1)S(1)} %multiply_convert_fusion, bf16[2048,256]{1,0:T(8,128)(2,1)S(1)} %copy-done.19), kind=kOutput, calls=%fused_computation.29 | convolution fusion | flops 2148007936 | bytes 10485760 | tf_op jit(solution)/shard_map/nk,nl->kl/dot_general | solution.py:96
  132.2 7.8 %convolution_add_fusion.2 = f32[2048,256]{1,0:T(8,128)} fusion(bf16[256,256]{1,0:T(8,128)(2,1)S(1)} %copy-done.14, bf16[2048,2048]{0,1:T(8,128)(2,1)} %copy-done.2, bf16[1,1,2048,256]{3,2,1,0:T(8,128)(2,1)} %param.25, bf16[2048,512]{1,0:T(8,128)(2,1)S(1)} %copy-done.6), kind=kOutput, calls=%fused_computation.16 | convolution fusion | flops 2417491968 | bytes 12713984 | tf_op jit(solution)/shard_map/dot_general | solution.py:29
  140.0 3.3 %fusion.6 = bf16[2048,256]{1,0:T(8,128)(2,1)S(1)} fusion(bf16[256,256]{1,0:T(8,128)(2,1)S(1)} %copy-done.15, f32[2048,256]{1,0:T(8,128)} %convolution_add_fusion.4, f32[2048,256]{1,0:T(8,128)} %convolution_add_fusion.2), kind=kOutput, calls=%fused_computation.21 | convolution fusion | flops 273678336 | bytes 5373952 | tf_op jit(solution)/shard_map/dot_general | solution.py:29
  144.8 4.5 %fusion.20 = f32[16,256,4,128]{3,1,2,0:T(8,128)} fusion(bf16[16,128,256,1]{2,1,3,0:T(8,128)(2,1)S(1)} %bitcast.101, s32[1,1,16,4,128,128]{5,4,3,2,1,0:T(8,128)S(1)} %copy-done.1), kind=kOutput, calls=%fused_computation.41 | convolution fusion | flops 537919488 | bytes 13631488 | tf_op jit(solution)/shard_map/bkij,bil->bkjl/dot_general | solution.py:112
  149.3 9.0 %copy.21 = f32[64,128,256]{2,1,0:T(8,128)} copy(f32[64,128,256]{1,2,0:T(8,128)} %bitcast.97) | data formatting | bytes 16777216 | tf_op jit(solution)/shard_map/reshape | solution.py:119
  158.3 5.3 %broadcast_in_dim.25 = f32[80,128,256]{2,1,0:T(8,128)} broadcast(f32[]{:T(128)} %constant.5.clone.1), dimensions={} | broadcast | bytes 10485764 | tf_op jit(solution)/shard_map/broadcast_in_dim | solution.py:118
  163.6 19.5 %scatter_fusion = f32[80,128,256]{2,1,0:T(8,128)} fusion(f32[80,128,256]{2,1,0:T(8,128)} %broadcast_in_dim.25, s32[64]{0:T(128)S(1)} %reshape.95, f32[64,128,256]{2,1,0:T(8,128)} %copy.21), kind=kCustom, calls=%fused_computation.1 | custom fusion | flops 2097152 | bytes 25166080 | tf_op jit(solution)/shard_map/scatter-add | solution.py:118
  183.1 4.8 %convert.9 = bf16[80,128,256]{2,1,0:T(8,128)(2,1)S(1)} convert(f32[80,128,256]{2,1,0:T(8,128)} %scatter_fusion) | non-fusion elementwise | flops 2621440 | bytes 15728640 | tf_op jit(solution)/shard_map/convert.2
  190.1 4.2 %collective-permute-start.4 = (bf16[2048,256]{1,0:T(8,128)(2,1)}, bf16[2048,256]{1,0:T(8,128)(2,1)}, u32[]{:S(2)}, u32[]{:S(2)}) collective-permute-start(bf16[2048,256]{1,0:T(8,128)(2,1)} %bitcast.23), channel_id=1, source_target_pairs={{16,0},{32,16},{48,32},{64,48},{80,64},{96,80},{112,96},{17,1},{33... | collective-permute-start | bytes 3145736 | tf_op jit(solution)/shard_map/ppermute | solution.py:25
  197.5 5.2 %collective-permute-start.7 = (bf16[2048,256]{1,0:T(8,128)(2,1)}, bf16[2048,256]{1,0:T(8,128)(2,1)}, u32[]{:S(2)}, u32[]{:S(2)}) collective-permute-start(bf16[2048,256]{1,0:T(8,128)(2,1)} %bitcast.26), channel_id=1, source_target_pairs={{0,1},{1,2},{2,3},{3,4},{4,5},{5,6},{6,7},{7,8},{8,9},{9,10},{10,1... | collective-permute-start | bytes 3145736 | tf_op jit(solution)/shard_map/ppermute | solution.py:25
  204.5 8.9 %all-to-all-start.1 = ((bf16[128,16,256]{2,1,0:T(8,128)(2,1)}), bf16[128,16,256]{2,1,0:T(8,128)(2,1)S(1)}, u32[]{:S(2)}, u32[]{:S(2)}) async-start(bf16[128,16,256]{2,1,0:T(8,128)(2,1)} %bitcast.28), calls=%async_computation.1 | async-start | bytes 2097152 | tf_op jit(solution)/shard_map/all_to_all | solution.py:99
  215.2 3.8 %convolution_add_fusion.1 = f32[2048,256]{1,0:T(8,128)} fusion(f32[2048,256]{1,0:T(8,128)} %convolution_add_fusion.2, bf16[2048,256]{1,0:T(8,128)(2,1)} %copy-done.4, bf16[512,256]{1,0:T(8,128)(2,1)} %param.20), kind=kOutput, calls=%fused_computation.14 | convolution fusion | flops 268959744 | bytes 5373952 | tf_op jit(solution)/shard_map/dot_general | solution.py:29
  219.0 31.3 %all-to-all-done.1 = bf16[128,16,256]{2,1,0:T(8,128)(2,1)S(1)} async-done(((bf16[128,16,256]{2,1,0:T(8,128)(2,1)}), bf16[128,16,256]{2,1,0:T(8,128)(2,1)S(1)}, u32[]{:S(2)}, u32[]{:S(2)}) %all-to-all-start.1) | async-done | bytes 1048608 | tf_op jit(solution)/shard_map/all_to_all | solution.py:99
  250.3 3.8 %fusion.19 = bf16[2048,256]{1,0:T(8,128)(2,1)} fusion(f32[16,128,256]{2,1,0:T(8,128)S(1)} %slice.54, bf16[2048,256]{1,0:T(8,128)(2,1)} %collective-permute-done.7, bf16[2048,256]{1,0:T(8,128)(2,1)} %collective-permute-done.6, bf16[2048,256]{1,0:T(8,128)(2,1)} %collective-permute-done.5, bf16[2048,256]{1,0:T(8,128)(2,1)} %collective-permute-done.4), kind=kLoop, calls=%fused_computation.39 | loop fusion | flops 4718592 | bytes 7340032 | tf_op jit(solution)/shard_map/convert_element_type | solution.py:130
  254.1 4.6 %fusion.12 = bf16[1,1,2048,256]{3,2,1,0:T(8,128)(2,1)} fusion(f32[2048,256]{1,0:T(8,128)} %convolution_add_fusion.1, bf16[256,256]{1,0:T(8,128)(2,1)S(1)} %copy-done.11, bf16[2048,256]{1,0:T(8,128)(2,1)} %fusion.19, bf16[256,256]{1,0:T(8,128)(2,1)} %param.19, f32[2048,256]{1,0:T(8,128)} %copy-done.5), kind=kOutput, calls=%fused_computation.31 | convolution fusion | flops 542638080 | bytes 6553600 | tf_op jit(solution)/shard_map/dot_general | solution.py:29
  (70 shorter events, 26.7 us)
Async XLA Ops:
  0.6 63.6 %copy-start = (bf16[256,512]{1,0:T(8,128)(2,1)S(1)}, bf16[256,512]{1,0:T(8,128)(2,1)}, u32[]{:S(2)}) copy-start(bf16[256,512]{1,0:T(8,128)(2,1)} %param.23) | copy-start | bytes 786436
  2.3 3.3 %copy-start.5 = (f32[2048,256]{1,0:T(8,128)}, f32[2048,256]{1,0:T(8,128)S(1)}, u32[]{:S(2)}) copy-start(f32[2048,256]{1,0:T(8,128)S(1)} %fusion.28) | copy-start | bytes 6291460
  2.4 27.3 %copy-start.13 = (s32[128,1]{0,1:T(1,128)S(1)}, s32[128,1]{0,1:T(1,128)}, u32[]{:S(2)}) copy-start(s32[128,1]{0,1:T(1,128)} %param.17) | copy-start | bytes 1540
  2.4 27.4 %copy-start.12 = (s32[1,1,16,4]{2,3,1,0:T(4,128)S(1)}, s32[1,1,16,4]{2,3,1,0:T(4,128)}, u32[]{:S(2)}) copy-start(s32[1,1,16,4]{2,3,1,0:T(4,128)} %param.14) | copy-start | bytes 772
  2.4 27.9 %copy-start.3 = (bf16[1,1,2048,256]{3,2,1,0:T(8,128)(2,1)S(1)}, bf16[1,1,2048,256]{3,2,1,0:T(8,128)(2,1)}, u32[]{:S(2)}) copy-start(bf16[1,1,2048,256]{3,2,1,0:T(8,128)(2,1)} %param.13) | copy-start | bytes 3145732
  5.6 26.0 %copy-start.10 = (bf16[256,256]{1,0:T(8,128)(2,1)S(1)}, bf16[256,256]{1,0:T(8,128)(2,1)}, u32[]{:S(2)}) copy-start(bf16[256,256]{1,0:T(8,128)(2,1)} %param.24) | copy-start | bytes 393220
  5.6 61.9 %collective-permute-start = (bf16[2048,256]{1,0:T(8,128)(2,1)}, bf16[2048,256]{1,0:T(8,128)(2,1)}, u32[]{:S(2)}, u32[]{:S(2)}) collective-permute-start(bf16[2048,256]{1,0:T(8,128)(2,1)} %get-tuple-element.7), channel_id=1, source_target_pairs={{0,16},{16,32},{32,48},{48,64},{64,80},{80,96},{96,112},{1,17},{17... | collective-permute-start | bytes 3145736 | tf_op jit(solution)/shard_map/ppermute | solution.py:25
  10.7 59.1 %collective-permute-start.1 = (bf16[2048,256]{1,0:T(8,128)(2,1)}, bf16[2048,256]{1,0:T(8,128)(2,1)}, u32[]{:S(2)}, u32[]{:S(2)}) collective-permute-start(bf16[2048,256]{1,0:T(8,128)(2,1)} %get-tuple-element.7), channel_id=1, source_target_pairs={{16,0},{32,16},{48,32},{64,48},{80,64},{96,80},{112,96},{17,1},{33... | collective-permute-start | bytes 3145736 | tf_op jit(solution)/shard_map/ppermute | solution.py:25
  12.6 59.5 %collective-permute-start.2 = (bf16[2048,256]{1,0:T(8,128)(2,1)}, bf16[2048,256]{1,0:T(8,128)(2,1)}, u32[]{:S(2)}, u32[]{:S(2)}) collective-permute-start(bf16[2048,256]{1,0:T(8,128)(2,1)} %get-tuple-element.7), channel_id=1, source_target_pairs={{0,1},{1,2},{2,3},{3,4},{4,5},{5,6},{6,7},{7,8},{8,9},{9,10},{10,1... | collective-permute-start | bytes 3145736 | tf_op jit(solution)/shard_map/ppermute | solution.py:25
  16.8 57.6 %collective-permute-start.3 = (bf16[2048,256]{1,0:T(8,128)(2,1)}, bf16[2048,256]{1,0:T(8,128)(2,1)}, u32[]{:S(2)}, u32[]{:S(2)}) collective-permute-start(bf16[2048,256]{1,0:T(8,128)(2,1)} %get-tuple-element.7), channel_id=1, source_target_pairs={{1,0},{2,1},{3,2},{4,3},{5,4},{6,5},{7,6},{8,7},{9,8},{10,9},{11,1... | collective-permute-start | bytes 3145736 | tf_op jit(solution)/shard_map/ppermute | solution.py:25
  18.1 46.2 %all-to-all-start = ((bf16[128,16,256]{2,1,0:T(8,128)(2,1)}), bf16[128,16,256]{2,1,0:T(8,128)(2,1)}, u32[]{:S(2)}, u32[]{:S(2)}) async-start(bf16[128,16,256]{2,1,0:T(8,128)(2,1)} %bitcast.16), calls=%async_computation | async-start | bytes 2097152 | tf_op jit(solution)/shard_map/all_to_all | solution.py:74
  82.0 4.3 %copy-start.8 = (bf16[512,256]{1,0:T(8,128)(2,1)S(1)}, bf16[512,256]{1,0:T(8,128)(2,1)}, u32[]{:S(2)}) copy-start(bf16[512,256]{1,0:T(8,128)(2,1)} %param.20) | copy-start | bytes 786436
  86.3 1.8 copy-start.14
  90.6 4.6 %copy-start.18 = (bf16[2048,256]{1,0:T(8,128)(2,1)}, bf16[2048,256]{1,0:T(8,128)(2,1)S(1)}, u32[]{:S(2)}) copy-start(bf16[2048,256]{1,0:T(8,128)(2,1)S(1)} %convolution_convert_fusion.4) | copy-start | bytes 3145732
  95.2 5.1 %copy-start.7 = (bf16[2048,256]{1,0:T(8,128)(2,1)S(1)}, bf16[2048,256]{1,0:T(8,128)(2,1)}, u32[]{:S(2)}) copy-start(bf16[2048,256]{1,0:T(8,128)(2,1)} %convolution_convert_fusion.3) | copy-start | bytes 3145732
  100.2 5.6 %copy-start.6 = (bf16[2048,512]{1,0:T(8,128)(2,1)S(1)}, bf16[2048,512]{1,0:T(8,128)(2,1)}, u32[]{:S(2)}) copy-start(bf16[2048,512]{1,0:T(8,128)(2,1)} %convolution_convert_fusion) | copy-start | bytes 6291460
  115.4 13.2 %copy-start.19 = (bf16[2048,256]{1,0:T(8,128)(2,1)S(1)}, bf16[2048,256]{1,0:T(8,128)(2,1)}, u32[]{:S(2)}) copy-start(bf16[2048,256]{1,0:T(8,128)(2,1)} %copy-done.18) | copy-start | bytes 3145732
  125.4 3.2 %copy-start.2 = (bf16[2048,2048]{0,1:T(8,128)(2,1)}, bf16[2048,2048]{0,1:T(8,128)(2,1)S(1)}, u32[]{:S(2)}) copy-start(bf16[2048,2048]{0,1:T(8,128)(2,1)S(1)} %multiply_convert_fusion) | copy-start | bytes 25165828
  132.2 7.8 %copy-start.15 = (bf16[256,256]{1,0:T(8,128)(2,1)S(1)}, bf16[256,256]{1,0:T(8,128)(2,1)}, u32[]{:S(2)}) copy-start(bf16[256,256]{1,0:T(8,128)(2,1)} %param.21) | copy-start | bytes 393220
  140.0 4.3 %copy-start.9 = (bf16[512,256]{1,0:T(8,128)(2,1)S(1)}, bf16[512,256]{1,0:T(8,128)(2,1)}, u32[]{:S(2)}) copy-start(bf16[512,256]{1,0:T(8,128)(2,1)} %param.20) | copy-start | bytes 786436
  140.0 4.8 %copy-start.1 = (s32[1,1,16,4,128,128]{5,4,3,2,1,0:T(8,128)S(1)}, s32[1,1,16,4,128,128]{5,4,3,2,1,0:T(8,128)}, u32[]{:S(2)}) copy-start(s32[1,1,16,4,128,128]{5,4,3,2,1,0:T(8,128)} %param.15) | copy-start | bytes 12582916
  143.3 1.0 copy-start.4
  187.9 14.9 %copy-start.16 = (bf16[2048,256]{1,0:T(8,128)(2,1)S(1)}, bf16[2048,256]{1,0:T(8,128)(2,1)}, u32[]{:S(2)}) copy-start(bf16[2048,256]{1,0:T(8,128)(2,1)} %fusion.9) | copy-start | bytes 3145732
  187.9 14.9 %copy-start.17 = (bf16[2048,256]{1,0:T(8,128)(2,1)S(1)}, bf16[2048,256]{1,0:T(8,128)(2,1)}, u32[]{:S(2)}) copy-start(bf16[2048,256]{1,0:T(8,128)(2,1)} %convolution_convert_fusion.6) | copy-start | bytes 3145732
  190.1 60.2 %collective-permute-start.4 = (bf16[2048,256]{1,0:T(8,128)(2,1)}, bf16[2048,256]{1,0:T(8,128)(2,1)}, u32[]{:S(2)}, u32[]{:S(2)}) collective-permute-start(bf16[2048,256]{1,0:T(8,128)(2,1)} %bitcast.23), channel_id=1, source_target_pairs={{16,0},{32,16},{48,32},{64,48},{80,64},{96,80},{112,96},{17,1},{33... | collective-permute-start | bytes 3145736 | tf_op jit(solution)/shard_map/ppermute | solution.py:25
  194.3 56.0 %collective-permute-start.5 = (bf16[2048,256]{1,0:T(8,128)(2,1)}, bf16[2048,256]{1,0:T(8,128)(2,1)}, u32[]{:S(2)}, u32[]{:S(2)}) collective-permute-start(bf16[2048,256]{1,0:T(8,128)(2,1)} %bitcast.24), channel_id=1, source_target_pairs={{0,16},{16,32},{32,48},{48,64},{64,80},{80,96},{96,112},{1,17},{17... | collective-permute-start | bytes 3145736 | tf_op jit(solution)/shard_map/ppermute | solution.py:25
  196.2 54.1 %collective-permute-start.6 = (bf16[2048,256]{1,0:T(8,128)(2,1)}, bf16[2048,256]{1,0:T(8,128)(2,1)}, u32[]{:S(2)}, u32[]{:S(2)}) collective-permute-start(bf16[2048,256]{1,0:T(8,128)(2,1)} %bitcast.25), channel_id=1, source_target_pairs={{1,0},{2,1},{3,2},{4,3},{5,4},{6,5},{7,6},{8,7},{9,8},{10,9},{11,1... | collective-permute-start | bytes 3145736 | tf_op jit(solution)/shard_map/ppermute | solution.py:25
  197.5 52.8 %collective-permute-start.7 = (bf16[2048,256]{1,0:T(8,128)(2,1)}, bf16[2048,256]{1,0:T(8,128)(2,1)}, u32[]{:S(2)}, u32[]{:S(2)}) collective-permute-start(bf16[2048,256]{1,0:T(8,128)(2,1)} %bitcast.26), channel_id=1, source_target_pairs={{0,1},{1,2},{2,3},{3,4},{4,5},{5,6},{6,7},{7,8},{8,9},{9,10},{10,1... | collective-permute-start | bytes 3145736 | tf_op jit(solution)/shard_map/ppermute | solution.py:25
  204.5 45.8 %all-to-all-start.1 = ((bf16[128,16,256]{2,1,0:T(8,128)(2,1)}), bf16[128,16,256]{2,1,0:T(8,128)(2,1)S(1)}, u32[]{:S(2)}, u32[]{:S(2)}) async-start(bf16[128,16,256]{2,1,0:T(8,128)(2,1)} %bitcast.28), calls=%async_computation.1 | async-start | bytes 2097152 | tf_op jit(solution)/shard_map/all_to_all | solution.py:99
  219.0 35.1 %copy-start.11 = (bf16[256,256]{1,0:T(8,128)(2,1)S(1)}, bf16[256,256]{1,0:T(8,128)(2,1)}, u32[]{:S(2)}) copy-start(bf16[256,256]{1,0:T(8,128)(2,1)} %param.18) | copy-start | bytes 393220

commit v2 on v1

--- a/solution.py
+++ b/solution.py
@@ -23,6 +23,13 @@
     count = lax.axis_size(axis)
     leading, last = (max(0, -steps), min(count, count - steps))
     return lax.ppermute(value, axis, [(source, source + steps) for source in range(leading, last)])
+
+
+def exchange_slots(groups, inner, outer):
+    staged = jnp.swapaxes(groups, 0, 1)
+    staged = lax.all_to_all(staged, inner, split_axis=0, concat_axis=0, tiled=True)
+    staged = jnp.swapaxes(staged, 0, 1)
+    return lax.all_to_all(staged, outer, split_axis=0, concat_axis=0, tiled=True)
 
 
 def dense(left, right):
@@ -70,10 +77,8 @@
     queries = dense(updated, w_q).astype(jnp.bfloat16)
     own_tokens = tokens[0]
     slot_count = own_tokens.shape[0] // devices
-    token_groups = own_tokens.reshape(devices, slot_count, latent_width)
-    arrived_tokens = lax.all_to_all(
-        token_groups, ("px", "py"), split_axis=0, concat_axis=0, tiled=True
-    )
+    token_groups = own_tokens.reshape(rows_px, rows_py, slot_count, latent_width)
+    arrived_tokens = exchange_slots(token_groups, "py", "px")
     arrived_tokens = arrived_tokens.reshape(devices * slot_count, latent_width)
     arrived = dense(arrived_tokens, w_kv).astype(jnp.bfloat16)
     key_rows = arrived[:, :latent_width]
@@ -96,12 +101,8 @@
     grad_keys = jnp.einsum("nk,nl->kl", grad_score, queries, preferred_element_type=jnp.float32)
     grad_kv = jnp.concatenate([grad_keys, grad_vals], axis=1).astype(jnp.bfloat16)
     grad_slots = dense(grad_kv, w_kv.T).astype(jnp.bfloat16)
-    returned = lax.all_to_all(
-        grad_slots.reshape(devices, slot_count, latent_width),
-        ("px", "py"),
-        split_axis=0,
-        concat_axis=0,
-        tiled=True,
+    returned = exchange_slots(
+        grad_slots.reshape(rows_px, rows_py, slot_count, latent_width), "py", "px"
     )
     grad_tokens = returned.reshape(devices * slot_count, latent_width)
     grad_update = cotangent[0, 0].astype(jnp.float32) + dense(grad_query, w_q.T)

time: 261 us -> 281 us (1.077)
  starting transfers between devices: 45.6 us -> 53.8 us
  waiting for transfers between devices: 61.3 us -> 66.7 us
    all_to_all x2 -> x4, starting transfers between devices: 20.5 us -> 28 us  [the longest x2 15.5 us: exchange_slots(): lax.all_to_all(staged, inner, split_axis=0, concat_axis=0, tiled=True)]
    all_to_all x2 -> x4, waiting for transfers between devices: 61.3 us -> 66.6 us  [the longest x2 60.2 us: exchange_slots(): lax.all_to_all(staged, inner, split_axis=0, concat_axis=0, tiled=True)]
    all_to_all x0 -> x2, local copies, waits for them, and re-layouts: none -> 3.37 us  [exchange_slots(): lax.all_to_all(staged, inner, split_axis=0, concat_axis=0, tiled=True)]
    unnamed x45 -> x43, local copies, waits for them, and re-layouts: 12.2 us -> 8.88 us
    dot_general x1, matrix products: 3.55 us -> 6.81 us  [on_device(): jnp.einsum('nk,nl->kl', grad_score, queries, preferred_element_type=jnp.f...]
  transfers between devices with their start and end apart: 10 -> 12, of which waited for: 2 -> 3; matrix products, arithmetic and copies ran while one was open for 8% -> 17% of each run, Pallas kernels for 0% -> 0%
where the time goes in v2:
time: 281 us; the launch traced here: 280 us
  matrix products  71.6 us (25%)
  waiting for transfers between devices  66.7 us (24%)
  starting transfers between devices  53.8 us (19%)
  other arithmetic  45.9 us (16%)
  local copies, waits for them, and re-layouts  40.6 us (14%)
    all_to_all x2, waiting for transfers between devices, exchange_slots(): lax.all_to_all(staged, inner, split_axis=0, concat_axis=0, tiled=True)  60.2 us
    dot_general x13, matrix products, dense(): return jnp.dot(left, right, preferred_element_type=jnp.float32)  35.5 us
    ppermute x8, starting transfers between devices, passed_along(): lax.ppermute(value, axis, [(source, source + steps) for source in range(l...  25.8 us
    scatter-add x1, other arithmetic, on_device(): jax.ops.segment_sum(grad_parts.reshape(block_count * tile_count, blk_rows...  19.7 us
    all_to_all x2, starting transfers between devices, exchange_slots(): lax.all_to_all(staged, inner, split_axis=0, concat_axis=0, tiled=True)  15.5 us
    all_to_all x2, starting transfers between devices, exchange_slots(): lax.all_to_all(staged, outer, split_axis=0, concat_axis=0, tiled=True)  12.5 us
    convert_element_type x1, other arithmetic, on_device(): (probability * (grad_prob - spread) * score_scale).astype(jnp.bfloat16)  12.5 us
    dot_general x1, matrix products, on_device(): jnp.einsum('nl,kl->nk', grad_out, value_rows, preferred_element_type=jnp....  9.64 us
  transfers between devices with their start and end apart: 12, of which 3 were waited for; matrix products, arithmetic and copies ran while one was open for 17% of the time, Pallas kernels for 0%

profile of v2, /device:TPU:1, one launch (start us, length us, event | category | flops | bytes accessed | tf_op | source)
XLA Modules:
  0.0 279.5 jit_solution(8891144448037645208)
XLA Ops:
  2.4 3.2 %bitcast_dynamic-update-slice_fusion.4 = (bf16[5,2048,256]{2,1,0:T(8,128)(2,1)}, bf16[2048,256]{1,0:T(8,128)(2,1)}) fusion(bf16[256,256]{1,0:T(8,128)(2,1)} %param.19, f32[2048,256]{1,0:T(8,128)S(1)} %fusion.28), kind=kOutput, calls=%fused_computation.55 | convolution fusion | flops 271581184 | bytes 4325376 | tf_op jit(solution)/shard_map/dot_general | solution.py:36
  5.6 5.1 %collective-permute-start = (bf16[2048,256]{1,0:T(8,128)(2,1)}, bf16[2048,256]{1,0:T(8,128)(2,1)}, u32[]{:S(2)}, u32[]{:S(2)}) collective-permute-start(bf16[2048,256]{1,0:T(8,128)(2,1)} %get-tuple-element.7), channel_id=1, source_target_pairs={{0,16},{16,32},{32,48},{48,64},{64,80},{80,96},{96,112},{1,17},{17... | collective-permute-start | bytes 3145736 | tf_op jit(solution)/shard_map/ppermute | solution.py:25
  12.6 4.2 %collective-permute-start.2 = (bf16[2048,256]{1,0:T(8,128)(2,1)}, bf16[2048,256]{1,0:T(8,128)(2,1)}, u32[]{:S(2)}, u32[]{:S(2)}) collective-permute-start(bf16[2048,256]{1,0:T(8,128)(2,1)} %get-tuple-element.7), channel_id=1, source_target_pairs={{0,1},{1,2},{2,3},{3,4},{4,5},{5,6},{6,7},{7,8},{8,9},{9,10},{10,1... | collective-permute-start | bytes 3145736 | tf_op jit(solution)/shard_map/ppermute | solution.py:25
  19.1 7.2 %all-to-all-start = ((bf16[16,8,16,256]{3,2,1,0:T(8,128)(2,1)}), bf16[16,8,16,256]{3,2,1,0:T(8,128)(2,1)}, u32[]{:S(2)}, u32[]{:S(2)}) async-start(bf16[16,8,16,256]{3,2,1,0:T(8,128)(2,1)} %copy.28), calls=%async_computation | async-start | bytes 2097152 | tf_op jit(solution)/shard_map/all_to_all | solution.py:30
  29.7 29.8 %all-to-all-done = bf16[16,8,16,256]{3,2,1,0:T(8,128)(2,1)} async-done(((bf16[16,8,16,256]{3,2,1,0:T(8,128)(2,1)}), bf16[16,8,16,256]{3,2,1,0:T(8,128)(2,1)}, u32[]{:S(2)}, u32[]{:S(2)}) %all-to-all-start) | async-done | bytes 1048608 | tf_op jit(solution)/shard_map/all_to_all | solution.py:30
  59.5 2.3 copy.44
  61.8 6.7 %all-to-all-start.1 = ((bf16[8,16,16,256]{3,2,1,0:T(8,128)(2,1)}), bf16[8,16,16,256]{3,2,1,0:T(8,128)(2,1)}, u32[]{:S(2)}, u32[]{:S(2)}) async-start(bf16[8,16,16,256]{3,2,1,0:T(8,128)(2,1)} %bitcast.110), calls=%async_computation.1 | async-start | bytes 2097152 | tf_op jit(solution)/shard_map/all_to_all | solution.py:32
  77.5 5.3 %gather_fusion = bf16[64,128,256]{2,1,0:T(8,128)(2,1)} fusion(bf16[80,128,256]{2,1,0:T(8,128)(2,1)} %bitcast.115, s32[1024]{0:T(1024)S(1)} %pad_clamp_fusion), kind=kCustom, calls=%fused_computation | custom fusion | bytes 8388864 | tf_op jit(solution)/shard_map/gather | solution.py:71
  82.9 4.3 %bitcast_convert_fusion = bf16[16,256,128]{1,2,0:T(8,128)(2,1)S(1)} fusion(bf16[16,4,128,256]{3,2,1,0:T(8,128)(2,1)} %bitcast.109, s32[1,1,16,4,128,128]{5,4,3,2,1,0:T(8,128)} %param.15), kind=kOutput, calls=%fused_computation.40 | convolution fusion | flops 538443776 | bytes 9437184 | tf_op jit(solution)/shard_map/bkij,bkjl->bil/dot_general | solution.py:72
  88.9 3.5 %convolution_convert_fusion.4 = bf16[2048,256]{1,0:T(8,128)(2,1)} fusion(bf16[256,256]{1,0:T(8,128)(2,1)} %param.22, bf16[256,256]{1,0:T(8,128)(2,1)} %param.21, f32[2048,256]{1,0:T(8,128)} %convolution_add_fusion.4, bf16[1,1,2048,256]{3,2,1,0:T(8,128)(2,1)S(1)} %copy-done.2), kind=kOutput, calls=%fused_computation.26 | convolution fusion | flops 541589504 | bytes 4456448 | tf_op jit(solution)/shard_map/dot_general | solution.py:36
  94.4 3.6 %fusion = (f32[2048]{0:T(1024)S(1)}, f32[2048,2048]{0,1:T(8,128)S(1)}) fusion(pred[2048]{0:T(1024)(128)(4,1)S(1)} %lt.39, bf16[2048,256]{1,0:T(8,128)(2,1)} %convolution_convert_fusion.4, bf16[2048,512]{1,0:T(8,128)(2,1)S(1)} %convolution_convert_fusion), kind=kOutput, calls=%fused_computation.6 | convolution fusion | flops 2160064512 | bytes 18884608 | tf_op jit(solution)/shard_map/nl,kl->nk/dot_general | solution.py:88
  98.0 5.0 %fusion.2 = f32[2048]{0:T(1024)S(1)} fusion(f32[2048,2048]{0,1:T(8,128)S(1)} %get-tuple-element.9, f32[2048]{0:T(1024)S(1)} %get-tuple-element.8, pred[2048]{0:T(1024)(128)(4,1)S(1)} %lt.39), kind=kLoop, calls=%fused_computation.8 | loop fusion | flops 16775168 | bytes 16795648 | tf_op jit(solution)/shard_map/reduce_sum | solution.py:93
  103.1 7.1 %fusion.9 = bf16[2048,256]{0,1:T(8,128)(2,1)} fusion(bf16[2048,256]{1,0:T(8,128)(2,1)S(1)} %copy-done.7, f32[2048,2048]{0,1:T(8,128)S(1)} %get-tuple-element.9, f32[2048]{0:T(1024)S(1)} %fusion.2, f32[2048]{0:T(1024)S(1)} %get-tuple-element.8, pred[2048]{0:T(1024)(128)(4,1)S(1)} %lt.39), kind=kOutput, calls=%fused_computation.28 | convolution fusion | flops 2168979456 | bytes 18892800 | tf_op jit(solution)/shard_map/nk,nl->kl/dot_general | solution.py:97
  110.1 9.6 %multiply_reduce_fusion = (f32[2048]{0:T(1024)S(1)}, f32[2048,2048]{0,1:T(8,128)}) fusion(f32[2048]{0:T(1024)S(1)} %fusion.2, f32[2048]{0:T(1024)S(1)} %get-tuple-element.8, f32[2048,2048]{0,1:T(8,128)S(1)} %get-tuple-element.9, pred[2048]{0:T(1024)(128)(4,1)S(1)} %lt.39, bf16[2048,256]{1,0:T(8,128)(2,1)} %convolution_convert_fusion.3, ...), kind=kOutput, calls=%fused_computation.3 | convolution fusion | flops 2172647424 | bytes 35678208 | tf_op jit(solution)/shard_map/nl,kl->nk/dot_general | solution.py:96
  119.8 12.5 %multiply_convert_fusion = bf16[2048,2048]{0,1:T(8,128)(2,1)} fusion(f32[2048,2048]{0,1:T(8,128)} %get-tuple-element.11, f32[2048]{0:T(1024)S(1)} %get-tuple-element.10, f32[2048]{0:T(1024)S(1)} %fusion.2, f32[2048]{0:T(1024)S(1)} %get-tuple-element.8, f32[2048,2048]{0,1:T(8,128)S(1)} %get-tuple-element.9, pred[2048]{0:T(1024)(128)(4,1)S(1)} %lt.39), kind=kLoop, calls=%fused_computation.2 | loop fusion | flops 33554432 | bytes 41969664 | tf_op jit(solution)/shard_map/convert_element_type | solution.py:99
  132.3 6.8 %convolution_convert_fusion.6 = bf16[2048,256]{0,1:T(8,128)(2,1)} fusion(bf16[2048,2048]{0,1:T(8,128)(2,1)} %multiply_convert_fusion, bf16[2048,256]{1,0:T(8,128)(2,1)S(1)} %copy-done.18), kind=kOutput, calls=%fused_computation.29 | convolution fusion | flops 2148007936 | bytes 10485760 | tf_op jit(solution)/shard_map/nk,nl->kl/dot_general | solution.py:101
  139.1 7.8 %convolution_add_fusion.2 = f32[2048,256]{1,0:T(8,128)} fusion(bf16[256,256]{1,0:T(8,128)(2,1)S(1)} %copy-done.14, bf16[2048,2048]{0,1:T(8,128)(2,1)} %multiply_convert_fusion, bf16[1,1,2048,256]{3,2,1,0:T(8,128)(2,1)} %param.25, bf16[2048,512]{1,0:T(8,128)(2,1)S(1)} %convolution_convert_fusion), kind=kOutput, calls=%fused_computation.16 | convolution fusion | flops 2417491968 | bytes 12713984 | tf_op jit(solution)/shard_map/dot_general | solution.py:36
  146.9 3.3 %fusion.6 = bf16[2048,256]{1,0:T(8,128)(2,1)S(1)} fusion(bf16[256,256]{1,0:T(8,128)(2,1)S(1)} %copy-done.15, f32[2048,256]{1,0:T(8,128)} %convolution_add_fusion.4, f32[2048,256]{1,0:T(8,128)} %convolution_add_fusion.2), kind=kOutput, calls=%fused_computation.21 | convolution fusion | flops 273678336 | bytes 5373952 | tf_op jit(solution)/shard_map/dot_general | solution.py:36
  151.6 4.6 %fusion.20 = f32[16,256,4,128]{3,1,2,0:T(8,128)} fusion(bf16[16,128,256,1]{2,1,3,0:T(8,128)(2,1)S(1)} %bitcast.114, s32[1,1,16,4,128,128]{5,4,3,2,1,0:T(8,128)S(1)} %copy-done.1), kind=kOutput, calls=%fused_computation.41 | convolution fusion | flops 537919488 | bytes 13631488 | tf_op jit(solution)/shard_map/bkij,bil->bkjl/dot_general | solution.py:113
  156.2 9.0 %copy.32 = f32[64,128,256]{2,1,0:T(8,128)} copy(f32[64,128,256]{1,2,0:T(8,128)} %bitcast.108) | data formatting | bytes 16777216 | tf_op jit(solution)/shard_map/reshape | solution.py:120
  165.2 5.3 %broadcast_in_dim.25 = f32[80,128,256]{2,1,0:T(8,128)} broadcast(f32[]{:T(128)} %constant.5.clone.1), dimensions={} | broadcast | bytes 10485764 | tf_op jit(solution)/shard_map/broadcast_in_dim | solution.py:119
  170.5 19.7 %scatter_fusion = f32[80,128,256]{2,1,0:T(8,128)} fusion(f32[80,128,256]{2,1,0:T(8,128)} %broadcast_in_dim.25, s32[64]{0:T(128)S(1)} %reshape.95, f32[64,128,256]{2,1,0:T(8,128)} %copy.32), kind=kCustom, calls=%fused_computation.1 | custom fusion | flops 2097152 | bytes 25166080 | tf_op jit(solution)/shard_map/scatter-add | solution.py:119
  190.2 4.8 %convert.9 = bf16[80,128,256]{2,1,0:T(8,128)(2,1)S(1)} convert(f32[80,128,256]{2,1,0:T(8,128)} %scatter_fusion) | non-fusion elementwise | flops 2621440 | bytes 15728640 | tf_op jit(solution)/shard_map/convert.2
  199.1 3.6 %collective-permute-start.5 = (bf16[2048,256]{1,0:T(8,128)(2,1)}, bf16[2048,256]{1,0:T(8,128)(2,1)}, u32[]{:S(2)}, u32[]{:S(2)}) collective-permute-start(bf16[2048,256]{1,0:T(8,128)(2,1)} %bitcast.26), channel_id=1, source_target_pairs={{0,16},{16,32},{32,48},{48,64},{64,80},{80,96},{96,112},{1,17},{17... | collective-permute-start | bytes 3145736 | tf_op jit(solution)/shard_map/ppermute | solution.py:25
  204.0 6.5 %collective-permute-start.7 = (bf16[2048,256]{1,0:T(8,128)(2,1)}, bf16[2048,256]{1,0:T(8,128)(2,1)}, u32[]{:S(2)}, u32[]{:S(2)}) collective-permute-start(bf16[2048,256]{1,0:T(8,128)(2,1)} %bitcast.28), channel_id=1, source_target_pairs={{0,1},{1,2},{2,3},{3,4},{4,5},{5,6},{6,7},{7,8},{8,9},{9,10},{10,1... | collective-permute-start | bytes 3145736 | tf_op jit(solution)/shard_map/ppermute | solution.py:25
  212.3 8.4 %all-to-all-start.2 = ((bf16[16,8,16,256]{3,2,1,0:T(8,128)(2,1)}), bf16[16,8,16,256]{3,2,1,0:T(8,128)(2,1)S(1)}, u32[]{:S(2)}, u32[]{:S(2)}) async-start(bf16[16,8,16,256]{3,2,1,0:T(8,128)(2,1)} %bitcast.106), calls=%async_computation.2 | async-start | bytes 2097152 | tf_op jit(solution)/shard_map/all_to_all | solution.py:30
  222.5 3.8 %convolution_add_fusion.1 = f32[2048,256]{1,0:T(8,128)} fusion(f32[2048,256]{1,0:T(8,128)} %convolution_add_fusion.2, bf16[2048,256]{1,0:T(8,128)(2,1)} %copy-done.3, bf16[512,256]{1,0:T(8,128)(2,1)} %param.20), kind=kOutput, calls=%fused_computation.14 | convolution fusion | flops 268959744 | bytes 5373952 | tf_op jit(solution)/shard_map/dot_general | solution.py:36
  226.3 30.4 %all-to-all-done.2 = bf16[16,8,16,256]{3,2,1,0:T(8,128)(2,1)S(1)} async-done(((bf16[16,8,16,256]{3,2,1,0:T(8,128)(2,1)}), bf16[16,8,16,256]{3,2,1,0:T(8,128)(2,1)S(1)}, u32[]{:S(2)}, u32[]{:S(2)}) %all-to-all-start.2) | async-done | bytes 1048608 | tf_op jit(solution)/shard_map/all_to_all | solution.py:30
  257.7 5.9 %all-to-all-start.3 = ((bf16[8,16,16,256]{3,2,1,0:T(8,128)(2,1)}), bf16[8,16,16,256]{3,2,1,0:T(8,128)(2,1)S(1)}, u32[]{:S(2)}, u32[]{:S(2)}) async-start(bf16[8,16,16,256]{3,2,1,0:T(8,128)(2,1)} %bitcast.112), calls=%async_computation.3 | async-start | bytes 2097152 | tf_op jit(solution)/shard_map/all_to_all | solution.py:32
  263.6 3.8 %fusion.19 = bf16[2048,256]{1,0:T(8,128)(2,1)} fusion(f32[16,128,256]{2,1,0:T(8,128)S(1)} %slice.54, bf16[2048,256]{1,0:T(8,128)(2,1)} %collective-permute-done.7, bf16[2048,256]{1,0:T(8,128)(2,1)} %collective-permute-done.6, bf16[2048,256]{1,0:T(8,128)(2,1)} %collective-permute-done.5, bf16[2048,256]{1,0:T(8,128)(2,1)} %collective-permute-done.4), kind=kLoop, calls=%fused_computation.39 | loop fusion | flops 4718592 | bytes 7340032 | tf_op jit(solution)/shard_map/convert_element_type | solution.py:131
  267.5 4.6 %fusion.12 = bf16[1,1,2048,256]{3,2,1,0:T(8,128)(2,1)} fusion(f32[2048,256]{1,0:T(8,128)} %convolution_add_fusion.1, bf16[256,256]{1,0:T(8,128)(2,1)S(1)} %copy-done.11, bf16[2048,256]{1,0:T(8,128)(2,1)} %fusion.19, bf16[256,256]{1,0:T(8,128)(2,1)} %param.19, f32[2048,256]{1,0:T(8,128)} %copy-done.4), kind=kOutput, calls=%fused_computation.31 | convolution fusion | flops 542638080 | bytes 6553600 | tf_op jit(solution)/shard_map/dot_general | solution.py:36
  272.1 6.5 %all-to-all-done.3 = bf16[8,16,16,256]{3,2,1,0:T(8,128)(2,1)S(1)} async-done(((bf16[8,16,16,256]{3,2,1,0:T(8,128)(2,1)}), bf16[8,16,16,256]{3,2,1,0:T(8,128)(2,1)S(1)}, u32[]{:S(2)}, u32[]{:S(2)}) %all-to-all-start.3) | async-done | bytes 1048608 | tf_op jit(solution)/shard_map/all_to_all | solution.py:32
  (76 shorter events, 34.5 us)
Async XLA Ops:
  0.6 91.8 %copy-start = (bf16[256,512]{1,0:T(8,128)(2,1)S(1)}, bf16[256,512]{1,0:T(8,128)(2,1)}, u32[]{:S(2)}) copy-start(bf16[256,512]{1,0:T(8,128)(2,1)} %param.23) | copy-start | bytes 786436
  2.3 3.2 %copy-start.4 = (f32[2048,256]{1,0:T(8,128)}, f32[2048,256]{1,0:T(8,128)S(1)}, u32[]{:S(2)}) copy-start(f32[2048,256]{1,0:T(8,128)S(1)} %fusion.28) | copy-start | bytes 6291460
  2.4 15.7 %copy-start.5 = (bf16[1,2048,256]{2,1,0:T(8,128)(2,1)S(1)}, bf16[1,2048,256]{2,1,0:T(8,128)(2,1)}, u32[]{:S(2)}) copy-start(bf16[1,2048,256]{2,1,0:T(8,128)(2,1)} %param.16) | copy-start | bytes 3145732
  5.6 20.7 %copy-start.12 = (s32[1,1,16,4]{2,3,1,0:T(4,128)S(1)}, s32[1,1,16,4]{2,3,1,0:T(4,128)}, u32[]{:S(2)}) copy-start(s32[1,1,16,4]{2,3,1,0:T(4,128)} %param.14) | copy-start | bytes 772
  5.6 20.9 %copy-start.6 = (bf16[1,1,2048,256]{3,2,1,0:T(8,128)(2,1)S(1)}, bf16[1,1,2048,256]{3,2,1,0:T(8,128)(2,1)}, u32[]{:S(2)}) copy-start(bf16[1,1,2048,256]{3,2,1,0:T(8,128)(2,1)} %param.25) | copy-start | bytes 3145732
  5.6 20.9 %copy-start.10 = (bf16[256,256]{1,0:T(8,128)(2,1)S(1)}, bf16[256,256]{1,0:T(8,128)(2,1)}, u32[]{:S(2)}) copy-start(bf16[256,256]{1,0:T(8,128)(2,1)} %param.24) | copy-start | bytes 393220
  5.6 22.4 %copy-start.13 = (s32[128,1]{0,1:T(1,128)S(1)}, s32[128,1]{0,1:T(1,128)}, u32[]{:S(2)}) copy-start(s32[128,1]{0,1:T(1,128)} %param.17) | copy-start | bytes 1540
  5.6 22.5 %copy-start.2 = (bf16[1,1,2048,256]{3,2,1,0:T(8,128)(2,1)S(1)}, bf16[1,1,2048,256]{3,2,1,0:T(8,128)(2,1)}, u32[]{:S(2)}) copy-start(bf16[1,1,2048,256]{3,2,1,0:T(8,128)(2,1)} %param.13) | copy-start | bytes 3145732
  5.6 62.8 %collective-permute-start = (bf16[2048,256]{1,0:T(8,128)(2,1)}, bf16[2048,256]{1,0:T(8,128)(2,1)}, u32[]{:S(2)}, u32[]{:S(2)}) collective-permute-start(bf16[2048,256]{1,0:T(8,128)(2,1)} %get-tuple-element.7), channel_id=1, source_target_pairs={{0,16},{16,32},{32,48},{48,64},{64,80},{80,96},{96,112},{1,17},{17... | collective-permute-start | bytes 3145736 | tf_op jit(solution)/shard_map/ppermute | solution.py:25
  10.7 60.0 %collective-permute-start.1 = (bf16[2048,256]{1,0:T(8,128)(2,1)}, bf16[2048,256]{1,0:T(8,128)(2,1)}, u32[]{:S(2)}, u32[]{:S(2)}) collective-permute-start(bf16[2048,256]{1,0:T(8,128)(2,1)} %get-tuple-element.7), channel_id=1, source_target_pairs={{16,0},{32,16},{48,32},{64,48},{80,64},{96,80},{112,96},{17,1},{33... | collective-permute-start | bytes 3145736 | tf_op jit(solution)/shard_map/ppermute | solution.py:25
  12.6 60.4 %collective-permute-start.2 = (bf16[2048,256]{1,0:T(8,128)(2,1)}, bf16[2048,256]{1,0:T(8,128)(2,1)}, u32[]{:S(2)}, u32[]{:S(2)}) collective-permute-start(bf16[2048,256]{1,0:T(8,128)(2,1)} %get-tuple-element.7), channel_id=1, source_target_pairs={{0,1},{1,2},{2,3},{3,4},{4,5},{5,6},{6,7},{7,8},{8,9},{9,10},{10,1... | collective-permute-start | bytes 3145736 | tf_op jit(solution)/shard_map/ppermute | solution.py:25
  16.8 58.5 %collective-permute-start.3 = (bf16[2048,256]{1,0:T(8,128)(2,1)}, bf16[2048,256]{1,0:T(8,128)(2,1)}, u32[]{:S(2)}, u32[]{:S(2)}) collective-permute-start(bf16[2048,256]{1,0:T(8,128)(2,1)} %get-tuple-element.7), channel_id=1, source_target_pairs={{1,0},{2,1},{3,2},{4,3},{5,4},{6,5},{7,6},{8,7},{9,8},{10,9},{11,1... | collective-permute-start | bytes 3145736 | tf_op jit(solution)/shard_map/ppermute | solution.py:25
  19.1 40.3 %all-to-all-start = ((bf16[16,8,16,256]{3,2,1,0:T(8,128)(2,1)}), bf16[16,8,16,256]{3,2,1,0:T(8,128)(2,1)}, u32[]{:S(2)}, u32[]{:S(2)}) async-start(bf16[16,8,16,256]{3,2,1,0:T(8,128)(2,1)} %copy.28), calls=%async_computation | async-start | bytes 2097152 | tf_op jit(solution)/shard_map/all_to_all | solution.py:30
  61.8 30.7 %all-to-all-start.1 = ((bf16[8,16,16,256]{3,2,1,0:T(8,128)(2,1)}), bf16[8,16,16,256]{3,2,1,0:T(8,128)(2,1)}, u32[]{:S(2)}, u32[]{:S(2)}) async-start(bf16[8,16,16,256]{3,2,1,0:T(8,128)(2,1)} %bitcast.110), calls=%async_computation.1 | async-start | bytes 2097152 | tf_op jit(solution)/shard_map/all_to_all | solution.py:32
  82.9 4.3 %copy-start.8 = (bf16[512,256]{1,0:T(8,128)(2,1)S(1)}, bf16[512,256]{1,0:T(8,128)(2,1)}, u32[]{:S(2)}) copy-start(bf16[512,256]{1,0:T(8,128)(2,1)} %param.20) | copy-start | bytes 786436
  98.0 5.1 %copy-start.7 = (bf16[2048,256]{1,0:T(8,128)(2,1)S(1)}, bf16[2048,256]{1,0:T(8,128)(2,1)}, u32[]{:S(2)}) copy-start(bf16[2048,256]{1,0:T(8,128)(2,1)} %convolution_convert_fusion.3) | copy-start | bytes 3145732
  119.8 12.5 %copy-start.18 = (bf16[2048,256]{1,0:T(8,128)(2,1)S(1)}, bf16[2048,256]{1,0:T(8,128)(2,1)}, u32[]{:S(2)}) copy-start(bf16[2048,256]{1,0:T(8,128)(2,1)} %convolution_convert_fusion.4) | copy-start | bytes 3145732
  132.3 6.8 %copy-start.14 = (bf16[256,256]{1,0:T(8,128)(2,1)S(1)}, bf16[256,256]{1,0:T(8,128)(2,1)}, u32[]{:S(2)}) copy-start(bf16[256,256]{1,0:T(8,128)(2,1)} %param.22) | copy-start | bytes 393220
  139.1 7.8 %copy-start.15 = (bf16[256,256]{1,0:T(8,128)(2,1)S(1)}, bf16[256,256]{1,0:T(8,128)(2,1)}, u32[]{:S(2)}) copy-start(bf16[256,256]{1,0:T(8,128)(2,1)} %param.21) | copy-start | bytes 393220
  146.9 4.3 %copy-start.9 = (bf16[512,256]{1,0:T(8,128)(2,1)S(1)}, bf16[512,256]{1,0:T(8,128)(2,1)}, u32[]{:S(2)}) copy-start(bf16[512,256]{1,0:T(8,128)(2,1)} %param.20) | copy-start | bytes 786436
  146.9 4.8 %copy-start.1 = (s32[1,1,16,4,128,128]{5,4,3,2,1,0:T(8,128)S(1)}, s32[1,1,16,4,128,128]{5,4,3,2,1,0:T(8,128)}, u32[]{:S(2)}) copy-start(s32[1,1,16,4,128,128]{5,4,3,2,1,0:T(8,128)} %param.15) | copy-start | bytes 12582916
  150.2 1.0 copy-start.3
  195.0 15.5 %copy-start.16 = (bf16[2048,256]{0,1:T(8,128)(2,1)S(1)}, bf16[2048,256]{0,1:T(8,128)(2,1)}, u32[]{:S(2)}) copy-start(bf16[2048,256]{0,1:T(8,128)(2,1)} %fusion.9) | copy-start | bytes 3145732
  195.0 15.5 %copy-start.17 = (bf16[2048,256]{0,1:T(8,128)(2,1)S(1)}, bf16[2048,256]{0,1:T(8,128)(2,1)}, u32[]{:S(2)}) copy-start(bf16[2048,256]{0,1:T(8,128)(2,1)} %convolution_convert_fusion.6) | copy-start | bytes 3145732
  197.1 66.5 %collective-permute-start.4 = (bf16[2048,256]{1,0:T(8,128)(2,1)}, bf16[2048,256]{1,0:T(8,128)(2,1)}, u32[]{:S(2)}, u32[]{:S(2)}) collective-permute-start(bf16[2048,256]{1,0:T(8,128)(2,1)} %bitcast.25), channel_id=1, source_target_pairs={{16,0},{32,16},{48,32},{64,48},{80,64},{96,80},{112,96},{17,1},{33... | collective-permute-start | bytes 3145736 | tf_op jit(solution)/shard_map/ppermute | solution.py:25
  199.1 64.5 %collective-permute-start.5 = (bf16[2048,256]{1,0:T(8,128)(2,1)}, bf16[2048,256]{1,0:T(8,128)(2,1)}, u32[]{:S(2)}, u32[]{:S(2)}) collective-permute-start(bf16[2048,256]{1,0:T(8,128)(2,1)} %bitcast.26), channel_id=1, source_target_pairs={{0,16},{16,32},{32,48},{48,64},{64,80},{80,96},{96,112},{1,17},{17... | collective-permute-start | bytes 3145736 | tf_op jit(solution)/shard_map/ppermute | solution.py:25
  202.7 60.9 %collective-permute-start.6 = (bf16[2048,256]{1,0:T(8,128)(2,1)}, bf16[2048,256]{1,0:T(8,128)(2,1)}, u32[]{:S(2)}, u32[]{:S(2)}) collective-permute-start(bf16[2048,256]{1,0:T(8,128)(2,1)} %bitcast.27), channel_id=1, source_target_pairs={{1,0},{2,1},{3,2},{4,3},{5,4},{6,5},{7,6},{8,7},{9,8},{10,9},{11,1... | collective-permute-start | bytes 3145736 | tf_op jit(solution)/shard_map/ppermute | solution.py:25
  204.0 59.6 %collective-permute-start.7 = (bf16[2048,256]{1,0:T(8,128)(2,1)}, bf16[2048,256]{1,0:T(8,128)(2,1)}, u32[]{:S(2)}, u32[]{:S(2)}) collective-permute-start(bf16[2048,256]{1,0:T(8,128)(2,1)} %bitcast.28), channel_id=1, source_target_pairs={{0,1},{1,2},{2,3},{3,4},{4,5},{5,6},{6,7},{7,8},{8,9},{9,10},{10,1... | collective-permute-start | bytes 3145736 | tf_op jit(solution)/shard_map/ppermute | solution.py:25
  212.3 44.3 %all-to-all-start.2 = ((bf16[16,8,16,256]{3,2,1,0:T(8,128)(2,1)}), bf16[16,8,16,256]{3,2,1,0:T(8,128)(2,1)S(1)}, u32[]{:S(2)}, u32[]{:S(2)}) async-start(bf16[16,8,16,256]{3,2,1,0:T(8,128)(2,1)} %bitcast.106), calls=%async_computation.2 | async-start | bytes 2097152 | tf_op jit(solution)/shard_map/all_to_all | solution.py:30
  257.7 20.8 %all-to-all-start.3 = ((bf16[8,16,16,256]{3,2,1,0:T(8,128)(2,1)}), bf16[8,16,16,256]{3,2,1,0:T(8,128)(2,1)S(1)}, u32[]{:S(2)}, u32[]{:S(2)}) async-start(bf16[8,16,16,256]{3,2,1,0:T(8,128)(2,1)} %bitcast.112), calls=%async_computation.3 | async-start | bytes 2097152 | tf_op jit(solution)/shard_map/all_to_all | solution.py:32
  263.6 3.9 %copy-start.11 = (bf16[256,256]{1,0:T(8,128)(2,1)S(1)}, bf16[256,256]{1,0:T(8,128)(2,1)}, u32[]{:S(2)}) copy-start(bf16[256,256]{1,0:T(8,128)(2,1)} %param.18) | copy-start | bytes 393220

commit v3 on v1

--- a/solution.py
+++ b/solution.py
@@ -3,6 +3,8 @@
 import jax
 import jax.numpy as jnp
 from jax import lax
+from jax.experimental import pallas as pl
+from jax.experimental.pallas import tpu as pltpu
 from jax.sharding import PartitionSpec as P
 
 
@@ -23,6 +25,89 @@
     count = lax.axis_size(axis)
     leading, last = (max(0, -steps), min(count, count - steps))
     return lax.ppermute(value, axis, [(source, source + steps) for source in range(leading, last)])
+
+
+def gather_kernel(src_ids, mask_ref, own, up, down, left, right, out_ref):
+    b = pl.program_id(0)
+    tiles = mask_ref.shape[1]
+    per_side = own.shape[0]
+    total = jnp.zeros(out_ref.shape, jnp.float32)
+    for k in range(tiles):
+        picked = src_ids[b * tiles + k]
+        side = picked // per_side
+        block = picked % per_side
+        bits = mask_ref[0, k].astype(jnp.float32).astype(jnp.bfloat16)
+        rows = own[block]
+        for index, ref in enumerate((up, down, left, right)):
+            rows = jnp.where(side == index + 1, ref[block], rows)
+        total = total + jnp.dot(bits, rows, preferred_element_type=jnp.float32)
+    out_ref[...] = total.astype(out_ref.dtype)
+
+
+def tile_gather(src_ids, tile_mask, sources):
+    blocks, tiles, blk, _ = tile_mask.shape
+    width = sources[0].shape[-1]
+    whole = pl.BlockSpec((blocks, blk, width), lambda b, ids: (0, 0, 0))
+    return pl.pallas_call(
+        gather_kernel,
+        grid_spec=pltpu.PrefetchScalarGridSpec(
+            num_scalar_prefetch=1,
+            grid=(blocks,),
+            in_specs=[pl.BlockSpec((1, tiles, blk, blk), lambda b, ids: (b, 0, 0, 0))]
+            + [whole] * len(sources),
+            out_specs=pl.BlockSpec((blk, width), lambda b, ids: (b, 0)),
+        ),
+        out_shape=jax.ShapeDtypeStruct((blocks * blk, width), jnp.bfloat16),
+    )(src_ids, tile_mask, *sources)
+
+
+def scatter_kernel(src_ids, mask_ref, grad_ref, own_ref, out_ref, total):
+    b = pl.program_id(0)
+    tiles = mask_ref.shape[1]
+    per_side = own_ref.shape[0]
+
+    @pl.when(b == 0)
+    def _():
+        total[...] = jnp.zeros(total.shape, jnp.float32)
+
+    grad_rows = grad_ref[...]
+    for k in range(tiles):
+        picked = src_ids[b * tiles + k]
+        bits = mask_ref[0, k].astype(jnp.float32).T.astype(jnp.bfloat16)
+        total[picked] += jnp.dot(bits, grad_rows, preferred_element_type=jnp.float32)
+
+    @pl.when(b == pl.num_programs(0) - 1)
+    def _():
+        own_ref[...] = total[0:per_side]
+        for side in range(out_ref.shape[0]):
+            start = (side + 1) * per_side
+            out_ref[side] = total[start : start + per_side].astype(out_ref.dtype)
+
+
+def tile_scatter(src_ids, tile_mask, grad_agg, sides):
+    blocks, tiles, blk, _ = tile_mask.shape
+    width = grad_agg.shape[-1]
+    return pl.pallas_call(
+        scatter_kernel,
+        grid_spec=pltpu.PrefetchScalarGridSpec(
+            num_scalar_prefetch=1,
+            grid=(blocks,),
+            in_specs=[
+                pl.BlockSpec((1, tiles, blk, blk), lambda b, ids: (b, 0, 0, 0)),
+                pl.BlockSpec((blk, width), lambda b, ids: (b, 0)),
+            ],
+            out_specs=[
+                pl.BlockSpec((blocks, blk, width), lambda b, ids: (0, 0, 0)),
+                pl.BlockSpec((sides - 1, blocks, blk, width), lambda b, ids: (0, 0, 0, 0)),
+            ],
+            scratch_shapes=[pltpu.VMEM((sides * blocks, blk, width), jnp.float32)],
+        ),
+        out_shape=(
+            jax.ShapeDtypeStruct((blocks, blk, width), jnp.float32),
+            jax.ShapeDtypeStruct((sides - 1, blocks, blk, width), jnp.bfloat16),
+        ),
+        compiler_params=pltpu.CompilerParams(dimension_semantics=("arbitrary",)),
+    )(src_ids, tile_mask, grad_agg)
 
 
 def dense(left, right):
@@ -50,20 +135,19 @@
     pre_act = dense(latent, w_e1)
     activation = jax.nn.silu(pre_act).astype(jnp.bfloat16)
     message = dense(activation, w_e2).astype(jnp.bfloat16)
-    sources = jnp.stack(
-        [
-            message,
-            passed_along(message, "px", 1),
-            passed_along(message, "px", -1),
-            passed_along(message, "py", 1),
-            passed_along(message, "py", -1),
-        ]
-    )
-    picked_ids = tile_src[0, 0]
-    tile_bf16 = tile_mask[0, 0].astype(jnp.bfloat16)
-    picked = sources.reshape(5 * block_count, blk_rows, latent_width)[picked_ids]
-    gathered = jnp.einsum("bkij,bkjl->bil", tile_bf16, picked, preferred_element_type=jnp.float32)
-    gathered = gathered.reshape(node_rows, latent_width).astype(jnp.bfloat16)
+    sources = [
+        message,
+        passed_along(message, "px", 1),
+        passed_along(message, "px", -1),
+        passed_along(message, "py", 1),
+        passed_along(message, "py", -1),
+    ]
+    src_ids = tile_src[0, 0].reshape(-1)
+    gathered = tile_gather(
+        src_ids,
+        tile_mask[0, 0],
+        [part.reshape(block_count, blk_rows, latent_width) for part in sources],
+    )
     zvalue = dense(latent, w_n1[:latent_width]) + dense(gathered, w_n1[latent_width:])
     hidden = jax.nn.silu(zvalue).astype(jnp.bfloat16)
     updated = (latent.astype(jnp.float32) + dense(hidden, w_n2)).astype(jnp.bfloat16)
@@ -109,20 +193,9 @@
     grad_z = (dense(update_low, w_n2.T) * silu_slope(zvalue)).astype(jnp.bfloat16)
     grad_agg = dense(grad_z, w_n1[latent_width:].T).astype(jnp.bfloat16)
     grad_node = grad_update + dense(grad_z, w_n1[:latent_width].T)
-    grad_parts = jnp.einsum(
-        "bkij,bil->bkjl",
-        tile_bf16,
-        grad_agg.reshape(block_count, blk_rows, latent_width),
-        preferred_element_type=jnp.float32,
-    )
-    grad_src = jax.ops.segment_sum(
-        grad_parts.reshape(block_count * tile_count, blk_rows, latent_width),
-        picked_ids.reshape(-1),
-        num_segments=5 * block_count,
-    )
-    grad_src = grad_src.reshape(5, node_rows, latent_width)
-    outbound = grad_src[1:].astype(jnp.bfloat16)
-    collected = grad_src[0]
+    own_part, outbound = tile_scatter(src_ids, tile_mask[0, 0], grad_agg, len(sources))
+    outbound = outbound.reshape(len(sources) - 1, node_rows, latent_width)
+    collected = own_part.reshape(node_rows, latent_width)
     for member, offset in ((0, -1), (1, 1)):
         collected = collected + passed_along(outbound[member], "px", offset).astype(jnp.float32)
     for member, offset in ((2, -1), (3, 1)):

time: 261 us -> 209 us (0.80)
  local copies, waits for them, and re-layouts: 38.4 us -> 6.77 us
  Pallas kernels: 0 us -> 28.4 us
  other arithmetic: 43.2 us -> 20.6 us
  waiting for transfers between devices: 61.3 us -> 44.3 us
  matrix products: 70.2 us -> 60.4 us
    all_to_all x1, waiting for transfers between devices: 30 us -> 0.01 us  [on_device(): lax.all_to_all(token_groups, ('px', 'py'), split_axis=0, concat_axis=0, t...]
    pallas_call x0 -> x2, Pallas kernels: none -> 28.4 us  [the longest x1 15 us: tile_scatter(): pl.pallas_call(scatter_kernel, grid_spec=pltpu.PrefetchScalarGridSpec(num...]
    scatter-add x1 -> x0, other arithmetic: 19.5 us -> none  [on_device(): jax.ops.segment_sum(grad_parts.reshape(block_count * tile_count, blk_rows...]
    ppermute x8, waiting for transfers between devices: 0.02 us -> 12.9 us  [passed_along(): lax.ppermute(value, axis, [(source, source + steps) for source in range(l...]
    unnamed x45 -> x38, local copies, waits for them, and re-layouts: 12.2 us -> 1.59 us
    reshape x1 -> x0, local copies, waits for them, and re-layouts: 9 us -> none  [on_device(): grad_parts.reshape(block_count * tile_count, blk_rows, latent_width)]
    dot_general x2 -> x0, matrix products: 8.86 us -> none  [the longest x1 4.55 us: on_device(): jnp.einsum('bkij,bil->bkjl', tile_bf16, grad_agg.reshape(block_count, blk...]
    gather x1 -> x0, local copies, waits for them, and re-layouts: 5.32 us -> none  [on_device(): sources.reshape(5 * block_count, blk_rows, latent_width)[picked_ids]]
  transfers between devices with their start and end apart: 10 -> 10, of which waited for: 2 -> 2; matrix products, arithmetic and copies ran while one was open for 8% -> 7% of each run, Pallas kernels for 0% -> 0%
where the time goes in v3:
time: 209 us; the launch traced here: 208 us
  matrix products  60.4 us (29%)
  starting transfers between devices  46.6 us (22%)
  waiting for transfers between devices  44.3 us (21%)
  Pallas kernels  28.4 us (14%)
  other arithmetic  20.6 us (10%)
  local copies, waits for them, and re-layouts  6.77 us (3%)
    dot_general x13, matrix products, dense(): return jnp.dot(left, right, preferred_element_type=jnp.float32)  34.6 us
    all_to_all x1, waiting for transfers between devices, on_device(): lax.all_to_all(grad_slots.reshape(devices, slot_count, latent_width), ('p...  31.4 us
    ppermute x8, starting transfers between devices, passed_along(): lax.ppermute(value, axis, [(source, source + steps) for source in range(l...  23.3 us
    pallas_call x1, Pallas kernels, tile_scatter(): pl.pallas_call(scatter_kernel, grid_spec=pltpu.PrefetchScalarGridSpec(num...  15 us
    pallas_call x1, Pallas kernels, tile_gather(): pl.pallas_call(gather_kernel, grid_spec=pltpu.PrefetchScalarGridSpec(num_...  13.5 us
    ppermute x8, waiting for transfers between devices, passed_along(): lax.ppermute(value, axis, [(source, source + steps) for source in range(l...  12.9 us
    convert_element_type x1, other arithmetic, on_device(): (probability * (grad_prob - spread) * score_scale).astype(jnp.bfloat16)  12.4 us
    all_to_all x1, starting transfers between devices, on_device(): lax.all_to_all(token_groups, ('px', 'py'), split_axis=0, concat_axis=0, t...  12 us
  transfers between devices with their start and end apart: 10, of which 2 were waited for; matrix products, arithmetic and copies ran while one was open for 7% of the time, Pallas kernels for 0%

profile of v3, /device:TPU:1, one launch (start us, length us, event | category | flops | bytes accessed | tf_op | source)
XLA Modules:
  0.0 208.0 jit_solution(2237083463343284235)
XLA Ops:
  0.7 12.0 %all-to-all-start = ((bf16[128,16,256]{2,1,0:T(8,128)(2,1)}), bf16[128,16,256]{2,1,0:T(8,128)(2,1)}, u32[]{:S(2)}, u32[]{:S(2)}) async-start(bf16[128,16,256]{2,1,0:T(8,128)(2,1)} %bitcast.67), calls=%async_computation | async-start | bytes 2097152 | tf_op jit(solution)/shard_map/all_to_all | solution.py:158
  13.6 1.7 convolution_convert_fusion.5
  16.5 5.0 %collective-permute-start.2 = (bf16[2048,256]{1,0:T(8,128)(2,1)}, bf16[2048,256]{1,0:T(8,128)(2,1)}, u32[]{:S(2)}, u32[]{:S(2)}) collective-permute-start(bf16[2048,256]{1,0:T(8,128)(2,1)} %convolution_convert_fusion.5), channel_id=1, source_target_pairs={{0,1},{1,2},{2,3},{3,4},{4,5},{5,6},{6,7},{7,8},{8,9},{9,10},{10,1... | collective-permute-start | bytes 3145736 | tf_op jit(solution)/shard_map/ppermute | solution.py:27
  21.5 3.6 %collective-permute-start.1 = (bf16[2048,256]{1,0:T(8,128)(2,1)}, bf16[2048,256]{1,0:T(8,128)(2,1)}, u32[]{:S(2)}, u32[]{:S(2)}) collective-permute-start(bf16[2048,256]{1,0:T(8,128)(2,1)} %convolution_convert_fusion.5), channel_id=1, source_target_pairs={{16,0},{32,16},{48,32},{64,48},{80,64},{96,80},{112,96},{17,1},{33... | collective-permute-start | bytes 3145736 | tf_op jit(solution)/shard_map/ppermute | solution.py:27
  25.1 2.5 %collective-permute-start = (bf16[2048,256]{1,0:T(8,128)(2,1)}, bf16[2048,256]{1,0:T(8,128)(2,1)}, u32[]{:S(2)}, u32[]{:S(2)}) collective-permute-start(bf16[2048,256]{1,0:T(8,128)(2,1)} %convolution_convert_fusion.5), channel_id=1, source_target_pairs={{0,16},{16,32},{32,48},{48,64},{64,80},{80,96},{96,112},{1,17},{17... | collective-permute-start | bytes 3145736 | tf_op jit(solution)/shard_map/ppermute | solution.py:27
  28.6 1.5 convolution_convert_fusion.3
  30.1 1.3 fusion.24
  31.4 3.3 %convolution_convert_fusion = bf16[2048,512]{1,0:T(8,128)(2,1)} fusion(bf16[2048,256]{1,0:T(8,128)(2,1)} %bitcast.10, bf16[256,512]{1,0:T(8,128)(2,1)S(1)} %copy-done), kind=kOutput, calls=%fused_computation.9 | convolution fusion | flops 537919488 | bytes 3407872 | tf_op jit(solution)/shard_map/dot_general | solution.py:114
  34.7 12.9 %collective-permute-done.3 = bf16[2048,256]{1,0:T(8,128)(2,1)} collective-permute-done((bf16[2048,256]{1,0:T(8,128)(2,1)}, bf16[2048,256]{1,0:T(8,128)(2,1)}, u32[]{:S(2)}, u32[]{:S(2)}) %collective-permute-start.3) | collective-permute-done | bytes 1048608 | tf_op jit(solution)/shard_map/ppermute | solution.py:27
  47.6 13.5 %shard_map.140 = bf16[2048,256]{1,0:T(8,128)(2,1)} custom-call(s32[64]{0:T(128)} %reshape_squeeze.6.src_ids, s32[16,4,128,128]{3,2,1,0:T(8,128)} %bitcast.64, bf16[16,128,256]{2,1,0:T(8,128)(2,1)} %bitcast.4.own, bf16[16,128,256]{2,1,0:T(8,128)(2,1)} %bitcast.5.up, bf16[16,128,256]{2,1,0:T(8,128)(2,1)} %bitcast.6.down, bf16[16,128,256]{2,1,0:T(8,128)(2,1)} %bitcast.7.left, ...), custom_call_target="tpu_custom_call" | custom-call | tf_op jit(solution)/shard_map/pallas_call | solution.py:51
  61.1 3.0 %convolution_add_fusion.4 = f32[2048,256]{1,0:T(8,128)} fusion(f32[2048,256]{1,0:T(8,128)S(1)} %fusion.24, bf16[2048,256]{1,0:T(8,128)(2,1)} %shard_map.140, bf16[512,256]{1,0:T(8,128)(2,1)} %param.20), kind=kOutput, calls=%fused_computation.16 | convolution fusion | flops 268959744 | bytes 5373952 | tf_op jit(solution)/shard_map/dot_general | solution.py:114
  64.1 3.6 %convolution_convert_fusion.4 = bf16[2048,256]{1,0:T(8,128)(2,1)} fusion(bf16[256,256]{1,0:T(8,128)(2,1)} %param.22, bf16[256,256]{1,0:T(8,128)(2,1)} %param.21, f32[2048,256]{1,0:T(8,128)} %convolution_add_fusion.4, bf16[1,1,2048,256]{3,2,1,0:T(8,128)(2,1)S(1)} %copy-done.1), kind=kOutput, calls=%fused_computation.24 | convolution fusion | flops 541589504 | bytes 4456448 | tf_op jit(solution)/shard_map/dot_general | solution.py:114
  67.7 3.6 %fusion = (f32[2048]{0:T(1024)S(1)}, f32[2048,2048]{0,1:T(8,128)S(1)}) fusion(pred[2048]{0:T(1024)(128)(4,1)S(1)} %lt.26, bf16[2048,256]{1,0:T(8,128)(2,1)} %convolution_convert_fusion.4, bf16[2048,512]{1,0:T(8,128)(2,1)S(1)} %copy-done.3), kind=kOutput, calls=%fused_computation.4 | convolution fusion | flops 2160064512 | bytes 18884608 | tf_op jit(solution)/shard_map/nl,kl->nk/dot_general | solution.py:167
  71.4 5.0 %fusion.2 = f32[2048]{0:T(1024)S(1)} fusion(f32[2048,2048]{0,1:T(8,128)S(1)} %get-tuple-element.11, f32[2048]{0:T(1024)S(1)} %get-tuple-element.10, pred[2048]{0:T(1024)(128)(4,1)S(1)} %lt.26), kind=kLoop, calls=%fused_computation.6 | loop fusion | flops 16775168 | bytes 16795648 | tf_op jit(solution)/shard_map/reduce_sum | solution.py:172
  76.4 5.6 %fusion.9 = bf16[2048,256]{1,0:T(8,128)(2,1)} fusion(bf16[2048,256]{1,0:T(8,128)(2,1)S(1)} %copy-done.7, f32[2048,2048]{0,1:T(8,128)S(1)} %get-tuple-element.11, f32[2048]{0:T(1024)S(1)} %fusion.2, f32[2048]{0:T(1024)S(1)} %get-tuple-element.10, pred[2048]{0:T(1024)(128)(4,1)S(1)} %lt.26), kind=kOutput, calls=%fused_computation.26 | convolution fusion | flops 2168979456 | bytes 18892800 | tf_op jit(solution)/shard_map/nk,nl->kl/dot_general | solution.py:176
  82.0 9.6 %multiply_reduce_fusion = (f32[2048]{0:T(1024)S(1)}, f32[2048,2048]{0,1:T(8,128)}) fusion(f32[2048]{0:T(1024)S(1)} %fusion.2, f32[2048]{0:T(1024)S(1)} %get-tuple-element.10, f32[2048,2048]{0,1:T(8,128)S(1)} %get-tuple-element.11, pred[2048]{0:T(1024)(128)(4,1)S(1)} %lt.26, bf16[2048,256]{1,0:T(8,128)(2,1)} %convolution_convert_fusion.3, ...), kind=kOutput, calls=%fused_computation.1 | convolution fusion | flops 2172647424 | bytes 35678208 | tf_op jit(solution)/shard_map/nl,kl->nk/dot_general | solution.py:175
  91.6 12.4 %multiply_convert_fusion = bf16[2048,2048]{0,1:T(8,128)(2,1)} fusion(f32[2048,2048]{0,1:T(8,128)} %get-tuple-element.13, f32[2048]{0:T(1024)S(1)} %get-tuple-element.12, f32[2048]{0:T(1024)S(1)} %fusion.2, f32[2048]{0:T(1024)S(1)} %get-tuple-element.10, f32[2048,2048]{0,1:T(8,128)S(1)} %get-tuple-element.11, pred[2048]{0:T(1024)(128)(4,1)S(1)} %lt.26), kind=kLoop, calls=%fused_computation | loop fusion | flops 33554432 | bytes 41969664 | tf_op jit(solution)/shard_map/convert_element_type | solution.py:178
  104.0 7.9 %convolution_add_fusion.2 = f32[2048,256]{1,0:T(8,128)} fusion(bf16[256,256]{1,0:T(8,128)(2,1)} %param.22, bf16[2048,2048]{0,1:T(8,128)(2,1)} %multiply_convert_fusion, bf16[1,1,2048,256]{3,2,1,0:T(8,128)(2,1)} %param.25, bf16[2048,512]{1,0:T(8,128)(2,1)S(1)} %copy-done.3), kind=kOutput, calls=%fused_computation.14 | convolution fusion | flops 2417491968 | bytes 12713984 | tf_op jit(solution)/shard_map/dot_general | solution.py:114
  111.9 7.0 %convolution_convert_fusion.6 = bf16[2048,256]{1,0:T(8,128)(2,1)} fusion(bf16[2048,2048]{0,1:T(8,128)(2,1)} %multiply_convert_fusion, bf16[2048,256]{1,0:T(8,128)(2,1)S(1)} %copy-done.17), kind=kOutput, calls=%fused_computation.27 | convolution fusion | flops 2148007936 | bytes 10485760 | tf_op jit(solution)/shard_map/nk,nl->kl/dot_general | solution.py:180
  119.9 1.4 convolution_convert_fusion.2.grad_ref
  121.3 15.0 %shard_map.141 = (f32[16,128,256]{2,1,0:T(8,128)}, bf16[4,16,128,256]{3,2,1,0:T(8,128)(2,1)}) custom-call(s32[64]{0:T(128)} %reshape_squeeze.6.src_ids, s32[16,4,128,128]{3,2,1,0:T(8,128)} %bitcast.65, bf16[2048,256]{1,0:T(8,128)(2,1)} %convolution_convert_fusion.2.grad_ref), custom_call_target="tpu_custom_call" | custom-call | tf_op jit(solution)/shard_map/pallas_call | solution.py:90
  136.3 4.5 %fusion.45 = (bf16[1,16,128,256]{3,2,1,0:T(8,128)(2,1)}, bf16[1,16,128,256]{3,2,1,0:T(8,128)(2,1)}, bf16[1,16,128,256]{3,2,1,0:T(8,128)(2,1)}, bf16[1,16,128,256]{3,2,1,0:T(8,128)(2,1)}) fusion(bf16[4,16,128,256]{3,2,1,0:T(8,128)(2,1)} %get-tuple-element.5), kind=kLoop, calls=%fused_computation.64 | loop fusion | bytes 8388608 | tf_op jit(solution)/shard_map/slice | solution.py:200
  140.8 3.5 %collective-permute-start.7 = (bf16[2048,256]{1,0:T(8,128)(2,1)}, bf16[2048,256]{1,0:T(8,128)(2,1)S(1)}, u32[]{:S(2)}, u32[]{:S(2)}) collective-permute-start(bf16[2048,256]{1,0:T(8,128)(2,1)} %bitcast.15), channel_id=1, source_target_pairs={{0,1},{1,2},{2,3},{3,4},{4,5},{5,6},{6,7},{7,8},{8,9},{9,10},{10,1... | collective-permute-start | bytes 3145736 | tf_op jit(solution)/shard_map/ppermute | solution.py:27
  144.3 2.8 %collective-permute-start.4 = (bf16[2048,256]{1,0:T(8,128)(2,1)}, bf16[2048,256]{1,0:T(8,128)(2,1)}, u32[]{:S(2)}, u32[]{:S(2)}) collective-permute-start(bf16[2048,256]{1,0:T(8,128)(2,1)} %bitcast.12), channel_id=1, source_target_pairs={{16,0},{32,16},{48,32},{64,48},{80,64},{96,80},{112,96},{17,1},{33... | collective-permute-start | bytes 3145736 | tf_op jit(solution)/shard_map/ppermute | solution.py:27
  147.1 1.3 collective-permute-start.6
  148.4 3.3 %collective-permute-start.5 = (bf16[2048,256]{1,0:T(8,128)(2,1)}, bf16[2048,256]{1,0:T(8,128)(2,1)}, u32[]{:S(2)}, u32[]{:S(2)}) collective-permute-start(bf16[2048,256]{1,0:T(8,128)(2,1)} %bitcast.13), channel_id=1, source_target_pairs={{0,16},{16,32},{32,48},{48,64},{64,80},{80,96},{96,112},{1,17},{17... | collective-permute-start | bytes 3145736 | tf_op jit(solution)/shard_map/ppermute | solution.py:27
  151.7 1.7 convolution_convert_fusion.1
  153.4 11.3 %all-to-all-start.1 = ((bf16[128,16,256]{2,1,0:T(8,128)(2,1)}), bf16[128,16,256]{2,1,0:T(8,128)(2,1)S(1)}, u32[]{:S(2)}, u32[]{:S(2)}) async-start(bf16[128,16,256]{2,1,0:T(8,128)(2,1)} %bitcast.68), calls=%async_computation.1 | async-start | bytes 2097152 | tf_op jit(solution)/shard_map/all_to_all | solution.py:183
  164.7 3.5 %convolution_add_fusion.1 = f32[2048,256]{1,0:T(8,128)} fusion(f32[2048,256]{1,0:T(8,128)} %convolution_add_fusion.2, bf16[2048,256]{1,0:T(8,128)(2,1)S(1)} %fusion.6, bf16[512,256]{1,0:T(8,128)(2,1)} %param.20), kind=kOutput, calls=%fused_computation.12 | convolution fusion | flops 268959744 | bytes 5373952 | tf_op jit(solution)/shard_map/dot_general | solution.py:114
  168.2 31.4 %all-to-all-done.1 = bf16[128,16,256]{2,1,0:T(8,128)(2,1)S(1)} async-done(((bf16[128,16,256]{2,1,0:T(8,128)(2,1)}), bf16[128,16,256]{2,1,0:T(8,128)(2,1)S(1)}, u32[]{:S(2)}, u32[]{:S(2)}) %all-to-all-start.1) | async-done | bytes 1048608 | tf_op jit(solution)/shard_map/all_to_all | solution.py:183
  199.7 3.1 %fusion.19 = bf16[2048,256]{1,0:T(8,128)(2,1)S(1)} fusion(f32[16,128,256]{2,1,0:T(8,128)} %get-tuple-element.4, bf16[2048,256]{1,0:T(8,128)(2,1)S(1)} %collective-permute-done.7, bf16[2048,256]{1,0:T(8,128)(2,1)} %collective-permute-done.6, bf16[2048,256]{1,0:T(8,128)(2,1)} %collective-permute-done.5, bf16[2048,256]{1,0:T(8,128)(2,1)} %collective-permute-done.4), kind=kLoop, calls=%fused_computation.37 | loop fusion | flops 4718592 | bytes 7340032 | tf_op jit(solution)/shard_map/convert_element_type | solution.py:203
  202.8 4.2 %fusion.12 = bf16[1,1,2048,256]{3,2,1,0:T(8,128)(2,1)} fusion(f32[2048,256]{1,0:T(8,128)} %convolution_add_fusion.1, bf16[256,256]{1,0:T(8,128)(2,1)S(1)} %copy-done.10, bf16[2048,256]{1,0:T(8,128)(2,1)S(1)} %fusion.19, bf16[256,256]{1,0:T(8,128)(2,1)} %param.19, f32[2048,256]{1,0:T(8,128)} %copy-done.2), kind=kOutput, calls=%fused_computation.29 | convolution fusion | flops 542638080 | bytes 6553600 | tf_op jit(solution)/shard_map/dot_general | solution.py:114
  (52 shorter events, 5.1 us)
Async XLA Ops:
  0.6 30.8 %copy-start = (bf16[256,512]{1,0:T(8,128)(2,1)S(1)}, bf16[256,512]{1,0:T(8,128)(2,1)}, u32[]{:S(2)}) copy-start(bf16[256,512]{1,0:T(8,128)(2,1)} %param.23) | copy-start | bytes 786436
  0.6 12.0 %copy-start.1 = (bf16[1,1,2048,256]{3,2,1,0:T(8,128)(2,1)S(1)}, bf16[1,1,2048,256]{3,2,1,0:T(8,128)(2,1)}, u32[]{:S(2)}) copy-start(bf16[1,1,2048,256]{3,2,1,0:T(8,128)(2,1)} %param.13) | copy-start | bytes 3145732
  0.7 12.0 %copy-start.10 = (bf16[256,256]{1,0:T(8,128)(2,1)S(1)}, bf16[256,256]{1,0:T(8,128)(2,1)}, u32[]{:S(2)}) copy-start(bf16[256,256]{1,0:T(8,128)(2,1)} %param.18) | copy-start | bytes 393220
  0.7 30.8 %all-to-all-start = ((bf16[128,16,256]{2,1,0:T(8,128)(2,1)}), bf16[128,16,256]{2,1,0:T(8,128)(2,1)}, u32[]{:S(2)}, u32[]{:S(2)}) async-start(bf16[128,16,256]{2,1,0:T(8,128)(2,1)} %bitcast.67), calls=%async_computation | async-start | bytes 2097152 | tf_op jit(solution)/shard_map/all_to_all | solution.py:158
  12.6 0.9 copy-start.14
  13.6 1.7 copy-start.2
  13.6 14.1 %copy-start.11 = (s32[1,1,16,4]{2,3,1,0:T(4,128)S(1)}, s32[1,1,16,4]{2,3,1,0:T(4,128)}, u32[]{:S(2)}) copy-start(s32[1,1,16,4]{2,3,1,0:T(4,128)} %param.14) | copy-start | bytes 772
  13.6 14.9 %copy-start.12 = (s32[128,1]{0,1:T(1,128)S(1)}, s32[128,1]{0,1:T(1,128)}, u32[]{:S(2)}) copy-start(s32[128,1]{0,1:T(1,128)} %param.17) | copy-start | bytes 1540
  13.6 15.0 %copy-start.6 = (bf16[1,1,2048,256]{3,2,1,0:T(8,128)(2,1)S(1)}, bf16[1,1,2048,256]{3,2,1,0:T(8,128)(2,1)}, u32[]{:S(2)}) copy-start(bf16[1,1,2048,256]{3,2,1,0:T(8,128)(2,1)} %param.25) | copy-start | bytes 3145732
  13.6 15.0 %copy-start.9 = (bf16[256,256]{1,0:T(8,128)(2,1)S(1)}, bf16[256,256]{1,0:T(8,128)(2,1)}, u32[]{:S(2)}) copy-start(bf16[256,256]{1,0:T(8,128)(2,1)} %param.24) | copy-start | bytes 393220
  15.2 32.3 %collective-permute-start.3 = (bf16[2048,256]{1,0:T(8,128)(2,1)}, bf16[2048,256]{1,0:T(8,128)(2,1)}, u32[]{:S(2)}, u32[]{:S(2)}) collective-permute-start(bf16[2048,256]{1,0:T(8,128)(2,1)} %convolution_convert_fusion.5), channel_id=1, source_target_pairs={{1,0},{2,1},{3,2},{4,3},{5,4},{6,5},{7,6},{8,7},{9,8},{10,9},{11,1... | collective-permute-start | bytes 3145736 | tf_op jit(solution)/shard_map/ppermute | solution.py:27
  16.5 31.0 %collective-permute-start.2 = (bf16[2048,256]{1,0:T(8,128)(2,1)}, bf16[2048,256]{1,0:T(8,128)(2,1)}, u32[]{:S(2)}, u32[]{:S(2)}) collective-permute-start(bf16[2048,256]{1,0:T(8,128)(2,1)} %convolution_convert_fusion.5), channel_id=1, source_target_pairs={{0,1},{1,2},{2,3},{3,4},{4,5},{5,6},{6,7},{7,8},{8,9},{9,10},{10,1... | collective-permute-start | bytes 3145736 | tf_op jit(solution)/shard_map/ppermute | solution.py:27
  21.5 26.0 %collective-permute-start.1 = (bf16[2048,256]{1,0:T(8,128)(2,1)}, bf16[2048,256]{1,0:T(8,128)(2,1)}, u32[]{:S(2)}, u32[]{:S(2)}) collective-permute-start(bf16[2048,256]{1,0:T(8,128)(2,1)} %convolution_convert_fusion.5), channel_id=1, source_target_pairs={{16,0},{32,16},{48,32},{64,48},{80,64},{96,80},{112,96},{17,1},{33... | collective-permute-start | bytes 3145736 | tf_op jit(solution)/shard_map/ppermute | solution.py:27
  25.1 22.4 %collective-permute-start = (bf16[2048,256]{1,0:T(8,128)(2,1)}, bf16[2048,256]{1,0:T(8,128)(2,1)}, u32[]{:S(2)}, u32[]{:S(2)}) collective-permute-start(bf16[2048,256]{1,0:T(8,128)(2,1)} %convolution_convert_fusion.5), channel_id=1, source_target_pairs={{0,16},{16,32},{32,48},{48,64},{64,80},{80,96},{96,112},{1,17},{17... | collective-permute-start | bytes 3145736 | tf_op jit(solution)/shard_map/ppermute | solution.py:27
  64.1 3.6 %copy-start.3 = (bf16[2048,512]{1,0:T(8,128)(2,1)S(1)}, bf16[2048,512]{1,0:T(8,128)(2,1)}, u32[]{:S(2)}) copy-start(bf16[2048,512]{1,0:T(8,128)(2,1)} %convolution_convert_fusion) | copy-start | bytes 6291460
  71.3 5.1 %copy-start.7 = (bf16[2048,256]{1,0:T(8,128)(2,1)S(1)}, bf16[2048,256]{1,0:T(8,128)(2,1)}, u32[]{:S(2)}) copy-start(bf16[2048,256]{1,0:T(8,128)(2,1)} %convolution_convert_fusion.3) | copy-start | bytes 3145732
  104.0 7.9 %copy-start.17 = (bf16[2048,256]{1,0:T(8,128)(2,1)S(1)}, bf16[2048,256]{1,0:T(8,128)(2,1)}, u32[]{:S(2)}) copy-start(bf16[2048,256]{1,0:T(8,128)(2,1)} %convolution_convert_fusion.4) | copy-start | bytes 3145732
  111.9 7.0 %copy-start.4 = (f32[2048,256]{1,0:T(8,128)S(1)}, f32[2048,256]{1,0:T(8,128)}, u32[]{:S(2)}) copy-start(f32[2048,256]{1,0:T(8,128)} %convolution_add_fusion.2) | copy-start | bytes 6291460
  111.9 7.0 %copy-start.5 = (f32[2048,256]{1,0:T(8,128)S(1)}, f32[2048,256]{1,0:T(8,128)}, u32[]{:S(2)}) copy-start(f32[2048,256]{1,0:T(8,128)} %convolution_add_fusion.4) | copy-start | bytes 6291460
  111.9 7.0 %copy-start.13 = (bf16[256,256]{1,0:T(8,128)(2,1)S(1)}, bf16[256,256]{1,0:T(8,128)(2,1)}, u32[]{:S(2)}) copy-start(bf16[256,256]{1,0:T(8,128)(2,1)} %param.21) | copy-start | bytes 393220
  118.9 1.0 copy-start.8
  136.3 15.4 %copy-start.15 = (bf16[2048,256]{1,0:T(8,128)(2,1)S(1)}, bf16[2048,256]{1,0:T(8,128)(2,1)}, u32[]{:S(2)}) copy-start(bf16[2048,256]{1,0:T(8,128)(2,1)} %fusion.9) | copy-start | bytes 3145732
  136.3 15.4 %copy-start.16 = (bf16[2048,256]{1,0:T(8,128)(2,1)S(1)}, bf16[2048,256]{1,0:T(8,128)(2,1)}, u32[]{:S(2)}) copy-start(bf16[2048,256]{1,0:T(8,128)(2,1)} %convolution_convert_fusion.6) | copy-start | bytes 3145732
  140.8 58.9 %collective-permute-start.7 = (bf16[2048,256]{1,0:T(8,128)(2,1)}, bf16[2048,256]{1,0:T(8,128)(2,1)S(1)}, u32[]{:S(2)}, u32[]{:S(2)}) collective-permute-start(bf16[2048,256]{1,0:T(8,128)(2,1)} %bitcast.15), channel_id=1, source_target_pairs={{0,1},{1,2},{2,3},{3,4},{4,5},{5,6},{6,7},{7,8},{8,9},{9,10},{10,1... | collective-permute-start | bytes 3145736 | tf_op jit(solution)/shard_map/ppermute | solution.py:27
  144.3 55.4 %collective-permute-start.4 = (bf16[2048,256]{1,0:T(8,128)(2,1)}, bf16[2048,256]{1,0:T(8,128)(2,1)}, u32[]{:S(2)}, u32[]{:S(2)}) collective-permute-start(bf16[2048,256]{1,0:T(8,128)(2,1)} %bitcast.12), channel_id=1, source_target_pairs={{16,0},{32,16},{48,32},{64,48},{80,64},{96,80},{112,96},{17,1},{33... | collective-permute-start | bytes 3145736 | tf_op jit(solution)/shard_map/ppermute | solution.py:27
  147.1 52.6 %collective-permute-start.6 = (bf16[2048,256]{1,0:T(8,128)(2,1)}, bf16[2048,256]{1,0:T(8,128)(2,1)}, u32[]{:S(2)}, u32[]{:S(2)}) collective-permute-start(bf16[2048,256]{1,0:T(8,128)(2,1)} %bitcast.14), channel_id=1, source_target_pairs={{1,0},{2,1},{3,2},{4,3},{5,4},{6,5},{7,6},{8,7},{9,8},{10,9},{11,1... | collective-permute-start | bytes 3145736 | tf_op jit(solution)/shard_map/ppermute | solution.py:27
  148.4 51.3 %collective-permute-start.5 = (bf16[2048,256]{1,0:T(8,128)(2,1)}, bf16[2048,256]{1,0:T(8,128)(2,1)}, u32[]{:S(2)}, u32[]{:S(2)}) collective-permute-start(bf16[2048,256]{1,0:T(8,128)(2,1)} %bitcast.13), channel_id=1, source_target_pairs={{0,16},{16,32},{32,48},{48,64},{64,80},{80,96},{96,112},{1,17},{17... | collective-permute-start | bytes 3145736 | tf_op jit(solution)/shard_map/ppermute | solution.py:27
  153.4 46.2 %all-to-all-start.1 = ((bf16[128,16,256]{2,1,0:T(8,128)(2,1)}), bf16[128,16,256]{2,1,0:T(8,128)(2,1)S(1)}, u32[]{:S(2)}, u32[]{:S(2)}) async-start(bf16[128,16,256]{2,1,0:T(8,128)(2,1)} %bitcast.68), calls=%async_computation.1 | async-start | bytes 2097152 | tf_op jit(solution)/shard_map/all_to_all | solution.py:183

commit v4 on v3

--- a/solution.py
+++ b/solution.py
@@ -1,3 +1,4 @@
+import functools
 import math
 
 import jax
@@ -108,6 +109,72 @@
         ),
         compiler_params=pltpu.CompilerParams(dimension_semantics=("arbitrary",)),
     )(src_ids, tile_mask, grad_agg)
+
+
+def attend_kernel(scale, live_ref, q_ref, go_ref, kv_ref, gq_ref, gkv_ref, gk_acc, gv_acc):
+    step = pl.program_id(0)
+    width = q_ref.shape[1]
+
+    @pl.when(step == 0)
+    def _():
+        gk_acc[...] = jnp.zeros(gk_acc.shape, jnp.float32)
+        gv_acc[...] = jnp.zeros(gv_acc.shape, jnp.float32)
+
+    queries = q_ref[...]
+    grad_out = go_ref[...]
+    keys = kv_ref[:, 0:width]
+    values = kv_ref[:, width : 2 * width]
+    nt = (((1,), (1,)), ((), ()))
+    tn = (((0,), (0,)), ((), ()))
+    scores = lax.dot_general(queries, keys, nt, preferred_element_type=jnp.float32) * scale
+    scores = jnp.where(live_ref[...] > 0, scores, -jnp.inf)
+    highest = jnp.max(scores, axis=1, keepdims=True)
+    expo_terms = jnp.exp(scores - highest)
+    probability = expo_terms / jnp.sum(expo_terms, axis=1, keepdims=True)
+    prob_low = probability.astype(jnp.bfloat16)
+    grad_prob = lax.dot_general(grad_out, values, nt, preferred_element_type=jnp.float32)
+    spread = jnp.sum(probability * grad_prob, axis=1, keepdims=True)
+    grad_score = (probability * (grad_prob - spread) * scale).astype(jnp.bfloat16)
+    gq_ref[...] = jnp.dot(grad_score, keys, preferred_element_type=jnp.float32).astype(gq_ref.dtype)
+    gk_acc[...] += lax.dot_general(grad_score, queries, tn, preferred_element_type=jnp.float32)
+    gv_acc[...] += lax.dot_general(prob_low, grad_out, tn, preferred_element_type=jnp.float32)
+
+    @pl.when(step == pl.num_programs(0) - 1)
+    def _():
+        gkv_ref[:, 0:width] = gk_acc[...].astype(gkv_ref.dtype)
+        gkv_ref[:, width : 2 * width] = gv_acc[...].astype(gkv_ref.dtype)
+
+
+def attend_back(live, queries, grad_out, keyvals, scale, rows_per_step=256):
+    rows, width = queries.shape
+    slots = keyvals.shape[0]
+    steps = rows // rows_per_step
+    row_block = pl.BlockSpec((rows_per_step, width), lambda i: (i, 0))
+    return pl.pallas_call(
+        functools.partial(attend_kernel, scale),
+        grid=(steps,),
+        in_specs=[
+            pl.BlockSpec((1, slots), lambda i: (0, 0)),
+            row_block,
+            row_block,
+            pl.BlockSpec((slots, 2 * width), lambda i: (0, 0)),
+        ],
+        out_specs=[row_block, pl.BlockSpec((slots, 2 * width), lambda i: (0, 0))],
+        out_shape=(
+            jax.ShapeDtypeStruct((rows, width), jnp.bfloat16),
+            jax.ShapeDtypeStruct((slots, 2 * width), jnp.bfloat16),
+        ),
+        scratch_shapes=[
+            pltpu.VMEM((slots, width), jnp.float32),
+            pltpu.VMEM((slots, width), jnp.float32),
+        ],
+        compiler_params=pltpu.CompilerParams(dimension_semantics=("arbitrary",)),
+        cost_estimate=pl.CostEstimate(
+            flops=10 * rows * slots * width,
+            transcendentals=rows * slots,
+            bytes_accessed=2 * (3 * rows * width + 4 * slots * width),
+        ),
+    )(live, queries, grad_out, keyvals)
 
 
 def dense(left, right):
@@ -160,25 +227,11 @@
     )
     arrived_tokens = arrived_tokens.reshape(devices * slot_count, latent_width)
     arrived = dense(arrived_tokens, w_kv).astype(jnp.bfloat16)
-    key_rows = arrived[:, :latent_width]
-    value_rows = arrived[:, latent_width:]
-    live_keys = (jnp.arange(slot_count)[None, :] < tok_count[:, 0][:, None]).reshape(-1)
-    scores = (
-        jnp.einsum("nl,kl->nk", queries, key_rows, preferred_element_type=jnp.float32) * score_scale
-    )
-    scores = jnp.where(live_keys[None, :], scores, -jnp.inf)
-    highest = jnp.max(scores, axis=1, keepdims=True)
-    expo_terms = jnp.exp(scores - highest)
-    probability = expo_terms / jnp.sum(expo_terms, axis=1, keepdims=True)
-    prob_low = probability.astype(jnp.bfloat16)
+    live_keys = (jnp.arange(slot_count)[None, :] < tok_count[:, 0][:, None]).reshape(1, -1)
     grad_out = dense(cotangent[0, 0], w_o.T).astype(jnp.bfloat16)
-    grad_prob = jnp.einsum("nl,kl->nk", grad_out, value_rows, preferred_element_type=jnp.float32)
-    grad_vals = jnp.einsum("nk,nl->kl", prob_low, grad_out, preferred_element_type=jnp.float32)
-    spread = jnp.sum(probability * grad_prob, axis=1, keepdims=True)
-    grad_score = (probability * (grad_prob - spread) * score_scale).astype(jnp.bfloat16)
-    grad_query = dense(grad_score, key_rows).astype(jnp.bfloat16)
-    grad_keys = jnp.einsum("nk,nl->kl", grad_score, queries, preferred_element_type=jnp.float32)
-    grad_kv = jnp.concatenate([grad_keys, grad_vals], axis=1).astype(jnp.bfloat16)
+    grad_query, grad_kv = attend_back(
+        live_keys.astype(jnp.float32), queries, grad_out, arrived, score_scale
+    )
     grad_slots = dense(grad_kv, w_kv.T).astype(jnp.bfloat16)
     returned = lax.all_to_all(
         grad_slots.reshape(devices, slot_count, latent_width),

time: 209 us -> 184 us (0.88)
  matrix products: 60.4 us -> 27.7 us
  Pallas kernels: 28.4 us -> 50.6 us
  other arithmetic: 20.6 us -> 4.58 us
    dot_general x4 -> x0, matrix products: 25.8 us -> none  [the longest x1 9.63 us: on_device(): jnp.einsum('nl,kl->nk', grad_out, value_rows, preferred_element_type=jnp....]
    pallas_call x0 -> x1, Pallas kernels: none -> 22.1 us  [attend_back(): pl.pallas_call(functools.partial(attend_kernel, scale), grid=(steps,), in...]
    convert_element_type x1, other arithmetic: 12.4 us -> 0.08 us  [on_device(): live_keys.astype(jnp.float32)]
    dot_general x13, matrix products: 34.6 us -> 27.7 us  [dense(): return jnp.dot(left, right, preferred_element_type=jnp.float32)]
    reduce_sum x1 -> x0, other arithmetic: 5.04 us -> none  [on_device(): probability = expo_terms / jnp.sum(expo_terms, axis=1, keepdims=True)]
  transfers between devices with their start and end apart: 10 -> 10, of which waited for: 2 -> 2; matrix products, arithmetic and copies ran while one was open for 7% -> 8% of each run, Pallas kernels for 0% -> 0%
where the time goes in v4:
time: 184 us; the launch traced here: 182 us
  Pallas kernels  50.6 us (28%)
  starting transfers between devices  46.8 us (25%)
  waiting for transfers between devices  43.5 us (24%)
  matrix products  27.7 us (15%)
  local copies, waits for them, and re-layouts  8.44 us (5%)
  other arithmetic  4.58 us (2%)
    all_to_all x1, waiting for transfers between devices, on_device(): lax.all_to_all(grad_slots.reshape(devices, slot_count, latent_width), ('p...  31.2 us
    dot_general x13, matrix products, dense(): return jnp.dot(left, right, preferred_element_type=jnp.float32)  27.7 us
    ppermute x8, starting transfers between devices, passed_along(): lax.ppermute(value, axis, [(source, source + steps) for source in range(l...  24.5 us
    pallas_call x1, Pallas kernels, attend_back(): pl.pallas_call(functools.partial(attend_kernel, scale), grid=(steps,), in...  22.1 us
    pallas_call x1, Pallas kernels, tile_scatter(): pl.pallas_call(scatter_kernel, grid_spec=pltpu.PrefetchScalarGridSpec(num...  15 us
    pallas_call x1, Pallas kernels, tile_gather(): pl.pallas_call(gather_kernel, grid_spec=pltpu.PrefetchScalarGridSpec(num_...  13.5 us
    ppermute x8, waiting for transfers between devices, passed_along(): lax.ppermute(value, axis, [(source, source + steps) for source in range(l...  12.3 us
    all_to_all x1, starting transfers between devices, on_device(): lax.all_to_all(token_groups, ('px', 'py'), split_axis=0, concat_axis=0, t...  12 us
  transfers between devices with their start and end apart: 10, of which 2 were waited for; matrix products, arithmetic and copies ran while one was open for 8% of the time, Pallas kernels for 0%

profile of v4, /device:TPU:1, one launch (start us, length us, event | category | flops | bytes accessed | tf_op | source)
XLA Modules:
  0.0 182.5 jit_solution(1793071035891916622)
XLA Ops:
  0.7 12.0 %all-to-all-start = ((bf16[128,16,256]{2,1,0:T(8,128)(2,1)}), bf16[128,16,256]{2,1,0:T(8,128)(2,1)}, u32[]{:S(2)}, u32[]{:S(2)}) async-start(bf16[128,16,256]{2,1,0:T(8,128)(2,1)} %bitcast.64), calls=%async_computation | async-start | bytes 2097152 | tf_op jit(solution)/shard_map/all_to_all | solution.py:225
  13.6 1.7 convolution_convert_fusion.5
  15.2 1.3 collective-permute-start.3
  16.5 5.0 %collective-permute-start.2 = (bf16[2048,256]{1,0:T(8,128)(2,1)}, bf16[2048,256]{1,0:T(8,128)(2,1)}, u32[]{:S(2)}, u32[]{:S(2)}) collective-permute-start(bf16[2048,256]{1,0:T(8,128)(2,1)} %convolution_convert_fusion.5), channel_id=1, source_target_pairs={{0,1},{1,2},{2,3},{3,4},{4,5},{5,6},{6,7},{7,8},{8,9},{9,10},{10,1... | collective-permute-start | bytes 3145736 | tf_op jit(solution)/shard_map/ppermute | solution.py:28
  21.6 3.6 %collective-permute-start.1 = (bf16[2048,256]{1,0:T(8,128)(2,1)}, bf16[2048,256]{1,0:T(8,128)(2,1)}, u32[]{:S(2)}, u32[]{:S(2)}) collective-permute-start(bf16[2048,256]{1,0:T(8,128)(2,1)} %convolution_convert_fusion.5), channel_id=1, source_target_pairs={{16,0},{32,16},{48,32},{64,48},{80,64},{96,80},{112,96},{17,1},{33... | collective-permute-start | bytes 3145736 | tf_op jit(solution)/shard_map/ppermute | solution.py:28
  25.2 2.5 %collective-permute-start = (bf16[2048,256]{1,0:T(8,128)(2,1)}, bf16[2048,256]{1,0:T(8,128)(2,1)}, u32[]{:S(2)}, u32[]{:S(2)}) collective-permute-start(bf16[2048,256]{1,0:T(8,128)(2,1)} %convolution_convert_fusion.5), channel_id=1, source_target_pairs={{0,16},{16,32},{32,48},{48,64},{64,80},{80,96},{96,112},{1,17},{17... | collective-permute-start | bytes 3145736 | tf_op jit(solution)/shard_map/ppermute | solution.py:28
  28.6 0.7 reshape.73.live_ref
  29.3 1.4 convolution_convert_fusion.3.go_ref
  30.7 1.3 fusion.11
  32.0 3.3 %convolution_convert_fusion.kv_ref = bf16[2048,512]{1,0:T(8,128)(2,1)} fusion(bf16[2048,256]{1,0:T(8,128)(2,1)} %bitcast.10, bf16[256,512]{1,0:T(8,128)(2,1)S(1)} %copy-done), kind=kOutput, calls=%fused_computation | convolution fusion | flops 537919488 | bytes 3407872 | tf_op jit(solution)/shard_map/dot_general | solution.py:181
  35.3 12.3 %collective-permute-done.3 = bf16[2048,256]{1,0:T(8,128)(2,1)} collective-permute-done((bf16[2048,256]{1,0:T(8,128)(2,1)}, bf16[2048,256]{1,0:T(8,128)(2,1)}, u32[]{:S(2)}, u32[]{:S(2)}) %collective-permute-start.3) | collective-permute-done | bytes 1048608 | tf_op jit(solution)/shard_map/ppermute | solution.py:28
  47.6 13.5 %shard_map.140 = bf16[2048,256]{1,0:T(8,128)(2,1)} custom-call(s32[64]{0:T(128)} %reshape_squeeze.6.src_ids, s32[16,4,128,128]{3,2,1,0:T(8,128)} %bitcast.60, bf16[16,128,256]{2,1,0:T(8,128)(2,1)} %bitcast.4.own, bf16[16,128,256]{2,1,0:T(8,128)(2,1)} %bitcast.5.up, bf16[16,128,256]{2,1,0:T(8,128)(2,1)} %bitcast.6.down, bf16[16,128,256]{2,1,0:T(8,128)(2,1)} %bitcast.7.left, ...), custom_call_target="tpu_custom_call" | custom-call | tf_op jit(solution)/shard_map/pallas_call | solution.py:52
  61.1 3.1 %convolution_add_fusion.4 = f32[2048,256]{1,0:T(8,128)} fusion(f32[2048,256]{1,0:T(8,128)S(1)} %fusion.11, bf16[2048,256]{1,0:T(8,128)(2,1)} %shard_map.140, bf16[512,256]{1,0:T(8,128)(2,1)} %param.20), kind=kOutput, calls=%fused_computation.7 | convolution fusion | flops 268959744 | bytes 5373952 | tf_op jit(solution)/shard_map/dot_general | solution.py:181
  64.2 3.4 %convolution_convert_fusion.4.q_ref = bf16[2048,256]{1,0:T(8,128)(2,1)} fusion(bf16[256,256]{1,0:T(8,128)(2,1)S(1)} %copy-done.11, bf16[256,256]{1,0:T(8,128)(2,1)} %param.21, f32[2048,256]{1,0:T(8,128)} %convolution_add_fusion.4, bf16[1,1,2048,256]{3,2,1,0:T(8,128)(2,1)S(1)} %copy-done.1), kind=kOutput, calls=%fused_computation.15 | convolution fusion | flops 541589504 | bytes 4456448 | tf_op jit(solution)/shard_map/dot_general | solution.py:181
  67.6 22.1 %shard_map.141 = (bf16[2048,256]{1,0:T(8,128)(2,1)}, bf16[2048,512]{1,0:T(8,128)(2,1)}) custom-call(f32[1,2048]{1,0:T(1,128)} %reshape.73.live_ref, bf16[2048,256]{1,0:T(8,128)(2,1)} %convolution_convert_fusion.4.q_ref, bf16[2048,256]{1,0:T(8,128)(2,1)} %convolution_convert_fusion.3.go_ref, bf16[2048,512]{1,0:T(8,128)(2,1)} %convolution_convert_fusion.kv_ref), custom_call_target="tpu_custom_call" | custom-call | flops 10737418240 | bytes 7340032 | tf_op jit(solution)/shard_map/pallas_call | solution.py:153
  89.7 1.8 %convolution_add_fusion.2 = f32[2048,256]{1,0:T(8,128)S(1)} fusion(bf16[2048,256]{1,0:T(8,128)(2,1)} %get-tuple-element.6, bf16[256,256]{1,0:T(8,128)(2,1)S(1)} %copy-done.11, bf16[1,1,2048,256]{3,2,1,0:T(8,128)(2,1)S(1)} %copy-done.3), kind=kOutput, calls=%fused_computation.5 | convolution fusion | flops 269484032 | bytes 4325376 | tf_op jit(solution)/shard_map/dot_general | solution.py:181
  91.6 1.0 fusion.1
  92.6 1.0 copy-done.4
  93.6 1.4 convolution_convert_fusion.2.grad_ref
  95.0 15.0 %shard_map.142 = (f32[16,128,256]{2,1,0:T(8,128)}, bf16[4,16,128,256]{3,2,1,0:T(8,128)(2,1)}) custom-call(s32[64]{0:T(128)} %reshape_squeeze.6.src_ids, s32[16,4,128,128]{3,2,1,0:T(8,128)} %bitcast.61, bf16[2048,256]{1,0:T(8,128)(2,1)} %convolution_convert_fusion.2.grad_ref), custom_call_target="tpu_custom_call" | custom-call | tf_op jit(solution)/shard_map/pallas_call | solution.py:91
  110.0 4.5 %fusion.27 = (bf16[1,16,128,256]{3,2,1,0:T(8,128)(2,1)}, bf16[1,16,128,256]{3,2,1,0:T(8,128)(2,1)}, bf16[1,16,128,256]{3,2,1,0:T(8,128)(2,1)}, bf16[1,16,128,256]{3,2,1,0:T(8,128)(2,1)}) fusion(bf16[4,16,128,256]{3,2,1,0:T(8,128)(2,1)} %get-tuple-element.8), kind=kLoop, calls=%fused_computation.44 | loop fusion | bytes 8388608 | tf_op jit(solution)/shard_map/slice | solution.py:253
  114.5 4.5 %collective-permute-start.7 = (bf16[2048,256]{1,0:T(8,128)(2,1)}, bf16[2048,256]{1,0:T(8,128)(2,1)}, u32[]{:S(2)}, u32[]{:S(2)}) collective-permute-start(bf16[2048,256]{1,0:T(8,128)(2,1)} %bitcast.15), channel_id=1, source_target_pairs={{0,1},{1,2},{2,3},{3,4},{4,5},{5,6},{6,7},{7,8},{8,9},{9,10},{10,1... | collective-permute-start | bytes 3145736 | tf_op jit(solution)/shard_map/ppermute | solution.py:28
  119.0 2.9 %collective-permute-start.4 = (bf16[2048,256]{1,0:T(8,128)(2,1)}, bf16[2048,256]{1,0:T(8,128)(2,1)}, u32[]{:S(2)}, u32[]{:S(2)}) collective-permute-start(bf16[2048,256]{1,0:T(8,128)(2,1)} %bitcast.12), channel_id=1, source_target_pairs={{16,0},{32,16},{48,32},{64,48},{80,64},{96,80},{112,96},{17,1},{33... | collective-permute-start | bytes 3145736 | tf_op jit(solution)/shard_map/ppermute | solution.py:28
  121.8 1.3 collective-permute-start.6
  123.1 3.4 %collective-permute-start.5 = (bf16[2048,256]{1,0:T(8,128)(2,1)}, bf16[2048,256]{1,0:T(8,128)(2,1)}, u32[]{:S(2)}, u32[]{:S(2)}) collective-permute-start(bf16[2048,256]{1,0:T(8,128)(2,1)} %bitcast.13), channel_id=1, source_target_pairs={{0,16},{16,32},{32,48},{48,64},{64,80},{80,96},{96,112},{1,17},{17... | collective-permute-start | bytes 3145736 | tf_op jit(solution)/shard_map/ppermute | solution.py:28
  126.6 1.7 convolution_convert_fusion.1
  128.3 10.4 %all-to-all-start.1 = ((bf16[128,16,256]{2,1,0:T(8,128)(2,1)}), bf16[128,16,256]{2,1,0:T(8,128)(2,1)S(1)}, u32[]{:S(2)}, u32[]{:S(2)}) async-start(bf16[128,16,256]{2,1,0:T(8,128)(2,1)} %bitcast.63), calls=%async_computation.1 | async-start | bytes 2097152 | tf_op jit(solution)/shard_map/all_to_all | solution.py:236
  138.7 3.1 %convolution_add_fusion.1 = f32[2048,256]{1,0:T(8,128)} fusion(f32[2048,256]{1,0:T(8,128)S(1)} %convolution_add_fusion.2, bf16[2048,256]{1,0:T(8,128)(2,1)} %copy-done.4, bf16[512,256]{1,0:T(8,128)(2,1)} %param.20), kind=kOutput, calls=%fused_computation.3 | convolution fusion | flops 268959744 | bytes 5373952 | tf_op jit(solution)/shard_map/dot_general | solution.py:181
  141.8 31.2 %all-to-all-done.1 = bf16[128,16,256]{2,1,0:T(8,128)(2,1)S(1)} async-done(((bf16[128,16,256]{2,1,0:T(8,128)(2,1)}), bf16[128,16,256]{2,1,0:T(8,128)(2,1)S(1)}, u32[]{:S(2)}, u32[]{:S(2)}) %all-to-all-start.1) | async-done | bytes 1048608 | tf_op jit(solution)/shard_map/all_to_all | solution.py:236
  173.0 4.5 %fusion.8 = bf16[2048,256]{1,0:T(8,128)(2,1)} fusion(f32[16,128,256]{2,1,0:T(8,128)} %get-tuple-element.7, bf16[2048,256]{1,0:T(8,128)(2,1)} %collective-permute-done.7, bf16[2048,256]{1,0:T(8,128)(2,1)} %collective-permute-done.6, bf16[2048,256]{1,0:T(8,128)(2,1)} %collective-permute-done.5, bf16[2048,256]{1,0:T(8,128)(2,1)} %collective-permute-done.4), kind=kLoop, calls=%fused_computation.22 | loop fusion | flops 4718592 | bytes 7340032 | tf_op jit(solution)/shard_map/convert_element_type | solution.py:256
  177.5 4.0 %fusion.4 = bf16[1,1,2048,256]{3,2,1,0:T(8,128)(2,1)} fusion(f32[2048,256]{1,0:T(8,128)} %convolution_add_fusion.1, bf16[256,256]{1,0:T(8,128)(2,1)S(1)} %copy-done.13, bf16[2048,256]{1,0:T(8,128)(2,1)} %fusion.8, bf16[256,256]{1,0:T(8,128)(2,1)} %param.19, f32[2048,256]{1,0:T(8,128)S(1)} %copy-done.6), kind=kOutput, calls=%fused_computation.17 | convolution fusion | flops 542638080 | bytes 6553600 | tf_op jit(solution)/shard_map/dot_general | solution.py:181
  181.5 1.0 copy.18
  (47 shorter events, 1.9 us)
Async XLA Ops:
  0.6 31.4 %copy-start = (bf16[256,512]{1,0:T(8,128)(2,1)S(1)}, bf16[256,512]{1,0:T(8,128)(2,1)}, u32[]{:S(2)}) copy-start(bf16[256,512]{1,0:T(8,128)(2,1)} %param.23) | copy-start | bytes 786436
  0.6 12.0 %copy-start.1 = (bf16[1,1,2048,256]{3,2,1,0:T(8,128)(2,1)S(1)}, bf16[1,1,2048,256]{3,2,1,0:T(8,128)(2,1)}, u32[]{:S(2)}) copy-start(bf16[1,1,2048,256]{3,2,1,0:T(8,128)(2,1)} %param.13) | copy-start | bytes 3145732
  0.7 12.0 %copy-start.12 = (bf16[256,256]{1,0:T(8,128)(2,1)S(1)}, bf16[256,256]{1,0:T(8,128)(2,1)}, u32[]{:S(2)}) copy-start(bf16[256,256]{1,0:T(8,128)(2,1)} %param.18) | copy-start | bytes 393220
  0.7 31.4 %all-to-all-start = ((bf16[128,16,256]{2,1,0:T(8,128)(2,1)}), bf16[128,16,256]{2,1,0:T(8,128)(2,1)}, u32[]{:S(2)}, u32[]{:S(2)}) async-start(bf16[128,16,256]{2,1,0:T(8,128)(2,1)} %bitcast.64), calls=%async_computation | async-start | bytes 2097152 | tf_op jit(solution)/shard_map/all_to_all | solution.py:225
  12.6 0.9 copy-start.17
  13.6 1.7 copy-start.5
  13.6 14.2 %copy-start.14 = (s32[1,1,16,4]{2,3,1,0:T(4,128)S(1)}, s32[1,1,16,4]{2,3,1,0:T(4,128)}, u32[]{:S(2)}) copy-start(s32[1,1,16,4]{2,3,1,0:T(4,128)} %param.14) | copy-start | bytes 772
  13.6 14.9 %copy-start.15 = (s32[128,1]{0,1:T(1,128)S(1)}, s32[128,1]{0,1:T(1,128)}, u32[]{:S(2)}) copy-start(s32[128,1]{0,1:T(1,128)} %param.17) | copy-start | bytes 1540
  13.6 15.7 %copy-start.2 = (bf16[1,1,2048,256]{3,2,1,0:T(8,128)(2,1)S(1)}, bf16[1,1,2048,256]{3,2,1,0:T(8,128)(2,1)}, u32[]{:S(2)}) copy-start(bf16[1,1,2048,256]{3,2,1,0:T(8,128)(2,1)} %param.25) | copy-start | bytes 3145732
  13.6 15.7 %copy-start.10 = (bf16[256,256]{1,0:T(8,128)(2,1)S(1)}, bf16[256,256]{1,0:T(8,128)(2,1)}, u32[]{:S(2)}) copy-start(bf16[256,256]{1,0:T(8,128)(2,1)} %param.24) | copy-start | bytes 393220
  15.2 32.3 %collective-permute-start.3 = (bf16[2048,256]{1,0:T(8,128)(2,1)}, bf16[2048,256]{1,0:T(8,128)(2,1)}, u32[]{:S(2)}, u32[]{:S(2)}) collective-permute-start(bf16[2048,256]{1,0:T(8,128)(2,1)} %convolution_convert_fusion.5), channel_id=1, source_target_pairs={{1,0},{2,1},{3,2},{4,3},{5,4},{6,5},{7,6},{8,7},{9,8},{10,9},{11,1... | collective-permute-start | bytes 3145736 | tf_op jit(solution)/shard_map/ppermute | solution.py:28
  16.5 31.0 %collective-permute-start.2 = (bf16[2048,256]{1,0:T(8,128)(2,1)}, bf16[2048,256]{1,0:T(8,128)(2,1)}, u32[]{:S(2)}, u32[]{:S(2)}) collective-permute-start(bf16[2048,256]{1,0:T(8,128)(2,1)} %convolution_convert_fusion.5), channel_id=1, source_target_pairs={{0,1},{1,2},{2,3},{3,4},{4,5},{5,6},{6,7},{7,8},{8,9},{9,10},{10,1... | collective-permute-start | bytes 3145736 | tf_op jit(solution)/shard_map/ppermute | solution.py:28
  21.6 26.0 %collective-permute-start.1 = (bf16[2048,256]{1,0:T(8,128)(2,1)}, bf16[2048,256]{1,0:T(8,128)(2,1)}, u32[]{:S(2)}, u32[]{:S(2)}) collective-permute-start(bf16[2048,256]{1,0:T(8,128)(2,1)} %convolution_convert_fusion.5), channel_id=1, source_target_pairs={{16,0},{32,16},{48,32},{64,48},{80,64},{96,80},{112,96},{17,1},{33... | collective-permute-start | bytes 3145736 | tf_op jit(solution)/shard_map/ppermute | solution.py:28
  25.2 22.4 %collective-permute-start = (bf16[2048,256]{1,0:T(8,128)(2,1)}, bf16[2048,256]{1,0:T(8,128)(2,1)}, u32[]{:S(2)}, u32[]{:S(2)}) collective-permute-start(bf16[2048,256]{1,0:T(8,128)(2,1)} %convolution_convert_fusion.5), channel_id=1, source_target_pairs={{0,16},{16,32},{32,48},{48,64},{64,80},{80,96},{96,112},{1,17},{17... | collective-permute-start | bytes 3145736 | tf_op jit(solution)/shard_map/ppermute | solution.py:28
  61.1 3.1 %copy-start.11 = (bf16[256,256]{1,0:T(8,128)(2,1)S(1)}, bf16[256,256]{1,0:T(8,128)(2,1)}, u32[]{:S(2)}) copy-start(bf16[256,256]{1,0:T(8,128)(2,1)} %param.22) | copy-start | bytes 393220
  67.6 22.1 %copy-start.3 = (bf16[1,1,2048,256]{3,2,1,0:T(8,128)(2,1)S(1)}, bf16[1,1,2048,256]{3,2,1,0:T(8,128)(2,1)}, u32[]{:S(2)}) copy-start(bf16[1,1,2048,256]{3,2,1,0:T(8,128)(2,1)} %param.25) | copy-start | bytes 3145732
  89.7 1.9 %copy-start.8 = (f32[2048,256]{1,0:T(8,128)S(1)}, f32[2048,256]{1,0:T(8,128)}, u32[]{:S(2)}) copy-start(f32[2048,256]{1,0:T(8,128)} %convolution_add_fusion.4) | copy-start | bytes 6291460
  89.7 1.9 %copy-start.16 = (bf16[256,256]{1,0:T(8,128)(2,1)S(1)}, bf16[256,256]{1,0:T(8,128)(2,1)}, u32[]{:S(2)}) copy-start(bf16[256,256]{1,0:T(8,128)(2,1)} %param.21) | copy-start | bytes 393220
  91.6 2.0 %copy-start.9 = (bf16[512,256]{1,0:T(8,128)(2,1)S(1)}, bf16[512,256]{1,0:T(8,128)(2,1)}, u32[]{:S(2)}) copy-start(bf16[512,256]{1,0:T(8,128)(2,1)} %param.20) | copy-start | bytes 786436
  92.6 1.0 copy-start.4
  110.0 16.5 %copy-start.7 = (bf16[2048,512]{1,0:T(8,128)(2,1)S(1)}, bf16[2048,512]{1,0:T(8,128)(2,1)}, u32[]{:S(2)}) copy-start(bf16[2048,512]{1,0:T(8,128)(2,1)} %get-tuple-element.9) | copy-start | bytes 6291460
  114.5 58.5 %collective-permute-start.7 = (bf16[2048,256]{1,0:T(8,128)(2,1)}, bf16[2048,256]{1,0:T(8,128)(2,1)}, u32[]{:S(2)}, u32[]{:S(2)}) collective-permute-start(bf16[2048,256]{1,0:T(8,128)(2,1)} %bitcast.15), channel_id=1, source_target_pairs={{0,1},{1,2},{2,3},{3,4},{4,5},{5,6},{6,7},{7,8},{8,9},{9,10},{10,1... | collective-permute-start | bytes 3145736 | tf_op jit(solution)/shard_map/ppermute | solution.py:28
  119.0 54.0 %collective-permute-start.4 = (bf16[2048,256]{1,0:T(8,128)(2,1)}, bf16[2048,256]{1,0:T(8,128)(2,1)}, u32[]{:S(2)}, u32[]{:S(2)}) collective-permute-start(bf16[2048,256]{1,0:T(8,128)(2,1)} %bitcast.12), channel_id=1, source_target_pairs={{16,0},{32,16},{48,32},{64,48},{80,64},{96,80},{112,96},{17,1},{33... | collective-permute-start | bytes 3145736 | tf_op jit(solution)/shard_map/ppermute | solution.py:28
  121.8 51.2 %collective-permute-start.6 = (bf16[2048,256]{1,0:T(8,128)(2,1)}, bf16[2048,256]{1,0:T(8,128)(2,1)}, u32[]{:S(2)}, u32[]{:S(2)}) collective-permute-start(bf16[2048,256]{1,0:T(8,128)(2,1)} %bitcast.14), channel_id=1, source_target_pairs={{1,0},{2,1},{3,2},{4,3},{5,4},{6,5},{7,6},{8,7},{9,8},{10,9},{11,1... | collective-permute-start | bytes 3145736 | tf_op jit(solution)/shard_map/ppermute | solution.py:28
  123.1 49.9 %collective-permute-start.5 = (bf16[2048,256]{1,0:T(8,128)(2,1)}, bf16[2048,256]{1,0:T(8,128)(2,1)}, u32[]{:S(2)}, u32[]{:S(2)}) collective-permute-start(bf16[2048,256]{1,0:T(8,128)(2,1)} %bitcast.13), channel_id=1, source_target_pairs={{0,16},{16,32},{32,48},{48,64},{64,80},{80,96},{96,112},{1,17},{17... | collective-permute-start | bytes 3145736 | tf_op jit(solution)/shard_map/ppermute | solution.py:28
  128.3 44.7 %all-to-all-start.1 = ((bf16[128,16,256]{2,1,0:T(8,128)(2,1)}), bf16[128,16,256]{2,1,0:T(8,128)(2,1)S(1)}, u32[]{:S(2)}, u32[]{:S(2)}) async-start(bf16[128,16,256]{2,1,0:T(8,128)(2,1)} %bitcast.63), calls=%async_computation.1 | async-start | bytes 2097152 | tf_op jit(solution)/shard_map/all_to_all | solution.py:236
  173.0 4.5 %copy-start.6 = (f32[2048,256]{1,0:T(8,128)S(1)}, f32[2048,256]{1,0:T(8,128)}, u32[]{:S(2)}) copy-start(f32[2048,256]{1,0:T(8,128)} %copy-done.5) | copy-start | bytes 6291460
  173.0 4.5 %copy-start.13 = (bf16[256,256]{1,0:T(8,128)(2,1)S(1)}, bf16[256,256]{1,0:T(8,128)(2,1)}, u32[]{:S(2)}) copy-start(bf16[256,256]{1,0:T(8,128)(2,1)} %param.18) | copy-start | bytes 393220

commit v5 on v4

--- a/solution.py
+++ b/solution.py
@@ -28,56 +28,70 @@
     return lax.ppermute(value, axis, [(source, source + steps) for source in range(leading, last)])
 
 
-def gather_kernel(src_ids, mask_ref, own, up, down, left, right, out_ref):
-    b = pl.program_id(0)
+def gather_kernel(group, src_ids, mask_ref, own, up, down, left, right, out_ref, rhs):
+    step = pl.program_id(0)
     tiles = mask_ref.shape[1]
+    blk = mask_ref.shape[2]
     per_side = own.shape[0]
-    total = jnp.zeros(out_ref.shape, jnp.float32)
-    for k in range(tiles):
-        picked = src_ids[b * tiles + k]
-        side = picked // per_side
-        block = picked % per_side
-        bits = mask_ref[0, k].astype(jnp.float32).astype(jnp.bfloat16)
-        rows = own[block]
-        for index, ref in enumerate((up, down, left, right)):
-            rows = jnp.where(side == index + 1, ref[block], rows)
-        total = total + jnp.dot(bits, rows, preferred_element_type=jnp.float32)
-    out_ref[...] = total.astype(out_ref.dtype)
-
-
-def tile_gather(src_ids, tile_mask, sources):
+    for g in range(group):
+        for k in range(tiles):
+            picked = src_ids[(step * group + g) * tiles + k]
+            side = picked // per_side
+            block = picked % per_side
+            for index, ref in enumerate((own, up, down, left, right)):
+
+                @pl.when(side == index)
+                def _():
+                    rhs[k * blk : (k + 1) * blk, :] = ref[block]
+
+        bits = jnp.concatenate(
+            [mask_ref[g, k].astype(jnp.float32).astype(jnp.bfloat16) for k in range(tiles)], axis=1
+        )
+        total = jnp.dot(bits, rhs[...], preferred_element_type=jnp.float32)
+        out_ref[g * blk : (g + 1) * blk, :] = total.astype(out_ref.dtype)
+
+
+def tile_gather(src_ids, tile_mask, sources, group=4):
     blocks, tiles, blk, _ = tile_mask.shape
     width = sources[0].shape[-1]
-    whole = pl.BlockSpec((blocks, blk, width), lambda b, ids: (0, 0, 0))
+    whole = pl.BlockSpec((blocks, blk, width), lambda i, ids: (0, 0, 0))
     return pl.pallas_call(
-        gather_kernel,
+        functools.partial(gather_kernel, group),
         grid_spec=pltpu.PrefetchScalarGridSpec(
             num_scalar_prefetch=1,
-            grid=(blocks,),
-            in_specs=[pl.BlockSpec((1, tiles, blk, blk), lambda b, ids: (b, 0, 0, 0))]
+            grid=(blocks // group,),
+            in_specs=[pl.BlockSpec((group, tiles, blk, blk), lambda i, ids: (i, 0, 0, 0))]
             + [whole] * len(sources),
-            out_specs=pl.BlockSpec((blk, width), lambda b, ids: (b, 0)),
+            out_specs=pl.BlockSpec((group * blk, width), lambda i, ids: (i, 0)),
+            scratch_shapes=[pltpu.VMEM((tiles * blk, width), jnp.bfloat16)],
         ),
         out_shape=jax.ShapeDtypeStruct((blocks * blk, width), jnp.bfloat16),
+        compiler_params=pltpu.CompilerParams(dimension_semantics=("arbitrary",)),
     )(src_ids, tile_mask, *sources)
 
 
-def scatter_kernel(src_ids, mask_ref, grad_ref, own_ref, out_ref, total):
-    b = pl.program_id(0)
+def scatter_kernel(group, src_ids, mask_ref, grad_ref, own_ref, out_ref, total):
+    step = pl.program_id(0)
     tiles = mask_ref.shape[1]
+    blk = mask_ref.shape[2]
     per_side = own_ref.shape[0]
-
-    @pl.when(b == 0)
+    tn = (((0,), (0,)), ((), ()))
+
+    @pl.when(step == 0)
     def _():
         total[...] = jnp.zeros(total.shape, jnp.float32)
 
-    grad_rows = grad_ref[...]
-    for k in range(tiles):
-        picked = src_ids[b * tiles + k]
-        bits = mask_ref[0, k].astype(jnp.float32).T.astype(jnp.bfloat16)
-        total[picked] += jnp.dot(bits, grad_rows, preferred_element_type=jnp.float32)
-
-    @pl.when(b == pl.num_programs(0) - 1)
+    for g in range(group):
+        bits = jnp.concatenate(
+            [mask_ref[g, k].astype(jnp.float32).astype(jnp.bfloat16) for k in range(tiles)], axis=1
+        )
+        grad_rows = grad_ref[g * blk : (g + 1) * blk, :]
+        parts = lax.dot_general(bits, grad_rows, tn, preferred_element_type=jnp.float32)
+        for k in range(tiles):
+            picked = src_ids[(step * group + g) * tiles + k]
+            total[picked] += parts[k * blk : (k + 1) * blk]
+
+    @pl.when(step == pl.num_programs(0) - 1)
     def _():
         own_ref[...] = total[0:per_side]
         for side in range(out_ref.shape[0]):
@@ -85,21 +99,21 @@
             out_ref[side] = total[start : start + per_side].astype(out_ref.dtype)
 
 
-def tile_scatter(src_ids, tile_mask, grad_agg, sides):
+def tile_scatter(src_ids, tile_mask, grad_agg, sides, group=4):
     blocks, tiles, blk, _ = tile_mask.shape
     width = grad_agg.shape[-1]
     return pl.pallas_call(
-        scatter_kernel,
+        functools.partial(scatter_kernel, group),
         grid_spec=pltpu.PrefetchScalarGridSpec(
             num_scalar_prefetch=1,
-            grid=(blocks,),
+            grid=(blocks // group,),
             in_specs=[
-                pl.BlockSpec((1, tiles, blk, blk), lambda b, ids: (b, 0, 0, 0)),
-                pl.BlockSpec((blk, width), lambda b, ids: (b, 0)),
+                pl.BlockSpec((group, tiles, blk, blk), lambda i, ids: (i, 0, 0, 0)),
+                pl.BlockSpec((group * blk, width), lambda i, ids: (i, 0)),
             ],
             out_specs=[
-                pl.BlockSpec((blocks, blk, width), lambda b, ids: (0, 0, 0)),
-                pl.BlockSpec((sides - 1, blocks, blk, width), lambda b, ids: (0, 0, 0, 0)),
+                pl.BlockSpec((blocks, blk, width), lambda i, ids: (0, 0, 0)),
+                pl.BlockSpec((sides - 1, blocks, blk, width), lambda i, ids: (0, 0, 0, 0)),
             ],
             scratch_shapes=[pltpu.VMEM((sides * blocks, blk, width), jnp.float32)],
         ),

time: 184 us -> 173 us (0.940)
  Pallas kernels: 50.6 us -> 40.7 us
    pallas_call x2, Pallas kernels: 28.5 us -> 18.6 us  [the longest x1 9.84 us: tile_gather(): pl.pallas_call(functools.partial(gather_kernel, group), grid_spec=pltpu.P...]
where the time goes in v5:
time: 173 us
  starting transfers between devices  46.6 us (27%)
  waiting for transfers between devices  43.7 us (25%)
  Pallas kernels  40.7 us (24%)
  matrix products  27.7 us (16%)
  local copies, waits for them, and re-layouts  8.43 us (5%)
  other arithmetic  4.58 us (3%)
    all_to_all x1, waiting for transfers between devices, on_device(): lax.all_to_all(grad_slots.reshape(devices, slot_count, latent_width), ('p...  31.4 us
    dot_general x13, matrix products, dense(): return jnp.dot(left, right, preferred_element_type=jnp.float32)  27.7 us
    ppermute x8, starting transfers between devices, passed_along(): lax.ppermute(value, axis, [(source, source + steps) for source in range(l...  24.3 us
    pallas_call x1, Pallas kernels, attend_back(): pl.pallas_call(functools.partial(attend_kernel, scale), grid=(steps,), in...  22.1 us
    ppermute x8, waiting for transfers between devices, passed_along(): lax.ppermute(value, axis, [(source, source + steps) for source in range(l...  12.3 us
    all_to_all x1, starting transfers between devices, on_device(): lax.all_to_all(token_groups, ('px', 'py'), split_axis=0, concat_axis=0, t...  12 us
    all_to_all x1, starting transfers between devices, on_device(): lax.all_to_all(grad_slots.reshape(devices, slot_count, latent_width), ('p...  10.4 us
    pallas_call x1, Pallas kernels, tile_gather(): pl.pallas_call(functools.partial(gather_kernel, group), grid_spec=pltpu.P...  9.84 us
  transfers between devices with their start and end apart: 10, of which 2 were waited for; matrix products, arithmetic and copies ran while one was open for 8% of the time, Pallas kernels for 0%

profile of v5, /device:TPU:1, one launch (start us, length us, event | category | flops | bytes accessed | tf_op | source)
XLA Modules:
  0.0 172.6 jit_solution(4349408582824039604)
XLA Ops:
  0.7 12.0 %all-to-all-start = ((bf16[128,16,256]{2,1,0:T(8,128)(2,1)}), bf16[128,16,256]{2,1,0:T(8,128)(2,1)}, u32[]{:S(2)}, u32[]{:S(2)}) async-start(bf16[128,16,256]{2,1,0:T(8,128)(2,1)} %bitcast.64), calls=%async_computation | async-start | bytes 2097152 | tf_op jit(solution)/shard_map/all_to_all | solution.py:239
  13.6 1.7 convolution_convert_fusion.5
  15.2 1.3 collective-permute-start.3
  16.5 5.0 %collective-permute-start.2 = (bf16[2048,256]{1,0:T(8,128)(2,1)}, bf16[2048,256]{1,0:T(8,128)(2,1)}, u32[]{:S(2)}, u32[]{:S(2)}) collective-permute-start(bf16[2048,256]{1,0:T(8,128)(2,1)} %convolution_convert_fusion.5), channel_id=1, source_target_pairs={{0,1},{1,2},{2,3},{3,4},{4,5},{5,6},{6,7},{7,8},{8,9},{9,10},{10,1... | collective-permute-start | bytes 3145736 | tf_op jit(solution)/shard_map/ppermute | solution.py:28
  21.6 3.6 %collective-permute-start.1 = (bf16[2048,256]{1,0:T(8,128)(2,1)}, bf16[2048,256]{1,0:T(8,128)(2,1)}, u32[]{:S(2)}, u32[]{:S(2)}) collective-permute-start(bf16[2048,256]{1,0:T(8,128)(2,1)} %convolution_convert_fusion.5), channel_id=1, source_target_pairs={{16,0},{32,16},{48,32},{64,48},{80,64},{96,80},{112,96},{17,1},{33... | collective-permute-start | bytes 3145736 | tf_op jit(solution)/shard_map/ppermute | solution.py:28
  25.2 2.5 %collective-permute-start = (bf16[2048,256]{1,0:T(8,128)(2,1)}, bf16[2048,256]{1,0:T(8,128)(2,1)}, u32[]{:S(2)}, u32[]{:S(2)}) collective-permute-start(bf16[2048,256]{1,0:T(8,128)(2,1)} %convolution_convert_fusion.5), channel_id=1, source_target_pairs={{0,16},{16,32},{32,48},{48,64},{64,80},{80,96},{96,112},{1,17},{17... | collective-permute-start | bytes 3145736 | tf_op jit(solution)/shard_map/ppermute | solution.py:28
  28.6 0.7 reshape.73.live_ref
  29.3 1.4 convolution_convert_fusion.3.go_ref
  30.7 1.3 fusion.11
  32.0 3.3 %convolution_convert_fusion.kv_ref = bf16[2048,512]{1,0:T(8,128)(2,1)} fusion(bf16[2048,256]{1,0:T(8,128)(2,1)} %bitcast.10, bf16[256,512]{1,0:T(8,128)(2,1)S(1)} %copy-done), kind=kOutput, calls=%fused_computation | convolution fusion | flops 537919488 | bytes 3407872 | tf_op jit(solution)/shard_map/dot_general | solution.py:195
  35.3 12.3 %collective-permute-done.3 = bf16[2048,256]{1,0:T(8,128)(2,1)} collective-permute-done((bf16[2048,256]{1,0:T(8,128)(2,1)}, bf16[2048,256]{1,0:T(8,128)(2,1)}, u32[]{:S(2)}, u32[]{:S(2)}) %collective-permute-start.3) | collective-permute-done | bytes 1048608 | tf_op jit(solution)/shard_map/ppermute | solution.py:28
  47.6 9.8 %shard_map.140 = bf16[2048,256]{1,0:T(8,128)(2,1)} custom-call(s32[64]{0:T(128)} %reshape_squeeze.6.src_ids, s32[16,4,128,128]{3,2,1,0:T(8,128)} %bitcast.60, bf16[16,128,256]{2,1,0:T(8,128)(2,1)} %bitcast.4.own, bf16[16,128,256]{2,1,0:T(8,128)(2,1)} %bitcast.5.up, bf16[16,128,256]{2,1,0:T(8,128)(2,1)} %bitcast.6.down, bf16[16,128,256]{2,1,0:T(8,128)(2,1)} %bitcast.7.left, ...), custom_call_target="tpu_custom_call" | custom-call | tf_op jit(solution)/shard_map/pallas_call | solution.py:58
  57.4 3.1 %convolution_add_fusion.4 = f32[2048,256]{1,0:T(8,128)} fusion(f32[2048,256]{1,0:T(8,128)S(1)} %fusion.11, bf16[2048,256]{1,0:T(8,128)(2,1)} %shard_map.140, bf16[512,256]{1,0:T(8,128)(2,1)} %param.20), kind=kOutput, calls=%fused_computation.7 | convolution fusion | flops 268959744 | bytes 5373952 | tf_op jit(solution)/shard_map/dot_general | solution.py:195
  60.5 3.4 %convolution_convert_fusion.4.q_ref = bf16[2048,256]{1,0:T(8,128)(2,1)} fusion(bf16[256,256]{1,0:T(8,128)(2,1)S(1)} %copy-done.11, bf16[256,256]{1,0:T(8,128)(2,1)} %param.21, f32[2048,256]{1,0:T(8,128)} %convolution_add_fusion.4, bf16[1,1,2048,256]{3,2,1,0:T(8,128)(2,1)S(1)} %copy-done.1), kind=kOutput, calls=%fused_computation.15 | convolution fusion | flops 541589504 | bytes 4456448 | tf_op jit(solution)/shard_map/dot_general | solution.py:195
  64.0 22.1 %shard_map.141 = (bf16[2048,256]{1,0:T(8,128)(2,1)}, bf16[2048,512]{1,0:T(8,128)(2,1)}) custom-call(f32[1,2048]{1,0:T(1,128)} %reshape.73.live_ref, bf16[2048,256]{1,0:T(8,128)(2,1)} %convolution_convert_fusion.4.q_ref, bf16[2048,256]{1,0:T(8,128)(2,1)} %convolution_convert_fusion.3.go_ref, bf16[2048,512]{1,0:T(8,128)(2,1)} %convolution_convert_fusion.kv_ref), custom_call_target="tpu_custom_call" | custom-call | flops 10737418240 | bytes 7340032 | tf_op jit(solution)/shard_map/pallas_call | solution.py:167
  86.1 1.8 %convolution_add_fusion.2 = f32[2048,256]{1,0:T(8,128)S(1)} fusion(bf16[2048,256]{1,0:T(8,128)(2,1)} %get-tuple-element.6, bf16[256,256]{1,0:T(8,128)(2,1)S(1)} %copy-done.11, bf16[1,1,2048,256]{3,2,1,0:T(8,128)(2,1)S(1)} %copy-done.3), kind=kOutput, calls=%fused_computation.5 | convolution fusion | flops 269484032 | bytes 4325376 | tf_op jit(solution)/shard_map/dot_general | solution.py:195
  88.0 1.0 fusion.1
  89.0 1.0 copy-done.4
  89.9 1.4 convolution_convert_fusion.2.grad_ref
  91.4 8.8 %shard_map.142 = (f32[16,128,256]{2,1,0:T(8,128)}, bf16[4,16,128,256]{3,2,1,0:T(8,128)(2,1)}) custom-call(s32[64]{0:T(128)} %reshape_squeeze.6.src_ids, s32[16,4,128,128]{3,2,1,0:T(8,128)} %bitcast.61, bf16[2048,256]{1,0:T(8,128)(2,1)} %convolution_convert_fusion.2.grad_ref), custom_call_target="tpu_custom_call" | custom-call | tf_op jit(solution)/shard_map/pallas_call | solution.py:105
  100.2 4.5 %fusion.27 = (bf16[1,16,128,256]{3,2,1,0:T(8,128)(2,1)}, bf16[1,16,128,256]{3,2,1,0:T(8,128)(2,1)}, bf16[1,16,128,256]{3,2,1,0:T(8,128)(2,1)}, bf16[1,16,128,256]{3,2,1,0:T(8,128)(2,1)}) fusion(bf16[4,16,128,256]{3,2,1,0:T(8,128)(2,1)} %get-tuple-element.8), kind=kLoop, calls=%fused_computation.44 | loop fusion | bytes 8388608 | tf_op jit(solution)/shard_map/slice | solution.py:267
  104.7 4.5 %collective-permute-start.7 = (bf16[2048,256]{1,0:T(8,128)(2,1)}, bf16[2048,256]{1,0:T(8,128)(2,1)}, u32[]{:S(2)}, u32[]{:S(2)}) collective-permute-start(bf16[2048,256]{1,0:T(8,128)(2,1)} %bitcast.15), channel_id=1, source_target_pairs={{0,1},{1,2},{2,3},{3,4},{4,5},{5,6},{6,7},{7,8},{8,9},{9,10},{10,1... | collective-permute-start | bytes 3145736 | tf_op jit(solution)/shard_map/ppermute | solution.py:28
  109.1 2.8 %collective-permute-start.4 = (bf16[2048,256]{1,0:T(8,128)(2,1)}, bf16[2048,256]{1,0:T(8,128)(2,1)}, u32[]{:S(2)}, u32[]{:S(2)}) collective-permute-start(bf16[2048,256]{1,0:T(8,128)(2,1)} %bitcast.12), channel_id=1, source_target_pairs={{16,0},{32,16},{48,32},{64,48},{80,64},{96,80},{112,96},{17,1},{33... | collective-permute-start | bytes 3145736 | tf_op jit(solution)/shard_map/ppermute | solution.py:28
  112.0 1.3 collective-permute-start.6
  113.3 3.2 %collective-permute-start.5 = (bf16[2048,256]{1,0:T(8,128)(2,1)}, bf16[2048,256]{1,0:T(8,128)(2,1)}, u32[]{:S(2)}, u32[]{:S(2)}) collective-permute-start(bf16[2048,256]{1,0:T(8,128)(2,1)} %bitcast.13), channel_id=1, source_target_pairs={{0,16},{16,32},{32,48},{48,64},{64,80},{80,96},{96,112},{1,17},{17... | collective-permute-start | bytes 3145736 | tf_op jit(solution)/shard_map/ppermute | solution.py:28
  116.5 1.7 %convolution_convert_fusion.1 = bf16[2048,256]{1,0:T(8,128)(2,1)} fusion(bf16[2048,512]{1,0:T(8,128)(2,1)S(1)} %copy-done.7, bf16[256,512]{1,0:T(8,128)(2,1)S(1)} %copy-done), kind=kOutput, calls=%fused_computation.8 | convolution fusion | flops 537395200 | bytes 3407872 | tf_op jit(solution)/shard_map/dot_general | solution.py:195
  118.3 10.4 %all-to-all-start.1 = ((bf16[128,16,256]{2,1,0:T(8,128)(2,1)}), bf16[128,16,256]{2,1,0:T(8,128)(2,1)S(1)}, u32[]{:S(2)}, u32[]{:S(2)}) async-start(bf16[128,16,256]{2,1,0:T(8,128)(2,1)} %bitcast.63), calls=%async_computation.1 | async-start | bytes 2097152 | tf_op jit(solution)/shard_map/all_to_all | solution.py:250
  128.7 3.1 %convolution_add_fusion.1 = f32[2048,256]{1,0:T(8,128)} fusion(f32[2048,256]{1,0:T(8,128)S(1)} %convolution_add_fusion.2, bf16[2048,256]{1,0:T(8,128)(2,1)} %copy-done.4, bf16[512,256]{1,0:T(8,128)(2,1)} %param.20), kind=kOutput, calls=%fused_computation.3 | convolution fusion | flops 268959744 | bytes 5373952 | tf_op jit(solution)/shard_map/dot_general | solution.py:195
  131.7 31.4 %all-to-all-done.1 = bf16[128,16,256]{2,1,0:T(8,128)(2,1)S(1)} async-done(((bf16[128,16,256]{2,1,0:T(8,128)(2,1)}), bf16[128,16,256]{2,1,0:T(8,128)(2,1)S(1)}, u32[]{:S(2)}, u32[]{:S(2)}) %all-to-all-start.1) | async-done | bytes 1048608 | tf_op jit(solution)/shard_map/all_to_all | solution.py:250
  163.2 4.5 %fusion.8 = bf16[2048,256]{1,0:T(8,128)(2,1)} fusion(f32[16,128,256]{2,1,0:T(8,128)} %get-tuple-element.7, bf16[2048,256]{1,0:T(8,128)(2,1)} %collective-permute-done.7, bf16[2048,256]{1,0:T(8,128)(2,1)} %collective-permute-done.6, bf16[2048,256]{1,0:T(8,128)(2,1)} %collective-permute-done.5, bf16[2048,256]{1,0:T(8,128)(2,1)} %collective-permute-done.4), kind=kLoop, calls=%fused_computation.22 | loop fusion | flops 4718592 | bytes 7340032 | tf_op jit(solution)/shard_map/convert_element_type | solution.py:270
  167.7 4.0 %fusion.4 = bf16[1,1,2048,256]{3,2,1,0:T(8,128)(2,1)} fusion(f32[2048,256]{1,0:T(8,128)} %convolution_add_fusion.1, bf16[256,256]{1,0:T(8,128)(2,1)S(1)} %copy-done.13, bf16[2048,256]{1,0:T(8,128)(2,1)} %fusion.8, bf16[256,256]{1,0:T(8,128)(2,1)} %param.19, f32[2048,256]{1,0:T(8,128)S(1)} %copy-done.6), kind=kOutput, calls=%fused_computation.17 | convolution fusion | flops 542638080 | bytes 6553600 | tf_op jit(solution)/shard_map/dot_general | solution.py:195
  171.7 1.0 copy.18
  (47 shorter events, 1.9 us)
Async XLA Ops:
  0.6 31.4 %copy-start = (bf16[256,512]{1,0:T(8,128)(2,1)S(1)}, bf16[256,512]{1,0:T(8,128)(2,1)}, u32[]{:S(2)}) copy-start(bf16[256,512]{1,0:T(8,128)(2,1)} %param.23) | copy-start | bytes 786436
  0.6 12.0 %copy-start.1 = (bf16[1,1,2048,256]{3,2,1,0:T(8,128)(2,1)S(1)}, bf16[1,1,2048,256]{3,2,1,0:T(8,128)(2,1)}, u32[]{:S(2)}) copy-start(bf16[1,1,2048,256]{3,2,1,0:T(8,128)(2,1)} %param.13) | copy-start | bytes 3145732
  0.7 12.0 %copy-start.12 = (bf16[256,256]{1,0:T(8,128)(2,1)S(1)}, bf16[256,256]{1,0:T(8,128)(2,1)}, u32[]{:S(2)}) copy-start(bf16[256,256]{1,0:T(8,128)(2,1)} %param.18) | copy-start | bytes 393220
  0.7 31.4 %all-to-all-start = ((bf16[128,16,256]{2,1,0:T(8,128)(2,1)}), bf16[128,16,256]{2,1,0:T(8,128)(2,1)}, u32[]{:S(2)}, u32[]{:S(2)}) async-start(bf16[128,16,256]{2,1,0:T(8,128)(2,1)} %bitcast.64), calls=%async_computation | async-start | bytes 2097152 | tf_op jit(solution)/shard_map/all_to_all | solution.py:239
  12.6 0.9 copy-start.17
  13.6 1.7 copy-start.5
  13.6 14.2 %copy-start.14 = (s32[1,1,16,4]{2,3,1,0:T(4,128)S(1)}, s32[1,1,16,4]{2,3,1,0:T(4,128)}, u32[]{:S(2)}) copy-start(s32[1,1,16,4]{2,3,1,0:T(4,128)} %param.14) | copy-start | bytes 772
  13.6 14.9 %copy-start.15 = (s32[128,1]{0,1:T(1,128)S(1)}, s32[128,1]{0,1:T(1,128)}, u32[]{:S(2)}) copy-start(s32[128,1]{0,1:T(1,128)} %param.17) | copy-start | bytes 1540
  13.6 15.7 %copy-start.2 = (bf16[1,1,2048,256]{3,2,1,0:T(8,128)(2,1)S(1)}, bf16[1,1,2048,256]{3,2,1,0:T(8,128)(2,1)}, u32[]{:S(2)}) copy-start(bf16[1,1,2048,256]{3,2,1,0:T(8,128)(2,1)} %param.25) | copy-start | bytes 3145732
  13.6 15.7 %copy-start.10 = (bf16[256,256]{1,0:T(8,128)(2,1)S(1)}, bf16[256,256]{1,0:T(8,128)(2,1)}, u32[]{:S(2)}) copy-start(bf16[256,256]{1,0:T(8,128)(2,1)} %param.24) | copy-start | bytes 393220
  15.2 32.3 %collective-permute-start.3 = (bf16[2048,256]{1,0:T(8,128)(2,1)}, bf16[2048,256]{1,0:T(8,128)(2,1)}, u32[]{:S(2)}, u32[]{:S(2)}) collective-permute-start(bf16[2048,256]{1,0:T(8,128)(2,1)} %convolution_convert_fusion.5), channel_id=1, source_target_pairs={{1,0},{2,1},{3,2},{4,3},{5,4},{6,5},{7,6},{8,7},{9,8},{10,9},{11,1... | collective-permute-start | bytes 3145736 | tf_op jit(solution)/shard_map/ppermute | solution.py:28
  16.5 31.0 %collective-permute-start.2 = (bf16[2048,256]{1,0:T(8,128)(2,1)}, bf16[2048,256]{1,0:T(8,128)(2,1)}, u32[]{:S(2)}, u32[]{:S(2)}) collective-permute-start(bf16[2048,256]{1,0:T(8,128)(2,1)} %convolution_convert_fusion.5), channel_id=1, source_target_pairs={{0,1},{1,2},{2,3},{3,4},{4,5},{5,6},{6,7},{7,8},{8,9},{9,10},{10,1... | collective-permute-start | bytes 3145736 | tf_op jit(solution)/shard_map/ppermute | solution.py:28
  21.6 26.0 %collective-permute-start.1 = (bf16[2048,256]{1,0:T(8,128)(2,1)}, bf16[2048,256]{1,0:T(8,128)(2,1)}, u32[]{:S(2)}, u32[]{:S(2)}) collective-permute-start(bf16[2048,256]{1,0:T(8,128)(2,1)} %convolution_convert_fusion.5), channel_id=1, source_target_pairs={{16,0},{32,16},{48,32},{64,48},{80,64},{96,80},{112,96},{17,1},{33... | collective-permute-start | bytes 3145736 | tf_op jit(solution)/shard_map/ppermute | solution.py:28
  25.2 22.4 %collective-permute-start = (bf16[2048,256]{1,0:T(8,128)(2,1)}, bf16[2048,256]{1,0:T(8,128)(2,1)}, u32[]{:S(2)}, u32[]{:S(2)}) collective-permute-start(bf16[2048,256]{1,0:T(8,128)(2,1)} %convolution_convert_fusion.5), channel_id=1, source_target_pairs={{0,16},{16,32},{32,48},{48,64},{64,80},{80,96},{96,112},{1,17},{17... | collective-permute-start | bytes 3145736 | tf_op jit(solution)/shard_map/ppermute | solution.py:28
  57.4 3.1 %copy-start.11 = (bf16[256,256]{1,0:T(8,128)(2,1)S(1)}, bf16[256,256]{1,0:T(8,128)(2,1)}, u32[]{:S(2)}) copy-start(bf16[256,256]{1,0:T(8,128)(2,1)} %param.22) | copy-start | bytes 393220
  64.0 22.1 %copy-start.3 = (bf16[1,1,2048,256]{3,2,1,0:T(8,128)(2,1)S(1)}, bf16[1,1,2048,256]{3,2,1,0:T(8,128)(2,1)}, u32[]{:S(2)}) copy-start(bf16[1,1,2048,256]{3,2,1,0:T(8,128)(2,1)} %param.25) | copy-start | bytes 3145732
  86.1 1.9 %copy-start.8 = (f32[2048,256]{1,0:T(8,128)S(1)}, f32[2048,256]{1,0:T(8,128)}, u32[]{:S(2)}) copy-start(f32[2048,256]{1,0:T(8,128)} %convolution_add_fusion.4) | copy-start | bytes 6291460
  86.1 1.9 %copy-start.16 = (bf16[256,256]{1,0:T(8,128)(2,1)S(1)}, bf16[256,256]{1,0:T(8,128)(2,1)}, u32[]{:S(2)}) copy-start(bf16[256,256]{1,0:T(8,128)(2,1)} %param.21) | copy-start | bytes 393220
  88.0 2.0 %copy-start.9 = (bf16[512,256]{1,0:T(8,128)(2,1)S(1)}, bf16[512,256]{1,0:T(8,128)(2,1)}, u32[]{:S(2)}) copy-start(bf16[512,256]{1,0:T(8,128)(2,1)} %param.20) | copy-start | bytes 786436
  89.0 1.0 copy-start.4
  100.2 16.4 %copy-start.7 = (bf16[2048,512]{1,0:T(8,128)(2,1)S(1)}, bf16[2048,512]{1,0:T(8,128)(2,1)}, u32[]{:S(2)}) copy-start(bf16[2048,512]{1,0:T(8,128)(2,1)} %get-tuple-element.9) | copy-start | bytes 6291460
  104.7 58.5 %collective-permute-start.7 = (bf16[2048,256]{1,0:T(8,128)(2,1)}, bf16[2048,256]{1,0:T(8,128)(2,1)}, u32[]{:S(2)}, u32[]{:S(2)}) collective-permute-start(bf16[2048,256]{1,0:T(8,128)(2,1)} %bitcast.15), channel_id=1, source_target_pairs={{0,1},{1,2},{2,3},{3,4},{4,5},{5,6},{6,7},{7,8},{8,9},{9,10},{10,1... | collective-permute-start | bytes 3145736 | tf_op jit(solution)/shard_map/ppermute | solution.py:28
  109.1 54.0 %collective-permute-start.4 = (bf16[2048,256]{1,0:T(8,128)(2,1)}, bf16[2048,256]{1,0:T(8,128)(2,1)}, u32[]{:S(2)}, u32[]{:S(2)}) collective-permute-start(bf16[2048,256]{1,0:T(8,128)(2,1)} %bitcast.12), channel_id=1, source_target_pairs={{16,0},{32,16},{48,32},{64,48},{80,64},{96,80},{112,96},{17,1},{33... | collective-permute-start | bytes 3145736 | tf_op jit(solution)/shard_map/ppermute | solution.py:28
  112.0 51.2 %collective-permute-start.6 = (bf16[2048,256]{1,0:T(8,128)(2,1)}, bf16[2048,256]{1,0:T(8,128)(2,1)}, u32[]{:S(2)}, u32[]{:S(2)}) collective-permute-start(bf16[2048,256]{1,0:T(8,128)(2,1)} %bitcast.14), channel_id=1, source_target_pairs={{1,0},{2,1},{3,2},{4,3},{5,4},{6,5},{7,6},{8,7},{9,8},{10,9},{11,1... | collective-permute-start | bytes 3145736 | tf_op jit(solution)/shard_map/ppermute | solution.py:28
  113.3 49.9 %collective-permute-start.5 = (bf16[2048,256]{1,0:T(8,128)(2,1)}, bf16[2048,256]{1,0:T(8,128)(2,1)}, u32[]{:S(2)}, u32[]{:S(2)}) collective-permute-start(bf16[2048,256]{1,0:T(8,128)(2,1)} %bitcast.13), channel_id=1, source_target_pairs={{0,16},{16,32},{32,48},{48,64},{64,80},{80,96},{96,112},{1,17},{17... | collective-permute-start | bytes 3145736 | tf_op jit(solution)/shard_map/ppermute | solution.py:28
  118.3 44.9 %all-to-all-start.1 = ((bf16[128,16,256]{2,1,0:T(8,128)(2,1)}), bf16[128,16,256]{2,1,0:T(8,128)(2,1)S(1)}, u32[]{:S(2)}, u32[]{:S(2)}) async-start(bf16[128,16,256]{2,1,0:T(8,128)(2,1)} %bitcast.63), calls=%async_computation.1 | async-start | bytes 2097152 | tf_op jit(solution)/shard_map/all_to_all | solution.py:250
  163.2 4.5 %copy-start.6 = (f32[2048,256]{1,0:T(8,128)S(1)}, f32[2048,256]{1,0:T(8,128)}, u32[]{:S(2)}) copy-start(f32[2048,256]{1,0:T(8,128)} %copy-done.5) | copy-start | bytes 6291460
  163.2 4.5 %copy-start.13 = (bf16[256,256]{1,0:T(8,128)(2,1)S(1)}, bf16[256,256]{1,0:T(8,128)(2,1)}, u32[]{:S(2)}) copy-start(bf16[256,256]{1,0:T(8,128)(2,1)} %param.18) | copy-start | bytes 393220

commit v6 on v5

--- a/solution.py
+++ b/solution.py
@@ -189,6 +189,42 @@
             bytes_accessed=2 * (3 * rows * width + 4 * slots * width),
         ),
     )(live, queries, grad_out, keyvals)
+
+
+def slope_of(values):
+    sigma = 1.0 / (1.0 + jnp.exp(-values))
+    return sigma * (1.0 + values * (1.0 - sigma))
+
+
+def edge_back_kernel(lat_ref, own_ref, a_ref, b_ref, c_ref, d_ref, gn_ref, w1_ref, w2_ref, out_ref):
+    nt = (((1,), (1,)), ((), ()))
+    collected = own_ref[...]
+    for ref in (a_ref, b_ref, c_ref, d_ref):
+        collected = collected + ref[...].astype(jnp.float32)
+    grad_msg = collected.astype(jnp.bfloat16)
+    pre_act = jnp.dot(lat_ref[...], w1_ref[...], preferred_element_type=jnp.float32)
+    grad_pre = lax.dot_general(grad_msg, w2_ref[...], nt, preferred_element_type=jnp.float32)
+    grad_pre = (grad_pre * slope_of(pre_act)).astype(jnp.bfloat16)
+    total = gn_ref[...] + lax.dot_general(grad_pre, w1_ref[...], nt, preferred_element_type=jnp.float32)
+    out_ref[...] = total.astype(out_ref.dtype)
+
+
+def edge_back(latent, own_part, received, grad_node, w_e1, w_e2, rows_per_step=512):
+    rows, width = latent.shape
+    row_block = pl.BlockSpec((rows_per_step, width), lambda i: (i, 0))
+    weight = pl.BlockSpec(w_e1.shape, lambda i: (0, 0))
+    return pl.pallas_call(
+        edge_back_kernel,
+        grid=(rows // rows_per_step,),
+        in_specs=[row_block] * (3 + len(received)) + [weight, weight],
+        out_specs=row_block,
+        out_shape=jax.ShapeDtypeStruct((rows, width), jnp.bfloat16),
+        cost_estimate=pl.CostEstimate(
+            flops=6 * rows * width * width,
+            transcendentals=rows * width,
+            bytes_accessed=rows * width * (2 + 4 + 2 * len(received) + 4 + 2),
+        ),
+    )(latent, own_part, *received, grad_node, w_e1, w_e2)
 
 
 def dense(left, right):
@@ -262,14 +298,15 @@
     grad_node = grad_update + dense(grad_z, w_n1[:latent_width].T)
     own_part, outbound = tile_scatter(src_ids, tile_mask[0, 0], grad_agg, len(sources))
     outbound = outbound.reshape(len(sources) - 1, node_rows, latent_width)
-    collected = own_part.reshape(node_rows, latent_width)
-    for member, offset in ((0, -1), (1, 1)):
-        collected = collected + passed_along(outbound[member], "px", offset).astype(jnp.float32)
-    for member, offset in ((2, -1), (3, 1)):
-        collected = collected + passed_along(outbound[member], "py", offset).astype(jnp.float32)
-    grad_msg = collected.astype(jnp.bfloat16)
-    grad_pre = (dense(grad_msg, w_e2.T) * silu_slope(pre_act)).astype(jnp.bfloat16)
-    grad_nodes = (grad_node + dense(grad_pre, w_e1.T)).astype(jnp.bfloat16)
+    received = [
+        passed_along(outbound[0], "px", -1),
+        passed_along(outbound[1], "px", 1),
+        passed_along(outbound[2], "py", -1),
+        passed_along(outbound[3], "py", 1),
+    ]
+    grad_nodes = edge_back(
+        latent, own_part.reshape(node_rows, latent_width), received, grad_node, w_e1, w_e2
+    )
     return (grad_nodes[None, None], grad_tokens[None])
 
 

time: 173 us -> 165 us (0.954); the launches traced: 173 us -> 163 us
  waiting for transfers between devices: 43.7 us -> 36.5 us
  Pallas kernels: 40.7 us -> 47.2 us
  other arithmetic: 4.58 us -> 0.08 us
  matrix products: 27.7 us -> 23.3 us
    all_to_all x1, waiting for transfers between devices: 31.4 us -> 22.8 us  [on_device(): lax.all_to_all(grad_slots.reshape(devices, slot_count, latent_width), ('p...]
    pallas_call x0 -> x1, Pallas kernels: none -> 6.5 us  [edge_back(): pl.pallas_call(edge_back_kernel, grid=(rows // rows_per_step,), in_specs=...]
    convert_element_type x1 -> x0, other arithmetic: 4.5 us -> none  [on_device(): grad_msg = collected.astype(jnp.bfloat16)]
    dot_general x13 -> x11, matrix products: 27.7 us -> 23.3 us  [dense(): return jnp.dot(left, right, preferred_element_type=jnp.float32)]
  transfers between devices with their start and end apart: 10 -> 10, of which waited for: 2 -> 2; matrix products, arithmetic and copies ran while one was open for 8% -> 9% of each run, Pallas kernels for 0% -> 0%
where the time goes in v6:
time: 165 us; the launch traced here: 163 us
  Pallas kernels  47.2 us (29%)
  starting transfers between devices  46.8 us (28%)
  waiting for transfers between devices  36.5 us (22%)
  matrix products  23.3 us (14%)
  local copies, waits for them, and re-layouts  7.92 us (5%)
    ppermute x8, starting transfers between devices, passed_along(): lax.ppermute(value, axis, [(source, source + steps) for source in range(l...  25 us
    dot_general x11, matrix products, dense(): return jnp.dot(left, right, preferred_element_type=jnp.float32)  23.3 us
    all_to_all x1, waiting for transfers between devices, on_device(): lax.all_to_all(grad_slots.reshape(devices, slot_count, latent_width), ('p...  22.8 us
    pallas_call x1, Pallas kernels, attend_back(): pl.pallas_call(functools.partial(attend_kernel, scale), grid=(steps,), in...  22 us
    ppermute x8, waiting for transfers between devices, passed_along(): lax.ppermute(value, axis, [(source, source + steps) for source in range(l...  13.7 us
    all_to_all x1, starting transfers between devices, on_device(): lax.all_to_all(token_groups, ('px', 'py'), split_axis=0, concat_axis=0, t...  11.5 us
    all_to_all x1, starting transfers between devices, on_device(): lax.all_to_all(grad_slots.reshape(devices, slot_count, latent_width), ('p...  10.2 us
    pallas_call x1, Pallas kernels, tile_gather(): pl.pallas_call(functools.partial(gather_kernel, group), grid_spec=pltpu.P...  9.84 us
  transfers between devices with their start and end apart: 10, of which 2 were waited for; matrix products, arithmetic and copies ran while one was open for 9% of the time, Pallas kernels for 0%

profile of v6, /device:TPU:1, one launch (start us, length us, event | category | flops | bytes accessed | tf_op | source)
XLA Modules:
  0.0 162.6 jit_solution(5292630173340473084)
XLA Ops:
  0.7 11.5 %all-to-all-start = ((bf16[128,16,256]{2,1,0:T(8,128)(2,1)}), bf16[128,16,256]{2,1,0:T(8,128)(2,1)S(1)}, u32[]{:S(2)}, u32[]{:S(2)}) async-start(bf16[128,16,256]{2,1,0:T(8,128)(2,1)} %bitcast.58), calls=%async_computation | async-start | bytes 2097152 | tf_op jit(solution)/shard_map/all_to_all | solution.py:275
  12.2 2.8 %convolution_convert_fusion.5 = bf16[2048,256]{1,0:T(8,128)(2,1)} fusion(bf16[256,256]{1,0:T(8,128)(2,1)S(1)} %copy-done.11, bf16[256,256]{1,0:T(8,128)(2,1)} %w1_ref.1, bf16[1,1,2048,256]{3,2,1,0:T(8,128)(2,1)S(1)} %copy-done.4), kind=kOutput, calls=%fused_computation.12 | convolution fusion | flops 540016640 | bytes 2359296 | tf_op jit(solution)/shard_map/dot_general | solution.py:231
  15.0 1.3 collective-permute-start.3
  16.3 5.0 %collective-permute-start.2 = (bf16[2048,256]{1,0:T(8,128)(2,1)}, bf16[2048,256]{1,0:T(8,128)(2,1)}, u32[]{:S(2)}, u32[]{:S(2)}) collective-permute-start(bf16[2048,256]{1,0:T(8,128)(2,1)} %convolution_convert_fusion.5), channel_id=1, source_target_pairs={{0,1},{1,2},{2,3},{3,4},{4,5},{5,6},{6,7},{7,8},{8,9},{9,10},{10,1... | collective-permute-start | bytes 3145736 | tf_op jit(solution)/shard_map/ppermute | solution.py:28
  21.3 3.5 %collective-permute-start.1 = (bf16[2048,256]{1,0:T(8,128)(2,1)}, bf16[2048,256]{1,0:T(8,128)(2,1)}, u32[]{:S(2)}, u32[]{:S(2)}) collective-permute-start(bf16[2048,256]{1,0:T(8,128)(2,1)} %convolution_convert_fusion.5), channel_id=1, source_target_pairs={{16,0},{32,16},{48,32},{64,48},{80,64},{96,80},{112,96},{17,1},{33... | collective-permute-start | bytes 3145736 | tf_op jit(solution)/shard_map/ppermute | solution.py:28
  24.8 2.6 %collective-permute-start = (bf16[2048,256]{1,0:T(8,128)(2,1)}, bf16[2048,256]{1,0:T(8,128)(2,1)}, u32[]{:S(2)}, u32[]{:S(2)}) collective-permute-start(bf16[2048,256]{1,0:T(8,128)(2,1)} %convolution_convert_fusion.5), channel_id=1, source_target_pairs={{0,16},{16,32},{32,48},{48,64},{64,80},{80,96},{96,112},{1,17},{17... | collective-permute-start | bytes 3145736 | tf_op jit(solution)/shard_map/ppermute | solution.py:28
  27.5 0.6 reshape_squeeze.6.src_ids
  28.3 0.7 reshape.73.live_ref
  29.0 2.5 %convolution_convert_fusion.3.go_ref = bf16[2048,256]{1,0:T(8,128)(2,1)} fusion(bf16[256,256]{1,0:T(8,128)(2,1)} %param.24, bf16[1,1,2048,256]{3,2,1,0:T(8,128)(2,1)S(1)} %copy-done.1), kind=kOutput, calls=%fused_computation.10 | convolution fusion | flops 268959744 | bytes 2228224 | tf_op jit(solution)/shard_map/dot_general | solution.py:231
  31.5 0.4 fusion.9
  31.9 2.0 %convolution_convert_fusion.kv_ref = bf16[2048,512]{1,0:T(8,128)(2,1)} fusion(bf16[2048,256]{1,0:T(8,128)(2,1)S(1)} %bitcast.54, bf16[256,512]{1,0:T(8,128)(2,1)S(1)} %copy-done), kind=kOutput, calls=%fused_computation | convolution fusion | flops 537919488 | bytes 3407872 | tf_op jit(solution)/shard_map/dot_general | solution.py:231
  33.9 13.7 %collective-permute-done.3 = bf16[2048,256]{1,0:T(8,128)(2,1)} collective-permute-done((bf16[2048,256]{1,0:T(8,128)(2,1)}, bf16[2048,256]{1,0:T(8,128)(2,1)}, u32[]{:S(2)}, u32[]{:S(2)}) %collective-permute-start.3) | collective-permute-done | bytes 1048608 | tf_op jit(solution)/shard_map/ppermute | solution.py:28
  47.6 9.8 %shard_map.140 = bf16[2048,256]{1,0:T(8,128)(2,1)} custom-call(s32[64]{0:T(128)} %reshape_squeeze.6.src_ids, s32[16,4,128,128]{3,2,1,0:T(8,128)} %bitcast.51, bf16[16,128,256]{2,1,0:T(8,128)(2,1)} %bitcast.59, bf16[16,128,256]{2,1,0:T(8,128)(2,1)} %bitcast.5.up, bf16[16,128,256]{2,1,0:T(8,128)(2,1)} %bitcast.6.down, bf16[16,128,256]{2,1,0:T(8,128)(2,1)} %bitcast.7.left, ...), custom_call_target="tpu_custom_call" | custom-call | tf_op jit(solution)/shard_map/pallas_call | solution.py:58
  57.5 3.1 %convolution_add_fusion.3 = f32[2048,256]{1,0:T(8,128)} fusion(f32[2048,256]{1,0:T(8,128)S(1)} %fusion.9, bf16[2048,256]{1,0:T(8,128)(2,1)} %shard_map.140, bf16[512,256]{1,0:T(8,128)(2,1)} %param.20), kind=kOutput, calls=%fused_computation.5 | convolution fusion | flops 268959744 | bytes 5373952 | tf_op jit(solution)/shard_map/dot_general | solution.py:231
  60.5 3.4 %convolution_convert_fusion.4.q_ref = bf16[2048,256]{1,0:T(8,128)(2,1)} fusion(bf16[256,256]{1,0:T(8,128)(2,1)S(1)} %copy-done.12, bf16[256,256]{1,0:T(8,128)(2,1)} %param.21, f32[2048,256]{1,0:T(8,128)} %convolution_add_fusion.3, bf16[1,1,2048,256]{3,2,1,0:T(8,128)(2,1)S(1)} %copy-done.6), kind=kOutput, calls=%fused_computation.11 | convolution fusion | flops 541589504 | bytes 4456448 | tf_op jit(solution)/shard_map/dot_general | solution.py:231
  64.0 22.0 %shard_map.141 = (bf16[2048,256]{1,0:T(8,128)(2,1)}, bf16[2048,512]{1,0:T(8,128)(2,1)}) custom-call(f32[1,2048]{1,0:T(1,128)} %reshape.73.live_ref, bf16[2048,256]{1,0:T(8,128)(2,1)} %convolution_convert_fusion.4.q_ref, bf16[2048,256]{1,0:T(8,128)(2,1)} %convolution_convert_fusion.3.go_ref, bf16[2048,512]{1,0:T(8,128)(2,1)} %convolution_convert_fusion.kv_ref), custom_call_target="tpu_custom_call" | custom-call | flops 10737418240 | bytes 7340032 | tf_op jit(solution)/shard_map/pallas_call | solution.py:167
  86.0 1.8 %convolution_add_fusion.1 = f32[2048,256]{1,0:T(8,128)S(1)} fusion(bf16[2048,256]{1,0:T(8,128)(2,1)} %get-tuple-element.6, bf16[256,256]{1,0:T(8,128)(2,1)S(1)} %copy-done.12, bf16[1,1,2048,256]{3,2,1,0:T(8,128)(2,1)S(1)} %copy-done.2), kind=kOutput, calls=%fused_computation.3 | convolution fusion | flops 269484032 | bytes 4325376 | tf_op jit(solution)/shard_map/dot_general | solution.py:231
  87.9 1.0 fusion.1
  88.9 1.0 copy-done.3
  89.9 1.4 convolution_convert_fusion.2.grad_ref
  91.4 8.8 %shard_map.142 = (f32[16,128,256]{2,1,0:T(8,128)}, bf16[4,16,128,256]{3,2,1,0:T(8,128)(2,1)}) custom-call(s32[64]{0:T(128)} %reshape_squeeze.6.src_ids, s32[16,4,128,128]{3,2,1,0:T(8,128)} %bitcast.52, bf16[2048,256]{1,0:T(8,128)(2,1)} %convolution_convert_fusion.2.grad_ref), custom_call_target="tpu_custom_call" | custom-call | tf_op jit(solution)/shard_map/pallas_call | solution.py:105
  100.2 4.4 %fusion.23 = (bf16[1,16,128,256]{3,2,1,0:T(8,128)(2,1)}, bf16[1,16,128,256]{3,2,1,0:T(8,128)(2,1)}, bf16[1,16,128,256]{3,2,1,0:T(8,128)(2,1)}, bf16[1,16,128,256]{3,2,1,0:T(8,128)(2,1)}) fusion(bf16[4,16,128,256]{3,2,1,0:T(8,128)(2,1)} %get-tuple-element.8), kind=kLoop, calls=%fused_computation.32 | loop fusion | bytes 8388608 | tf_op jit(solution)/shard_map/slice | solution.py:305
  104.6 1.3 collective-permute-start.6
  105.9 5.2 %collective-permute-start.7 = (bf16[2048,256]{1,0:T(8,128)(2,1)}, bf16[2048,256]{1,0:T(8,128)(2,1)}, u32[]{:S(2)}, u32[]{:S(2)}) collective-permute-start(bf16[2048,256]{1,0:T(8,128)(2,1)} %bitcast.15), channel_id=1, source_target_pairs={{0,1},{1,2},{2,3},{3,4},{4,5},{5,6},{6,7},{7,8},{8,9},{9,10},{10,1... | collective-permute-start | bytes 3145736 | tf_op jit(solution)/shard_map/ppermute | solution.py:28
  111.1 4.3 %collective-permute-start.5 = (bf16[2048,256]{1,0:T(8,128)(2,1)}, bf16[2048,256]{1,0:T(8,128)(2,1)}, u32[]{:S(2)}, u32[]{:S(2)}) collective-permute-start(bf16[2048,256]{1,0:T(8,128)(2,1)} %bitcast.13), channel_id=1, source_target_pairs={{0,16},{16,32},{32,48},{48,64},{64,80},{80,96},{96,112},{1,17},{17... | collective-permute-start | bytes 3145736 | tf_op jit(solution)/shard_map/ppermute | solution.py:28
  115.3 1.9 %collective-permute-start.4 = (bf16[2048,256]{1,0:T(8,128)(2,1)}, bf16[2048,256]{1,0:T(8,128)(2,1)}, u32[]{:S(2)}, u32[]{:S(2)}) collective-permute-start(bf16[2048,256]{1,0:T(8,128)(2,1)} %bitcast.12), channel_id=1, source_target_pairs={{16,0},{32,16},{48,32},{64,48},{80,64},{96,80},{112,96},{17,1},{33... | collective-permute-start | bytes 3145736 | tf_op jit(solution)/shard_map/ppermute | solution.py:28
  117.3 1.7 %convolution_convert_fusion.1 = bf16[2048,256]{1,0:T(8,128)(2,1)} fusion(bf16[2048,512]{1,0:T(8,128)(2,1)S(1)} %copy-done.7, bf16[256,512]{1,0:T(8,128)(2,1)S(1)} %copy-done), kind=kOutput, calls=%fused_computation.6 | convolution fusion | flops 537395200 | bytes 3407872 | tf_op jit(solution)/shard_map/dot_general | solution.py:231
  119.0 10.2 %all-to-all-start.1 = ((bf16[128,16,256]{2,1,0:T(8,128)(2,1)}), bf16[128,16,256]{2,1,0:T(8,128)(2,1)S(1)}, u32[]{:S(2)}, u32[]{:S(2)}) async-start(bf16[128,16,256]{2,1,0:T(8,128)(2,1)} %bitcast.55), calls=%async_computation.1 | async-start | bytes 2097152 | tf_op jit(solution)/shard_map/all_to_all | solution.py:286
  129.3 3.1 %convolution_add_fusion.gn_ref = f32[2048,256]{1,0:T(8,128)} fusion(f32[2048,256]{1,0:T(8,128)S(1)} %convolution_add_fusion.1, bf16[2048,256]{1,0:T(8,128)(2,1)} %copy-done.3, bf16[512,256]{1,0:T(8,128)(2,1)} %param.20), kind=kOutput, calls=%fused_computation.1 | convolution fusion | flops 268959744 | bytes 5373952 | tf_op jit(solution)/shard_map/dot_general | solution.py:231
  132.3 22.8 %all-to-all-done.1 = bf16[128,16,256]{2,1,0:T(8,128)(2,1)S(1)} async-done(((bf16[128,16,256]{2,1,0:T(8,128)(2,1)}), bf16[128,16,256]{2,1,0:T(8,128)(2,1)S(1)}, u32[]{:S(2)}, u32[]{:S(2)}) %all-to-all-start.1) | async-done | bytes 1048608 | tf_op jit(solution)/shard_map/all_to_all | solution.py:286
  155.1 6.5 %shard_map.143 = bf16[2048,256]{1,0:T(8,128)(2,1)} custom-call(bf16[2048,256]{1,0:T(8,128)(2,1)} %bitcast.56, f32[2048,256]{1,0:T(8,128)} %bitcast.57, bf16[2048,256]{1,0:T(8,128)(2,1)} %collective-permute-done.4.a_ref, bf16[2048,256]{1,0:T(8,128)(2,1)} %collective-permute-done.5.b_ref, bf16[2048,256]{1,0:T(8,128)(2,1)} %collective-permute-done.6.c_ref, ...), custom_call_target="tpu_custom_call" | custom-call | flops 805306368 | bytes 10485760 | tf_op jit(solution)/shard_map/pallas_call | solution.py:216
  161.6 1.0 copy.18
  (41 shorter events, 0.3 us)
Async XLA Ops:
  0.6 31.3 %copy-start = (bf16[256,512]{1,0:T(8,128)(2,1)S(1)}, bf16[256,512]{1,0:T(8,128)(2,1)}, u32[]{:S(2)}) copy-start(bf16[256,512]{1,0:T(8,128)(2,1)} %param.23) | copy-start | bytes 786436
  0.6 11.5 %copy-start.4 = (bf16[1,1,2048,256]{3,2,1,0:T(8,128)(2,1)S(1)}, bf16[1,1,2048,256]{3,2,1,0:T(8,128)(2,1)}, u32[]{:S(2)}) copy-start(bf16[1,1,2048,256]{3,2,1,0:T(8,128)(2,1)} %param.13) | copy-start | bytes 3145732
  0.7 11.5 %copy-start.11 = (bf16[256,256]{1,0:T(8,128)(2,1)S(1)}, bf16[256,256]{1,0:T(8,128)(2,1)}, u32[]{:S(2)}) copy-start(bf16[256,256]{1,0:T(8,128)(2,1)} %w2_ref.1) | copy-start | bytes 393220
  0.7 31.2 %all-to-all-start = ((bf16[128,16,256]{2,1,0:T(8,128)(2,1)}), bf16[128,16,256]{2,1,0:T(8,128)(2,1)S(1)}, u32[]{:S(2)}, u32[]{:S(2)}) async-start(bf16[128,16,256]{2,1,0:T(8,128)(2,1)} %bitcast.58), calls=%async_computation | async-start | bytes 2097152 | tf_op jit(solution)/shard_map/all_to_all | solution.py:275
  12.2 15.3 %copy-start.13 = (s32[1,1,16,4]{2,3,1,0:T(4,128)S(1)}, s32[1,1,16,4]{2,3,1,0:T(4,128)}, u32[]{:S(2)}) copy-start(s32[1,1,16,4]{2,3,1,0:T(4,128)} %param.14) | copy-start | bytes 772
  12.2 16.0 %copy-start.14 = (s32[128,1]{0,1:T(1,128)S(1)}, s32[128,1]{0,1:T(1,128)}, u32[]{:S(2)}) copy-start(s32[128,1]{0,1:T(1,128)} %param.17) | copy-start | bytes 1540
  12.2 16.7 %copy-start.1 = (bf16[1,1,2048,256]{3,2,1,0:T(8,128)(2,1)S(1)}, bf16[1,1,2048,256]{3,2,1,0:T(8,128)(2,1)}, u32[]{:S(2)}) copy-start(bf16[1,1,2048,256]{3,2,1,0:T(8,128)(2,1)} %param.25) | copy-start | bytes 3145732
  15.0 32.6 %collective-permute-start.3 = (bf16[2048,256]{1,0:T(8,128)(2,1)}, bf16[2048,256]{1,0:T(8,128)(2,1)}, u32[]{:S(2)}, u32[]{:S(2)}) collective-permute-start(bf16[2048,256]{1,0:T(8,128)(2,1)} %convolution_convert_fusion.5), channel_id=1, source_target_pairs={{1,0},{2,1},{3,2},{4,3},{5,4},{6,5},{7,6},{8,7},{9,8},{10,9},{11,1... | collective-permute-start | bytes 3145736 | tf_op jit(solution)/shard_map/ppermute | solution.py:28
  16.3 31.3 %collective-permute-start.2 = (bf16[2048,256]{1,0:T(8,128)(2,1)}, bf16[2048,256]{1,0:T(8,128)(2,1)}, u32[]{:S(2)}, u32[]{:S(2)}) collective-permute-start(bf16[2048,256]{1,0:T(8,128)(2,1)} %convolution_convert_fusion.5), channel_id=1, source_target_pairs={{0,1},{1,2},{2,3},{3,4},{4,5},{5,6},{6,7},{7,8},{8,9},{9,10},{10,1... | collective-permute-start | bytes 3145736 | tf_op jit(solution)/shard_map/ppermute | solution.py:28
  21.3 26.3 %collective-permute-start.1 = (bf16[2048,256]{1,0:T(8,128)(2,1)}, bf16[2048,256]{1,0:T(8,128)(2,1)}, u32[]{:S(2)}, u32[]{:S(2)}) collective-permute-start(bf16[2048,256]{1,0:T(8,128)(2,1)} %convolution_convert_fusion.5), channel_id=1, source_target_pairs={{16,0},{32,16},{48,32},{64,48},{80,64},{96,80},{112,96},{17,1},{33... | collective-permute-start | bytes 3145736 | tf_op jit(solution)/shard_map/ppermute | solution.py:28
  24.8 22.8 %collective-permute-start = (bf16[2048,256]{1,0:T(8,128)(2,1)}, bf16[2048,256]{1,0:T(8,128)(2,1)}, u32[]{:S(2)}, u32[]{:S(2)}) collective-permute-start(bf16[2048,256]{1,0:T(8,128)(2,1)} %convolution_convert_fusion.5), channel_id=1, source_target_pairs={{0,16},{16,32},{32,48},{48,64},{64,80},{80,96},{96,112},{1,17},{17... | collective-permute-start | bytes 3145736 | tf_op jit(solution)/shard_map/ppermute | solution.py:28
  29.0 2.5 %copy-start.5 = (bf16[1,1,2048,256]{3,2,1,0:T(8,128)(2,1)S(1)}, bf16[1,1,2048,256]{3,2,1,0:T(8,128)(2,1)}, u32[]{:S(2)}) copy-start(bf16[1,1,2048,256]{3,2,1,0:T(8,128)(2,1)} %param.13) | copy-start | bytes 3145732
  29.0 2.5 %copy-start.9 = (bf16[512,256]{1,0:T(8,128)(2,1)S(1)}, bf16[512,256]{1,0:T(8,128)(2,1)}, u32[]{:S(2)}) copy-start(bf16[512,256]{1,0:T(8,128)(2,1)} %param.20) | copy-start | bytes 786436
  57.4 3.1 %copy-start.6 = (bf16[1,1,2048,256]{3,2,1,0:T(8,128)(2,1)S(1)}, bf16[1,1,2048,256]{3,2,1,0:T(8,128)(2,1)}, u32[]{:S(2)}) copy-start(bf16[1,1,2048,256]{3,2,1,0:T(8,128)(2,1)} %param.13) | copy-start | bytes 3145732
  57.4 3.1 %copy-start.12 = (bf16[256,256]{1,0:T(8,128)(2,1)S(1)}, bf16[256,256]{1,0:T(8,128)(2,1)}, u32[]{:S(2)}) copy-start(bf16[256,256]{1,0:T(8,128)(2,1)} %param.22) | copy-start | bytes 393220
  64.0 22.0 %copy-start.2 = (bf16[1,1,2048,256]{3,2,1,0:T(8,128)(2,1)S(1)}, bf16[1,1,2048,256]{3,2,1,0:T(8,128)(2,1)}, u32[]{:S(2)}) copy-start(bf16[1,1,2048,256]{3,2,1,0:T(8,128)(2,1)} %param.25) | copy-start | bytes 3145732
  86.0 1.9 %copy-start.8 = (f32[2048,256]{1,0:T(8,128)S(1)}, f32[2048,256]{1,0:T(8,128)}, u32[]{:S(2)}) copy-start(f32[2048,256]{1,0:T(8,128)} %convolution_add_fusion.3) | copy-start | bytes 6291460
  86.0 1.9 %copy-start.15 = (bf16[256,256]{1,0:T(8,128)(2,1)S(1)}, bf16[256,256]{1,0:T(8,128)(2,1)}, u32[]{:S(2)}) copy-start(bf16[256,256]{1,0:T(8,128)(2,1)} %param.21) | copy-start | bytes 393220
  87.9 2.0 %copy-start.10 = (bf16[512,256]{1,0:T(8,128)(2,1)S(1)}, bf16[512,256]{1,0:T(8,128)(2,1)}, u32[]{:S(2)}) copy-start(bf16[512,256]{1,0:T(8,128)(2,1)} %param.20) | copy-start | bytes 786436
  88.9 1.0 copy-start.3
  100.2 17.1 %copy-start.7 = (bf16[2048,512]{1,0:T(8,128)(2,1)S(1)}, bf16[2048,512]{1,0:T(8,128)(2,1)}, u32[]{:S(2)}) copy-start(bf16[2048,512]{1,0:T(8,128)(2,1)} %get-tuple-element.9) | copy-start | bytes 6291460
  104.6 50.5 %collective-permute-start.6 = (bf16[2048,256]{1,0:T(8,128)(2,1)}, bf16[2048,256]{1,0:T(8,128)(2,1)}, u32[]{:S(2)}, u32[]{:S(2)}) collective-permute-start(bf16[2048,256]{1,0:T(8,128)(2,1)} %bitcast.14), channel_id=1, source_target_pairs={{1,0},{2,1},{3,2},{4,3},{5,4},{6,5},{7,6},{8,7},{9,8},{10,9},{11,1... | collective-permute-start | bytes 3145736 | tf_op jit(solution)/shard_map/ppermute | solution.py:28
  105.9 49.2 %collective-permute-start.7 = (bf16[2048,256]{1,0:T(8,128)(2,1)}, bf16[2048,256]{1,0:T(8,128)(2,1)}, u32[]{:S(2)}, u32[]{:S(2)}) collective-permute-start(bf16[2048,256]{1,0:T(8,128)(2,1)} %bitcast.15), channel_id=1, source_target_pairs={{0,1},{1,2},{2,3},{3,4},{4,5},{5,6},{6,7},{7,8},{8,9},{9,10},{10,1... | collective-permute-start | bytes 3145736 | tf_op jit(solution)/shard_map/ppermute | solution.py:28
  111.1 44.0 %collective-permute-start.5 = (bf16[2048,256]{1,0:T(8,128)(2,1)}, bf16[2048,256]{1,0:T(8,128)(2,1)}, u32[]{:S(2)}, u32[]{:S(2)}) collective-permute-start(bf16[2048,256]{1,0:T(8,128)(2,1)} %bitcast.13), channel_id=1, source_target_pairs={{0,16},{16,32},{32,48},{48,64},{64,80},{80,96},{96,112},{1,17},{17... | collective-permute-start | bytes 3145736 | tf_op jit(solution)/shard_map/ppermute | solution.py:28
  115.3 39.8 %collective-permute-start.4 = (bf16[2048,256]{1,0:T(8,128)(2,1)}, bf16[2048,256]{1,0:T(8,128)(2,1)}, u32[]{:S(2)}, u32[]{:S(2)}) collective-permute-start(bf16[2048,256]{1,0:T(8,128)(2,1)} %bitcast.12), channel_id=1, source_target_pairs={{16,0},{32,16},{48,32},{64,48},{80,64},{96,80},{112,96},{17,1},{33... | collective-permute-start | bytes 3145736 | tf_op jit(solution)/shard_map/ppermute | solution.py:28
  119.0 36.1 %all-to-all-start.1 = ((bf16[128,16,256]{2,1,0:T(8,128)(2,1)}), bf16[128,16,256]{2,1,0:T(8,128)(2,1)S(1)}, u32[]{:S(2)}, u32[]{:S(2)}) async-start(bf16[128,16,256]{2,1,0:T(8,128)(2,1)} %bitcast.55), calls=%async_computation.1 | async-start | bytes 2097152 | tf_op jit(solution)/shard_map/all_to_all | solution.py:286

commit v7 on v6

--- a/solution.py
+++ b/solution.py
@@ -70,7 +70,8 @@
     )(src_ids, tile_mask, *sources)
 
 
-def scatter_kernel(group, src_ids, mask_ref, grad_ref, own_ref, out_ref, total):
+def scatter_kernel(group, src_ids, mask_ref, grad_ref, own_ref, *rest):
+    side_refs, total = rest[:-1], rest[-1]
     step = pl.program_id(0)
     tiles = mask_ref.shape[1]
     blk = mask_ref.shape[2]
@@ -94,9 +95,9 @@
     @pl.when(step == pl.num_programs(0) - 1)
     def _():
         own_ref[...] = total[0:per_side]
-        for side in range(out_ref.shape[0]):
+        for side, out_ref in enumerate(side_refs):
             start = (side + 1) * per_side
-            out_ref[side] = total[start : start + per_side].astype(out_ref.dtype)
+            out_ref[...] = total[start : start + per_side].astype(out_ref.dtype)
 
 
 def tile_scatter(src_ids, tile_mask, grad_agg, sides, group=4):
@@ -111,16 +112,11 @@
                 pl.BlockSpec((group, tiles, blk, blk), lambda i, ids: (i, 0, 0, 0)),
                 pl.BlockSpec((group * blk, width), lambda i, ids: (i, 0)),
             ],
-            out_specs=[
-                pl.BlockSpec((blocks, blk, width), lambda i, ids: (0, 0, 0)),
-                pl.BlockSpec((sides - 1, blocks, blk, width), lambda i, ids: (0, 0, 0, 0)),
-            ],
+            out_specs=[pl.BlockSpec((blocks, blk, width), lambda i, ids: (0, 0, 0))] * sides,
             scratch_shapes=[pltpu.VMEM((sides * blocks, blk, width), jnp.float32)],
         ),
-        out_shape=(
-            jax.ShapeDtypeStruct((blocks, blk, width), jnp.float32),
-            jax.ShapeDtypeStruct((sides - 1, blocks, blk, width), jnp.bfloat16),
-        ),
+        out_shape=[jax.ShapeDtypeStruct((blocks, blk, width), jnp.float32)]
+        + [jax.ShapeDtypeStruct((blocks, blk, width), jnp.bfloat16)] * (sides - 1),
         compiler_params=pltpu.CompilerParams(dimension_semantics=("arbitrary",)),
     )(src_ids, tile_mask, grad_agg)
 
@@ -296,8 +292,8 @@
     grad_z = (dense(update_low, w_n2.T) * silu_slope(zvalue)).astype(jnp.bfloat16)
     grad_agg = dense(grad_z, w_n1[latent_width:].T).astype(jnp.bfloat16)
     grad_node = grad_update + dense(grad_z, w_n1[:latent_width].T)
-    own_part, outbound = tile_scatter(src_ids, tile_mask[0, 0], grad_agg, len(sources))
-    outbound = outbound.reshape(len(sources) - 1, node_rows, latent_width)
+    own_part, *outbound = tile_scatter(src_ids, tile_mask[0, 0], grad_agg, len(sources))
+    outbound = [part.reshape(node_rows, latent_width) for part in outbound]
     received = [
         passed_along(outbound[0], "px", -1),
         passed_along(outbound[1], "px", 1),

time: 165 us -> 169 us (1.024); the launches traced: 163 us -> 169 us
  waiting for transfers between devices: 36.5 us -> 45.5 us
  local copies, waits for them, and re-layouts: 7.92 us -> 3.56 us
    all_to_all x1, waiting for transfers between devices: 22.8 us -> 31.8 us  [on_device(): lax.all_to_all(grad_slots.reshape(devices, slot_count, latent_width), ('p...]
    slice x1 -> x0, local copies, waits for them, and re-layouts: 4.42 us -> none  [on_device(): outbound[3]]
where the time goes in v7:
time: 169 us
  Pallas kernels  47.1 us (28%)
  starting transfers between devices  46.6 us (28%)
  waiting for transfers between devices  45.5 us (27%)
  matrix products  24.8 us (15%)
  local copies, waits for them, and re-layouts  3.56 us (2%)
    all_to_all x1, waiting for transfers between devices, on_device(): lax.all_to_all(grad_slots.reshape(devices, slot_count, latent_width), ('p...  31.8 us
    dot_general x11, matrix products, dense(): return jnp.dot(left, right, preferred_element_type=jnp.float32)  24.8 us
    ppermute x8, starting transfers between devices, passed_along(): lax.ppermute(value, axis, [(source, source + steps) for source in range(l...  24.6 us
    pallas_call x1, Pallas kernels, attend_back(): pl.pallas_call(functools.partial(attend_kernel, scale), grid=(steps,), in...  22 us
    ppermute x8, waiting for transfers between devices, passed_along(): lax.ppermute(value, axis, [(source, source + steps) for source in range(l...  13.7 us
    all_to_all x1, starting transfers between devices, on_device(): lax.all_to_all(token_groups, ('px', 'py'), split_axis=0, concat_axis=0, t...  11.5 us
    all_to_all x1, starting transfers between devices, on_device(): lax.all_to_all(grad_slots.reshape(devices, slot_count, latent_width), ('p...  10.5 us
    pallas_call x1, Pallas kernels, tile_gather(): pl.pallas_call(functools.partial(gather_kernel, group), grid_spec=pltpu.P...  9.83 us
  transfers between devices with their start and end apart: 10, of which 2 were waited for; matrix products, arithmetic and copies ran while one was open for 9% of the time, Pallas kernels for 0%

profile of v7, /device:TPU:1, one launch (start us, length us, event | category | flops | bytes accessed | tf_op | source)
XLA Modules:
  0.0 168.6 jit_solution(5104160270909232630)
XLA Ops:
  0.7 11.5 %all-to-all-start = ((bf16[128,16,256]{2,1,0:T(8,128)(2,1)}), bf16[128,16,256]{2,1,0:T(8,128)(2,1)S(1)}, u32[]{:S(2)}, u32[]{:S(2)}) async-start(bf16[128,16,256]{2,1,0:T(8,128)(2,1)} %bitcast.58), calls=%async_computation | async-start | bytes 2097152 | tf_op jit(solution)/shard_map/all_to_all | solution.py:271
  12.2 2.8 %convolution_convert_fusion.5 = bf16[2048,256]{1,0:T(8,128)(2,1)} fusion(bf16[256,256]{1,0:T(8,128)(2,1)S(1)} %copy-done.10, bf16[256,256]{1,0:T(8,128)(2,1)} %w1_ref.1, bf16[1,1,2048,256]{3,2,1,0:T(8,128)(2,1)S(1)} %copy-done.4), kind=kOutput, calls=%fused_computation.12 | convolution fusion | flops 540016640 | bytes 2359296 | tf_op jit(solution)/shard_map/dot_general | solution.py:227
  15.0 1.3 collective-permute-start.3
  16.3 5.0 %collective-permute-start.2 = (bf16[2048,256]{1,0:T(8,128)(2,1)}, bf16[2048,256]{1,0:T(8,128)(2,1)}, u32[]{:S(2)}, u32[]{:S(2)}) collective-permute-start(bf16[2048,256]{1,0:T(8,128)(2,1)} %convolution_convert_fusion.5), channel_id=1, source_target_pairs={{0,1},{1,2},{2,3},{3,4},{4,5},{5,6},{6,7},{7,8},{8,9},{9,10},{10,1... | collective-permute-start | bytes 3145736 | tf_op jit(solution)/shard_map/ppermute | solution.py:28
  21.3 3.5 %collective-permute-start.1 = (bf16[2048,256]{1,0:T(8,128)(2,1)}, bf16[2048,256]{1,0:T(8,128)(2,1)}, u32[]{:S(2)}, u32[]{:S(2)}) collective-permute-start(bf16[2048,256]{1,0:T(8,128)(2,1)} %convolution_convert_fusion.5), channel_id=1, source_target_pairs={{16,0},{32,16},{48,32},{64,48},{80,64},{96,80},{112,96},{17,1},{33... | collective-permute-start | bytes 3145736 | tf_op jit(solution)/shard_map/ppermute | solution.py:28
  24.9 2.6 %collective-permute-start = (bf16[2048,256]{1,0:T(8,128)(2,1)}, bf16[2048,256]{1,0:T(8,128)(2,1)}, u32[]{:S(2)}, u32[]{:S(2)}) collective-permute-start(bf16[2048,256]{1,0:T(8,128)(2,1)} %convolution_convert_fusion.5), channel_id=1, source_target_pairs={{0,16},{16,32},{32,48},{48,64},{64,80},{80,96},{96,112},{1,17},{17... | collective-permute-start | bytes 3145736 | tf_op jit(solution)/shard_map/ppermute | solution.py:28
  27.5 0.1 copy.16
  27.6 0.6 reshape_squeeze.6.src_ids
  28.3 0.7 reshape.80.live_ref
  29.0 2.4 %convolution_convert_fusion.3.go_ref = bf16[2048,256]{1,0:T(8,128)(2,1)} fusion(bf16[256,256]{1,0:T(8,128)(2,1)} %param.24, bf16[1,1,2048,256]{3,2,1,0:T(8,128)(2,1)S(1)} %copy-done.1), kind=kOutput, calls=%fused_computation.10 | convolution fusion | flops 268959744 | bytes 2228224 | tf_op jit(solution)/shard_map/dot_general | solution.py:227
  31.4 0.4 fusion.9
  31.9 2.0 %convolution_convert_fusion.kv_ref = bf16[2048,512]{1,0:T(8,128)(2,1)} fusion(bf16[2048,256]{1,0:T(8,128)(2,1)S(1)} %bitcast.54, bf16[256,512]{1,0:T(8,128)(2,1)S(1)} %copy-done), kind=kOutput, calls=%fused_computation | convolution fusion | flops 537919488 | bytes 3407872 | tf_op jit(solution)/shard_map/dot_general | solution.py:227
  33.9 13.7 %collective-permute-done.3 = bf16[2048,256]{1,0:T(8,128)(2,1)} collective-permute-done((bf16[2048,256]{1,0:T(8,128)(2,1)}, bf16[2048,256]{1,0:T(8,128)(2,1)}, u32[]{:S(2)}, u32[]{:S(2)}) %collective-permute-start.3) | collective-permute-done | bytes 1048608 | tf_op jit(solution)/shard_map/ppermute | solution.py:28
  47.6 9.8 %shard_map.140 = bf16[2048,256]{1,0:T(8,128)(2,1)} custom-call(s32[64]{0:T(128)} %reshape_squeeze.6.src_ids, s32[16,4,128,128]{3,2,1,0:T(8,128)} %bitcast.51, bf16[16,128,256]{2,1,0:T(8,128)(2,1)} %bitcast.59, bf16[16,128,256]{2,1,0:T(8,128)(2,1)} %bitcast.5.up, bf16[16,128,256]{2,1,0:T(8,128)(2,1)} %bitcast.6.down, bf16[16,128,256]{2,1,0:T(8,128)(2,1)} %bitcast.7.left, ...), custom_call_target="tpu_custom_call" | custom-call | tf_op jit(solution)/shard_map/pallas_call | solution.py:58
  57.4 3.1 %convolution_add_fusion.3 = f32[2048,256]{1,0:T(8,128)} fusion(f32[2048,256]{1,0:T(8,128)S(1)} %fusion.9, bf16[2048,256]{1,0:T(8,128)(2,1)} %shard_map.140, bf16[512,256]{1,0:T(8,128)(2,1)} %param.20), kind=kOutput, calls=%fused_computation.5 | convolution fusion | flops 268959744 | bytes 5373952 | tf_op jit(solution)/shard_map/dot_general | solution.py:227
  60.6 3.4 %convolution_convert_fusion.4.q_ref = bf16[2048,256]{1,0:T(8,128)(2,1)} fusion(bf16[256,256]{1,0:T(8,128)(2,1)S(1)} %copy-done.11, bf16[256,256]{1,0:T(8,128)(2,1)} %param.21, f32[2048,256]{1,0:T(8,128)} %convolution_add_fusion.3, bf16[1,1,2048,256]{3,2,1,0:T(8,128)(2,1)S(1)} %copy-done.6), kind=kOutput, calls=%fused_computation.11 | convolution fusion | flops 541589504 | bytes 4456448 | tf_op jit(solution)/shard_map/dot_general | solution.py:227
  64.0 22.0 %shard_map.141 = (bf16[2048,256]{1,0:T(8,128)(2,1)}, bf16[2048,512]{1,0:T(8,128)(2,1)}) custom-call(f32[1,2048]{1,0:T(1,128)} %reshape.80.live_ref, bf16[2048,256]{1,0:T(8,128)(2,1)} %convolution_convert_fusion.4.q_ref, bf16[2048,256]{1,0:T(8,128)(2,1)} %convolution_convert_fusion.3.go_ref, bf16[2048,512]{1,0:T(8,128)(2,1)} %convolution_convert_fusion.kv_ref), custom_call_target="tpu_custom_call" | custom-call | flops 10737418240 | bytes 7340032 | tf_op jit(solution)/shard_map/pallas_call | solution.py:163
  86.0 1.8 %convolution_add_fusion.1 = f32[2048,256]{1,0:T(8,128)S(1)} fusion(bf16[2048,256]{1,0:T(8,128)(2,1)} %get-tuple-element.9, bf16[256,256]{1,0:T(8,128)(2,1)S(1)} %copy-done.11, bf16[1,1,2048,256]{3,2,1,0:T(8,128)(2,1)S(1)} %copy-done.2), kind=kOutput, calls=%fused_computation.3 | convolution fusion | flops 269484032 | bytes 4325376 | tf_op jit(solution)/shard_map/dot_general | solution.py:227
  87.9 1.0 fusion.1
  88.9 1.1 copy-done.3
  90.0 1.4 convolution_convert_fusion.2.grad_ref
  91.5 8.8 %shard_map.142 = (f32[16,128,256]{2,1,0:T(8,128)}, bf16[16,128,256]{2,1,0:T(8,128)(2,1)}, bf16[16,128,256]{2,1,0:T(8,128)(2,1)}, bf16[16,128,256]{2,1,0:T(8,128)(2,1)}, bf16[16,128,256]{2,1,0:T(8,128)(2,1)}) custom-call(s32[64]{0:T(128)} %reshape_squeeze.6.src_ids, s32[16,4,128,128]{3,2,1,0:T(8,128)} %bitcast.52, ...), custom_call_target="tpu_custom_call" | custom-call | tf_op jit(solution)/shard_map/pallas_call | solution.py:106
  100.2 2.6 %collective-permute-start.4 = (bf16[2048,256]{1,0:T(8,128)(2,1)}, bf16[2048,256]{1,0:T(8,128)(2,1)}, u32[]{:S(2)}, u32[]{:S(2)}) collective-permute-start(bf16[2048,256]{1,0:T(8,128)(2,1)} %bitcast.65), channel_id=1, source_target_pairs={{16,0},{32,16},{48,32},{64,48},{80,64},{96,80},{112,96},{17,1},{33... | collective-permute-start | bytes 3145736 | tf_op jit(solution)/shard_map/ppermute | solution.py:28
  102.9 3.2 %collective-permute-start.5 = (bf16[2048,256]{1,0:T(8,128)(2,1)}, bf16[2048,256]{1,0:T(8,128)(2,1)}, u32[]{:S(2)}, u32[]{:S(2)}) collective-permute-start(bf16[2048,256]{1,0:T(8,128)(2,1)} %bitcast.64), channel_id=1, source_target_pairs={{0,16},{16,32},{32,48},{48,64},{64,80},{80,96},{96,112},{1,17},{17... | collective-permute-start | bytes 3145736 | tf_op jit(solution)/shard_map/ppermute | solution.py:28
  106.0 1.3 collective-permute-start.6
  107.3 5.1 %collective-permute-start.7 = (bf16[2048,256]{1,0:T(8,128)(2,1)}, bf16[2048,256]{1,0:T(8,128)(2,1)}, u32[]{:S(2)}, u32[]{:S(2)}) collective-permute-start(bf16[2048,256]{1,0:T(8,128)(2,1)} %bitcast.62), channel_id=1, source_target_pairs={{0,1},{1,2},{2,3},{3,4},{4,5},{5,6},{6,7},{7,8},{8,9},{9,10},{10,1... | collective-permute-start | bytes 3145736 | tf_op jit(solution)/shard_map/ppermute | solution.py:28
  112.5 3.3 %convolution_convert_fusion.1 = bf16[2048,256]{1,0:T(8,128)(2,1)} fusion(bf16[2048,512]{1,0:T(8,128)(2,1)} %get-tuple-element.15, bf16[256,512]{1,0:T(8,128)(2,1)S(1)} %copy-done), kind=kOutput, calls=%fused_computation.6 | convolution fusion | flops 537395200 | bytes 3407872 | tf_op jit(solution)/shard_map/dot_general | solution.py:227
  115.8 10.5 %all-to-all-start.1 = ((bf16[128,16,256]{2,1,0:T(8,128)(2,1)}), bf16[128,16,256]{2,1,0:T(8,128)(2,1)S(1)}, u32[]{:S(2)}, u32[]{:S(2)}) async-start(bf16[128,16,256]{2,1,0:T(8,128)(2,1)} %bitcast.55), calls=%async_computation.1 | async-start | bytes 2097152 | tf_op jit(solution)/shard_map/all_to_all | solution.py:282
  126.3 3.0 %convolution_add_fusion.gn_ref = f32[2048,256]{1,0:T(8,128)} fusion(f32[2048,256]{1,0:T(8,128)S(1)} %convolution_add_fusion.1, bf16[2048,256]{1,0:T(8,128)(2,1)} %copy-done.3, bf16[512,256]{1,0:T(8,128)(2,1)} %param.20), kind=kOutput, calls=%fused_computation.1 | convolution fusion | flops 268959744 | bytes 5373952 | tf_op jit(solution)/shard_map/dot_general | solution.py:227
  129.3 31.8 %all-to-all-done.1 = bf16[128,16,256]{2,1,0:T(8,128)(2,1)S(1)} async-done(((bf16[128,16,256]{2,1,0:T(8,128)(2,1)}), bf16[128,16,256]{2,1,0:T(8,128)(2,1)S(1)}, u32[]{:S(2)}, u32[]{:S(2)}) %all-to-all-start.1) | async-done | bytes 1048608 | tf_op jit(solution)/shard_map/all_to_all | solution.py:282
  161.1 6.5 %shard_map.143 = bf16[2048,256]{1,0:T(8,128)(2,1)} custom-call(bf16[2048,256]{1,0:T(8,128)(2,1)} %bitcast.56, f32[2048,256]{1,0:T(8,128)} %bitcast.57, bf16[2048,256]{1,0:T(8,128)(2,1)} %collective-permute-done.4.a_ref, bf16[2048,256]{1,0:T(8,128)(2,1)} %collective-permute-done.5.b_ref, bf16[2048,256]{1,0:T(8,128)(2,1)} %collective-permute-done.6.c_ref, ...), custom_call_target="tpu_custom_call" | custom-call | flops 805306368 | bytes 10485760 | tf_op jit(solution)/shard_map/pallas_call | solution.py:212
  167.6 1.0 copy.18
  (38 shorter events, 0.2 us)
Async XLA Ops:
  0.6 31.2 %copy-start = (bf16[256,512]{1,0:T(8,128)(2,1)S(1)}, bf16[256,512]{1,0:T(8,128)(2,1)}, u32[]{:S(2)}) copy-start(bf16[256,512]{1,0:T(8,128)(2,1)} %param.23) | copy-start | bytes 786436
  0.6 11.5 %copy-start.4 = (bf16[1,1,2048,256]{3,2,1,0:T(8,128)(2,1)S(1)}, bf16[1,1,2048,256]{3,2,1,0:T(8,128)(2,1)}, u32[]{:S(2)}) copy-start(bf16[1,1,2048,256]{3,2,1,0:T(8,128)(2,1)} %param.13) | copy-start | bytes 3145732
  0.7 11.5 %copy-start.10 = (bf16[256,256]{1,0:T(8,128)(2,1)S(1)}, bf16[256,256]{1,0:T(8,128)(2,1)}, u32[]{:S(2)}) copy-start(bf16[256,256]{1,0:T(8,128)(2,1)} %w2_ref.1) | copy-start | bytes 393220
  0.7 31.2 %all-to-all-start = ((bf16[128,16,256]{2,1,0:T(8,128)(2,1)}), bf16[128,16,256]{2,1,0:T(8,128)(2,1)S(1)}, u32[]{:S(2)}, u32[]{:S(2)}) async-start(bf16[128,16,256]{2,1,0:T(8,128)(2,1)} %bitcast.58), calls=%async_computation | async-start | bytes 2097152 | tf_op jit(solution)/shard_map/all_to_all | solution.py:271
  12.2 15.3 %copy-start.12 = (s32[1,1,16,4]{2,3,1,0:T(4,128)S(1)}, s32[1,1,16,4]{2,3,1,0:T(4,128)}, u32[]{:S(2)}) copy-start(s32[1,1,16,4]{2,3,1,0:T(4,128)} %param.14) | copy-start | bytes 772
  12.2 16.0 %copy-start.13 = (s32[128,1]{0,1:T(1,128)S(1)}, s32[128,1]{0,1:T(1,128)}, u32[]{:S(2)}) copy-start(s32[128,1]{0,1:T(1,128)} %param.17) | copy-start | bytes 1540
  12.2 16.8 %copy-start.1 = (bf16[1,1,2048,256]{3,2,1,0:T(8,128)(2,1)S(1)}, bf16[1,1,2048,256]{3,2,1,0:T(8,128)(2,1)}, u32[]{:S(2)}) copy-start(bf16[1,1,2048,256]{3,2,1,0:T(8,128)(2,1)} %param.25) | copy-start | bytes 3145732
  15.0 32.6 %collective-permute-start.3 = (bf16[2048,256]{1,0:T(8,128)(2,1)}, bf16[2048,256]{1,0:T(8,128)(2,1)}, u32[]{:S(2)}, u32[]{:S(2)}) collective-permute-start(bf16[2048,256]{1,0:T(8,128)(2,1)} %convolution_convert_fusion.5), channel_id=1, source_target_pairs={{1,0},{2,1},{3,2},{4,3},{5,4},{6,5},{7,6},{8,7},{9,8},{10,9},{11,1... | collective-permute-start | bytes 3145736 | tf_op jit(solution)/shard_map/ppermute | solution.py:28
  16.3 31.3 %collective-permute-start.2 = (bf16[2048,256]{1,0:T(8,128)(2,1)}, bf16[2048,256]{1,0:T(8,128)(2,1)}, u32[]{:S(2)}, u32[]{:S(2)}) collective-permute-start(bf16[2048,256]{1,0:T(8,128)(2,1)} %convolution_convert_fusion.5), channel_id=1, source_target_pairs={{0,1},{1,2},{2,3},{3,4},{4,5},{5,6},{6,7},{7,8},{8,9},{9,10},{10,1... | collective-permute-start | bytes 3145736 | tf_op jit(solution)/shard_map/ppermute | solution.py:28
  21.3 26.3 %collective-permute-start.1 = (bf16[2048,256]{1,0:T(8,128)(2,1)}, bf16[2048,256]{1,0:T(8,128)(2,1)}, u32[]{:S(2)}, u32[]{:S(2)}) collective-permute-start(bf16[2048,256]{1,0:T(8,128)(2,1)} %convolution_convert_fusion.5), channel_id=1, source_target_pairs={{16,0},{32,16},{48,32},{64,48},{80,64},{96,80},{112,96},{17,1},{33... | collective-permute-start | bytes 3145736 | tf_op jit(solution)/shard_map/ppermute | solution.py:28
  24.9 22.7 %collective-permute-start = (bf16[2048,256]{1,0:T(8,128)(2,1)}, bf16[2048,256]{1,0:T(8,128)(2,1)}, u32[]{:S(2)}, u32[]{:S(2)}) collective-permute-start(bf16[2048,256]{1,0:T(8,128)(2,1)} %convolution_convert_fusion.5), channel_id=1, source_target_pairs={{0,16},{16,32},{32,48},{48,64},{64,80},{80,96},{96,112},{1,17},{17... | collective-permute-start | bytes 3145736 | tf_op jit(solution)/shard_map/ppermute | solution.py:28
  29.0 2.5 %copy-start.5 = (bf16[1,1,2048,256]{3,2,1,0:T(8,128)(2,1)S(1)}, bf16[1,1,2048,256]{3,2,1,0:T(8,128)(2,1)}, u32[]{:S(2)}) copy-start(bf16[1,1,2048,256]{3,2,1,0:T(8,128)(2,1)} %param.13) | copy-start | bytes 3145732
  29.0 2.5 %copy-start.8 = (bf16[512,256]{1,0:T(8,128)(2,1)S(1)}, bf16[512,256]{1,0:T(8,128)(2,1)}, u32[]{:S(2)}) copy-start(bf16[512,256]{1,0:T(8,128)(2,1)} %param.20) | copy-start | bytes 786436
  57.4 3.1 %copy-start.6 = (bf16[1,1,2048,256]{3,2,1,0:T(8,128)(2,1)S(1)}, bf16[1,1,2048,256]{3,2,1,0:T(8,128)(2,1)}, u32[]{:S(2)}) copy-start(bf16[1,1,2048,256]{3,2,1,0:T(8,128)(2,1)} %param.13) | copy-start | bytes 3145732
  57.4 3.1 %copy-start.11 = (bf16[256,256]{1,0:T(8,128)(2,1)S(1)}, bf16[256,256]{1,0:T(8,128)(2,1)}, u32[]{:S(2)}) copy-start(bf16[256,256]{1,0:T(8,128)(2,1)} %param.22) | copy-start | bytes 393220
  64.0 22.0 %copy-start.2 = (bf16[1,1,2048,256]{3,2,1,0:T(8,128)(2,1)S(1)}, bf16[1,1,2048,256]{3,2,1,0:T(8,128)(2,1)}, u32[]{:S(2)}) copy-start(bf16[1,1,2048,256]{3,2,1,0:T(8,128)(2,1)} %param.25) | copy-start | bytes 3145732
  86.0 1.9 %copy-start.7 = (f32[2048,256]{1,0:T(8,128)S(1)}, f32[2048,256]{1,0:T(8,128)}, u32[]{:S(2)}) copy-start(f32[2048,256]{1,0:T(8,128)} %convolution_add_fusion.3) | copy-start | bytes 6291460
  86.0 1.9 %copy-start.14 = (bf16[256,256]{1,0:T(8,128)(2,1)S(1)}, bf16[256,256]{1,0:T(8,128)(2,1)}, u32[]{:S(2)}) copy-start(bf16[256,256]{1,0:T(8,128)(2,1)} %param.21) | copy-start | bytes 393220
  87.9 2.1 %copy-start.9 = (bf16[512,256]{1,0:T(8,128)(2,1)S(1)}, bf16[512,256]{1,0:T(8,128)(2,1)}, u32[]{:S(2)}) copy-start(bf16[512,256]{1,0:T(8,128)(2,1)} %param.20) | copy-start | bytes 786436
  88.9 1.1 copy-start.3
  100.2 60.9 %collective-permute-start.4 = (bf16[2048,256]{1,0:T(8,128)(2,1)}, bf16[2048,256]{1,0:T(8,128)(2,1)}, u32[]{:S(2)}, u32[]{:S(2)}) collective-permute-start(bf16[2048,256]{1,0:T(8,128)(2,1)} %bitcast.65), channel_id=1, source_target_pairs={{16,0},{32,16},{48,32},{64,48},{80,64},{96,80},{112,96},{17,1},{33... | collective-permute-start | bytes 3145736 | tf_op jit(solution)/shard_map/ppermute | solution.py:28
  102.9 58.2 %collective-permute-start.5 = (bf16[2048,256]{1,0:T(8,128)(2,1)}, bf16[2048,256]{1,0:T(8,128)(2,1)}, u32[]{:S(2)}, u32[]{:S(2)}) collective-permute-start(bf16[2048,256]{1,0:T(8,128)(2,1)} %bitcast.64), channel_id=1, source_target_pairs={{0,16},{16,32},{32,48},{48,64},{64,80},{80,96},{96,112},{1,17},{17... | collective-permute-start | bytes 3145736 | tf_op jit(solution)/shard_map/ppermute | solution.py:28
  106.0 55.1 %collective-permute-start.6 = (bf16[2048,256]{1,0:T(8,128)(2,1)}, bf16[2048,256]{1,0:T(8,128)(2,1)}, u32[]{:S(2)}, u32[]{:S(2)}) collective-permute-start(bf16[2048,256]{1,0:T(8,128)(2,1)} %bitcast.63), channel_id=1, source_target_pairs={{1,0},{2,1},{3,2},{4,3},{5,4},{6,5},{7,6},{8,7},{9,8},{10,9},{11,1... | collective-permute-start | bytes 3145736 | tf_op jit(solution)/shard_map/ppermute | solution.py:28
  107.3 53.8 %collective-permute-start.7 = (bf16[2048,256]{1,0:T(8,128)(2,1)}, bf16[2048,256]{1,0:T(8,128)(2,1)}, u32[]{:S(2)}, u32[]{:S(2)}) collective-permute-start(bf16[2048,256]{1,0:T(8,128)(2,1)} %bitcast.62), channel_id=1, source_target_pairs={{0,1},{1,2},{2,3},{3,4},{4,5},{5,6},{6,7},{7,8},{8,9},{9,10},{10,1... | collective-permute-start | bytes 3145736 | tf_op jit(solution)/shard_map/ppermute | solution.py:28
  115.8 45.3 %all-to-all-start.1 = ((bf16[128,16,256]{2,1,0:T(8,128)(2,1)}), bf16[128,16,256]{2,1,0:T(8,128)(2,1)S(1)}, u32[]{:S(2)}, u32[]{:S(2)}) async-start(bf16[128,16,256]{2,1,0:T(8,128)(2,1)} %bitcast.55), calls=%async_computation.1 | async-start | bytes 2097152 | tf_op jit(solution)/shard_map/all_to_all | solution.py:282

commit v8 on v7

--- a/solution.py
+++ b/solution.py
@@ -70,13 +70,27 @@
     )(src_ids, tile_mask, *sources)
 
 
-def scatter_kernel(group, src_ids, mask_ref, grad_ref, own_ref, *rest):
+def scatter_kernel(group, src_ids, mask_ref, gq_ref, cot_ref, z_ref, wq_ref, wn2_ref, wn1_ref, gn_ref, own_ref, *rest):
     side_refs, total = rest[:-1], rest[-1]
     step = pl.program_id(0)
     tiles = mask_ref.shape[1]
     blk = mask_ref.shape[2]
     per_side = own_ref.shape[0]
+    width = gq_ref.shape[1]
     tn = (((0,), (0,)), ((), ()))
+    nt = (((1,), (1,)), ((), ()))
+    grad_update = cot_ref[...].astype(jnp.float32) + lax.dot_general(
+        gq_ref[...], wq_ref[...], nt, preferred_element_type=jnp.float32
+    )
+    update_low = grad_update.astype(jnp.bfloat16)
+    grad_z = lax.dot_general(update_low, wn2_ref[...], nt, preferred_element_type=jnp.float32)
+    grad_z = (grad_z * slope_of(z_ref[...])).astype(jnp.bfloat16)
+    grad_agg = lax.dot_general(
+        grad_z, wn1_ref[width : 2 * width, :], nt, preferred_element_type=jnp.float32
+    ).astype(jnp.bfloat16)
+    gn_ref[...] = grad_update + lax.dot_general(
+        grad_z, wn1_ref[0:width, :], nt, preferred_element_type=jnp.float32
+    )
 
     @pl.when(step == 0)
     def _():
@@ -86,7 +100,7 @@
         bits = jnp.concatenate(
             [mask_ref[g, k].astype(jnp.float32).astype(jnp.bfloat16) for k in range(tiles)], axis=1
         )
-        grad_rows = grad_ref[g * blk : (g + 1) * blk, :]
+        grad_rows = grad_agg[g * blk : (g + 1) * blk, :]
         parts = lax.dot_general(bits, grad_rows, tn, preferred_element_type=jnp.float32)
         for k in range(tiles):
             picked = src_ids[(step * group + g) * tiles + k]
@@ -100,9 +114,10 @@
             out_ref[...] = total[start : start + per_side].astype(out_ref.dtype)
 
 
-def tile_scatter(src_ids, tile_mask, grad_agg, sides, group=4):
+def tile_scatter(src_ids, tile_mask, grad_query, cot, zvalue, w_q, w_n2, w_n1, sides, group=4):
     blocks, tiles, blk, _ = tile_mask.shape
-    width = grad_agg.shape[-1]
+    width = grad_query.shape[-1]
+    rows = pl.BlockSpec((group * blk, width), lambda i, ids: (i, 0))
     return pl.pallas_call(
         functools.partial(scatter_kernel, group),
         grid_spec=pltpu.PrefetchScalarGridSpec(
@@ -110,18 +125,25 @@
             grid=(blocks // group,),
             in_specs=[
                 pl.BlockSpec((group, tiles, blk, blk), lambda i, ids: (i, 0, 0, 0)),
-                pl.BlockSpec((group * blk, width), lambda i, ids: (i, 0)),
+                rows,
+                rows,
+                rows,
+                pl.BlockSpec(w_q.shape, lambda i, ids: (0, 0)),
+                pl.BlockSpec(w_n2.shape, lambda i, ids: (0, 0)),
+                pl.BlockSpec(w_n1.shape, lambda i, ids: (0, 0)),
             ],
-            out_specs=[pl.BlockSpec((blocks, blk, width), lambda i, ids: (0, 0, 0))] * sides,
+            out_specs=[rows]
+            + [pl.BlockSpec((blocks, blk, width), lambda i, ids: (0, 0, 0))] * sides,
             scratch_shapes=[pltpu.VMEM((sides * blocks, blk, width), jnp.float32)],
         ),
-        out_shape=[jax.ShapeDtypeStruct((blocks, blk, width), jnp.float32)]
+        out_shape=[jax.ShapeDtypeStruct((blocks * blk, width), jnp.float32)]
+        + [jax.ShapeDtypeStruct((blocks, blk, width), jnp.float32)]
         + [jax.ShapeDtypeStruct((blocks, blk, width), jnp.bfloat16)] * (sides - 1),
         compiler_params=pltpu.CompilerParams(dimension_semantics=("arbitrary",)),
-    )(src_ids, tile_mask, grad_agg)
-
-
-def attend_kernel(scale, live_ref, q_ref, go_ref, kv_ref, gq_ref, gkv_ref, gk_acc, gv_acc):
+    )(src_ids, tile_mask, grad_query, cot, zvalue, w_q, w_n2, w_n1)
+
+
+def attend_kernel(scale, live_ref, q_ref, go_ref, kv_ref, wkv_ref, gq_ref, slots_ref, gk_acc, gv_acc):
     step = pl.program_id(0)
     width = q_ref.shape[1]
 
@@ -151,11 +173,14 @@
 
     @pl.when(step == pl.num_programs(0) - 1)
     def _():
-        gkv_ref[:, 0:width] = gk_acc[...].astype(gkv_ref.dtype)
-        gkv_ref[:, width : 2 * width] = gv_acc[...].astype(gkv_ref.dtype)
-
-
-def attend_back(live, queries, grad_out, keyvals, scale, rows_per_step=256):
+        grad_keys = gk_acc[...].astype(jnp.bfloat16)
+        grad_vals = gv_acc[...].astype(jnp.bfloat16)
+        slots = lax.dot_general(grad_keys, wkv_ref[:, 0:width], nt, preferred_element_type=jnp.float32)
+        slots += lax.dot_general(grad_vals, wkv_ref[:, width : 2 * width], nt, preferred_element_type=jnp.float32)
+        slots_ref[...] = slots.astype(slots_ref.dtype)
+
+
+def attend_back(live, queries, grad_out, keyvals, w_kv, scale, rows_per_step=256):
     rows, width = queries.shape
     slots = keyvals.shape[0]
     steps = rows // rows_per_step
@@ -168,11 +193,12 @@
             row_block,
             row_block,
             pl.BlockSpec((slots, 2 * width), lambda i: (0, 0)),
+            pl.BlockSpec(w_kv.shape, lambda i: (0, 0)),
         ],
-        out_specs=[row_block, pl.BlockSpec((slots, 2 * width), lambda i: (0, 0))],
+        out_specs=[row_block, pl.BlockSpec((slots, width), lambda i: (0, 0))],
         out_shape=(
             jax.ShapeDtypeStruct((rows, width), jnp.bfloat16),
-            jax.ShapeDtypeStruct((slots, 2 * width), jnp.bfloat16),
+            jax.ShapeDtypeStruct((slots, width), jnp.bfloat16),
         ),
         scratch_shapes=[
             pltpu.VMEM((slots, width), jnp.float32),
@@ -184,7 +210,7 @@
             transcendentals=rows * slots,
             bytes_accessed=2 * (3 * rows * width + 4 * slots * width),
         ),
-    )(live, queries, grad_out, keyvals)
+    )(live, queries, grad_out, keyvals, w_kv)
 
 
 def slope_of(values):
@@ -275,10 +301,9 @@
     arrived = dense(arrived_tokens, w_kv).astype(jnp.bfloat16)
     live_keys = (jnp.arange(slot_count)[None, :] < tok_count[:, 0][:, None]).reshape(1, -1)
     grad_out = dense(cotangent[0, 0], w_o.T).astype(jnp.bfloat16)
-    grad_query, grad_kv = attend_back(
-        live_keys.astype(jnp.float32), queries, grad_out, arrived, score_scale
-    )
-    grad_slots = dense(grad_kv, w_kv.T).astype(jnp.bfloat16)
+    grad_query, grad_slots = attend_back(
+        live_keys.astype(jnp.float32), queries, grad_out, arrived, w_kv, score_scale
+    )
     returned = lax.all_to_all(
         grad_slots.reshape(devices, slot_count, latent_width),
         ("px", "py"),
@@ -287,12 +312,9 @@
         tiled=True,
     )
     grad_tokens = returned.reshape(devices * slot_count, latent_width)
-    grad_update = cotangent[0, 0].astype(jnp.float32) + dense(grad_query, w_q.T)
-    update_low = grad_update.astype(jnp.bfloat16)
-    grad_z = (dense(update_low, w_n2.T) * silu_slope(zvalue)).astype(jnp.bfloat16)
-    grad_agg = dense(grad_z, w_n1[latent_width:].T).astype(jnp.bfloat16)
-    grad_node = grad_update + dense(grad_z, w_n1[:latent_width].T)
-    own_part, *outbound = tile_scatter(src_ids, tile_mask[0, 0], grad_agg, len(sources))
+    grad_node, own_part, *outbound = tile_scatter(
+        src_ids, tile_mask[0, 0], grad_query, cotangent[0, 0], zvalue, w_q, w_n2, w_n1, len(sources)
+    )
     outbound = [part.reshape(node_rows, latent_width) for part in outbound]
     received = [
         passed_along(outbound[0], "px", -1),

time: 169 us -> 167 us (0.988)
  blocking collectives: 0 us -> 48.6 us
  waiting for transfers between devices: 45.5 us -> 12.7 us
  matrix products: 24.8 us -> 12.6 us
  starting transfers between devices: 46.6 us -> 36.2 us
  Pallas kernels: 47.1 us -> 50.3 us
    all_to_all x0 -> x1, blocking collectives: none -> 48.6 us  [on_device(): lax.all_to_all(grad_slots.reshape(devices, slot_count, latent_width), ('p...]
    all_to_all x1 -> x0, waiting for transfers between devices: 31.8 us -> none  [on_device(): lax.all_to_all(grad_slots.reshape(devices, slot_count, latent_width), ('p...]
    dot_general x11 -> x6, matrix products: 24.8 us -> 12.6 us  [dense(): return jnp.dot(left, right, preferred_element_type=jnp.float32)]
    all_to_all x1 -> x0, starting transfers between devices: 10.5 us -> none  [on_device(): lax.all_to_all(grad_slots.reshape(devices, slot_count, latent_width), ('p...]
    pallas_call x1, Pallas kernels: 8.78 us -> 11.9 us  [tile_scatter(): pl.pallas_call(functools.partial(scatter_kernel, group), grid_spec=pltpu....]
  transfers between devices with their start and end apart: 10 -> 9, of which waited for: 2 -> 1; matrix products, arithmetic and copies ran while one was open for 9% -> 6% of each run, Pallas kernels for 0% -> 0%
where the time goes in v8:
time: 167 us; the launch traced here: 166 us
  Pallas kernels  50.3 us (30%)
  blocking collectives  48.6 us (29%)
  starting transfers between devices  36.2 us (22%)
  waiting for transfers between devices  12.7 us (8%)
  matrix products  12.6 us (8%)
  local copies, waits for them, and re-layouts  4.23 us (3%)
    all_to_all x1, blocking collectives, on_device(): lax.all_to_all(grad_slots.reshape(devices, slot_count, latent_width), ('p...  48.6 us
    ppermute x8, starting transfers between devices, passed_along(): lax.ppermute(value, axis, [(source, source + steps) for source in range(l...  24.8 us
    pallas_call x1, Pallas kernels, attend_back(): pl.pallas_call(functools.partial(attend_kernel, scale), grid=(steps,), in...  22.1 us
    ppermute x8, waiting for transfers between devices, passed_along(): lax.ppermute(value, axis, [(source, source + steps) for source in range(l...  12.7 us
    dot_general x6, matrix products, dense(): return jnp.dot(left, right, preferred_element_type=jnp.float32)  12.6 us
    pallas_call x1, Pallas kernels, tile_scatter(): pl.pallas_call(functools.partial(scatter_kernel, group), grid_spec=pltpu....  11.9 us
    all_to_all x1, starting transfers between devices, on_device(): lax.all_to_all(token_groups, ('px', 'py'), split_axis=0, concat_axis=0, t...  11.5 us
    pallas_call x1, Pallas kernels, tile_gather(): pl.pallas_call(functools.partial(gather_kernel, group), grid_spec=pltpu.P...  9.84 us
  transfers between devices with their start and end apart: 9, of which 1 were waited for; matrix products, arithmetic and copies ran while one was open for 6% of the time, Pallas kernels for 0%

profile of v8, /device:TPU:1, one launch (start us, length us, event | category | flops | bytes accessed | tf_op | source)
XLA Modules:
  0.0 166.3 jit_solution(13990173199227951940)
XLA Ops:
  0.6 0.0 copy-start
  0.6 0.0 copy-start.3
  0.7 0.0 copy-start.10
  0.7 11.5 %all-to-all-start = ((bf16[128,16,256]{2,1,0:T(8,128)(2,1)}), bf16[128,16,256]{2,1,0:T(8,128)(2,1)S(1)}, u32[]{:S(2)}, u32[]{:S(2)}) async-start(bf16[128,16,256]{2,1,0:T(8,128)(2,1)} %bitcast.50), calls=%async_computation | async-start | bytes 2097152 | tf_op jit(solution)/shard_map/all_to_all | solution.py:297
  12.2 0.0 copy-start.12
  12.2 0.0 copy-start.2
  12.2 1.8 %convolution_convert_fusion.3 = bf16[2048,256]{1,0:T(8,128)(2,1)} fusion(bf16[256,256]{1,0:T(8,128)(2,1)S(1)} %copy-done.9, bf16[256,256]{1,0:T(8,128)(2,1)S(1)} %copy-done.10, bf16[1,1,2048,256]{3,2,1,0:T(8,128)(2,1)S(1)} %copy-done.3), kind=kOutput, calls=%fused_computation.6 | convolution fusion | flops 540016640 | bytes 2359296 | tf_op jit(solution)/shard_map/dot_general | solution.py:253
  14.1 1.4 collective-permute-start.3
  15.5 5.0 %collective-permute-start.2 = (bf16[2048,256]{1,0:T(8,128)(2,1)}, bf16[2048,256]{1,0:T(8,128)(2,1)}, u32[]{:S(2)}, u32[]{:S(2)}) collective-permute-start(bf16[2048,256]{1,0:T(8,128)(2,1)} %convolution_convert_fusion.3), channel_id=1, source_target_pairs={{0,1},{1,2},{2,3},{3,4},{4,5},{5,6},{6,7},{7,8},{8,9},{9,10},{10,1... | collective-permute-start | bytes 3145736 | tf_op jit(solution)/shard_map/ppermute | solution.py:28
  20.5 3.5 %collective-permute-start.1 = (bf16[2048,256]{1,0:T(8,128)(2,1)}, bf16[2048,256]{1,0:T(8,128)(2,1)}, u32[]{:S(2)}, u32[]{:S(2)}) collective-permute-start(bf16[2048,256]{1,0:T(8,128)(2,1)} %convolution_convert_fusion.3), channel_id=1, source_target_pairs={{16,0},{32,16},{48,32},{64,48},{80,64},{96,80},{112,96},{17,1},{33... | collective-permute-start | bytes 3145736 | tf_op jit(solution)/shard_map/ppermute | solution.py:28
  24.1 2.6 %collective-permute-start = (bf16[2048,256]{1,0:T(8,128)(2,1)}, bf16[2048,256]{1,0:T(8,128)(2,1)}, u32[]{:S(2)}, u32[]{:S(2)}) collective-permute-start(bf16[2048,256]{1,0:T(8,128)(2,1)} %convolution_convert_fusion.3), channel_id=1, source_target_pairs={{0,16},{16,32},{32,48},{48,64},{64,80},{80,96},{96,112},{1,17},{17... | collective-permute-start | bytes 3145736 | tf_op jit(solution)/shard_map/ppermute | solution.py:28
  26.7 0.1 copy.16
  26.8 0.6 reshape_squeeze.6.src_ids
  27.4 0.7 fusion.6
  28.1 1.5 reshape.80.live_ref
  29.7 1.5 convolution_convert_fusion.1.go_ref
  31.1 1.8 %fusion.4 = f32[2048,256]{1,0:T(8,128)} fusion(bf16[512,256]{1,0:T(8,128)(2,1)S(1)} %copy-done.7, bf16[1,1,2048,256]{3,2,1,0:T(8,128)(2,1)S(1)} %copy-done.3), kind=kOutput, calls=%fused_computation.11 | convolution fusion | flops 268435456 | bytes 3276800 | tf_op jit(solution)/shard_map/dot_general | solution.py:253
  32.9 2.0 %convolution_convert_fusion.kv_ref = bf16[2048,512]{1,0:T(8,128)(2,1)} fusion(bf16[2048,256]{1,0:T(8,128)(2,1)S(1)} %bitcast.46, bf16[256,512]{1,0:T(8,128)(2,1)S(1)} %copy-done.8), kind=kOutput, calls=%fused_computation | convolution fusion | flops 537919488 | bytes 3407872 | tf_op jit(solution)/shard_map/dot_general | solution.py:253
  34.9 12.7 %collective-permute-done.3 = bf16[2048,256]{1,0:T(8,128)(2,1)} collective-permute-done((bf16[2048,256]{1,0:T(8,128)(2,1)}, bf16[2048,256]{1,0:T(8,128)(2,1)}, u32[]{:S(2)}, u32[]{:S(2)}) %collective-permute-start.3) | collective-permute-done | bytes 1048608 | tf_op jit(solution)/shard_map/ppermute | solution.py:28
  47.6 9.8 %shard_map.140 = bf16[2048,256]{1,0:T(8,128)(2,1)} custom-call(s32[64]{0:T(128)} %reshape_squeeze.6.src_ids, s32[16,4,128,128]{3,2,1,0:T(8,128)} %bitcast.43, bf16[16,128,256]{2,1,0:T(8,128)(2,1)} %bitcast.52, bf16[16,128,256]{2,1,0:T(8,128)(2,1)} %bitcast.4.up, bf16[16,128,256]{2,1,0:T(8,128)(2,1)} %bitcast.5.down, bf16[16,128,256]{2,1,0:T(8,128)(2,1)} %bitcast.6.left, ...), custom_call_target="tpu_custom_call" | custom-call | tf_op jit(solution)/shard_map/pallas_call | solution.py:58
  57.5 2.4 %convolution_add_fusion.1.z_ref = f32[2048,256]{1,0:T(8,128)S(1)} fusion(f32[2048,256]{1,0:T(8,128)} %fusion.4, bf16[2048,256]{1,0:T(8,128)(2,1)} %shard_map.140, bf16[512,256]{1,0:T(8,128)(2,1)S(1)} %copy-done.7), kind=kOutput, calls=%fused_computation.2 | convolution fusion | flops 268959744 | bytes 5373952 | tf_op jit(solution)/shard_map/dot_general | solution.py:253
  59.9 3.1 %convolution_convert_fusion.2.q_ref = bf16[2048,256]{1,0:T(8,128)(2,1)} fusion(bf16[256,256]{1,0:T(8,128)(2,1)} %wq_ref.1, bf16[256,256]{1,0:T(8,128)(2,1)} %wn2_ref.1, f32[2048,256]{1,0:T(8,128)S(1)} %convolution_add_fusion.1.z_ref, bf16[1,1,2048,256]{3,2,1,0:T(8,128)(2,1)S(1)} %copy-done.4), kind=kOutput, calls=%fused_computation.5 | convolution fusion | flops 541589504 | bytes 4456448 | tf_op jit(solution)/shard_map/dot_general | solution.py:253
  63.1 22.1 %shard_map.141 = (bf16[2048,256]{1,0:T(8,128)(2,1)}, bf16[2048,256]{1,0:T(8,128)(2,1)}) custom-call(f32[1,2048]{1,0:T(1,128)} %reshape.80.live_ref, bf16[2048,256]{1,0:T(8,128)(2,1)} %convolution_convert_fusion.2.q_ref, bf16[2048,256]{1,0:T(8,128)(2,1)} %convolution_convert_fusion.1.go_ref, bf16[2048,512]{1,0:T(8,128)(2,1)} %convolution_convert_fusion.kv_ref, ...), custom_call_target="tpu_custom_call" | custom-call | flops 10737418240 | bytes 7340032 | tf_op jit(solution)/shard_map/pallas_call | solution.py:188
  85.2 11.9 %shard_map.142 = (f32[2048,256]{1,0:T(8,128)}, f32[16,128,256]{2,1,0:T(8,128)}, bf16[16,128,256]{2,1,0:T(8,128)(2,1)}, bf16[16,128,256]{2,1,0:T(8,128)(2,1)}, bf...) custom-call(s32[64]{0:T(128)} %reshape_squeeze.6.src_ids, s32[16,4,128,128]{3,2,1,0:T(8,128)} %bitcast.44, ...), custom_call_target="tpu_custom_call" | custom-call | tf_op jit(solution)/shard_map/pallas_call | solution.py:121
  97.0 2.6 %collective-permute-start.4 = (bf16[2048,256]{1,0:T(8,128)(2,1)}, bf16[2048,256]{1,0:T(8,128)(2,1)S(1)}, u32[]{:S(2)}, u32[]{:S(2)}) collective-permute-start(bf16[2048,256]{1,0:T(8,128)(2,1)} %bitcast.58), channel_id=1, source_target_pairs={{16,0},{32,16},{48,32},{64,48},{80,64},{96,80},{112,96},{17,1},{33... | collective-permute-start | bytes 3145736 | tf_op jit(solution)/shard_map/ppermute | solution.py:28
  99.7 3.1 %collective-permute-start.5 = (bf16[2048,256]{1,0:T(8,128)(2,1)}, bf16[2048,256]{1,0:T(8,128)(2,1)}, u32[]{:S(2)}, u32[]{:S(2)}) collective-permute-start(bf16[2048,256]{1,0:T(8,128)(2,1)} %bitcast.57), channel_id=1, source_target_pairs={{0,16},{16,32},{32,48},{48,64},{64,80},{80,96},{96,112},{1,17},{17... | collective-permute-start | bytes 3145736 | tf_op jit(solution)/shard_map/ppermute | solution.py:28
  102.8 1.3 collective-permute-start.6
  104.1 5.1 %collective-permute-start.7 = (bf16[2048,256]{1,0:T(8,128)(2,1)}, bf16[2048,256]{1,0:T(8,128)(2,1)}, u32[]{:S(2)}, u32[]{:S(2)}) collective-permute-start(bf16[2048,256]{1,0:T(8,128)(2,1)} %bitcast.55), channel_id=1, source_target_pairs={{0,1},{1,2},{2,3},{3,4},{4,5},{5,6},{6,7},{7,8},{8,9},{9,10},{10,1... | collective-permute-start | bytes 3145736 | tf_op jit(solution)/shard_map/ppermute | solution.py:28
  109.2 48.6 %all_to_all.10 = bf16[128,16,256]{2,1,0:T(8,128)(2,1)S(1)} all-to-all(bf16[128,16,256]{2,1,0:T(8,128)(2,1)S(1)} %bitcast.51), channel_id=1, replica_groups=mesh['px'=8,'py'=16] {'px','py'}, dimensions={0} | all-to-all | bytes 2097152 | tf_op jit(solution)/shard_map/all_to_all | solution.py:307
  157.9 0.9 copy-done.6
  158.8 6.5 %shard_map.143 = bf16[2048,256]{1,0:T(8,128)(2,1)} custom-call(bf16[2048,256]{1,0:T(8,128)(2,1)} %bitcast.48, f32[2048,256]{1,0:T(8,128)} %bitcast.49, bf16[2048,256]{1,0:T(8,128)(2,1)} %copy-done.6, bf16[2048,256]{1,0:T(8,128)(2,1)} %collective-permute-done.5.b_ref, bf16[2048,256]{1,0:T(8,128)(2,1)} %collective-permute-done.6.c_ref, ...), custom_call_target="tpu_custom_call" | custom-call | flops 805306368 | bytes 10485760 | tf_op jit(solution)/shard_map/pallas_call | solution.py:238
  165.3 1.0 copy.18
  (28 shorter events, 0.1 us)
Async XLA Ops:
  0.6 29.0 %copy-start = (bf16[256,256]{1,0:T(8,128)(2,1)S(1)}, bf16[256,256]{1,0:T(8,128)(2,1)}, u32[]{:S(2)}) copy-start(bf16[256,256]{1,0:T(8,128)(2,1)} %param.24) | copy-start | bytes 393220
  0.6 11.5 %copy-start.3 = (bf16[1,1,2048,256]{3,2,1,0:T(8,128)(2,1)S(1)}, bf16[1,1,2048,256]{3,2,1,0:T(8,128)(2,1)}, u32[]{:S(2)}) copy-start(bf16[1,1,2048,256]{3,2,1,0:T(8,128)(2,1)} %param.13) | copy-start | bytes 3145732
  0.7 11.5 %copy-start.9 = (bf16[256,256]{1,0:T(8,128)(2,1)S(1)}, bf16[256,256]{1,0:T(8,128)(2,1)}, u32[]{:S(2)}) copy-start(bf16[256,256]{1,0:T(8,128)(2,1)} %w2_ref.1) | copy-start | bytes 393220
  0.7 11.5 %copy-start.10 = (bf16[256,256]{1,0:T(8,128)(2,1)S(1)}, bf16[256,256]{1,0:T(8,128)(2,1)}, u32[]{:S(2)}) copy-start(bf16[256,256]{1,0:T(8,128)(2,1)} %w1_ref.1) | copy-start | bytes 393220
  0.7 32.2 %all-to-all-start = ((bf16[128,16,256]{2,1,0:T(8,128)(2,1)}), bf16[128,16,256]{2,1,0:T(8,128)(2,1)S(1)}, u32[]{:S(2)}, u32[]{:S(2)}) async-start(bf16[128,16,256]{2,1,0:T(8,128)(2,1)} %bitcast.50), calls=%async_computation | async-start | bytes 2097152 | tf_op jit(solution)/shard_map/all_to_all | solution.py:297
  12.2 14.5 %copy-start.11 = (s32[1,1,16,4]{2,3,1,0:T(4,128)S(1)}, s32[1,1,16,4]{2,3,1,0:T(4,128)}, u32[]{:S(2)}) copy-start(s32[1,1,16,4]{2,3,1,0:T(4,128)} %param.14) | copy-start | bytes 772
  12.2 15.2 %copy-start.12 = (s32[128,1]{0,1:T(1,128)S(1)}, s32[128,1]{0,1:T(1,128)}, u32[]{:S(2)}) copy-start(s32[128,1]{0,1:T(1,128)} %param.17) | copy-start | bytes 1540
  12.2 17.4 %copy-start.2 = (bf16[1,1,2048,256]{3,2,1,0:T(8,128)(2,1)S(1)}, bf16[1,1,2048,256]{3,2,1,0:T(8,128)(2,1)}, u32[]{:S(2)}) copy-start(bf16[1,1,2048,256]{3,2,1,0:T(8,128)(2,1)} %param.25) | copy-start | bytes 3145732
  14.1 17.1 %copy-start.7 = (bf16[512,256]{1,0:T(8,128)(2,1)S(1)}, bf16[512,256]{1,0:T(8,128)(2,1)}, u32[]{:S(2)}) copy-start(bf16[512,256]{1,0:T(8,128)(2,1)} %wn1_ref.1) | copy-start | bytes 786436
  14.1 33.6 %collective-permute-start.3 = (bf16[2048,256]{1,0:T(8,128)(2,1)}, bf16[2048,256]{1,0:T(8,128)(2,1)}, u32[]{:S(2)}, u32[]{:S(2)}) collective-permute-start(bf16[2048,256]{1,0:T(8,128)(2,1)} %convolution_convert_fusion.3), channel_id=1, source_target_pairs={{1,0},{2,1},{3,2},{4,3},{5,4},{6,5},{7,6},{8,7},{9,8},{10,9},{11,1... | collective-permute-start | bytes 3145736 | tf_op jit(solution)/shard_map/ppermute | solution.py:28
  15.5 32.2 %collective-permute-start.2 = (bf16[2048,256]{1,0:T(8,128)(2,1)}, bf16[2048,256]{1,0:T(8,128)(2,1)}, u32[]{:S(2)}, u32[]{:S(2)}) collective-permute-start(bf16[2048,256]{1,0:T(8,128)(2,1)} %convolution_convert_fusion.3), channel_id=1, source_target_pairs={{0,1},{1,2},{2,3},{3,4},{4,5},{5,6},{6,7},{7,8},{8,9},{9,10},{10,1... | collective-permute-start | bytes 3145736 | tf_op jit(solution)/shard_map/ppermute | solution.py:28
  20.5 27.1 %collective-permute-start.1 = (bf16[2048,256]{1,0:T(8,128)(2,1)}, bf16[2048,256]{1,0:T(8,128)(2,1)}, u32[]{:S(2)}, u32[]{:S(2)}) collective-permute-start(bf16[2048,256]{1,0:T(8,128)(2,1)} %convolution_convert_fusion.3), channel_id=1, source_target_pairs={{16,0},{32,16},{48,32},{64,48},{80,64},{96,80},{112,96},{17,1},{33... | collective-permute-start | bytes 3145736 | tf_op jit(solution)/shard_map/ppermute | solution.py:28
  24.1 23.6 %collective-permute-start = (bf16[2048,256]{1,0:T(8,128)(2,1)}, bf16[2048,256]{1,0:T(8,128)(2,1)}, u32[]{:S(2)}, u32[]{:S(2)}) collective-permute-start(bf16[2048,256]{1,0:T(8,128)(2,1)} %convolution_convert_fusion.3), channel_id=1, source_target_pairs={{0,16},{16,32},{32,48},{48,64},{64,80},{80,96},{96,112},{1,17},{17... | collective-permute-start | bytes 3145736 | tf_op jit(solution)/shard_map/ppermute | solution.py:28
  31.1 1.8 %copy-start.8 = (bf16[256,512]{1,0:T(8,128)(2,1)S(1)}, bf16[256,512]{1,0:T(8,128)(2,1)}, u32[]{:S(2)}) copy-start(bf16[256,512]{1,0:T(8,128)(2,1)} %wkv_ref.1) | copy-start | bytes 786436
  57.5 2.4 %copy-start.4 = (bf16[1,1,2048,256]{3,2,1,0:T(8,128)(2,1)S(1)}, bf16[1,1,2048,256]{3,2,1,0:T(8,128)(2,1)}, u32[]{:S(2)}) copy-start(bf16[1,1,2048,256]{3,2,1,0:T(8,128)(2,1)} %param.13) | copy-start | bytes 3145732
  59.9 3.1 %copy-start.1 = (f32[2048,256]{1,0:T(8,128)}, f32[2048,256]{1,0:T(8,128)S(1)}, u32[]{:S(2)}) copy-start(f32[2048,256]{1,0:T(8,128)S(1)} %convolution_add_fusion.1.z_ref) | copy-start | bytes 6291460
  85.1 24.1 %copy-start.5 = (bf16[2048,256]{1,0:T(8,128)(2,1)S(1)}, bf16[2048,256]{1,0:T(8,128)(2,1)}, u32[]{:S(2)}) copy-start(bf16[2048,256]{1,0:T(8,128)(2,1)} %get-tuple-element.17) | copy-start | bytes 3145732
  97.0 60.8 %collective-permute-start.4 = (bf16[2048,256]{1,0:T(8,128)(2,1)}, bf16[2048,256]{1,0:T(8,128)(2,1)S(1)}, u32[]{:S(2)}, u32[]{:S(2)}) collective-permute-start(bf16[2048,256]{1,0:T(8,128)(2,1)} %bitcast.58), channel_id=1, source_target_pairs={{16,0},{32,16},{48,32},{64,48},{80,64},{96,80},{112,96},{17,1},{33... | collective-permute-start | bytes 3145736 | tf_op jit(solution)/shard_map/ppermute | solution.py:28
  99.7 58.2 %collective-permute-start.5 = (bf16[2048,256]{1,0:T(8,128)(2,1)}, bf16[2048,256]{1,0:T(8,128)(2,1)}, u32[]{:S(2)}, u32[]{:S(2)}) collective-permute-start(bf16[2048,256]{1,0:T(8,128)(2,1)} %bitcast.57), channel_id=1, source_target_pairs={{0,16},{16,32},{32,48},{48,64},{64,80},{80,96},{96,112},{1,17},{17... | collective-permute-start | bytes 3145736 | tf_op jit(solution)/shard_map/ppermute | solution.py:28
  102.8 55.0 %collective-permute-start.6 = (bf16[2048,256]{1,0:T(8,128)(2,1)}, bf16[2048,256]{1,0:T(8,128)(2,1)}, u32[]{:S(2)}, u32[]{:S(2)}) collective-permute-start(bf16[2048,256]{1,0:T(8,128)(2,1)} %bitcast.56), channel_id=1, source_target_pairs={{1,0},{2,1},{3,2},{4,3},{5,4},{6,5},{7,6},{8,7},{9,8},{10,9},{11,1... | collective-permute-start | bytes 3145736 | tf_op jit(solution)/shard_map/ppermute | solution.py:28
  104.1 53.8 %collective-permute-start.7 = (bf16[2048,256]{1,0:T(8,128)(2,1)}, bf16[2048,256]{1,0:T(8,128)(2,1)}, u32[]{:S(2)}, u32[]{:S(2)}) collective-permute-start(bf16[2048,256]{1,0:T(8,128)(2,1)} %bitcast.55), channel_id=1, source_target_pairs={{0,1},{1,2},{2,3},{3,4},{4,5},{5,6},{6,7},{7,8},{8,9},{9,10},{10,1... | collective-permute-start | bytes 3145736 | tf_op jit(solution)/shard_map/ppermute | solution.py:28
  157.9 1.0 copy-start.6

commit v9 on v8

--- a/solution.py
+++ b/solution.py
@@ -28,7 +28,10 @@
     return lax.ppermute(value, axis, [(source, source + steps) for source in range(leading, last)])
 
 
-def gather_kernel(group, src_ids, mask_ref, own, up, down, left, right, out_ref, rhs):
+def gather_kernel(
+    group, src_ids, mask_ref, own, up, down, left, right, lat_ref, wn1_ref, wn2_ref, wq_ref,
+    z_ref, q_ref, rhs, gath
+):
     step = pl.program_id(0)
     tiles = mask_ref.shape[1]
     blk = mask_ref.shape[2]
@@ -48,26 +51,44 @@
             [mask_ref[g, k].astype(jnp.float32).astype(jnp.bfloat16) for k in range(tiles)], axis=1
         )
         total = jnp.dot(bits, rhs[...], preferred_element_type=jnp.float32)
-        out_ref[g * blk : (g + 1) * blk, :] = total.astype(out_ref.dtype)
-
-
-def tile_gather(src_ids, tile_mask, sources, group=4):
+        gath[g * blk : (g + 1) * blk, :] = total.astype(gath.dtype)
+    width = lat_ref.shape[1]
+    latent = lat_ref[...]
+    zvalue = jnp.dot(latent, wn1_ref[0:width, :], preferred_element_type=jnp.float32)
+    zvalue += jnp.dot(gath[...], wn1_ref[width : 2 * width, :], preferred_element_type=jnp.float32)
+    z_ref[...] = zvalue
+    hidden = (zvalue / (1.0 + jnp.exp(-zvalue))).astype(jnp.bfloat16)
+    updated = latent.astype(jnp.float32) + jnp.dot(hidden, wn2_ref[...], preferred_element_type=jnp.float32)
+    queries = jnp.dot(updated.astype(jnp.bfloat16), wq_ref[...], preferred_element_type=jnp.float32)
+    q_ref[...] = queries.astype(q_ref.dtype)
+
+
+def tile_gather(src_ids, tile_mask, sources, latent, w_n1, w_n2, w_q, group=4):
     blocks, tiles, blk, _ = tile_mask.shape
     width = sources[0].shape[-1]
     whole = pl.BlockSpec((blocks, blk, width), lambda i, ids: (0, 0, 0))
+    rows = pl.BlockSpec((group * blk, width), lambda i, ids: (i, 0))
     return pl.pallas_call(
         functools.partial(gather_kernel, group),
         grid_spec=pltpu.PrefetchScalarGridSpec(
             num_scalar_prefetch=1,
             grid=(blocks // group,),
             in_specs=[pl.BlockSpec((group, tiles, blk, blk), lambda i, ids: (i, 0, 0, 0))]
-            + [whole] * len(sources),
-            out_specs=pl.BlockSpec((group * blk, width), lambda i, ids: (i, 0)),
-            scratch_shapes=[pltpu.VMEM((tiles * blk, width), jnp.bfloat16)],
-        ),
-        out_shape=jax.ShapeDtypeStruct((blocks * blk, width), jnp.bfloat16),
+            + [whole] * len(sources)
+            + [rows]
+            + [pl.BlockSpec(w.shape, lambda i, ids: (0, 0)) for w in (w_n1, w_n2, w_q)],
+            out_specs=[rows, rows],
+            scratch_shapes=[
+                pltpu.VMEM((tiles * blk, width), jnp.bfloat16),
+                pltpu.VMEM((group * blk, width), jnp.bfloat16),
+            ],
+        ),
+        out_shape=(
+            jax.ShapeDtypeStruct((blocks * blk, width), jnp.float32),
+            jax.ShapeDtypeStruct((blocks * blk, width), jnp.bfloat16),
+        ),
         compiler_params=pltpu.CompilerParams(dimension_semantics=("arbitrary",)),
-    )(src_ids, tile_mask, *sources)
+    )(src_ids, tile_mask, *sources, latent, w_n1, w_n2, w_q)
 
 
 def scatter_kernel(group, src_ids, mask_ref, gq_ref, cot_ref, z_ref, wq_ref, wn2_ref, wn1_ref, gn_ref, own_ref, *rest):
@@ -282,15 +303,15 @@
         passed_along(message, "py", -1),
     ]
     src_ids = tile_src[0, 0].reshape(-1)
-    gathered = tile_gather(
+    zvalue, queries = tile_gather(
         src_ids,
         tile_mask[0, 0],
         [part.reshape(block_count, blk_rows, latent_width) for part in sources],
-    )
-    zvalue = dense(latent, w_n1[:latent_width]) + dense(gathered, w_n1[latent_width:])
-    hidden = jax.nn.silu(zvalue).astype(jnp.bfloat16)
-    updated = (latent.astype(jnp.float32) + dense(hidden, w_n2)).astype(jnp.bfloat16)
-    queries = dense(updated, w_q).astype(jnp.bfloat16)
+        latent,
+        w_n1,
+        w_n2,
+        w_q,
+    )
     own_tokens = tokens[0]
     slot_count = own_tokens.shape[0] // devices
     token_groups = own_tokens.reshape(devices, slot_count, latent_width)

time: 167 us -> 165 us (0.988)
  matrix products: 12.6 us -> 5.32 us
  waiting for transfers between devices: 12.7 us -> 16.1 us
  Pallas kernels: 50.3 us -> 52.7 us
    dot_general x6 -> x3, matrix products: 12.6 us -> 5.32 us  [dense(): return jnp.dot(left, right, preferred_element_type=jnp.float32)]
    pallas_call x1, Pallas kernels: 9.84 us -> 12.3 us  [tile_gather(): pl.pallas_call(functools.partial(gather_kernel, group), grid_spec=pltpu.P...]
    ppermute x8, waiting for transfers between devices: 12.7 us -> 14.5 us  [passed_along(): lax.ppermute(value, axis, [(source, source + steps) for source in range(l...]
  transfers between devices with their start and end apart: 9 -> 9, of which waited for: 1 -> 2; matrix products, arithmetic and copies ran while one was open for 6% -> 4% of each run, Pallas kernels for 0% -> 0%
where the time goes in v9:
time: 165 us; the launch traced here: 164 us
  Pallas kernels  52.7 us (32%)
  blocking collectives  48.6 us (29%)
  starting transfers between devices  36 us (22%)
  waiting for transfers between devices  16.1 us (10%)
  matrix products  5.32 us (3%)
  local copies, waits for them, and re-layouts  4.3 us (3%)
    all_to_all x1, blocking collectives, on_device(): lax.all_to_all(grad_slots.reshape(devices, slot_count, latent_width), ('p...  48.6 us
    ppermute x8, starting transfers between devices, passed_along(): lax.ppermute(value, axis, [(source, source + steps) for source in range(l...  24.6 us
    pallas_call x1, Pallas kernels, attend_back(): pl.pallas_call(functools.partial(attend_kernel, scale), grid=(steps,), in...  22.1 us
    ppermute x8, waiting for transfers between devices, passed_along(): lax.ppermute(value, axis, [(source, source + steps) for source in range(l...  14.5 us
    pallas_call x1, Pallas kernels, tile_gather(): pl.pallas_call(functools.partial(gather_kernel, group), grid_spec=pltpu.P...  12.3 us
    pallas_call x1, Pallas kernels, tile_scatter(): pl.pallas_call(functools.partial(scatter_kernel, group), grid_spec=pltpu....  11.9 us
    all_to_all x1, starting transfers between devices, on_device(): lax.all_to_all(token_groups, ('px', 'py'), split_axis=0, concat_axis=0, t...  11.5 us
    pallas_call x1, Pallas kernels, edge_back(): pl.pallas_call(edge_back_kernel, grid=(rows // rows_per_step,), in_specs=...  6.48 us
  transfers between devices with their start and end apart: 9, of which 2 were waited for; matrix products, arithmetic and copies ran while one was open for 4% of the time, Pallas kernels for 0%

profile of v9, /device:TPU:1, one launch (start us, length us, event | category | flops | bytes accessed | tf_op | source)
XLA Modules:
  0.0 164.0 jit_solution(13676193526859837899)
XLA Ops:
  0.6 0.0 copy-start
  0.6 0.0 copy-start.7
  0.7 0.0 copy-start.8
  0.7 0.0 copy-start.2
  0.7 11.5 %all-to-all-start = ((bf16[128,16,256]{2,1,0:T(8,128)(2,1)}), bf16[128,16,256]{2,1,0:T(8,128)(2,1)S(1)}, u32[]{:S(2)}, u32[]{:S(2)}) async-start(bf16[128,16,256]{2,1,0:T(8,128)(2,1)} %bitcast.42), calls=%async_computation | async-start | bytes 2097152 | tf_op jit(solution)/shard_map/all_to_all | solution.py:318
  12.2 0.0 copy-start.10
  12.2 0.0 copy-start.1
  12.2 1.8 %convolution_convert_fusion.2 = bf16[2048,256]{1,0:T(8,128)(2,1)} fusion(bf16[256,256]{1,0:T(8,128)(2,1)S(1)} %copy-done.7, bf16[256,256]{1,0:T(8,128)(2,1)S(1)} %copy-done.8, bf16[1,1,2048,256]{3,2,1,0:T(8,128)(2,1)S(1)} %copy-done.2), kind=kOutput, calls=%fused_computation.2 | convolution fusion | flops 540016640 | bytes 2359296 | tf_op jit(solution)/shard_map/dot_general | solution.py:274
  14.1 1.3 collective-permute-start.3
  15.3 5.0 %collective-permute-start.2 = (bf16[2048,256]{1,0:T(8,128)(2,1)}, bf16[2048,256]{1,0:T(8,128)(2,1)}, u32[]{:S(2)}, u32[]{:S(2)}) collective-permute-start(bf16[2048,256]{1,0:T(8,128)(2,1)} %convolution_convert_fusion.2), channel_id=1, source_target_pairs={{0,1},{1,2},{2,3},{3,4},{4,5},{5,6},{6,7},{7,8},{8,9},{9,10},{10,1... | collective-permute-start | bytes 3145736 | tf_op jit(solution)/shard_map/ppermute | solution.py:28
  20.3 3.5 %collective-permute-start.1 = (bf16[2048,256]{1,0:T(8,128)(2,1)}, bf16[2048,256]{1,0:T(8,128)(2,1)}, u32[]{:S(2)}, u32[]{:S(2)}) collective-permute-start(bf16[2048,256]{1,0:T(8,128)(2,1)} %convolution_convert_fusion.2), channel_id=1, source_target_pairs={{16,0},{32,16},{48,32},{64,48},{80,64},{96,80},{112,96},{17,1},{33... | collective-permute-start | bytes 3145736 | tf_op jit(solution)/shard_map/ppermute | solution.py:28
  23.8 2.6 %collective-permute-start = (bf16[2048,256]{1,0:T(8,128)(2,1)}, bf16[2048,256]{1,0:T(8,128)(2,1)}, u32[]{:S(2)}, u32[]{:S(2)}) collective-permute-start(bf16[2048,256]{1,0:T(8,128)(2,1)} %convolution_convert_fusion.2), channel_id=1, source_target_pairs={{0,16},{16,32},{32,48},{48,64},{64,80},{80,96},{96,112},{1,17},{17... | collective-permute-start | bytes 3145736 | tf_op jit(solution)/shard_map/ppermute | solution.py:28
  26.5 0.1 copy.16
  26.5 0.6 reshape_squeeze.6.src_ids
  27.2 0.1 fusion
  27.2 0.7 reshape.80.live_ref
  27.9 1.5 convolution_convert_fusion.1.go_ref
  29.5 1.5 all-to-all-done
  31.0 2.0 %convolution_convert_fusion.kv_ref = bf16[2048,512]{1,0:T(8,128)(2,1)} fusion(bf16[2048,256]{1,0:T(8,128)(2,1)S(1)} %bitcast.37, bf16[256,512]{1,0:T(8,128)(2,1)S(1)} %copy-done.6), kind=kOutput, calls=%fused_computation | convolution fusion | flops 537919488 | bytes 3407872 | tf_op jit(solution)/shard_map/dot_general | solution.py:274
  33.0 14.5 %collective-permute-done.3 = bf16[2048,256]{1,0:T(8,128)(2,1)S(1)} collective-permute-done((bf16[2048,256]{1,0:T(8,128)(2,1)}, bf16[2048,256]{1,0:T(8,128)(2,1)S(1)}, u32[]{:S(2)}, u32[]{:S(2)}) %collective-permute-start.3) | collective-permute-done | bytes 1048608 | tf_op jit(solution)/shard_map/ppermute | solution.py:28
  47.5 0.9 copy-done.4
  48.5 12.3 %shard_map.140 = (f32[2048,256]{1,0:T(8,128)}, bf16[2048,256]{1,0:T(8,128)(2,1)}) custom-call(s32[64]{0:T(128)} %reshape_squeeze.6.src_ids, s32[16,4,128,128]{3,2,1,0:T(8,128)} %bitcast.34, bf16[16,128,256]{2,1,0:T(8,128)(2,1)} %bitcast.44, bf16[16,128,256]{2,1,0:T(8,128)(2,1)} %bitcast.4.up, bf16[16,128,256]{2,1,0:T(8,128)(2,1)} %bitcast.5.down, ...), custom_call_target="tpu_custom_call" | custom-call | tf_op jit(solution)/shard_map/pallas_call | solution.py:71
  60.8 22.1 %shard_map.141 = (bf16[2048,256]{1,0:T(8,128)(2,1)}, bf16[2048,256]{1,0:T(8,128)(2,1)}) custom-call(f32[1,2048]{1,0:T(1,128)} %reshape.80.live_ref, bf16[2048,256]{1,0:T(8,128)(2,1)} %get-tuple-element.12.q_ref, bf16[2048,256]{1,0:T(8,128)(2,1)} %convolution_convert_fusion.1.go_ref, bf16[2048,512]{1,0:T(8,128)(2,1)} %convolution_convert_fusion.kv_ref, ...), custom_call_target="tpu_custom_call" | custom-call | flops 10737418240 | bytes 7340032 | tf_op jit(solution)/shard_map/pallas_call | solution.py:209
  82.8 11.9 %shard_map.142 = (f32[2048,256]{1,0:T(8,128)}, f32[16,128,256]{2,1,0:T(8,128)}, bf16[16,128,256]{2,1,0:T(8,128)(2,1)}, bf16[16,128,256]{2,1,0:T(8,128)(2,1)}, bf...) custom-call(s32[64]{0:T(128)} %reshape_squeeze.6.src_ids, s32[16,4,128,128]{3,2,1,0:T(8,128)} %bitcast.35, ...), custom_call_target="tpu_custom_call" | custom-call | tf_op jit(solution)/shard_map/pallas_call | solution.py:142
  94.8 2.6 %collective-permute-start.4 = (bf16[2048,256]{1,0:T(8,128)(2,1)}, bf16[2048,256]{1,0:T(8,128)(2,1)S(1)}, u32[]{:S(2)}, u32[]{:S(2)}) collective-permute-start(bf16[2048,256]{1,0:T(8,128)(2,1)} %bitcast.51), channel_id=1, source_target_pairs={{16,0},{32,16},{48,32},{64,48},{80,64},{96,80},{112,96},{17,1},{33... | collective-permute-start | bytes 3145736 | tf_op jit(solution)/shard_map/ppermute | solution.py:28
  97.4 3.2 %collective-permute-start.5 = (bf16[2048,256]{1,0:T(8,128)(2,1)}, bf16[2048,256]{1,0:T(8,128)(2,1)}, u32[]{:S(2)}, u32[]{:S(2)}) collective-permute-start(bf16[2048,256]{1,0:T(8,128)(2,1)} %bitcast.50), channel_id=1, source_target_pairs={{0,16},{16,32},{32,48},{48,64},{64,80},{80,96},{96,112},{1,17},{17... | collective-permute-start | bytes 3145736 | tf_op jit(solution)/shard_map/ppermute | solution.py:28
  100.6 1.3 collective-permute-start.6
  101.9 5.1 %collective-permute-start.7 = (bf16[2048,256]{1,0:T(8,128)(2,1)}, bf16[2048,256]{1,0:T(8,128)(2,1)}, u32[]{:S(2)}, u32[]{:S(2)}) collective-permute-start(bf16[2048,256]{1,0:T(8,128)(2,1)} %bitcast.48), channel_id=1, source_target_pairs={{0,1},{1,2},{2,3},{3,4},{4,5},{5,6},{6,7},{7,8},{8,9},{9,10},{10,1... | collective-permute-start | bytes 3145736 | tf_op jit(solution)/shard_map/ppermute | solution.py:28
  107.0 48.6 %all_to_all.10 = bf16[128,16,256]{2,1,0:T(8,128)(2,1)S(1)} all-to-all(bf16[128,16,256]{2,1,0:T(8,128)(2,1)S(1)} %bitcast.43), channel_id=1, replica_groups=mesh['px'=8,'py'=16] {'px','py'}, dimensions={0} | all-to-all | bytes 2097152 | tf_op jit(solution)/shard_map/all_to_all | solution.py:328
  155.6 0.9 copy-done.5
  156.6 6.5 %shard_map.143 = bf16[2048,256]{1,0:T(8,128)(2,1)} custom-call(bf16[2048,256]{1,0:T(8,128)(2,1)} %bitcast.40, f32[2048,256]{1,0:T(8,128)} %bitcast.41, bf16[2048,256]{1,0:T(8,128)(2,1)} %copy-done.5, bf16[2048,256]{1,0:T(8,128)(2,1)} %collective-permute-done.5.b_ref, bf16[2048,256]{1,0:T(8,128)(2,1)} %collective-permute-done.6.c_ref, ...), custom_call_target="tpu_custom_call" | custom-call | flops 805306368 | bytes 10485760 | tf_op jit(solution)/shard_map/pallas_call | solution.py:259
  163.1 1.0 copy.18
  (21 shorter events, 0.0 us)
Async XLA Ops:
  0.6 27.3 %copy-start = (bf16[256,256]{1,0:T(8,128)(2,1)S(1)}, bf16[256,256]{1,0:T(8,128)(2,1)}, u32[]{:S(2)}) copy-start(bf16[256,256]{1,0:T(8,128)(2,1)} %param.24) | copy-start | bytes 393220
  0.6 11.5 %copy-start.7 = (bf16[256,256]{1,0:T(8,128)(2,1)S(1)}, bf16[256,256]{1,0:T(8,128)(2,1)}, u32[]{:S(2)}) copy-start(bf16[256,256]{1,0:T(8,128)(2,1)} %w2_ref.1) | copy-start | bytes 393220
  0.7 11.5 %copy-start.8 = (bf16[256,256]{1,0:T(8,128)(2,1)S(1)}, bf16[256,256]{1,0:T(8,128)(2,1)}, u32[]{:S(2)}) copy-start(bf16[256,256]{1,0:T(8,128)(2,1)} %w1_ref.1) | copy-start | bytes 393220
  0.7 11.5 %copy-start.2 = (bf16[1,1,2048,256]{3,2,1,0:T(8,128)(2,1)S(1)}, bf16[1,1,2048,256]{3,2,1,0:T(8,128)(2,1)}, u32[]{:S(2)}) copy-start(bf16[1,1,2048,256]{3,2,1,0:T(8,128)(2,1)} %param.13) | copy-start | bytes 3145732
  0.7 30.3 %all-to-all-start = ((bf16[128,16,256]{2,1,0:T(8,128)(2,1)}), bf16[128,16,256]{2,1,0:T(8,128)(2,1)S(1)}, u32[]{:S(2)}, u32[]{:S(2)}) async-start(bf16[128,16,256]{2,1,0:T(8,128)(2,1)} %bitcast.42), calls=%async_computation | async-start | bytes 2097152 | tf_op jit(solution)/shard_map/all_to_all | solution.py:318
  12.2 14.2 %copy-start.9 = (s32[1,1,16,4]{2,3,1,0:T(4,128)S(1)}, s32[1,1,16,4]{2,3,1,0:T(4,128)}, u32[]{:S(2)}) copy-start(s32[1,1,16,4]{2,3,1,0:T(4,128)} %param.14) | copy-start | bytes 772
  12.2 14.9 %copy-start.10 = (s32[128,1]{0,1:T(1,128)S(1)}, s32[128,1]{0,1:T(1,128)}, u32[]{:S(2)}) copy-start(s32[128,1]{0,1:T(1,128)} %param.17) | copy-start | bytes 1540
  12.2 15.7 %copy-start.1 = (bf16[1,1,2048,256]{3,2,1,0:T(8,128)(2,1)S(1)}, bf16[1,1,2048,256]{3,2,1,0:T(8,128)(2,1)}, u32[]{:S(2)}) copy-start(bf16[1,1,2048,256]{3,2,1,0:T(8,128)(2,1)} %param.25) | copy-start | bytes 3145732
  14.1 33.5 %collective-permute-start.3 = (bf16[2048,256]{1,0:T(8,128)(2,1)}, bf16[2048,256]{1,0:T(8,128)(2,1)S(1)}, u32[]{:S(2)}, u32[]{:S(2)}) collective-permute-start(bf16[2048,256]{1,0:T(8,128)(2,1)} %convolution_convert_fusion.2), channel_id=1, source_target_pairs={{1,0},{2,1},{3,2},{4,3},{5,4},{6,5},{7,6},{8,7},{9,8},{10,9},{11,1... | collective-permute-start | bytes 3145736 | tf_op jit(solution)/shard_map/ppermute | solution.py:28
  15.3 32.2 %collective-permute-start.2 = (bf16[2048,256]{1,0:T(8,128)(2,1)}, bf16[2048,256]{1,0:T(8,128)(2,1)}, u32[]{:S(2)}, u32[]{:S(2)}) collective-permute-start(bf16[2048,256]{1,0:T(8,128)(2,1)} %convolution_convert_fusion.2), channel_id=1, source_target_pairs={{0,1},{1,2},{2,3},{3,4},{4,5},{5,6},{6,7},{7,8},{8,9},{9,10},{10,1... | collective-permute-start | bytes 3145736 | tf_op jit(solution)/shard_map/ppermute | solution.py:28
  20.3 27.2 %collective-permute-start.1 = (bf16[2048,256]{1,0:T(8,128)(2,1)}, bf16[2048,256]{1,0:T(8,128)(2,1)}, u32[]{:S(2)}, u32[]{:S(2)}) collective-permute-start(bf16[2048,256]{1,0:T(8,128)(2,1)} %convolution_convert_fusion.2), channel_id=1, source_target_pairs={{16,0},{32,16},{48,32},{64,48},{80,64},{96,80},{112,96},{17,1},{33... | collective-permute-start | bytes 3145736 | tf_op jit(solution)/shard_map/ppermute | solution.py:28
  23.8 23.7 %collective-permute-start = (bf16[2048,256]{1,0:T(8,128)(2,1)}, bf16[2048,256]{1,0:T(8,128)(2,1)}, u32[]{:S(2)}, u32[]{:S(2)}) collective-permute-start(bf16[2048,256]{1,0:T(8,128)(2,1)} %convolution_convert_fusion.2), channel_id=1, source_target_pairs={{0,16},{16,32},{32,48},{48,64},{64,80},{80,96},{96,112},{1,17},{17... | collective-permute-start | bytes 3145736 | tf_op jit(solution)/shard_map/ppermute | solution.py:28
  27.9 3.1 %copy-start.6 = (bf16[256,512]{1,0:T(8,128)(2,1)S(1)}, bf16[256,512]{1,0:T(8,128)(2,1)}, u32[]{:S(2)}) copy-start(bf16[256,512]{1,0:T(8,128)(2,1)} %wkv_ref.1) | copy-start | bytes 786436
  47.5 1.0 copy-start.4
  82.8 24.1 %copy-start.3 = (bf16[2048,256]{1,0:T(8,128)(2,1)S(1)}, bf16[2048,256]{1,0:T(8,128)(2,1)}, u32[]{:S(2)}) copy-start(bf16[2048,256]{1,0:T(8,128)(2,1)} %get-tuple-element.21) | copy-start | bytes 3145732
  94.8 60.8 %collective-permute-start.4 = (bf16[2048,256]{1,0:T(8,128)(2,1)}, bf16[2048,256]{1,0:T(8,128)(2,1)S(1)}, u32[]{:S(2)}, u32[]{:S(2)}) collective-permute-start(bf16[2048,256]{1,0:T(8,128)(2,1)} %bitcast.51), channel_id=1, source_target_pairs={{16,0},{32,16},{48,32},{64,48},{80,64},{96,80},{112,96},{17,1},{33... | collective-permute-start | bytes 3145736 | tf_op jit(solution)/shard_map/ppermute | solution.py:28
  97.4 58.2 %collective-permute-start.5 = (bf16[2048,256]{1,0:T(8,128)(2,1)}, bf16[2048,256]{1,0:T(8,128)(2,1)}, u32[]{:S(2)}, u32[]{:S(2)}) collective-permute-start(bf16[2048,256]{1,0:T(8,128)(2,1)} %bitcast.50), channel_id=1, source_target_pairs={{0,16},{16,32},{32,48},{48,64},{64,80},{80,96},{96,112},{1,17},{17... | collective-permute-start | bytes 3145736 | tf_op jit(solution)/shard_map/ppermute | solution.py:28
  100.6 55.0 %collective-permute-start.6 = (bf16[2048,256]{1,0:T(8,128)(2,1)}, bf16[2048,256]{1,0:T(8,128)(2,1)}, u32[]{:S(2)}, u32[]{:S(2)}) collective-permute-start(bf16[2048,256]{1,0:T(8,128)(2,1)} %bitcast.49), channel_id=1, source_target_pairs={{1,0},{2,1},{3,2},{4,3},{5,4},{6,5},{7,6},{8,7},{9,8},{10,9},{11,1... | collective-permute-start | bytes 3145736 | tf_op jit(solution)/shard_map/ppermute | solution.py:28
  101.9 53.7 %collective-permute-start.7 = (bf16[2048,256]{1,0:T(8,128)(2,1)}, bf16[2048,256]{1,0:T(8,128)(2,1)}, u32[]{:S(2)}, u32[]{:S(2)}) collective-permute-start(bf16[2048,256]{1,0:T(8,128)(2,1)} %bitcast.48), channel_id=1, source_target_pairs={{0,1},{1,2},{2,3},{3,4},{4,5},{5,6},{6,7},{7,8},{8,9},{9,10},{10,1... | collective-permute-start | bytes 3145736 | tf_op jit(solution)/shard_map/ppermute | solution.py:28
  155.6 1.0 copy-start.5

commit v10 on v9

--- a/solution.py
+++ b/solution.py
@@ -302,6 +302,7 @@
         passed_along(message, "py", 1),
         passed_along(message, "py", -1),
     ]
+    held_tokens, sources[1] = lax.optimization_barrier((tokens, sources[1]))
     src_ids = tile_src[0, 0].reshape(-1)
     zvalue, queries = tile_gather(
         src_ids,
@@ -312,7 +313,7 @@
         w_n2,
         w_q,
     )
-    own_tokens = tokens[0]
+    own_tokens = held_tokens[0]
     slot_count = own_tokens.shape[0] // devices
     token_groups = own_tokens.reshape(devices, slot_count, latent_width)
     arrived_tokens = lax.all_to_all(

time: 165 us -> 165 us (level)
  blocking collectives: 48.6 us -> 44.7 us
  waiting for transfers between devices: 16.1 us -> 20 us
    all_to_all x1, waiting for transfers between devices: 1.55 us -> 11.8 us  [on_device(): lax.all_to_all(token_groups, ('px', 'py'), split_axis=0, concat_axis=0, t...]
    ppermute x8, waiting for transfers between devices: 14.5 us -> 8.14 us  [passed_along(): lax.ppermute(value, axis, [(source, source + steps) for source in range(l...]
    all_to_all x1, blocking collectives: 48.6 us -> 44.7 us  [on_device(): lax.all_to_all(grad_slots.reshape(devices, slot_count, latent_width), ('p...]
  transfers between devices with their start and end apart: 9 -> 9, of which waited for: 2 -> 3; matrix products, arithmetic and copies ran while one was open for 4% -> 2% of each run, Pallas kernels for 0% -> 8%
where the time goes in v10:
time: 165 us; the launch traced here: 164 us
  Pallas kernels  52.9 us (32%)
  blocking collectives  44.7 us (27%)
  starting transfers between devices  36 us (22%)
  waiting for transfers between devices  20 us (12%)
  matrix products  5.61 us (3%)
  local copies, waits for them, and re-layouts  4.38 us (3%)
    all_to_all x1, blocking collectives, on_device(): lax.all_to_all(grad_slots.reshape(devices, slot_count, latent_width), ('p...  44.7 us
    ppermute x8, starting transfers between devices, passed_along(): lax.ppermute(value, axis, [(source, source + steps) for source in range(l...  25.1 us
    pallas_call x1, Pallas kernels, attend_back(): pl.pallas_call(functools.partial(attend_kernel, scale), grid=(steps,), in...  22.1 us
    pallas_call x1, Pallas kernels, tile_gather(): pl.pallas_call(functools.partial(gather_kernel, group), grid_spec=pltpu.P...  12.4 us
    pallas_call x1, Pallas kernels, tile_scatter(): pl.pallas_call(functools.partial(scatter_kernel, group), grid_spec=pltpu....  11.9 us
    all_to_all x1, waiting for transfers between devices, on_device(): lax.all_to_all(token_groups, ('px', 'py'), split_axis=0, concat_axis=0, t...  11.8 us
    all_to_all x1, starting transfers between devices, on_device(): lax.all_to_all(token_groups, ('px', 'py'), split_axis=0, concat_axis=0, t...  10.9 us
    ppermute x8, waiting for transfers between devices, passed_along(): lax.ppermute(value, axis, [(source, source + steps) for source in range(l...  8.14 us
  transfers between devices with their start and end apart: 9, of which 3 were waited for; matrix products, arithmetic and copies ran while one was open for 2% of the time, Pallas kernels for 8%

profile of v10, /device:TPU:1, one launch (start us, length us, event | category | flops | bytes accessed | tf_op | source)
XLA Modules:
  0.0 164.4 jit_solution(9898773194637073325)
XLA Ops:
  0.6 0.0 copy-start
  0.6 2.2 %convolution_convert_fusion.2 = bf16[2048,256]{1,0:T(8,128)(2,1)S(1)} fusion(bf16[256,256]{1,0:T(8,128)(2,1)} %w2_ref.1, bf16[256,256]{1,0:T(8,128)(2,1)} %w1_ref.1, bf16[1,1,2048,256]{3,2,1,0:T(8,128)(2,1)} %param.13), kind=kOutput, calls=%fused_computation.2 | convolution fusion | flops 540016640 | bytes 2359296 | tf_op jit(solution)/shard_map/dot_general | solution.py:274
  2.8 0.0 copy-start.3
  2.8 0.0 copy-start.7
  2.8 0.0 copy-start.8
  2.9 0.0 copy-start.1
  2.9 5.1 %collective-permute-start = (bf16[2048,256]{1,0:T(8,128)(2,1)S(1)}, bf16[2048,256]{1,0:T(8,128)(2,1)S(1)}, u32[]{:S(2)}, u32[]{:S(2)}) collective-permute-start(bf16[2048,256]{1,0:T(8,128)(2,1)S(1)} %convolution_convert_fusion.2), channel_id=1, source_target_pairs={{0,16},{16,32},{32,48},{48,64},{64,80},{80,96},{96,112},{1,17},{17... | collective-permute-start | bytes 3145736 | tf_op jit(solution)/shard_map/ppermute | solution.py:28
  7.9 1.3 collective-permute-start.3
  9.2 5.0 %collective-permute-start.2 = (bf16[2048,256]{1,0:T(8,128)(2,1)S(1)}, bf16[2048,256]{1,0:T(8,128)(2,1)}, u32[]{:S(2)}, u32[]{:S(2)}) collective-permute-start(bf16[2048,256]{1,0:T(8,128)(2,1)S(1)} %convolution_convert_fusion.2), channel_id=1, source_target_pairs={{0,1},{1,2},{2,3},{3,4},{4,5},{5,6},{6,7},{7,8},{8,9},{9,10},{10,1... | collective-permute-start | bytes 3145736 | tf_op jit(solution)/shard_map/ppermute | solution.py:28
  14.2 1.9 %collective-permute-start.1 = (bf16[2048,256]{1,0:T(8,128)(2,1)S(1)}, bf16[2048,256]{1,0:T(8,128)(2,1)}, u32[]{:S(2)}, u32[]{:S(2)}) collective-permute-start(bf16[2048,256]{1,0:T(8,128)(2,1)S(1)} %convolution_convert_fusion.2), channel_id=1, source_target_pairs={{16,0},{32,16},{48,32},{64,48},{80,64},{96,80},{112,96},{17,1},{33... | collective-permute-start | bytes 3145736 | tf_op jit(solution)/shard_map/ppermute | solution.py:28
  16.1 3.5 %collective-permute-done = bf16[2048,256]{1,0:T(8,128)(2,1)S(1)} collective-permute-done((bf16[2048,256]{1,0:T(8,128)(2,1)S(1)}, bf16[2048,256]{1,0:T(8,128)(2,1)S(1)}, u32[]{:S(2)}, u32[]{:S(2)}) %collective-permute-start) | collective-permute-done | bytes 1048608 | tf_op jit(solution)/shard_map/ppermute | solution.py:28
  19.7 1.0 copy-done.4
  20.6 10.9 %all-to-all-start = ((bf16[128,16,256]{2,1,0:T(8,128)(2,1)}), bf16[128,16,256]{2,1,0:T(8,128)(2,1)S(1)}, u32[]{:S(2)}, u32[]{:S(2)}) async-start(bf16[128,16,256]{2,1,0:T(8,128)(2,1)} %bitcast.9), calls=%async_computation | async-start | bytes 2097152 | tf_op jit(solution)/shard_map/all_to_all | solution.py:319
  31.6 0.1 copy.16
  31.7 0.7 reshape_squeeze.6.src_ids
  32.4 0.1 fusion
  32.4 0.7 reshape.80.live_ref
  33.1 1.4 convolution_convert_fusion.1.go_ref
  34.6 4.6 %collective-permute-done.2 = bf16[2048,256]{1,0:T(8,128)(2,1)} collective-permute-done((bf16[2048,256]{1,0:T(8,128)(2,1)S(1)}, bf16[2048,256]{1,0:T(8,128)(2,1)}, u32[]{:S(2)}, u32[]{:S(2)}) %collective-permute-start.2) | collective-permute-done | bytes 1048608 | tf_op jit(solution)/shard_map/ppermute | solution.py:28
  39.2 12.4 %shard_map.140 = (f32[2048,256]{1,0:T(8,128)}, bf16[2048,256]{1,0:T(8,128)(2,1)}) custom-call(s32[64]{0:T(128)} %reshape_squeeze.6.src_ids, s32[16,4,128,128]{3,2,1,0:T(8,128)} %bitcast.34, bf16[16,128,256]{2,1,0:T(8,128)(2,1)} %bitcast.43, bf16[16,128,256]{2,1,0:T(8,128)(2,1)} %bitcast.44, bf16[16,128,256]{2,1,0:T(8,128)(2,1)} %bitcast.5.down, ...), custom_call_target="tpu_custom_call" | custom-call | tf_op jit(solution)/shard_map/pallas_call | solution.py:71
  51.6 11.8 %all-to-all-done = bf16[128,16,256]{2,1,0:T(8,128)(2,1)S(1)} async-done(((bf16[128,16,256]{2,1,0:T(8,128)(2,1)}), bf16[128,16,256]{2,1,0:T(8,128)(2,1)S(1)}, u32[]{:S(2)}, u32[]{:S(2)}) %all-to-all-start) | async-done | bytes 1048608 | tf_op jit(solution)/shard_map/all_to_all | solution.py:319
  63.4 2.0 %convolution_convert_fusion.kv_ref = bf16[2048,512]{1,0:T(8,128)(2,1)} fusion(bf16[2048,256]{1,0:T(8,128)(2,1)S(1)} %bitcast.37, bf16[256,512]{1,0:T(8,128)(2,1)S(1)} %copy-done.6), kind=kOutput, calls=%fused_computation | convolution fusion | flops 537919488 | bytes 3407872 | tf_op jit(solution)/shard_map/dot_general | solution.py:274
  65.4 22.1 %shard_map.141 = (bf16[2048,256]{1,0:T(8,128)(2,1)}, bf16[2048,256]{1,0:T(8,128)(2,1)}) custom-call(f32[1,2048]{1,0:T(1,128)} %reshape.80.live_ref, bf16[2048,256]{1,0:T(8,128)(2,1)} %get-tuple-element.15.q_ref, bf16[2048,256]{1,0:T(8,128)(2,1)} %convolution_convert_fusion.1.go_ref, bf16[2048,512]{1,0:T(8,128)(2,1)} %convolution_convert_fusion.kv_ref, ...), custom_call_target="tpu_custom_call" | custom-call | flops 10737418240 | bytes 7340032 | tf_op jit(solution)/shard_map/pallas_call | solution.py:209
  87.5 11.9 %shard_map.142 = (f32[2048,256]{1,0:T(8,128)}, f32[16,128,256]{2,1,0:T(8,128)}, bf16[16,128,256]{2,1,0:T(8,128)(2,1)}, bf16[16,128,256]{2,1,0:T(8,128)(2,1)}, bf...) custom-call(s32[64]{0:T(128)} %reshape_squeeze.6.src_ids, s32[16,4,128,128]{3,2,1,0:T(8,128)} %bitcast.35, ...), custom_call_target="tpu_custom_call" | custom-call | tf_op jit(solution)/shard_map/pallas_call | solution.py:142
  99.4 1.9 %collective-permute-start.4 = (bf16[2048,256]{1,0:T(8,128)(2,1)}, bf16[2048,256]{1,0:T(8,128)(2,1)S(1)}, u32[]{:S(2)}, u32[]{:S(2)}) collective-permute-start(bf16[2048,256]{1,0:T(8,128)(2,1)} %bitcast.50), channel_id=1, source_target_pairs={{16,0},{32,16},{48,32},{64,48},{80,64},{96,80},{112,96},{17,1},{33... | collective-permute-start | bytes 3145736 | tf_op jit(solution)/shard_map/ppermute | solution.py:28
  101.3 3.6 %collective-permute-start.5 = (bf16[2048,256]{1,0:T(8,128)(2,1)}, bf16[2048,256]{1,0:T(8,128)(2,1)}, u32[]{:S(2)}, u32[]{:S(2)}) collective-permute-start(bf16[2048,256]{1,0:T(8,128)(2,1)} %bitcast.49), channel_id=1, source_target_pairs={{0,16},{16,32},{32,48},{48,64},{64,80},{80,96},{96,112},{1,17},{17... | collective-permute-start | bytes 3145736 | tf_op jit(solution)/shard_map/ppermute | solution.py:28
  105.0 1.3 collective-permute-start.6
  106.3 5.0 %collective-permute-start.7 = (bf16[2048,256]{1,0:T(8,128)(2,1)}, bf16[2048,256]{1,0:T(8,128)(2,1)}, u32[]{:S(2)}, u32[]{:S(2)}) collective-permute-start(bf16[2048,256]{1,0:T(8,128)(2,1)} %bitcast.47), channel_id=1, source_target_pairs={{0,1},{1,2},{2,3},{3,4},{4,5},{5,6},{6,7},{7,8},{8,9},{9,10},{10,1... | collective-permute-start | bytes 3145736 | tf_op jit(solution)/shard_map/ppermute | solution.py:28
  111.3 44.7 %all_to_all.10 = bf16[128,16,256]{2,1,0:T(8,128)(2,1)S(1)} all-to-all(bf16[128,16,256]{2,1,0:T(8,128)(2,1)S(1)} %bitcast.42), channel_id=1, replica_groups=mesh['px'=8,'py'=16] {'px','py'}, dimensions={0} | all-to-all | bytes 2097152 | tf_op jit(solution)/shard_map/all_to_all | solution.py:329
  156.0 0.9 copy-done.5
  156.9 6.5 %shard_map.143 = bf16[2048,256]{1,0:T(8,128)(2,1)} custom-call(bf16[2048,256]{1,0:T(8,128)(2,1)} %bitcast.40, f32[2048,256]{1,0:T(8,128)} %bitcast.41, bf16[2048,256]{1,0:T(8,128)(2,1)} %copy-done.5, bf16[2048,256]{1,0:T(8,128)(2,1)} %collective-permute-done.5.b_ref, bf16[2048,256]{1,0:T(8,128)(2,1)} %collective-permute-done.6.c_ref, ...), custom_call_target="tpu_custom_call" | custom-call | flops 805306368 | bytes 10485760 | tf_op jit(solution)/shard_map/pallas_call | solution.py:259
  163.4 1.0 copy.18
  (17 shorter events, 0.0 us)
Async XLA Ops:
  0.6 32.5 %copy-start = (bf16[256,256]{1,0:T(8,128)(2,1)S(1)}, bf16[256,256]{1,0:T(8,128)(2,1)}, u32[]{:S(2)}) copy-start(bf16[256,256]{1,0:T(8,128)(2,1)} %param.24) | copy-start | bytes 393220
  2.8 31.8 %copy-start.3 = (bf16[2048,256]{1,0:T(8,128)(2,1)}, bf16[2048,256]{1,0:T(8,128)(2,1)S(1)}, u32[]{:S(2)}) copy-start(bf16[2048,256]{1,0:T(8,128)(2,1)S(1)} %convolution_convert_fusion.2) | copy-start | bytes 3145732
  2.8 28.8 %copy-start.7 = (s32[1,1,16,4]{2,3,1,0:T(4,128)S(1)}, s32[1,1,16,4]{2,3,1,0:T(4,128)}, u32[]{:S(2)}) copy-start(s32[1,1,16,4]{2,3,1,0:T(4,128)} %param.14) | copy-start | bytes 772
  2.8 29.5 %copy-start.8 = (s32[128,1]{0,1:T(1,128)S(1)}, s32[128,1]{0,1:T(1,128)}, u32[]{:S(2)}) copy-start(s32[128,1]{0,1:T(1,128)} %param.17) | copy-start | bytes 1540
  2.9 30.3 %copy-start.1 = (bf16[1,1,2048,256]{3,2,1,0:T(8,128)(2,1)S(1)}, bf16[1,1,2048,256]{3,2,1,0:T(8,128)(2,1)}, u32[]{:S(2)}) copy-start(bf16[1,1,2048,256]{3,2,1,0:T(8,128)(2,1)} %param.25) | copy-start | bytes 3145732
  2.9 16.8 %collective-permute-start = (bf16[2048,256]{1,0:T(8,128)(2,1)S(1)}, bf16[2048,256]{1,0:T(8,128)(2,1)S(1)}, u32[]{:S(2)}, u32[]{:S(2)}) collective-permute-start(bf16[2048,256]{1,0:T(8,128)(2,1)S(1)} %convolution_convert_fusion.2), channel_id=1, source_target_pairs={{0,16},{16,32},{32,48},{48,64},{64,80},{80,96},{96,112},{1,17},{17... | collective-permute-start | bytes 3145736 | tf_op jit(solution)/shard_map/ppermute | solution.py:28
  7.9 26.7 %collective-permute-start.3 = (bf16[2048,256]{1,0:T(8,128)(2,1)S(1)}, bf16[2048,256]{1,0:T(8,128)(2,1)}, u32[]{:S(2)}, u32[]{:S(2)}) collective-permute-start(bf16[2048,256]{1,0:T(8,128)(2,1)S(1)} %convolution_convert_fusion.2), channel_id=1, source_target_pairs={{1,0},{2,1},{3,2},{4,3},{5,4},{6,5},{7,6},{8,7},{9,8},{10,9},{11,1... | collective-permute-start | bytes 3145736 | tf_op jit(solution)/shard_map/ppermute | solution.py:28
  9.2 29.9 %collective-permute-start.2 = (bf16[2048,256]{1,0:T(8,128)(2,1)S(1)}, bf16[2048,256]{1,0:T(8,128)(2,1)}, u32[]{:S(2)}, u32[]{:S(2)}) collective-permute-start(bf16[2048,256]{1,0:T(8,128)(2,1)S(1)} %convolution_convert_fusion.2), channel_id=1, source_target_pairs={{0,1},{1,2},{2,3},{3,4},{4,5},{5,6},{6,7},{7,8},{8,9},{9,10},{10,1... | collective-permute-start | bytes 3145736 | tf_op jit(solution)/shard_map/ppermute | solution.py:28
  14.2 25.0 %collective-permute-start.1 = (bf16[2048,256]{1,0:T(8,128)(2,1)S(1)}, bf16[2048,256]{1,0:T(8,128)(2,1)}, u32[]{:S(2)}, u32[]{:S(2)}) collective-permute-start(bf16[2048,256]{1,0:T(8,128)(2,1)S(1)} %convolution_convert_fusion.2), channel_id=1, source_target_pairs={{16,0},{32,16},{48,32},{64,48},{80,64},{96,80},{112,96},{17,1},{33... | collective-permute-start | bytes 3145736 | tf_op jit(solution)/shard_map/ppermute | solution.py:28
  19.7 1.0 copy-start.4
  20.6 42.8 %all-to-all-start = ((bf16[128,16,256]{2,1,0:T(8,128)(2,1)}), bf16[128,16,256]{2,1,0:T(8,128)(2,1)S(1)}, u32[]{:S(2)}, u32[]{:S(2)}) async-start(bf16[128,16,256]{2,1,0:T(8,128)(2,1)} %bitcast.9), calls=%async_computation | async-start | bytes 2097152 | tf_op jit(solution)/shard_map/all_to_all | solution.py:319
  39.2 24.2 %copy-start.6 = (bf16[256,512]{1,0:T(8,128)(2,1)S(1)}, bf16[256,512]{1,0:T(8,128)(2,1)}, u32[]{:S(2)}) copy-start(bf16[256,512]{1,0:T(8,128)(2,1)} %wkv_ref.1) | copy-start | bytes 786436
  87.5 23.8 %copy-start.2 = (bf16[2048,256]{1,0:T(8,128)(2,1)S(1)}, bf16[2048,256]{1,0:T(8,128)(2,1)}, u32[]{:S(2)}) copy-start(bf16[2048,256]{1,0:T(8,128)(2,1)} %get-tuple-element.25) | copy-start | bytes 3145732
  99.4 56.5 %collective-permute-start.4 = (bf16[2048,256]{1,0:T(8,128)(2,1)}, bf16[2048,256]{1,0:T(8,128)(2,1)S(1)}, u32[]{:S(2)}, u32[]{:S(2)}) collective-permute-start(bf16[2048,256]{1,0:T(8,128)(2,1)} %bitcast.50), channel_id=1, source_target_pairs={{16,0},{32,16},{48,32},{64,48},{80,64},{96,80},{112,96},{17,1},{33... | collective-permute-start | bytes 3145736 | tf_op jit(solution)/shard_map/ppermute | solution.py:28
  101.3 54.6 %collective-permute-start.5 = (bf16[2048,256]{1,0:T(8,128)(2,1)}, bf16[2048,256]{1,0:T(8,128)(2,1)}, u32[]{:S(2)}, u32[]{:S(2)}) collective-permute-start(bf16[2048,256]{1,0:T(8,128)(2,1)} %bitcast.49), channel_id=1, source_target_pairs={{0,16},{16,32},{32,48},{48,64},{64,80},{80,96},{96,112},{1,17},{17... | collective-permute-start | bytes 3145736 | tf_op jit(solution)/shard_map/ppermute | solution.py:28
  105.0 51.0 %collective-permute-start.6 = (bf16[2048,256]{1,0:T(8,128)(2,1)}, bf16[2048,256]{1,0:T(8,128)(2,1)}, u32[]{:S(2)}, u32[]{:S(2)}) collective-permute-start(bf16[2048,256]{1,0:T(8,128)(2,1)} %bitcast.48), channel_id=1, source_target_pairs={{1,0},{2,1},{3,2},{4,3},{5,4},{6,5},{7,6},{8,7},{9,8},{10,9},{11,1... | collective-permute-start | bytes 3145736 | tf_op jit(solution)/shard_map/ppermute | solution.py:28
  106.3 49.7 %collective-permute-start.7 = (bf16[2048,256]{1,0:T(8,128)(2,1)}, bf16[2048,256]{1,0:T(8,128)(2,1)}, u32[]{:S(2)}, u32[]{:S(2)}) collective-permute-start(bf16[2048,256]{1,0:T(8,128)(2,1)} %bitcast.47), channel_id=1, source_target_pairs={{0,1},{1,2},{2,3},{3,4},{4,5},{5,6},{6,7},{7,8},{8,9},{9,10},{10,1... | collective-permute-start | bytes 3145736 | tf_op jit(solution)/shard_map/ppermute | solution.py:28
  155.9 1.0 copy-start.5

commit v11 on v9

--- a/solution.py
+++ b/solution.py
@@ -201,7 +201,7 @@
         slots_ref[...] = slots.astype(slots_ref.dtype)
 
 
-def attend_back(live, queries, grad_out, keyvals, w_kv, scale, rows_per_step=256):
+def attend_back(live, queries, grad_out, keyvals, w_kv, scale, rows_per_step=512):
     rows, width = queries.shape
     slots = keyvals.shape[0]
     steps = rows // rows_per_step

time: 165 us -> 163 us (0.988)
  Pallas kernels: 52.7 us -> 50.9 us
    pallas_call x1, Pallas kernels: 22.1 us -> 20.3 us  [attend_back(): pl.pallas_call(functools.partial(attend_kernel, scale), grid=(steps,), in...]
where the time goes in v11:
time: 163 us; the launch traced here: 162 us
  Pallas kernels  50.9 us (31%)
  blocking collectives  48.6 us (30%)
  starting transfers between devices  36 us (22%)
  waiting for transfers between devices  16.1 us (10%)
  matrix products  5.32 us (3%)
  local copies, waits for them, and re-layouts  4.3 us (3%)
    all_to_all x1, blocking collectives, on_device(): lax.all_to_all(grad_slots.reshape(devices, slot_count, latent_width), ('p...  48.6 us
    ppermute x8, starting transfers between devices, passed_along(): lax.ppermute(value, axis, [(source, source + steps) for source in range(l...  24.5 us
    pallas_call x1, Pallas kernels, attend_back(): pl.pallas_call(functools.partial(attend_kernel, scale), grid=(steps,), in...  20.3 us
    ppermute x8, waiting for transfers between devices, passed_along(): lax.ppermute(value, axis, [(source, source + steps) for source in range(l...  14.5 us
    pallas_call x1, Pallas kernels, tile_gather(): pl.pallas_call(functools.partial(gather_kernel, group), grid_spec=pltpu.P...  12.3 us
    pallas_call x1, Pallas kernels, tile_scatter(): pl.pallas_call(functools.partial(scatter_kernel, group), grid_spec=pltpu....  11.9 us
    all_to_all x1, starting transfers between devices, on_device(): lax.all_to_all(token_groups, ('px', 'py'), split_axis=0, concat_axis=0, t...  11.5 us
    pallas_call x1, Pallas kernels, edge_back(): pl.pallas_call(edge_back_kernel, grid=(rows // rows_per_step,), in_specs=...  6.48 us
  transfers between devices with their start and end apart: 9, of which 2 were waited for; matrix products, arithmetic and copies ran while one was open for 4% of the time, Pallas kernels for 0%

profile of v11, /device:TPU:1, one launch (start us, length us, event | category | flops | bytes accessed | tf_op | source)
XLA Modules:
  0.0 162.2 jit_solution(8902319557818943729)
XLA Ops:
  0.6 0.0 copy-start
  0.6 0.0 copy-start.7
  0.7 0.0 copy-start.8
  0.7 0.0 copy-start.2
  0.7 11.5 %all-to-all-start = ((bf16[128,16,256]{2,1,0:T(8,128)(2,1)}), bf16[128,16,256]{2,1,0:T(8,128)(2,1)S(1)}, u32[]{:S(2)}, u32[]{:S(2)}) async-start(bf16[128,16,256]{2,1,0:T(8,128)(2,1)} %bitcast.42), calls=%async_computation | async-start | bytes 2097152 | tf_op jit(solution)/shard_map/all_to_all | solution.py:318
  12.2 0.0 copy-start.10
  12.2 0.0 copy-start.1
  12.2 1.8 %convolution_convert_fusion.2 = bf16[2048,256]{1,0:T(8,128)(2,1)} fusion(bf16[256,256]{1,0:T(8,128)(2,1)S(1)} %copy-done.7, bf16[256,256]{1,0:T(8,128)(2,1)S(1)} %copy-done.8, bf16[1,1,2048,256]{3,2,1,0:T(8,128)(2,1)S(1)} %copy-done.2), kind=kOutput, calls=%fused_computation.2 | convolution fusion | flops 540016640 | bytes 2359296 | tf_op jit(solution)/shard_map/dot_general | solution.py:274
  14.1 1.3 collective-permute-start.3
  15.3 5.0 %collective-permute-start.2 = (bf16[2048,256]{1,0:T(8,128)(2,1)}, bf16[2048,256]{1,0:T(8,128)(2,1)}, u32[]{:S(2)}, u32[]{:S(2)}) collective-permute-start(bf16[2048,256]{1,0:T(8,128)(2,1)} %convolution_convert_fusion.2), channel_id=1, source_target_pairs={{0,1},{1,2},{2,3},{3,4},{4,5},{5,6},{6,7},{7,8},{8,9},{9,10},{10,1... | collective-permute-start | bytes 3145736 | tf_op jit(solution)/shard_map/ppermute | solution.py:28
  20.3 3.5 %collective-permute-start.1 = (bf16[2048,256]{1,0:T(8,128)(2,1)}, bf16[2048,256]{1,0:T(8,128)(2,1)}, u32[]{:S(2)}, u32[]{:S(2)}) collective-permute-start(bf16[2048,256]{1,0:T(8,128)(2,1)} %convolution_convert_fusion.2), channel_id=1, source_target_pairs={{16,0},{32,16},{48,32},{64,48},{80,64},{96,80},{112,96},{17,1},{33... | collective-permute-start | bytes 3145736 | tf_op jit(solution)/shard_map/ppermute | solution.py:28
  23.8 2.6 %collective-permute-start = (bf16[2048,256]{1,0:T(8,128)(2,1)}, bf16[2048,256]{1,0:T(8,128)(2,1)}, u32[]{:S(2)}, u32[]{:S(2)}) collective-permute-start(bf16[2048,256]{1,0:T(8,128)(2,1)} %convolution_convert_fusion.2), channel_id=1, source_target_pairs={{0,16},{16,32},{32,48},{48,64},{64,80},{80,96},{96,112},{1,17},{17... | collective-permute-start | bytes 3145736 | tf_op jit(solution)/shard_map/ppermute | solution.py:28
  26.5 0.1 copy.16
  26.5 0.6 reshape_squeeze.6.src_ids
  27.2 0.1 fusion
  27.2 0.7 reshape.80.live_ref
  27.9 1.5 convolution_convert_fusion.1.go_ref
  29.5 1.5 all-to-all-done
  31.0 2.0 %convolution_convert_fusion.kv_ref = bf16[2048,512]{1,0:T(8,128)(2,1)} fusion(bf16[2048,256]{1,0:T(8,128)(2,1)S(1)} %bitcast.37, bf16[256,512]{1,0:T(8,128)(2,1)S(1)} %copy-done.6), kind=kOutput, calls=%fused_computation | convolution fusion | flops 537919488 | bytes 3407872 | tf_op jit(solution)/shard_map/dot_general | solution.py:274
  33.0 14.5 %collective-permute-done.3 = bf16[2048,256]{1,0:T(8,128)(2,1)S(1)} collective-permute-done((bf16[2048,256]{1,0:T(8,128)(2,1)}, bf16[2048,256]{1,0:T(8,128)(2,1)S(1)}, u32[]{:S(2)}, u32[]{:S(2)}) %collective-permute-start.3) | collective-permute-done | bytes 1048608 | tf_op jit(solution)/shard_map/ppermute | solution.py:28
  47.5 0.9 copy-done.4
  48.5 12.3 %shard_map.140 = (f32[2048,256]{1,0:T(8,128)}, bf16[2048,256]{1,0:T(8,128)(2,1)}) custom-call(s32[64]{0:T(128)} %reshape_squeeze.6.src_ids, s32[16,4,128,128]{3,2,1,0:T(8,128)} %bitcast.34, bf16[16,128,256]{2,1,0:T(8,128)(2,1)} %bitcast.44, bf16[16,128,256]{2,1,0:T(8,128)(2,1)} %bitcast.4.up, bf16[16,128,256]{2,1,0:T(8,128)(2,1)} %bitcast.5.down, ...), custom_call_target="tpu_custom_call" | custom-call | tf_op jit(solution)/shard_map/pallas_call | solution.py:71
  60.8 20.3 %shard_map.141 = (bf16[2048,256]{1,0:T(8,128)(2,1)}, bf16[2048,256]{1,0:T(8,128)(2,1)}) custom-call(f32[1,2048]{1,0:T(1,128)} %reshape.80.live_ref, bf16[2048,256]{1,0:T(8,128)(2,1)} %get-tuple-element.12.q_ref, bf16[2048,256]{1,0:T(8,128)(2,1)} %convolution_convert_fusion.1.go_ref, bf16[2048,512]{1,0:T(8,128)(2,1)} %convolution_convert_fusion.kv_ref, ...), custom_call_target="tpu_custom_call" | custom-call | flops 10737418240 | bytes 7340032 | tf_op jit(solution)/shard_map/pallas_call | solution.py:209
  81.0 11.9 %shard_map.142 = (f32[2048,256]{1,0:T(8,128)}, f32[16,128,256]{2,1,0:T(8,128)}, bf16[16,128,256]{2,1,0:T(8,128)(2,1)}, bf16[16,128,256]{2,1,0:T(8,128)(2,1)}, bf...) custom-call(s32[64]{0:T(128)} %reshape_squeeze.6.src_ids, s32[16,4,128,128]{3,2,1,0:T(8,128)} %bitcast.35, ...), custom_call_target="tpu_custom_call" | custom-call | tf_op jit(solution)/shard_map/pallas_call | solution.py:142
  92.9 2.6 %collective-permute-start.4 = (bf16[2048,256]{1,0:T(8,128)(2,1)}, bf16[2048,256]{1,0:T(8,128)(2,1)S(1)}, u32[]{:S(2)}, u32[]{:S(2)}) collective-permute-start(bf16[2048,256]{1,0:T(8,128)(2,1)} %bitcast.51), channel_id=1, source_target_pairs={{16,0},{32,16},{48,32},{64,48},{80,64},{96,80},{112,96},{17,1},{33... | collective-permute-start | bytes 3145736 | tf_op jit(solution)/shard_map/ppermute | solution.py:28
  95.6 3.2 %collective-permute-start.5 = (bf16[2048,256]{1,0:T(8,128)(2,1)}, bf16[2048,256]{1,0:T(8,128)(2,1)}, u32[]{:S(2)}, u32[]{:S(2)}) collective-permute-start(bf16[2048,256]{1,0:T(8,128)(2,1)} %bitcast.50), channel_id=1, source_target_pairs={{0,16},{16,32},{32,48},{48,64},{64,80},{80,96},{96,112},{1,17},{17... | collective-permute-start | bytes 3145736 | tf_op jit(solution)/shard_map/ppermute | solution.py:28
  98.7 1.3 collective-permute-start.6
  100.0 5.1 %collective-permute-start.7 = (bf16[2048,256]{1,0:T(8,128)(2,1)}, bf16[2048,256]{1,0:T(8,128)(2,1)}, u32[]{:S(2)}, u32[]{:S(2)}) collective-permute-start(bf16[2048,256]{1,0:T(8,128)(2,1)} %bitcast.48), channel_id=1, source_target_pairs={{0,1},{1,2},{2,3},{3,4},{4,5},{5,6},{6,7},{7,8},{8,9},{9,10},{10,1... | collective-permute-start | bytes 3145736 | tf_op jit(solution)/shard_map/ppermute | solution.py:28
  105.1 48.6 %all_to_all.10 = bf16[128,16,256]{2,1,0:T(8,128)(2,1)S(1)} all-to-all(bf16[128,16,256]{2,1,0:T(8,128)(2,1)S(1)} %bitcast.43), channel_id=1, replica_groups=mesh['px'=8,'py'=16] {'px','py'}, dimensions={0} | all-to-all | bytes 2097152 | tf_op jit(solution)/shard_map/all_to_all | solution.py:328
  153.8 0.9 copy-done.5
  154.7 6.5 %shard_map.143 = bf16[2048,256]{1,0:T(8,128)(2,1)} custom-call(bf16[2048,256]{1,0:T(8,128)(2,1)} %bitcast.40, f32[2048,256]{1,0:T(8,128)} %bitcast.41, bf16[2048,256]{1,0:T(8,128)(2,1)} %copy-done.5, bf16[2048,256]{1,0:T(8,128)(2,1)} %collective-permute-done.5.b_ref, bf16[2048,256]{1,0:T(8,128)(2,1)} %collective-permute-done.6.c_ref, ...), custom_call_target="tpu_custom_call" | custom-call | flops 805306368 | bytes 10485760 | tf_op jit(solution)/shard_map/pallas_call | solution.py:259
  161.2 1.0 copy.18
  (21 shorter events, 0.0 us)
Async XLA Ops:
  0.6 27.3 %copy-start = (bf16[256,256]{1,0:T(8,128)(2,1)S(1)}, bf16[256,256]{1,0:T(8,128)(2,1)}, u32[]{:S(2)}) copy-start(bf16[256,256]{1,0:T(8,128)(2,1)} %param.24) | copy-start | bytes 393220
  0.6 11.5 %copy-start.7 = (bf16[256,256]{1,0:T(8,128)(2,1)S(1)}, bf16[256,256]{1,0:T(8,128)(2,1)}, u32[]{:S(2)}) copy-start(bf16[256,256]{1,0:T(8,128)(2,1)} %w2_ref.1) | copy-start | bytes 393220
  0.7 11.5 %copy-start.8 = (bf16[256,256]{1,0:T(8,128)(2,1)S(1)}, bf16[256,256]{1,0:T(8,128)(2,1)}, u32[]{:S(2)}) copy-start(bf16[256,256]{1,0:T(8,128)(2,1)} %w1_ref.1) | copy-start | bytes 393220
  0.7 11.5 %copy-start.2 = (bf16[1,1,2048,256]{3,2,1,0:T(8,128)(2,1)S(1)}, bf16[1,1,2048,256]{3,2,1,0:T(8,128)(2,1)}, u32[]{:S(2)}) copy-start(bf16[1,1,2048,256]{3,2,1,0:T(8,128)(2,1)} %param.13) | copy-start | bytes 3145732
  0.7 30.3 %all-to-all-start = ((bf16[128,16,256]{2,1,0:T(8,128)(2,1)}), bf16[128,16,256]{2,1,0:T(8,128)(2,1)S(1)}, u32[]{:S(2)}, u32[]{:S(2)}) async-start(bf16[128,16,256]{2,1,0:T(8,128)(2,1)} %bitcast.42), calls=%async_computation | async-start | bytes 2097152 | tf_op jit(solution)/shard_map/all_to_all | solution.py:318
  12.2 14.2 %copy-start.9 = (s32[1,1,16,4]{2,3,1,0:T(4,128)S(1)}, s32[1,1,16,4]{2,3,1,0:T(4,128)}, u32[]{:S(2)}) copy-start(s32[1,1,16,4]{2,3,1,0:T(4,128)} %param.14) | copy-start | bytes 772
  12.2 14.9 %copy-start.10 = (s32[128,1]{0,1:T(1,128)S(1)}, s32[128,1]{0,1:T(1,128)}, u32[]{:S(2)}) copy-start(s32[128,1]{0,1:T(1,128)} %param.17) | copy-start | bytes 1540
  12.2 15.7 %copy-start.1 = (bf16[1,1,2048,256]{3,2,1,0:T(8,128)(2,1)S(1)}, bf16[1,1,2048,256]{3,2,1,0:T(8,128)(2,1)}, u32[]{:S(2)}) copy-start(bf16[1,1,2048,256]{3,2,1,0:T(8,128)(2,1)} %param.25) | copy-start | bytes 3145732
  14.1 33.5 %collective-permute-start.3 = (bf16[2048,256]{1,0:T(8,128)(2,1)}, bf16[2048,256]{1,0:T(8,128)(2,1)S(1)}, u32[]{:S(2)}, u32[]{:S(2)}) collective-permute-start(bf16[2048,256]{1,0:T(8,128)(2,1)} %convolution_convert_fusion.2), channel_id=1, source_target_pairs={{1,0},{2,1},{3,2},{4,3},{5,4},{6,5},{7,6},{8,7},{9,8},{10,9},{11,1... | collective-permute-start | bytes 3145736 | tf_op jit(solution)/shard_map/ppermute | solution.py:28
  15.3 32.2 %collective-permute-start.2 = (bf16[2048,256]{1,0:T(8,128)(2,1)}, bf16[2048,256]{1,0:T(8,128)(2,1)}, u32[]{:S(2)}, u32[]{:S(2)}) collective-permute-start(bf16[2048,256]{1,0:T(8,128)(2,1)} %convolution_convert_fusion.2), channel_id=1, source_target_pairs={{0,1},{1,2},{2,3},{3,4},{4,5},{5,6},{6,7},{7,8},{8,9},{9,10},{10,1... | collective-permute-start | bytes 3145736 | tf_op jit(solution)/shard_map/ppermute | solution.py:28
  20.3 27.2 %collective-permute-start.1 = (bf16[2048,256]{1,0:T(8,128)(2,1)}, bf16[2048,256]{1,0:T(8,128)(2,1)}, u32[]{:S(2)}, u32[]{:S(2)}) collective-permute-start(bf16[2048,256]{1,0:T(8,128)(2,1)} %convolution_convert_fusion.2), channel_id=1, source_target_pairs={{16,0},{32,16},{48,32},{64,48},{80,64},{96,80},{112,96},{17,1},{33... | collective-permute-start | bytes 3145736 | tf_op jit(solution)/shard_map/ppermute | solution.py:28
  23.8 23.7 %collective-permute-start = (bf16[2048,256]{1,0:T(8,128)(2,1)}, bf16[2048,256]{1,0:T(8,128)(2,1)}, u32[]{:S(2)}, u32[]{:S(2)}) collective-permute-start(bf16[2048,256]{1,0:T(8,128)(2,1)} %convolution_convert_fusion.2), channel_id=1, source_target_pairs={{0,16},{16,32},{32,48},{48,64},{64,80},{80,96},{96,112},{1,17},{17... | collective-permute-start | bytes 3145736 | tf_op jit(solution)/shard_map/ppermute | solution.py:28
  27.9 3.1 %copy-start.6 = (bf16[256,512]{1,0:T(8,128)(2,1)S(1)}, bf16[256,512]{1,0:T(8,128)(2,1)}, u32[]{:S(2)}) copy-start(bf16[256,512]{1,0:T(8,128)(2,1)} %wkv_ref.1) | copy-start | bytes 786436
  47.5 1.0 copy-start.4
  81.0 24.1 %copy-start.3 = (bf16[2048,256]{1,0:T(8,128)(2,1)S(1)}, bf16[2048,256]{1,0:T(8,128)(2,1)}, u32[]{:S(2)}) copy-start(bf16[2048,256]{1,0:T(8,128)(2,1)} %get-tuple-element.21) | copy-start | bytes 3145732
  92.9 60.8 %collective-permute-start.4 = (bf16[2048,256]{1,0:T(8,128)(2,1)}, bf16[2048,256]{1,0:T(8,128)(2,1)S(1)}, u32[]{:S(2)}, u32[]{:S(2)}) collective-permute-start(bf16[2048,256]{1,0:T(8,128)(2,1)} %bitcast.51), channel_id=1, source_target_pairs={{16,0},{32,16},{48,32},{64,48},{80,64},{96,80},{112,96},{17,1},{33... | collective-permute-start | bytes 3145736 | tf_op jit(solution)/shard_map/ppermute | solution.py:28
  95.6 58.2 %collective-permute-start.5 = (bf16[2048,256]{1,0:T(8,128)(2,1)}, bf16[2048,256]{1,0:T(8,128)(2,1)}, u32[]{:S(2)}, u32[]{:S(2)}) collective-permute-start(bf16[2048,256]{1,0:T(8,128)(2,1)} %bitcast.50), channel_id=1, source_target_pairs={{0,16},{16,32},{32,48},{48,64},{64,80},{80,96},{96,112},{1,17},{17... | collective-permute-start | bytes 3145736 | tf_op jit(solution)/shard_map/ppermute | solution.py:28
  98.7 55.0 %collective-permute-start.6 = (bf16[2048,256]{1,0:T(8,128)(2,1)}, bf16[2048,256]{1,0:T(8,128)(2,1)}, u32[]{:S(2)}, u32[]{:S(2)}) collective-permute-start(bf16[2048,256]{1,0:T(8,128)(2,1)} %bitcast.49), channel_id=1, source_target_pairs={{1,0},{2,1},{3,2},{4,3},{5,4},{6,5},{7,6},{8,7},{9,8},{10,9},{11,1... | collective-permute-start | bytes 3145736 | tf_op jit(solution)/shard_map/ppermute | solution.py:28
  100.0 53.7 %collective-permute-start.7 = (bf16[2048,256]{1,0:T(8,128)(2,1)}, bf16[2048,256]{1,0:T(8,128)(2,1)}, u32[]{:S(2)}, u32[]{:S(2)}) collective-permute-start(bf16[2048,256]{1,0:T(8,128)(2,1)} %bitcast.48), channel_id=1, source_target_pairs={{0,1},{1,2},{2,3},{3,4},{4,5},{5,6},{6,7},{7,8},{8,9},{9,10},{10,1... | collective-permute-start | bytes 3145736 | tf_op jit(solution)/shard_map/ppermute | solution.py:28
  153.7 1.0 copy-start.5

commit v12 on v11

--- a/solution.py
+++ b/solution.py
@@ -201,7 +201,7 @@
         slots_ref[...] = slots.astype(slots_ref.dtype)
 
 
-def attend_back(live, queries, grad_out, keyvals, w_kv, scale, rows_per_step=512):
+def attend_back(live, queries, grad_out, keyvals, w_kv, scale, rows_per_step=1024):
     rows, width = queries.shape
     slots = keyvals.shape[0]
     steps = rows // rows_per_step

time: 163 us -> 162 us (level)
  no operation moved by 1% of the time
where the time goes in v12:
time: 162 us
  Pallas kernels  50.3 us (31%)
  blocking collectives  48.6 us (30%)
  starting transfers between devices  36 us (22%)
  waiting for transfers between devices  16.1 us (10%)
  matrix products  5.33 us (3%)
  local copies, waits for them, and re-layouts  4.3 us (3%)
    all_to_all x1, blocking collectives, on_device(): lax.all_to_all(grad_slots.reshape(devices, slot_count, latent_width), ('p...  48.6 us
    ppermute x8, starting transfers between devices, passed_along(): lax.ppermute(value, axis, [(source, source + steps) for source in range(l...  24.5 us
    pallas_call x1, Pallas kernels, attend_back(): pl.pallas_call(functools.partial(attend_kernel, scale), grid=(steps,), in...  19.4 us
    ppermute x8, waiting for transfers between devices, passed_along(): lax.ppermute(value, axis, [(source, source + steps) for source in range(l...  14.5 us
    pallas_call x1, Pallas kernels, tile_gather(): pl.pallas_call(functools.partial(gather_kernel, group), grid_spec=pltpu.P...  12.3 us
    pallas_call x1, Pallas kernels, tile_scatter(): pl.pallas_call(functools.partial(scatter_kernel, group), grid_spec=pltpu....  12.1 us
    all_to_all x1, starting transfers between devices, on_device(): lax.all_to_all(token_groups, ('px', 'py'), split_axis=0, concat_axis=0, t...  11.5 us
    pallas_call x1, Pallas kernels, edge_back(): pl.pallas_call(edge_back_kernel, grid=(rows // rows_per_step,), in_specs=...  6.48 us
  transfers between devices with their start and end apart: 9, of which 2 were waited for; matrix products, arithmetic and copies ran while one was open for 4% of the time, Pallas kernels for 0%

profile of v12, /device:TPU:1, one launch (start us, length us, event | category | flops | bytes accessed | tf_op | source)
XLA Modules:
  0.0 161.5 jit_solution(14094673939763166251)
XLA Ops:
  0.6 0.0 copy-start
  0.6 0.0 copy-start.7
  0.7 0.0 copy-start.8
  0.7 0.0 copy-start.2
  0.7 11.5 %all-to-all-start = ((bf16[128,16,256]{2,1,0:T(8,128)(2,1)}), bf16[128,16,256]{2,1,0:T(8,128)(2,1)S(1)}, u32[]{:S(2)}, u32[]{:S(2)}) async-start(bf16[128,16,256]{2,1,0:T(8,128)(2,1)} %bitcast.42), calls=%async_computation | async-start | bytes 2097152 | tf_op jit(solution)/shard_map/all_to_all | solution.py:318
  12.2 0.0 copy-start.9
  12.2 0.0 copy-start.10
  12.2 1.8 %convolution_convert_fusion.2 = bf16[2048,256]{1,0:T(8,128)(2,1)} fusion(bf16[256,256]{1,0:T(8,128)(2,1)S(1)} %copy-done.7, bf16[256,256]{1,0:T(8,128)(2,1)S(1)} %copy-done.8, bf16[1,1,2048,256]{3,2,1,0:T(8,128)(2,1)S(1)} %copy-done.2), kind=kOutput, calls=%fused_computation.2 | convolution fusion | flops 540016640 | bytes 2359296 | tf_op jit(solution)/shard_map/dot_general | solution.py:274
  14.1 1.3 collective-permute-start.3
  15.3 5.0 %collective-permute-start.2 = (bf16[2048,256]{1,0:T(8,128)(2,1)}, bf16[2048,256]{1,0:T(8,128)(2,1)}, u32[]{:S(2)}, u32[]{:S(2)}) collective-permute-start(bf16[2048,256]{1,0:T(8,128)(2,1)} %convolution_convert_fusion.2), channel_id=1, source_target_pairs={{0,1},{1,2},{2,3},{3,4},{4,5},{5,6},{6,7},{7,8},{8,9},{9,10},{10,1... | collective-permute-start | bytes 3145736 | tf_op jit(solution)/shard_map/ppermute | solution.py:28
  20.3 3.5 %collective-permute-start.1 = (bf16[2048,256]{1,0:T(8,128)(2,1)}, bf16[2048,256]{1,0:T(8,128)(2,1)}, u32[]{:S(2)}, u32[]{:S(2)}) collective-permute-start(bf16[2048,256]{1,0:T(8,128)(2,1)} %convolution_convert_fusion.2), channel_id=1, source_target_pairs={{16,0},{32,16},{48,32},{64,48},{80,64},{96,80},{112,96},{17,1},{33... | collective-permute-start | bytes 3145736 | tf_op jit(solution)/shard_map/ppermute | solution.py:28
  23.8 2.6 %collective-permute-start = (bf16[2048,256]{1,0:T(8,128)(2,1)}, bf16[2048,256]{1,0:T(8,128)(2,1)}, u32[]{:S(2)}, u32[]{:S(2)}) collective-permute-start(bf16[2048,256]{1,0:T(8,128)(2,1)} %convolution_convert_fusion.2), channel_id=1, source_target_pairs={{0,16},{16,32},{32,48},{48,64},{64,80},{80,96},{96,112},{1,17},{17... | collective-permute-start | bytes 3145736 | tf_op jit(solution)/shard_map/ppermute | solution.py:28
  26.5 0.1 copy.16
  26.5 0.6 reshape_squeeze.6.src_ids
  27.2 0.1 fusion
  27.2 0.7 reshape.80.live_ref
  27.9 1.5 convolution_convert_fusion.1.go_ref
  29.5 1.5 all-to-all-done
  31.0 2.0 %convolution_convert_fusion.kv_ref = bf16[2048,512]{1,0:T(8,128)(2,1)} fusion(bf16[2048,256]{1,0:T(8,128)(2,1)S(1)} %bitcast.37, bf16[256,512]{1,0:T(8,128)(2,1)S(1)} %copy-done.6), kind=kOutput, calls=%fused_computation | convolution fusion | flops 537919488 | bytes 3407872 | tf_op jit(solution)/shard_map/dot_general | solution.py:274
  33.0 14.5 %collective-permute-done.3 = bf16[2048,256]{1,0:T(8,128)(2,1)S(1)} collective-permute-done((bf16[2048,256]{1,0:T(8,128)(2,1)}, bf16[2048,256]{1,0:T(8,128)(2,1)S(1)}, u32[]{:S(2)}, u32[]{:S(2)}) %collective-permute-start.3) | collective-permute-done | bytes 1048608 | tf_op jit(solution)/shard_map/ppermute | solution.py:28
  47.5 0.9 copy-done.4
  48.5 12.3 %shard_map.140 = (f32[2048,256]{1,0:T(8,128)}, bf16[2048,256]{1,0:T(8,128)(2,1)}) custom-call(s32[64]{0:T(128)} %reshape_squeeze.6.src_ids, s32[16,4,128,128]{3,2,1,0:T(8,128)} %bitcast.34, bf16[16,128,256]{2,1,0:T(8,128)(2,1)} %bitcast.44, bf16[16,128,256]{2,1,0:T(8,128)(2,1)} %bitcast.4.up, bf16[16,128,256]{2,1,0:T(8,128)(2,1)} %bitcast.5.down, ...), custom_call_target="tpu_custom_call" | custom-call | tf_op jit(solution)/shard_map/pallas_call | solution.py:71
  60.8 19.4 %shard_map.141 = (bf16[2048,256]{1,0:T(8,128)(2,1)}, bf16[2048,256]{1,0:T(8,128)(2,1)}) custom-call(f32[1,2048]{1,0:T(1,128)} %reshape.80.live_ref, bf16[2048,256]{1,0:T(8,128)(2,1)} %get-tuple-element.12.q_ref, bf16[2048,256]{1,0:T(8,128)(2,1)} %convolution_convert_fusion.1.go_ref, bf16[2048,512]{1,0:T(8,128)(2,1)} %convolution_convert_fusion.kv_ref, ...), custom_call_target="tpu_custom_call" | custom-call | flops 10737418240 | bytes 7340032 | tf_op jit(solution)/shard_map/pallas_call | solution.py:209
  80.2 12.1 %shard_map.142 = (f32[2048,256]{1,0:T(8,128)}, f32[16,128,256]{2,1,0:T(8,128)}, bf16[16,128,256]{2,1,0:T(8,128)(2,1)}, bf16[16,128,256]{2,1,0:T(8,128)(2,1)}, bf...) custom-call(s32[64]{0:T(128)} %reshape_squeeze.6.src_ids, s32[16,4,128,128]{3,2,1,0:T(8,128)} %bitcast.35, ...), custom_call_target="tpu_custom_call" | custom-call | tf_op jit(solution)/shard_map/pallas_call | solution.py:142
  92.3 2.6 %collective-permute-start.4 = (bf16[2048,256]{1,0:T(8,128)(2,1)}, bf16[2048,256]{1,0:T(8,128)(2,1)S(1)}, u32[]{:S(2)}, u32[]{:S(2)}) collective-permute-start(bf16[2048,256]{1,0:T(8,128)(2,1)} %bitcast.51), channel_id=1, source_target_pairs={{16,0},{32,16},{48,32},{64,48},{80,64},{96,80},{112,96},{17,1},{33... | collective-permute-start | bytes 3145736 | tf_op jit(solution)/shard_map/ppermute | solution.py:28
  94.9 3.2 %collective-permute-start.5 = (bf16[2048,256]{1,0:T(8,128)(2,1)}, bf16[2048,256]{1,0:T(8,128)(2,1)}, u32[]{:S(2)}, u32[]{:S(2)}) collective-permute-start(bf16[2048,256]{1,0:T(8,128)(2,1)} %bitcast.50), channel_id=1, source_target_pairs={{0,16},{16,32},{32,48},{48,64},{64,80},{80,96},{96,112},{1,17},{17... | collective-permute-start | bytes 3145736 | tf_op jit(solution)/shard_map/ppermute | solution.py:28
  98.1 1.3 collective-permute-start.6
  99.4 5.1 %collective-permute-start.7 = (bf16[2048,256]{1,0:T(8,128)(2,1)}, bf16[2048,256]{1,0:T(8,128)(2,1)}, u32[]{:S(2)}, u32[]{:S(2)}) collective-permute-start(bf16[2048,256]{1,0:T(8,128)(2,1)} %bitcast.48), channel_id=1, source_target_pairs={{0,1},{1,2},{2,3},{3,4},{4,5},{5,6},{6,7},{7,8},{8,9},{9,10},{10,1... | collective-permute-start | bytes 3145736 | tf_op jit(solution)/shard_map/ppermute | solution.py:28
  104.5 48.6 %all_to_all.10 = bf16[128,16,256]{2,1,0:T(8,128)(2,1)S(1)} all-to-all(bf16[128,16,256]{2,1,0:T(8,128)(2,1)S(1)} %bitcast.43), channel_id=1, replica_groups=mesh['px'=8,'py'=16] {'px','py'}, dimensions={0} | all-to-all | bytes 2097152 | tf_op jit(solution)/shard_map/all_to_all | solution.py:328
  153.2 0.9 copy-done.5
  154.1 6.5 %shard_map.143 = bf16[2048,256]{1,0:T(8,128)(2,1)} custom-call(bf16[2048,256]{1,0:T(8,128)(2,1)} %bitcast.40, f32[2048,256]{1,0:T(8,128)} %bitcast.41, bf16[2048,256]{1,0:T(8,128)(2,1)} %copy-done.5, bf16[2048,256]{1,0:T(8,128)(2,1)} %collective-permute-done.5.b_ref, bf16[2048,256]{1,0:T(8,128)(2,1)} %collective-permute-done.6.c_ref, ...), custom_call_target="tpu_custom_call" | custom-call | flops 805306368 | bytes 10485760 | tf_op jit(solution)/shard_map/pallas_call | solution.py:259
  160.6 1.0 copy.18
  (21 shorter events, 0.0 us)
Async XLA Ops:
  0.6 27.3 %copy-start = (bf16[256,256]{1,0:T(8,128)(2,1)S(1)}, bf16[256,256]{1,0:T(8,128)(2,1)}, u32[]{:S(2)}) copy-start(bf16[256,256]{1,0:T(8,128)(2,1)} %param.24) | copy-start | bytes 393220
  0.6 11.5 %copy-start.7 = (bf16[256,256]{1,0:T(8,128)(2,1)S(1)}, bf16[256,256]{1,0:T(8,128)(2,1)}, u32[]{:S(2)}) copy-start(bf16[256,256]{1,0:T(8,128)(2,1)} %w2_ref.1) | copy-start | bytes 393220
  0.7 11.5 %copy-start.8 = (bf16[256,256]{1,0:T(8,128)(2,1)S(1)}, bf16[256,256]{1,0:T(8,128)(2,1)}, u32[]{:S(2)}) copy-start(bf16[256,256]{1,0:T(8,128)(2,1)} %w1_ref.1) | copy-start | bytes 393220
  0.7 11.5 %copy-start.2 = (bf16[1,1,2048,256]{3,2,1,0:T(8,128)(2,1)S(1)}, bf16[1,1,2048,256]{3,2,1,0:T(8,128)(2,1)}, u32[]{:S(2)}) copy-start(bf16[1,1,2048,256]{3,2,1,0:T(8,128)(2,1)} %param.13) | copy-start | bytes 3145732
  0.7 30.3 %all-to-all-start = ((bf16[128,16,256]{2,1,0:T(8,128)(2,1)}), bf16[128,16,256]{2,1,0:T(8,128)(2,1)S(1)}, u32[]{:S(2)}, u32[]{:S(2)}) async-start(bf16[128,16,256]{2,1,0:T(8,128)(2,1)} %bitcast.42), calls=%async_computation | async-start | bytes 2097152 | tf_op jit(solution)/shard_map/all_to_all | solution.py:318
  12.2 14.2 %copy-start.9 = (s32[1,1,16,4]{2,3,1,0:T(4,128)S(1)}, s32[1,1,16,4]{2,3,1,0:T(4,128)}, u32[]{:S(2)}) copy-start(s32[1,1,16,4]{2,3,1,0:T(4,128)} %param.14) | copy-start | bytes 772
  12.2 14.9 %copy-start.10 = (s32[128,1]{0,1:T(1,128)S(1)}, s32[128,1]{0,1:T(1,128)}, u32[]{:S(2)}) copy-start(s32[128,1]{0,1:T(1,128)} %param.17) | copy-start | bytes 1540
  12.2 15.7 %copy-start.1 = (bf16[1,1,2048,256]{3,2,1,0:T(8,128)(2,1)S(1)}, bf16[1,1,2048,256]{3,2,1,0:T(8,128)(2,1)}, u32[]{:S(2)}) copy-start(bf16[1,1,2048,256]{3,2,1,0:T(8,128)(2,1)} %param.25) | copy-start | bytes 3145732
  14.1 33.5 %collective-permute-start.3 = (bf16[2048,256]{1,0:T(8,128)(2,1)}, bf16[2048,256]{1,0:T(8,128)(2,1)S(1)}, u32[]{:S(2)}, u32[]{:S(2)}) collective-permute-start(bf16[2048,256]{1,0:T(8,128)(2,1)} %convolution_convert_fusion.2), channel_id=1, source_target_pairs={{1,0},{2,1},{3,2},{4,3},{5,4},{6,5},{7,6},{8,7},{9,8},{10,9},{11,1... | collective-permute-start | bytes 3145736 | tf_op jit(solution)/shard_map/ppermute | solution.py:28
  15.3 32.2 %collective-permute-start.2 = (bf16[2048,256]{1,0:T(8,128)(2,1)}, bf16[2048,256]{1,0:T(8,128)(2,1)}, u32[]{:S(2)}, u32[]{:S(2)}) collective-permute-start(bf16[2048,256]{1,0:T(8,128)(2,1)} %convolution_convert_fusion.2), channel_id=1, source_target_pairs={{0,1},{1,2},{2,3},{3,4},{4,5},{5,6},{6,7},{7,8},{8,9},{9,10},{10,1... | collective-permute-start | bytes 3145736 | tf_op jit(solution)/shard_map/ppermute | solution.py:28
  20.3 27.2 %collective-permute-start.1 = (bf16[2048,256]{1,0:T(8,128)(2,1)}, bf16[2048,256]{1,0:T(8,128)(2,1)}, u32[]{:S(2)}, u32[]{:S(2)}) collective-permute-start(bf16[2048,256]{1,0:T(8,128)(2,1)} %convolution_convert_fusion.2), channel_id=1, source_target_pairs={{16,0},{32,16},{48,32},{64,48},{80,64},{96,80},{112,96},{17,1},{33... | collective-permute-start | bytes 3145736 | tf_op jit(solution)/shard_map/ppermute | solution.py:28
  23.8 23.7 %collective-permute-start = (bf16[2048,256]{1,0:T(8,128)(2,1)}, bf16[2048,256]{1,0:T(8,128)(2,1)}, u32[]{:S(2)}, u32[]{:S(2)}) collective-permute-start(bf16[2048,256]{1,0:T(8,128)(2,1)} %convolution_convert_fusion.2), channel_id=1, source_target_pairs={{0,16},{16,32},{32,48},{48,64},{64,80},{80,96},{96,112},{1,17},{17... | collective-permute-start | bytes 3145736 | tf_op jit(solution)/shard_map/ppermute | solution.py:28
  27.9 3.1 %copy-start.6 = (bf16[256,512]{1,0:T(8,128)(2,1)S(1)}, bf16[256,512]{1,0:T(8,128)(2,1)}, u32[]{:S(2)}) copy-start(bf16[256,512]{1,0:T(8,128)(2,1)} %wkv_ref.1) | copy-start | bytes 786436
  47.5 1.0 copy-start.4
  80.2 24.3 %copy-start.3 = (bf16[2048,256]{1,0:T(8,128)(2,1)S(1)}, bf16[2048,256]{1,0:T(8,128)(2,1)}, u32[]{:S(2)}) copy-start(bf16[2048,256]{1,0:T(8,128)(2,1)} %get-tuple-element.21) | copy-start | bytes 3145732
  92.3 60.8 %collective-permute-start.4 = (bf16[2048,256]{1,0:T(8,128)(2,1)}, bf16[2048,256]{1,0:T(8,128)(2,1)S(1)}, u32[]{:S(2)}, u32[]{:S(2)}) collective-permute-start(bf16[2048,256]{1,0:T(8,128)(2,1)} %bitcast.51), channel_id=1, source_target_pairs={{16,0},{32,16},{48,32},{64,48},{80,64},{96,80},{112,96},{17,1},{33... | collective-permute-start | bytes 3145736 | tf_op jit(solution)/shard_map/ppermute | solution.py:28
  94.9 58.2 %collective-permute-start.5 = (bf16[2048,256]{1,0:T(8,128)(2,1)}, bf16[2048,256]{1,0:T(8,128)(2,1)}, u32[]{:S(2)}, u32[]{:S(2)}) collective-permute-start(bf16[2048,256]{1,0:T(8,128)(2,1)} %bitcast.50), channel_id=1, source_target_pairs={{0,16},{16,32},{32,48},{48,64},{64,80},{80,96},{96,112},{1,17},{17... | collective-permute-start | bytes 3145736 | tf_op jit(solution)/shard_map/ppermute | solution.py:28
  98.1 55.0 %collective-permute-start.6 = (bf16[2048,256]{1,0:T(8,128)(2,1)}, bf16[2048,256]{1,0:T(8,128)(2,1)}, u32[]{:S(2)}, u32[]{:S(2)}) collective-permute-start(bf16[2048,256]{1,0:T(8,128)(2,1)} %bitcast.49), channel_id=1, source_target_pairs={{1,0},{2,1},{3,2},{4,3},{5,4},{6,5},{7,6},{8,7},{9,8},{10,9},{11,1... | collective-permute-start | bytes 3145736 | tf_op jit(solution)/shard_map/ppermute | solution.py:28
  99.4 53.7 %collective-permute-start.7 = (bf16[2048,256]{1,0:T(8,128)(2,1)}, bf16[2048,256]{1,0:T(8,128)(2,1)}, u32[]{:S(2)}, u32[]{:S(2)}) collective-permute-start(bf16[2048,256]{1,0:T(8,128)(2,1)} %bitcast.48), channel_id=1, source_target_pairs={{0,1},{1,2},{2,3},{3,4},{4,5},{5,6},{6,7},{7,8},{8,9},{9,10},{10,1... | collective-permute-start | bytes 3145736 | tf_op jit(solution)/shard_map/ppermute | solution.py:28
  153.1 1.0 copy-start.5

commit v13 on v12

--- a/solution.py
+++ b/solution.py
@@ -239,21 +239,20 @@
     return sigma * (1.0 + values * (1.0 - sigma))
 
 
-def edge_back_kernel(lat_ref, own_ref, a_ref, b_ref, c_ref, d_ref, gn_ref, w1_ref, w2_ref, out_ref):
+def edge_back_kernel(slope_ref, own_ref, a_ref, b_ref, c_ref, d_ref, gn_ref, w1_ref, w2_ref, out_ref):
     nt = (((1,), (1,)), ((), ()))
     collected = own_ref[...]
     for ref in (a_ref, b_ref, c_ref, d_ref):
         collected = collected + ref[...].astype(jnp.float32)
     grad_msg = collected.astype(jnp.bfloat16)
-    pre_act = jnp.dot(lat_ref[...], w1_ref[...], preferred_element_type=jnp.float32)
     grad_pre = lax.dot_general(grad_msg, w2_ref[...], nt, preferred_element_type=jnp.float32)
-    grad_pre = (grad_pre * slope_of(pre_act)).astype(jnp.bfloat16)
+    grad_pre = (grad_pre * slope_ref[...]).astype(jnp.bfloat16)
     total = gn_ref[...] + lax.dot_general(grad_pre, w1_ref[...], nt, preferred_element_type=jnp.float32)
     out_ref[...] = total.astype(out_ref.dtype)
 
 
-def edge_back(latent, own_part, received, grad_node, w_e1, w_e2, rows_per_step=512):
-    rows, width = latent.shape
+def edge_back(edge_slope, own_part, received, grad_node, w_e1, w_e2, rows_per_step=512):
+    rows, width = edge_slope.shape
     row_block = pl.BlockSpec((rows_per_step, width), lambda i: (i, 0))
     weight = pl.BlockSpec(w_e1.shape, lambda i: (0, 0))
     return pl.pallas_call(
@@ -265,9 +264,9 @@
         cost_estimate=pl.CostEstimate(
             flops=6 * rows * width * width,
             transcendentals=rows * width,
-            bytes_accessed=rows * width * (2 + 4 + 2 * len(received) + 4 + 2),
-        ),
-    )(latent, own_part, *received, grad_node, w_e1, w_e2)
+            bytes_accessed=rows * width * (4 + 4 + 2 * len(received) + 4 + 2),
+        ),
+    )(edge_slope, own_part, *received, grad_node, w_e1, w_e2)
 
 
 def dense(left, right):
@@ -343,8 +342,10 @@
         passed_along(outbound[2], "py", -1),
         passed_along(outbound[3], "py", 1),
     ]
+    late_pre_act, own_part = lax.optimization_barrier((pre_act, own_part))
+    edge_slope = silu_slope(late_pre_act)
     grad_nodes = edge_back(
-        latent, own_part.reshape(node_rows, latent_width), received, grad_node, w_e1, w_e2
+        edge_slope, own_part.reshape(node_rows, latent_width), received, grad_node, w_e1, w_e2
     )
     return (grad_nodes[None, None], grad_tokens[None])
 

time: 162 us -> 160 us (0.988)
  blocking collectives: 48.6 us -> 0 us
  waiting for transfers between devices: 16.1 us -> 49.8 us
  starting transfers between devices: 36 us -> 46.9 us
  other arithmetic: 0.08 us -> 2.11 us
    all_to_all x1 -> x0, blocking collectives: 48.6 us -> none  [on_device(): lax.all_to_all(grad_slots.reshape(devices, slot_count, latent_width), ('p...]
    all_to_all x0 -> x1, waiting for transfers between devices: none -> 36.2 us  [on_device(): lax.all_to_all(grad_slots.reshape(devices, slot_count, latent_width), ('p...]
    all_to_all x0 -> x1, starting transfers between devices: none -> 10.4 us  [on_device(): lax.all_to_all(grad_slots.reshape(devices, slot_count, latent_width), ('p...]
    mul x0 -> x1, other arithmetic: none -> 2.03 us  [silu_slope(): return sigma * (1.0 + values * (1.0 - sigma))]
    dot_general x3 -> x4, matrix products: 5.33 us -> 6.86 us  [dense(): return jnp.dot(left, right, preferred_element_type=jnp.float32)]
  transfers between devices with their start and end apart: 9 -> 10, of which waited for: 2 -> 3; matrix products, arithmetic and copies ran while one was open for 4% -> 7% of each run, Pallas kernels for 0% -> 0%
where the time goes in v13:
time: 160 us
  Pallas kernels  50.3 us (31%)
  waiting for transfers between devices  49.8 us (31%)
  starting transfers between devices  46.9 us (29%)
  matrix products  6.86 us (4%)
  local copies, waits for them, and re-layouts  2.91 us (2%)
  other arithmetic  2.11 us (1%)
    all_to_all x1, waiting for transfers between devices, on_device(): lax.all_to_all(grad_slots.reshape(devices, slot_count, latent_width), ('p...  36.2 us
    ppermute x8, starting transfers between devices, passed_along(): lax.ppermute(value, axis, [(source, source + steps) for source in range(l...  24.6 us
    pallas_call x1, Pallas kernels, attend_back(): pl.pallas_call(functools.partial(attend_kernel, scale), grid=(steps,), in...  19.5 us
    ppermute x8, waiting for transfers between devices, passed_along(): lax.ppermute(value, axis, [(source, source + steps) for source in range(l...  13.3 us
    pallas_call x1, Pallas kernels, tile_gather(): pl.pallas_call(functools.partial(gather_kernel, group), grid_spec=pltpu.P...  12.3 us
    all_to_all x1, starting transfers between devices, on_device(): lax.all_to_all(token_groups, ('px', 'py'), split_axis=0, concat_axis=0, t...  12 us
    pallas_call x1, Pallas kernels, tile_scatter(): pl.pallas_call(functools.partial(scatter_kernel, group), grid_spec=pltpu....  11.9 us
    all_to_all x1, starting transfers between devices, on_device(): lax.all_to_all(grad_slots.reshape(devices, slot_count, latent_width), ('p...  10.4 us
  transfers between devices with their start and end apart: 10, of which 3 were waited for; matrix products, arithmetic and copies ran while one was open for 7% of the time, Pallas kernels for 0%

profile of v13, /device:TPU:1, one launch (start us, length us, event | category | flops | bytes accessed | tf_op | source)
XLA Modules:
  0.0 159.7 jit_solution(2574449873954054833)
XLA Ops:
  0.6 0.0 copy-start
  0.6 0.0 copy-start.3
  0.7 0.0 copy-start.2
  0.7 12.0 %all-to-all-start = ((bf16[128,16,256]{2,1,0:T(8,128)(2,1)}), bf16[128,16,256]{2,1,0:T(8,128)(2,1)}, u32[]{:S(2)}, u32[]{:S(2)}) async-start(bf16[128,16,256]{2,1,0:T(8,128)(2,1)} %bitcast.37), calls=%async_computation | async-start | bytes 2097152 | tf_op jit(solution)/shard_map/all_to_all | solution.py:317
  12.6 0.0 copy-start.5
  12.7 0.4 fusion.2
  13.1 0.5 copy-done.5
  13.6 1.7 %convolution_convert_fusion.2 = bf16[2048,256]{1,0:T(8,128)(2,1)} fusion(bf16[256,256]{1,0:T(8,128)(2,1)S(1)} %copy-done.5, f32[2048,256]{1,0:T(8,128)S(1)} %fusion.2), kind=kOutput, calls=%fused_computation.2 | convolution fusion | flops 271581184 | bytes 3276800 | tf_op jit(solution)/shard_map/dot_general | solution.py:273
  15.2 1.3 collective-permute-start.3
  16.5 5.0 %collective-permute-start.2 = (bf16[2048,256]{1,0:T(8,128)(2,1)}, bf16[2048,256]{1,0:T(8,128)(2,1)}, u32[]{:S(2)}, u32[]{:S(2)}) collective-permute-start(bf16[2048,256]{1,0:T(8,128)(2,1)} %convolution_convert_fusion.2), channel_id=1, source_target_pairs={{0,1},{1,2},{2,3},{3,4},{4,5},{5,6},{6,7},{7,8},{8,9},{9,10},{10,1... | collective-permute-start | bytes 3145736 | tf_op jit(solution)/shard_map/ppermute | solution.py:28
  21.5 3.6 %collective-permute-start.1 = (bf16[2048,256]{1,0:T(8,128)(2,1)}, bf16[2048,256]{1,0:T(8,128)(2,1)}, u32[]{:S(2)}, u32[]{:S(2)}) collective-permute-start(bf16[2048,256]{1,0:T(8,128)(2,1)} %convolution_convert_fusion.2), channel_id=1, source_target_pairs={{16,0},{32,16},{48,32},{64,48},{80,64},{96,80},{112,96},{17,1},{33... | collective-permute-start | bytes 3145736 | tf_op jit(solution)/shard_map/ppermute | solution.py:28
  25.1 2.5 %collective-permute-start = (bf16[2048,256]{1,0:T(8,128)(2,1)}, bf16[2048,256]{1,0:T(8,128)(2,1)}, u32[]{:S(2)}, u32[]{:S(2)}) collective-permute-start(bf16[2048,256]{1,0:T(8,128)(2,1)} %convolution_convert_fusion.2), channel_id=1, source_target_pairs={{0,16},{16,32},{32,48},{48,64},{64,80},{80,96},{96,112},{1,17},{17... | collective-permute-start | bytes 3145736 | tf_op jit(solution)/shard_map/ppermute | solution.py:28
  27.6 0.1 copy.16
  27.7 0.7 reshape_squeeze.6.src_ids
  28.4 0.1 fusion
  28.5 0.7 reshape.80.live_ref
  29.2 1.5 convolution_convert_fusion.1.go_ref
  30.7 0.4 all-to-all-done
  31.1 3.2 %convolution_convert_fusion.kv_ref = bf16[2048,512]{1,0:T(8,128)(2,1)} fusion(bf16[2048,256]{1,0:T(8,128)(2,1)} %bitcast.10, bf16[256,512]{1,0:T(8,128)(2,1)S(1)} %copy-done.4), kind=kOutput, calls=%fused_computation | convolution fusion | flops 537919488 | bytes 3407872 | tf_op jit(solution)/shard_map/dot_general | solution.py:273
  34.3 13.2 %collective-permute-done.3 = bf16[2048,256]{1,0:T(8,128)(2,1)} collective-permute-done((bf16[2048,256]{1,0:T(8,128)(2,1)}, bf16[2048,256]{1,0:T(8,128)(2,1)}, u32[]{:S(2)}, u32[]{:S(2)}) %collective-permute-start.3) | collective-permute-done | bytes 1048608 | tf_op jit(solution)/shard_map/ppermute | solution.py:28
  47.6 12.3 %shard_map.140 = (f32[2048,256]{1,0:T(8,128)}, bf16[2048,256]{1,0:T(8,128)(2,1)}) custom-call(s32[64]{0:T(128)} %reshape_squeeze.6.src_ids, s32[16,4,128,128]{3,2,1,0:T(8,128)} %bitcast.30, bf16[16,128,256]{2,1,0:T(8,128)(2,1)} %bitcast.3.own, bf16[16,128,256]{2,1,0:T(8,128)(2,1)} %bitcast.4.up, bf16[16,128,256]{2,1,0:T(8,128)(2,1)} %bitcast.5.down, ...), custom_call_target="tpu_custom_call" | custom-call | tf_op jit(solution)/shard_map/pallas_call | solution.py:71
  59.9 19.5 %shard_map.141 = (bf16[2048,256]{1,0:T(8,128)(2,1)}, bf16[2048,256]{1,0:T(8,128)(2,1)}) custom-call(f32[1,2048]{1,0:T(1,128)} %reshape.80.live_ref, bf16[2048,256]{1,0:T(8,128)(2,1)} %get-tuple-element.14.q_ref, bf16[2048,256]{1,0:T(8,128)(2,1)} %convolution_convert_fusion.1.go_ref, bf16[2048,512]{1,0:T(8,128)(2,1)} %convolution_convert_fusion.kv_ref, ...), custom_call_target="tpu_custom_call" | custom-call | flops 10737418240 | bytes 7340032 | tf_op jit(solution)/shard_map/pallas_call | solution.py:209
  79.3 11.9 %shard_map.142 = (f32[2048,256]{1,0:T(8,128)}, f32[16,128,256]{2,1,0:T(8,128)}, bf16[16,128,256]{2,1,0:T(8,128)(2,1)}, bf16[16,128,256]{2,1,0:T(8,128)(2,1)}, bf...) custom-call(s32[64]{0:T(128)} %reshape_squeeze.6.src_ids, s32[16,4,128,128]{3,2,1,0:T(8,128)} %bitcast.31, ...), custom_call_target="tpu_custom_call" | custom-call | tf_op jit(solution)/shard_map/pallas_call | solution.py:142
  91.2 2.6 %collective-permute-start.4 = (bf16[2048,256]{1,0:T(8,128)(2,1)}, bf16[2048,256]{1,0:T(8,128)(2,1)}, u32[]{:S(2)}, u32[]{:S(2)}) collective-permute-start(bf16[2048,256]{1,0:T(8,128)(2,1)} %bitcast.43), channel_id=1, source_target_pairs={{16,0},{32,16},{48,32},{64,48},{80,64},{96,80},{112,96},{17,1},{33... | collective-permute-start | bytes 3145736 | tf_op jit(solution)/shard_map/ppermute | solution.py:28
  93.9 3.2 %collective-permute-start.5 = (bf16[2048,256]{1,0:T(8,128)(2,1)}, bf16[2048,256]{1,0:T(8,128)(2,1)}, u32[]{:S(2)}, u32[]{:S(2)}) collective-permute-start(bf16[2048,256]{1,0:T(8,128)(2,1)} %bitcast.42), channel_id=1, source_target_pairs={{0,16},{16,32},{32,48},{48,64},{64,80},{80,96},{96,112},{1,17},{17... | collective-permute-start | bytes 3145736 | tf_op jit(solution)/shard_map/ppermute | solution.py:28
  97.1 1.3 collective-permute-start.6
  98.4 5.1 %collective-permute-start.7 = (bf16[2048,256]{1,0:T(8,128)(2,1)}, bf16[2048,256]{1,0:T(8,128)(2,1)}, u32[]{:S(2)}, u32[]{:S(2)}) collective-permute-start(bf16[2048,256]{1,0:T(8,128)(2,1)} %bitcast.40), channel_id=1, source_target_pairs={{0,1},{1,2},{2,3},{3,4},{4,5},{5,6},{6,7},{7,8},{8,9},{9,10},{10,1... | collective-permute-start | bytes 3145736 | tf_op jit(solution)/shard_map/ppermute | solution.py:28
  103.5 10.4 %all-to-all-start.1 = ((bf16[128,16,256]{2,1,0:T(8,128)(2,1)}), bf16[128,16,256]{2,1,0:T(8,128)(2,1)S(1)}, u32[]{:S(2)}, u32[]{:S(2)}) async-start(bf16[128,16,256]{2,1,0:T(8,128)(2,1)} %bitcast.38), calls=%async_computation.1 | async-start | bytes 2097152 | tf_op jit(solution)/shard_map/all_to_all | solution.py:327
  113.9 2.0 %add_multiply_fusion.slope_ref = f32[2048,256]{1,0:T(8,128)} fusion(f32[2048,256]{1,0:T(8,128)S(1)} %fusion.2), kind=kLoop, calls=%fused_computation.3 | loop fusion | flops 3670016 | bytes 4194304 | tf_op jit(solution)/shard_map/mul | solution.py:278
  115.9 36.2 %all-to-all-done.1 = bf16[128,16,256]{2,1,0:T(8,128)(2,1)S(1)} async-done(((bf16[128,16,256]{2,1,0:T(8,128)(2,1)}), bf16[128,16,256]{2,1,0:T(8,128)(2,1)S(1)}, u32[]{:S(2)}, u32[]{:S(2)}) %all-to-all-start.1) | async-done | bytes 1048608 | tf_op jit(solution)/shard_map/all_to_all | solution.py:327
  152.1 6.6 %shard_map.143 = bf16[2048,256]{1,0:T(8,128)(2,1)} custom-call(f32[2048,256]{1,0:T(8,128)} %add_multiply_fusion.slope_ref, f32[2048,256]{1,0:T(8,128)} %bitcast.35, bf16[2048,256]{1,0:T(8,128)(2,1)} %collective-permute-done.4.a_ref, bf16[2048,256]{1,0:T(8,128)(2,1)} %collective-permute-done.5.b_ref, bf16[2048,256]{1,0:T(8,128)(2,1)} %collective-permute-done.6.c_ref, ...), custom_call_target="tpu_custom_call" | custom-call | flops 805306368 | bytes 11534336 | tf_op jit(solution)/shard_map/pallas_call | solution.py:258
  158.7 1.0 copy.18
  (18 shorter events, 0.0 us)
Async XLA Ops:
  0.6 28.5 %copy-start = (bf16[256,256]{1,0:T(8,128)(2,1)S(1)}, bf16[256,256]{1,0:T(8,128)(2,1)}, u32[]{:S(2)}) copy-start(bf16[256,256]{1,0:T(8,128)(2,1)} %param.24) | copy-start | bytes 393220
  0.6 12.0 %copy-start.3 = (bf16[256,256]{1,0:T(8,128)(2,1)S(1)}, bf16[256,256]{1,0:T(8,128)(2,1)}, u32[]{:S(2)}) copy-start(bf16[256,256]{1,0:T(8,128)(2,1)} %w1_ref.1) | copy-start | bytes 393220
  0.7 12.0 %copy-start.2 = (bf16[1,1,2048,256]{3,2,1,0:T(8,128)(2,1)S(1)}, bf16[1,1,2048,256]{3,2,1,0:T(8,128)(2,1)}, u32[]{:S(2)}) copy-start(bf16[1,1,2048,256]{3,2,1,0:T(8,128)(2,1)} %param.13) | copy-start | bytes 3145732
  0.7 30.4 %all-to-all-start = ((bf16[128,16,256]{2,1,0:T(8,128)(2,1)}), bf16[128,16,256]{2,1,0:T(8,128)(2,1)}, u32[]{:S(2)}, u32[]{:S(2)}) async-start(bf16[128,16,256]{2,1,0:T(8,128)(2,1)} %bitcast.37), calls=%async_computation | async-start | bytes 2097152 | tf_op jit(solution)/shard_map/all_to_all | solution.py:317
  12.6 0.9 copy-start.5
  13.6 14.1 %copy-start.6 = (s32[1,1,16,4]{2,3,1,0:T(4,128)S(1)}, s32[1,1,16,4]{2,3,1,0:T(4,128)}, u32[]{:S(2)}) copy-start(s32[1,1,16,4]{2,3,1,0:T(4,128)} %param.14) | copy-start | bytes 772
  13.6 14.8 %copy-start.7 = (s32[128,1]{0,1:T(1,128)S(1)}, s32[128,1]{0,1:T(1,128)}, u32[]{:S(2)}) copy-start(s32[128,1]{0,1:T(1,128)} %param.17) | copy-start | bytes 1540
  13.6 15.6 %copy-start.1 = (bf16[1,1,2048,256]{3,2,1,0:T(8,128)(2,1)S(1)}, bf16[1,1,2048,256]{3,2,1,0:T(8,128)(2,1)}, u32[]{:S(2)}) copy-start(bf16[1,1,2048,256]{3,2,1,0:T(8,128)(2,1)} %param.25) | copy-start | bytes 3145732
  15.2 32.4 %collective-permute-start.3 = (bf16[2048,256]{1,0:T(8,128)(2,1)}, bf16[2048,256]{1,0:T(8,128)(2,1)}, u32[]{:S(2)}, u32[]{:S(2)}) collective-permute-start(bf16[2048,256]{1,0:T(8,128)(2,1)} %convolution_convert_fusion.2), channel_id=1, source_target_pairs={{1,0},{2,1},{3,2},{4,3},{5,4},{6,5},{7,6},{8,7},{9,8},{10,9},{11,1... | collective-permute-start | bytes 3145736 | tf_op jit(solution)/shard_map/ppermute | solution.py:28
  16.5 31.1 %collective-permute-start.2 = (bf16[2048,256]{1,0:T(8,128)(2,1)}, bf16[2048,256]{1,0:T(8,128)(2,1)}, u32[]{:S(2)}, u32[]{:S(2)}) collective-permute-start(bf16[2048,256]{1,0:T(8,128)(2,1)} %convolution_convert_fusion.2), channel_id=1, source_target_pairs={{0,1},{1,2},{2,3},{3,4},{4,5},{5,6},{6,7},{7,8},{8,9},{9,10},{10,1... | collective-permute-start | bytes 3145736 | tf_op jit(solution)/shard_map/ppermute | solution.py:28
  21.5 26.1 %collective-permute-start.1 = (bf16[2048,256]{1,0:T(8,128)(2,1)}, bf16[2048,256]{1,0:T(8,128)(2,1)}, u32[]{:S(2)}, u32[]{:S(2)}) collective-permute-start(bf16[2048,256]{1,0:T(8,128)(2,1)} %convolution_convert_fusion.2), channel_id=1, source_target_pairs={{16,0},{32,16},{48,32},{64,48},{80,64},{96,80},{112,96},{17,1},{33... | collective-permute-start | bytes 3145736 | tf_op jit(solution)/shard_map/ppermute | solution.py:28
  25.1 22.5 %collective-permute-start = (bf16[2048,256]{1,0:T(8,128)(2,1)}, bf16[2048,256]{1,0:T(8,128)(2,1)}, u32[]{:S(2)}, u32[]{:S(2)}) collective-permute-start(bf16[2048,256]{1,0:T(8,128)(2,1)} %convolution_convert_fusion.2), channel_id=1, source_target_pairs={{0,16},{16,32},{32,48},{48,64},{64,80},{80,96},{96,112},{1,17},{17... | collective-permute-start | bytes 3145736 | tf_op jit(solution)/shard_map/ppermute | solution.py:28
  29.2 1.9 %copy-start.4 = (bf16[256,512]{1,0:T(8,128)(2,1)S(1)}, bf16[256,512]{1,0:T(8,128)(2,1)}, u32[]{:S(2)}) copy-start(bf16[256,512]{1,0:T(8,128)(2,1)} %wkv_ref.1) | copy-start | bytes 786436
  91.2 60.8 %collective-permute-start.4 = (bf16[2048,256]{1,0:T(8,128)(2,1)}, bf16[2048,256]{1,0:T(8,128)(2,1)}, u32[]{:S(2)}, u32[]{:S(2)}) collective-permute-start(bf16[2048,256]{1,0:T(8,128)(2,1)} %bitcast.43), channel_id=1, source_target_pairs={{16,0},{32,16},{48,32},{64,48},{80,64},{96,80},{112,96},{17,1},{33... | collective-permute-start | bytes 3145736 | tf_op jit(solution)/shard_map/ppermute | solution.py:28
  93.9 58.2 %collective-permute-start.5 = (bf16[2048,256]{1,0:T(8,128)(2,1)}, bf16[2048,256]{1,0:T(8,128)(2,1)}, u32[]{:S(2)}, u32[]{:S(2)}) collective-permute-start(bf16[2048,256]{1,0:T(8,128)(2,1)} %bitcast.42), channel_id=1, source_target_pairs={{0,16},{16,32},{32,48},{48,64},{64,80},{80,96},{96,112},{1,17},{17... | collective-permute-start | bytes 3145736 | tf_op jit(solution)/shard_map/ppermute | solution.py:28
  97.1 55.0 %collective-permute-start.6 = (bf16[2048,256]{1,0:T(8,128)(2,1)}, bf16[2048,256]{1,0:T(8,128)(2,1)}, u32[]{:S(2)}, u32[]{:S(2)}) collective-permute-start(bf16[2048,256]{1,0:T(8,128)(2,1)} %bitcast.41), channel_id=1, source_target_pairs={{1,0},{2,1},{3,2},{4,3},{5,4},{6,5},{7,6},{8,7},{9,8},{10,9},{11,1... | collective-permute-start | bytes 3145736 | tf_op jit(solution)/shard_map/ppermute | solution.py:28
  98.4 53.7 %collective-permute-start.7 = (bf16[2048,256]{1,0:T(8,128)(2,1)}, bf16[2048,256]{1,0:T(8,128)(2,1)}, u32[]{:S(2)}, u32[]{:S(2)}) collective-permute-start(bf16[2048,256]{1,0:T(8,128)(2,1)} %bitcast.40), channel_id=1, source_target_pairs={{0,1},{1,2},{2,3},{3,4},{4,5},{5,6},{6,7},{7,8},{8,9},{9,10},{10,1... | collective-permute-start | bytes 3145736 | tf_op jit(solution)/shard_map/ppermute | solution.py:28
  103.5 48.6 %all-to-all-start.1 = ((bf16[128,16,256]{2,1,0:T(8,128)(2,1)}), bf16[128,16,256]{2,1,0:T(8,128)(2,1)S(1)}, u32[]{:S(2)}, u32[]{:S(2)}) async-start(bf16[128,16,256]{2,1,0:T(8,128)(2,1)} %bitcast.38), calls=%async_computation.1 | async-start | bytes 2097152 | tf_op jit(solution)/shard_map/all_to_all | solution.py:327

commit v14 on v13

--- a/solution.py
+++ b/solution.py
@@ -251,7 +251,7 @@
     out_ref[...] = total.astype(out_ref.dtype)
 
 
-def edge_back(edge_slope, own_part, received, grad_node, w_e1, w_e2, rows_per_step=512):
+def edge_back(edge_slope, own_part, received, grad_node, w_e1, w_e2, rows_per_step=256):
     rows, width = edge_slope.shape
     row_block = pl.BlockSpec((rows_per_step, width), lambda i: (i, 0))
     weight = pl.BlockSpec(w_e1.shape, lambda i: (0, 0))

time: 160 us -> 162 us (1.012)
  Pallas kernels: 50.3 us -> 52.3 us
    pallas_call x1, Pallas kernels: 6.61 us -> 8.67 us  [edge_back(): pl.pallas_call(edge_back_kernel, grid=(rows // rows_per_step,), in_specs=...]
  transfers between devices with their start and end apart: 10 -> 10, of which waited for: 3 -> 3; matrix products, arithmetic and copies ran while one was open for 7% -> 6% of each run, Pallas kernels for 0% -> 0%
where the time goes in v14:
time: 162 us
  Pallas kernels  52.3 us (32%)
  waiting for transfers between devices  49.8 us (31%)
  starting transfers between devices  46.9 us (29%)
  matrix products  6.86 us (4%)
  local copies, waits for them, and re-layouts  2.91 us (2%)
  other arithmetic  2.11 us (1%)
    all_to_all x1, waiting for transfers between devices, on_device(): lax.all_to_all(grad_slots.reshape(devices, slot_count, latent_width), ('p...  36.1 us
    ppermute x8, starting transfers between devices, passed_along(): lax.ppermute(value, axis, [(source, source + steps) for source in range(l...  24.6 us
    pallas_call x1, Pallas kernels, attend_back(): pl.pallas_call(functools.partial(attend_kernel, scale), grid=(steps,), in...  19.5 us
    ppermute x8, waiting for transfers between devices, passed_along(): lax.ppermute(value, axis, [(source, source + steps) for source in range(l...  13.3 us
    pallas_call x1, Pallas kernels, tile_gather(): pl.pallas_call(functools.partial(gather_kernel, group), grid_spec=pltpu.P...  12.3 us
    all_to_all x1, starting transfers between devices, on_device(): lax.all_to_all(token_groups, ('px', 'py'), split_axis=0, concat_axis=0, t...  12 us
    pallas_call x1, Pallas kernels, tile_scatter(): pl.pallas_call(functools.partial(scatter_kernel, group), grid_spec=pltpu....  11.9 us
    all_to_all x1, starting transfers between devices, on_device(): lax.all_to_all(grad_slots.reshape(devices, slot_count, latent_width), ('p...  10.4 us
  transfers between devices with their start and end apart: 10, of which 3 were waited for; matrix products, arithmetic and copies ran while one was open for 6% of the time, Pallas kernels for 0%

profile of v14, /device:TPU:1, one launch (start us, length us, event | category | flops | bytes accessed | tf_op | source)
XLA Modules:
  0.0 161.7 jit_solution(4414971497409182130)
XLA Ops:
  0.6 0.0 copy-start
  0.6 0.0 copy-start.3
  0.7 0.0 copy-start.2
  0.7 12.0 %all-to-all-start = ((bf16[128,16,256]{2,1,0:T(8,128)(2,1)}), bf16[128,16,256]{2,1,0:T(8,128)(2,1)}, u32[]{:S(2)}, u32[]{:S(2)}) async-start(bf16[128,16,256]{2,1,0:T(8,128)(2,1)} %bitcast.37), calls=%async_computation | async-start | bytes 2097152 | tf_op jit(solution)/shard_map/all_to_all | solution.py:317
  12.6 0.0 copy-start.5
  12.7 0.4 fusion.2
  13.1 0.5 copy-done.5
  13.6 1.7 %convolution_convert_fusion.2 = bf16[2048,256]{1,0:T(8,128)(2,1)} fusion(bf16[256,256]{1,0:T(8,128)(2,1)S(1)} %copy-done.5, f32[2048,256]{1,0:T(8,128)S(1)} %fusion.2), kind=kOutput, calls=%fused_computation.2 | convolution fusion | flops 271581184 | bytes 3276800 | tf_op jit(solution)/shard_map/dot_general | solution.py:273
  15.2 1.3 collective-permute-start.3
  16.5 5.0 %collective-permute-start.2 = (bf16[2048,256]{1,0:T(8,128)(2,1)}, bf16[2048,256]{1,0:T(8,128)(2,1)}, u32[]{:S(2)}, u32[]{:S(2)}) collective-permute-start(bf16[2048,256]{1,0:T(8,128)(2,1)} %convolution_convert_fusion.2), channel_id=1, source_target_pairs={{0,1},{1,2},{2,3},{3,4},{4,5},{5,6},{6,7},{7,8},{8,9},{9,10},{10,1... | collective-permute-start | bytes 3145736 | tf_op jit(solution)/shard_map/ppermute | solution.py:28
  21.5 3.6 %collective-permute-start.1 = (bf16[2048,256]{1,0:T(8,128)(2,1)}, bf16[2048,256]{1,0:T(8,128)(2,1)}, u32[]{:S(2)}, u32[]{:S(2)}) collective-permute-start(bf16[2048,256]{1,0:T(8,128)(2,1)} %convolution_convert_fusion.2), channel_id=1, source_target_pairs={{16,0},{32,16},{48,32},{64,48},{80,64},{96,80},{112,96},{17,1},{33... | collective-permute-start | bytes 3145736 | tf_op jit(solution)/shard_map/ppermute | solution.py:28
  25.1 2.5 %collective-permute-start = (bf16[2048,256]{1,0:T(8,128)(2,1)}, bf16[2048,256]{1,0:T(8,128)(2,1)}, u32[]{:S(2)}, u32[]{:S(2)}) collective-permute-start(bf16[2048,256]{1,0:T(8,128)(2,1)} %convolution_convert_fusion.2), channel_id=1, source_target_pairs={{0,16},{16,32},{32,48},{48,64},{64,80},{80,96},{96,112},{1,17},{17... | collective-permute-start | bytes 3145736 | tf_op jit(solution)/shard_map/ppermute | solution.py:28
  27.6 0.1 copy.16
  27.7 0.7 reshape_squeeze.6.src_ids
  28.4 0.1 fusion
  28.5 0.7 reshape.80.live_ref
  29.2 1.5 convolution_convert_fusion.1.go_ref
  30.7 0.4 all-to-all-done
  31.1 3.2 %convolution_convert_fusion.kv_ref = bf16[2048,512]{1,0:T(8,128)(2,1)} fusion(bf16[2048,256]{1,0:T(8,128)(2,1)} %bitcast.10, bf16[256,512]{1,0:T(8,128)(2,1)S(1)} %copy-done.4), kind=kOutput, calls=%fused_computation | convolution fusion | flops 537919488 | bytes 3407872 | tf_op jit(solution)/shard_map/dot_general | solution.py:273
  34.3 13.2 %collective-permute-done.3 = bf16[2048,256]{1,0:T(8,128)(2,1)} collective-permute-done((bf16[2048,256]{1,0:T(8,128)(2,1)}, bf16[2048,256]{1,0:T(8,128)(2,1)}, u32[]{:S(2)}, u32[]{:S(2)}) %collective-permute-start.3) | collective-permute-done | bytes 1048608 | tf_op jit(solution)/shard_map/ppermute | solution.py:28
  47.6 12.3 %shard_map.140 = (f32[2048,256]{1,0:T(8,128)}, bf16[2048,256]{1,0:T(8,128)(2,1)}) custom-call(s32[64]{0:T(128)} %reshape_squeeze.6.src_ids, s32[16,4,128,128]{3,2,1,0:T(8,128)} %bitcast.30, bf16[16,128,256]{2,1,0:T(8,128)(2,1)} %bitcast.3.own, bf16[16,128,256]{2,1,0:T(8,128)(2,1)} %bitcast.4.up, bf16[16,128,256]{2,1,0:T(8,128)(2,1)} %bitcast.5.down, ...), custom_call_target="tpu_custom_call" | custom-call | tf_op jit(solution)/shard_map/pallas_call | solution.py:71
  59.9 19.5 %shard_map.141 = (bf16[2048,256]{1,0:T(8,128)(2,1)}, bf16[2048,256]{1,0:T(8,128)(2,1)}) custom-call(f32[1,2048]{1,0:T(1,128)} %reshape.80.live_ref, bf16[2048,256]{1,0:T(8,128)(2,1)} %get-tuple-element.14.q_ref, bf16[2048,256]{1,0:T(8,128)(2,1)} %convolution_convert_fusion.1.go_ref, bf16[2048,512]{1,0:T(8,128)(2,1)} %convolution_convert_fusion.kv_ref, ...), custom_call_target="tpu_custom_call" | custom-call | flops 10737418240 | bytes 7340032 | tf_op jit(solution)/shard_map/pallas_call | solution.py:209
  79.3 11.9 %shard_map.142 = (f32[2048,256]{1,0:T(8,128)}, f32[16,128,256]{2,1,0:T(8,128)}, bf16[16,128,256]{2,1,0:T(8,128)(2,1)}, bf16[16,128,256]{2,1,0:T(8,128)(2,1)}, bf...) custom-call(s32[64]{0:T(128)} %reshape_squeeze.6.src_ids, s32[16,4,128,128]{3,2,1,0:T(8,128)} %bitcast.31, ...), custom_call_target="tpu_custom_call" | custom-call | tf_op jit(solution)/shard_map/pallas_call | solution.py:142
  91.2 2.7 %collective-permute-start.4 = (bf16[2048,256]{1,0:T(8,128)(2,1)}, bf16[2048,256]{1,0:T(8,128)(2,1)}, u32[]{:S(2)}, u32[]{:S(2)}) collective-permute-start(bf16[2048,256]{1,0:T(8,128)(2,1)} %bitcast.43), channel_id=1, source_target_pairs={{16,0},{32,16},{48,32},{64,48},{80,64},{96,80},{112,96},{17,1},{33... | collective-permute-start | bytes 3145736 | tf_op jit(solution)/shard_map/ppermute | solution.py:28
  93.9 3.2 %collective-permute-start.5 = (bf16[2048,256]{1,0:T(8,128)(2,1)}, bf16[2048,256]{1,0:T(8,128)(2,1)}, u32[]{:S(2)}, u32[]{:S(2)}) collective-permute-start(bf16[2048,256]{1,0:T(8,128)(2,1)} %bitcast.42), channel_id=1, source_target_pairs={{0,16},{16,32},{32,48},{48,64},{64,80},{80,96},{96,112},{1,17},{17... | collective-permute-start | bytes 3145736 | tf_op jit(solution)/shard_map/ppermute | solution.py:28
  97.1 1.3 collective-permute-start.6
  98.4 5.1 %collective-permute-start.7 = (bf16[2048,256]{1,0:T(8,128)(2,1)}, bf16[2048,256]{1,0:T(8,128)(2,1)}, u32[]{:S(2)}, u32[]{:S(2)}) collective-permute-start(bf16[2048,256]{1,0:T(8,128)(2,1)} %bitcast.40), channel_id=1, source_target_pairs={{0,1},{1,2},{2,3},{3,4},{4,5},{5,6},{6,7},{7,8},{8,9},{9,10},{10,1... | collective-permute-start | bytes 3145736 | tf_op jit(solution)/shard_map/ppermute | solution.py:28
  103.5 10.4 %all-to-all-start.1 = ((bf16[128,16,256]{2,1,0:T(8,128)(2,1)}), bf16[128,16,256]{2,1,0:T(8,128)(2,1)S(1)}, u32[]{:S(2)}, u32[]{:S(2)}) async-start(bf16[128,16,256]{2,1,0:T(8,128)(2,1)} %bitcast.38), calls=%async_computation.1 | async-start | bytes 2097152 | tf_op jit(solution)/shard_map/all_to_all | solution.py:327
  113.9 2.0 %add_multiply_fusion.slope_ref = f32[2048,256]{1,0:T(8,128)} fusion(f32[2048,256]{1,0:T(8,128)S(1)} %fusion.2), kind=kLoop, calls=%fused_computation.3 | loop fusion | flops 3670016 | bytes 4194304 | tf_op jit(solution)/shard_map/mul | solution.py:278
  115.9 36.1 %all-to-all-done.1 = bf16[128,16,256]{2,1,0:T(8,128)(2,1)S(1)} async-done(((bf16[128,16,256]{2,1,0:T(8,128)(2,1)}), bf16[128,16,256]{2,1,0:T(8,128)(2,1)S(1)}, u32[]{:S(2)}, u32[]{:S(2)}) %all-to-all-start.1) | async-done | bytes 1048608 | tf_op jit(solution)/shard_map/all_to_all | solution.py:327
  152.1 8.7 %shard_map.143 = bf16[2048,256]{1,0:T(8,128)(2,1)} custom-call(f32[2048,256]{1,0:T(8,128)} %add_multiply_fusion.slope_ref, f32[2048,256]{1,0:T(8,128)} %bitcast.35, bf16[2048,256]{1,0:T(8,128)(2,1)} %collective-permute-done.4.a_ref, bf16[2048,256]{1,0:T(8,128)(2,1)} %collective-permute-done.5.b_ref, bf16[2048,256]{1,0:T(8,128)(2,1)} %collective-permute-done.6.c_ref, ...), custom_call_target="tpu_custom_call" | custom-call | flops 805306368 | bytes 11534336 | tf_op jit(solution)/shard_map/pallas_call | solution.py:258
  160.7 1.0 copy.18
  (18 shorter events, 0.0 us)
Async XLA Ops:
  0.6 28.5 %copy-start = (bf16[256,256]{1,0:T(8,128)(2,1)S(1)}, bf16[256,256]{1,0:T(8,128)(2,1)}, u32[]{:S(2)}) copy-start(bf16[256,256]{1,0:T(8,128)(2,1)} %param.24) | copy-start | bytes 393220
  0.6 12.0 %copy-start.3 = (bf16[256,256]{1,0:T(8,128)(2,1)S(1)}, bf16[256,256]{1,0:T(8,128)(2,1)}, u32[]{:S(2)}) copy-start(bf16[256,256]{1,0:T(8,128)(2,1)} %w1_ref.1) | copy-start | bytes 393220
  0.7 12.0 %copy-start.2 = (bf16[1,1,2048,256]{3,2,1,0:T(8,128)(2,1)S(1)}, bf16[1,1,2048,256]{3,2,1,0:T(8,128)(2,1)}, u32[]{:S(2)}) copy-start(bf16[1,1,2048,256]{3,2,1,0:T(8,128)(2,1)} %param.13) | copy-start | bytes 3145732
  0.7 30.4 %all-to-all-start = ((bf16[128,16,256]{2,1,0:T(8,128)(2,1)}), bf16[128,16,256]{2,1,0:T(8,128)(2,1)}, u32[]{:S(2)}, u32[]{:S(2)}) async-start(bf16[128,16,256]{2,1,0:T(8,128)(2,1)} %bitcast.37), calls=%async_computation | async-start | bytes 2097152 | tf_op jit(solution)/shard_map/all_to_all | solution.py:317
  12.6 0.9 copy-start.5
  13.6 14.1 %copy-start.6 = (s32[1,1,16,4]{2,3,1,0:T(4,128)S(1)}, s32[1,1,16,4]{2,3,1,0:T(4,128)}, u32[]{:S(2)}) copy-start(s32[1,1,16,4]{2,3,1,0:T(4,128)} %param.14) | copy-start | bytes 772
  13.6 14.8 %copy-start.7 = (s32[128,1]{0,1:T(1,128)S(1)}, s32[128,1]{0,1:T(1,128)}, u32[]{:S(2)}) copy-start(s32[128,1]{0,1:T(1,128)} %param.17) | copy-start | bytes 1540
  13.6 15.6 %copy-start.1 = (bf16[1,1,2048,256]{3,2,1,0:T(8,128)(2,1)S(1)}, bf16[1,1,2048,256]{3,2,1,0:T(8,128)(2,1)}, u32[]{:S(2)}) copy-start(bf16[1,1,2048,256]{3,2,1,0:T(8,128)(2,1)} %param.25) | copy-start | bytes 3145732
  15.2 32.4 %collective-permute-start.3 = (bf16[2048,256]{1,0:T(8,128)(2,1)}, bf16[2048,256]{1,0:T(8,128)(2,1)}, u32[]{:S(2)}, u32[]{:S(2)}) collective-permute-start(bf16[2048,256]{1,0:T(8,128)(2,1)} %convolution_convert_fusion.2), channel_id=1, source_target_pairs={{1,0},{2,1},{3,2},{4,3},{5,4},{6,5},{7,6},{8,7},{9,8},{10,9},{11,1... | collective-permute-start | bytes 3145736 | tf_op jit(solution)/shard_map/ppermute | solution.py:28
  16.5 31.1 %collective-permute-start.2 = (bf16[2048,256]{1,0:T(8,128)(2,1)}, bf16[2048,256]{1,0:T(8,128)(2,1)}, u32[]{:S(2)}, u32[]{:S(2)}) collective-permute-start(bf16[2048,256]{1,0:T(8,128)(2,1)} %convolution_convert_fusion.2), channel_id=1, source_target_pairs={{0,1},{1,2},{2,3},{3,4},{4,5},{5,6},{6,7},{7,8},{8,9},{9,10},{10,1... | collective-permute-start | bytes 3145736 | tf_op jit(solution)/shard_map/ppermute | solution.py:28
  21.5 26.1 %collective-permute-start.1 = (bf16[2048,256]{1,0:T(8,128)(2,1)}, bf16[2048,256]{1,0:T(8,128)(2,1)}, u32[]{:S(2)}, u32[]{:S(2)}) collective-permute-start(bf16[2048,256]{1,0:T(8,128)(2,1)} %convolution_convert_fusion.2), channel_id=1, source_target_pairs={{16,0},{32,16},{48,32},{64,48},{80,64},{96,80},{112,96},{17,1},{33... | collective-permute-start | bytes 3145736 | tf_op jit(solution)/shard_map/ppermute | solution.py:28
  25.1 22.5 %collective-permute-start = (bf16[2048,256]{1,0:T(8,128)(2,1)}, bf16[2048,256]{1,0:T(8,128)(2,1)}, u32[]{:S(2)}, u32[]{:S(2)}) collective-permute-start(bf16[2048,256]{1,0:T(8,128)(2,1)} %convolution_convert_fusion.2), channel_id=1, source_target_pairs={{0,16},{16,32},{32,48},{48,64},{64,80},{80,96},{96,112},{1,17},{17... | collective-permute-start | bytes 3145736 | tf_op jit(solution)/shard_map/ppermute | solution.py:28
  29.2 1.9 %copy-start.4 = (bf16[256,512]{1,0:T(8,128)(2,1)S(1)}, bf16[256,512]{1,0:T(8,128)(2,1)}, u32[]{:S(2)}) copy-start(bf16[256,512]{1,0:T(8,128)(2,1)} %wkv_ref.1) | copy-start | bytes 786436
  91.2 60.8 %collective-permute-start.4 = (bf16[2048,256]{1,0:T(8,128)(2,1)}, bf16[2048,256]{1,0:T(8,128)(2,1)}, u32[]{:S(2)}, u32[]{:S(2)}) collective-permute-start(bf16[2048,256]{1,0:T(8,128)(2,1)} %bitcast.43), channel_id=1, source_target_pairs={{16,0},{32,16},{48,32},{64,48},{80,64},{96,80},{112,96},{17,1},{33... | collective-permute-start | bytes 3145736 | tf_op jit(solution)/shard_map/ppermute | solution.py:28
  93.9 58.2 %collective-permute-start.5 = (bf16[2048,256]{1,0:T(8,128)(2,1)}, bf16[2048,256]{1,0:T(8,128)(2,1)}, u32[]{:S(2)}, u32[]{:S(2)}) collective-permute-start(bf16[2048,256]{1,0:T(8,128)(2,1)} %bitcast.42), channel_id=1, source_target_pairs={{0,16},{16,32},{32,48},{48,64},{64,80},{80,96},{96,112},{1,17},{17... | collective-permute-start | bytes 3145736 | tf_op jit(solution)/shard_map/ppermute | solution.py:28
  97.1 55.0 %collective-permute-start.6 = (bf16[2048,256]{1,0:T(8,128)(2,1)}, bf16[2048,256]{1,0:T(8,128)(2,1)}, u32[]{:S(2)}, u32[]{:S(2)}) collective-permute-start(bf16[2048,256]{1,0:T(8,128)(2,1)} %bitcast.41), channel_id=1, source_target_pairs={{1,0},{2,1},{3,2},{4,3},{5,4},{6,5},{7,6},{8,7},{9,8},{10,9},{11,1... | collective-permute-start | bytes 3145736 | tf_op jit(solution)/shard_map/ppermute | solution.py:28
  98.4 53.7 %collective-permute-start.7 = (bf16[2048,256]{1,0:T(8,128)(2,1)}, bf16[2048,256]{1,0:T(8,128)(2,1)}, u32[]{:S(2)}, u32[]{:S(2)}) collective-permute-start(bf16[2048,256]{1,0:T(8,128)(2,1)} %bitcast.40), channel_id=1, source_target_pairs={{0,1},{1,2},{2,3},{3,4},{4,5},{5,6},{6,7},{7,8},{8,9},{9,10},{10,1... | collective-permute-start | bytes 3145736 | tf_op jit(solution)/shard_map/ppermute | solution.py:28
  103.5 48.6 %all-to-all-start.1 = ((bf16[128,16,256]{2,1,0:T(8,128)(2,1)}), bf16[128,16,256]{2,1,0:T(8,128)(2,1)S(1)}, u32[]{:S(2)}, u32[]{:S(2)}) async-start(bf16[128,16,256]{2,1,0:T(8,128)(2,1)} %bitcast.38), calls=%async_computation.1 | async-start | bytes 2097152 | tf_op jit(solution)/shard_map/all_to_all | solution.py:327

commit v15 on v14

--- a/solution.py
+++ b/solution.py
@@ -251,7 +251,7 @@
     out_ref[...] = total.astype(out_ref.dtype)
 
 
-def edge_back(edge_slope, own_part, received, grad_node, w_e1, w_e2, rows_per_step=256):
+def edge_back(edge_slope, own_part, received, grad_node, w_e1, w_e2, rows_per_step=1024):
     rows, width = edge_slope.shape
     row_block = pl.BlockSpec((rows_per_step, width), lambda i: (i, 0))
     weight = pl.BlockSpec(w_e1.shape, lambda i: (0, 0))

time: 162 us -> 159 us (0.981)
  Pallas kernels: 52.3 us -> 49.1 us
    pallas_call x1, Pallas kernels: 8.67 us -> 5.49 us  [edge_back(): pl.pallas_call(edge_back_kernel, grid=(rows // rows_per_step,), in_specs=...]
  transfers between devices with their start and end apart: 10 -> 10, of which waited for: 3 -> 3; matrix products, arithmetic and copies ran while one was open for 6% -> 7% of each run, Pallas kernels for 0% -> 0%
where the time goes in v15:
time: 159 us
  waiting for transfers between devices  49.8 us (31%)
  Pallas kernels  49.1 us (31%)
  starting transfers between devices  46.9 us (29%)
  matrix products  6.86 us (4%)
  local copies, waits for them, and re-layouts  2.91 us (2%)
  other arithmetic  2.11 us (1%)
    all_to_all x1, waiting for transfers between devices, on_device(): lax.all_to_all(grad_slots.reshape(devices, slot_count, latent_width), ('p...  36.2 us
    ppermute x8, starting transfers between devices, passed_along(): lax.ppermute(value, axis, [(source, source + steps) for source in range(l...  24.6 us
    pallas_call x1, Pallas kernels, attend_back(): pl.pallas_call(functools.partial(attend_kernel, scale), grid=(steps,), in...  19.5 us
    ppermute x8, waiting for transfers between devices, passed_along(): lax.ppermute(value, axis, [(source, source + steps) for source in range(l...  13.3 us
    pallas_call x1, Pallas kernels, tile_gather(): pl.pallas_call(functools.partial(gather_kernel, group), grid_spec=pltpu.P...  12.3 us
    all_to_all x1, starting transfers between devices, on_device(): lax.all_to_all(token_groups, ('px', 'py'), split_axis=0, concat_axis=0, t...  12 us
    pallas_call x1, Pallas kernels, tile_scatter(): pl.pallas_call(functools.partial(scatter_kernel, group), grid_spec=pltpu....  11.9 us
    all_to_all x1, starting transfers between devices, on_device(): lax.all_to_all(grad_slots.reshape(devices, slot_count, latent_width), ('p...  10.4 us
  transfers between devices with their start and end apart: 10, of which 3 were waited for; matrix products, arithmetic and copies ran while one was open for 7% of the time, Pallas kernels for 0%

profile of v15, /device:TPU:1, one launch (start us, length us, event | category | flops | bytes accessed | tf_op | source)
XLA Modules:
  0.0 158.5 jit_solution(10454596833647734242)
XLA Ops:
  0.6 0.0 copy-start
  0.6 0.0 copy-start.3
  0.7 0.0 copy-start.2
  0.7 12.0 %all-to-all-start = ((bf16[128,16,256]{2,1,0:T(8,128)(2,1)}), bf16[128,16,256]{2,1,0:T(8,128)(2,1)}, u32[]{:S(2)}, u32[]{:S(2)}) async-start(bf16[128,16,256]{2,1,0:T(8,128)(2,1)} %bitcast.37), calls=%async_computation | async-start | bytes 2097152 | tf_op jit(solution)/shard_map/all_to_all | solution.py:317
  12.6 0.0 copy-start.5
  12.7 0.4 fusion.2
  13.1 0.5 copy-done.5
  13.6 1.7 %convolution_convert_fusion.2 = bf16[2048,256]{1,0:T(8,128)(2,1)} fusion(bf16[256,256]{1,0:T(8,128)(2,1)S(1)} %copy-done.5, f32[2048,256]{1,0:T(8,128)S(1)} %fusion.2), kind=kOutput, calls=%fused_computation.2 | convolution fusion | flops 271581184 | bytes 3276800 | tf_op jit(solution)/shard_map/dot_general | solution.py:273
  15.2 1.3 collective-permute-start.3
  16.5 5.0 %collective-permute-start.2 = (bf16[2048,256]{1,0:T(8,128)(2,1)}, bf16[2048,256]{1,0:T(8,128)(2,1)}, u32[]{:S(2)}, u32[]{:S(2)}) collective-permute-start(bf16[2048,256]{1,0:T(8,128)(2,1)} %convolution_convert_fusion.2), channel_id=1, source_target_pairs={{0,1},{1,2},{2,3},{3,4},{4,5},{5,6},{6,7},{7,8},{8,9},{9,10},{10,1... | collective-permute-start | bytes 3145736 | tf_op jit(solution)/shard_map/ppermute | solution.py:28
  21.5 3.6 %collective-permute-start.1 = (bf16[2048,256]{1,0:T(8,128)(2,1)}, bf16[2048,256]{1,0:T(8,128)(2,1)}, u32[]{:S(2)}, u32[]{:S(2)}) collective-permute-start(bf16[2048,256]{1,0:T(8,128)(2,1)} %convolution_convert_fusion.2), channel_id=1, source_target_pairs={{16,0},{32,16},{48,32},{64,48},{80,64},{96,80},{112,96},{17,1},{33... | collective-permute-start | bytes 3145736 | tf_op jit(solution)/shard_map/ppermute | solution.py:28
  25.1 2.5 %collective-permute-start = (bf16[2048,256]{1,0:T(8,128)(2,1)}, bf16[2048,256]{1,0:T(8,128)(2,1)}, u32[]{:S(2)}, u32[]{:S(2)}) collective-permute-start(bf16[2048,256]{1,0:T(8,128)(2,1)} %convolution_convert_fusion.2), channel_id=1, source_target_pairs={{0,16},{16,32},{32,48},{48,64},{64,80},{80,96},{96,112},{1,17},{17... | collective-permute-start | bytes 3145736 | tf_op jit(solution)/shard_map/ppermute | solution.py:28
  27.6 0.1 copy.16
  27.7 0.7 reshape_squeeze.6.src_ids
  28.4 0.1 fusion
  28.5 0.7 reshape.80.live_ref
  29.2 1.5 convolution_convert_fusion.1.go_ref
  30.7 0.4 all-to-all-done
  31.1 3.2 %convolution_convert_fusion.kv_ref = bf16[2048,512]{1,0:T(8,128)(2,1)} fusion(bf16[2048,256]{1,0:T(8,128)(2,1)} %bitcast.10, bf16[256,512]{1,0:T(8,128)(2,1)S(1)} %copy-done.4), kind=kOutput, calls=%fused_computation | convolution fusion | flops 537919488 | bytes 3407872 | tf_op jit(solution)/shard_map/dot_general | solution.py:273
  34.3 13.2 %collective-permute-done.3 = bf16[2048,256]{1,0:T(8,128)(2,1)} collective-permute-done((bf16[2048,256]{1,0:T(8,128)(2,1)}, bf16[2048,256]{1,0:T(8,128)(2,1)}, u32[]{:S(2)}, u32[]{:S(2)}) %collective-permute-start.3) | collective-permute-done | bytes 1048608 | tf_op jit(solution)/shard_map/ppermute | solution.py:28
  47.6 12.3 %shard_map.140 = (f32[2048,256]{1,0:T(8,128)}, bf16[2048,256]{1,0:T(8,128)(2,1)}) custom-call(s32[64]{0:T(128)} %reshape_squeeze.6.src_ids, s32[16,4,128,128]{3,2,1,0:T(8,128)} %bitcast.30, bf16[16,128,256]{2,1,0:T(8,128)(2,1)} %bitcast.3.own, bf16[16,128,256]{2,1,0:T(8,128)(2,1)} %bitcast.4.up, bf16[16,128,256]{2,1,0:T(8,128)(2,1)} %bitcast.5.down, ...), custom_call_target="tpu_custom_call" | custom-call | tf_op jit(solution)/shard_map/pallas_call | solution.py:71
  59.9 19.5 %shard_map.141 = (bf16[2048,256]{1,0:T(8,128)(2,1)}, bf16[2048,256]{1,0:T(8,128)(2,1)}) custom-call(f32[1,2048]{1,0:T(1,128)} %reshape.80.live_ref, bf16[2048,256]{1,0:T(8,128)(2,1)} %get-tuple-element.14.q_ref, bf16[2048,256]{1,0:T(8,128)(2,1)} %convolution_convert_fusion.1.go_ref, bf16[2048,512]{1,0:T(8,128)(2,1)} %convolution_convert_fusion.kv_ref, ...), custom_call_target="tpu_custom_call" | custom-call | flops 10737418240 | bytes 7340032 | tf_op jit(solution)/shard_map/pallas_call | solution.py:209
  79.3 11.9 %shard_map.142 = (f32[2048,256]{1,0:T(8,128)}, f32[16,128,256]{2,1,0:T(8,128)}, bf16[16,128,256]{2,1,0:T(8,128)(2,1)}, bf16[16,128,256]{2,1,0:T(8,128)(2,1)}, bf...) custom-call(s32[64]{0:T(128)} %reshape_squeeze.6.src_ids, s32[16,4,128,128]{3,2,1,0:T(8,128)} %bitcast.31, ...), custom_call_target="tpu_custom_call" | custom-call | tf_op jit(solution)/shard_map/pallas_call | solution.py:142
  91.2 2.6 %collective-permute-start.4 = (bf16[2048,256]{1,0:T(8,128)(2,1)}, bf16[2048,256]{1,0:T(8,128)(2,1)}, u32[]{:S(2)}, u32[]{:S(2)}) collective-permute-start(bf16[2048,256]{1,0:T(8,128)(2,1)} %bitcast.43), channel_id=1, source_target_pairs={{16,0},{32,16},{48,32},{64,48},{80,64},{96,80},{112,96},{17,1},{33... | collective-permute-start | bytes 3145736 | tf_op jit(solution)/shard_map/ppermute | solution.py:28
  93.9 3.2 %collective-permute-start.5 = (bf16[2048,256]{1,0:T(8,128)(2,1)}, bf16[2048,256]{1,0:T(8,128)(2,1)}, u32[]{:S(2)}, u32[]{:S(2)}) collective-permute-start(bf16[2048,256]{1,0:T(8,128)(2,1)} %bitcast.42), channel_id=1, source_target_pairs={{0,16},{16,32},{32,48},{48,64},{64,80},{80,96},{96,112},{1,17},{17... | collective-permute-start | bytes 3145736 | tf_op jit(solution)/shard_map/ppermute | solution.py:28
  97.1 1.3 collective-permute-start.6
  98.4 5.1 %collective-permute-start.7 = (bf16[2048,256]{1,0:T(8,128)(2,1)}, bf16[2048,256]{1,0:T(8,128)(2,1)}, u32[]{:S(2)}, u32[]{:S(2)}) collective-permute-start(bf16[2048,256]{1,0:T(8,128)(2,1)} %bitcast.40), channel_id=1, source_target_pairs={{0,1},{1,2},{2,3},{3,4},{4,5},{5,6},{6,7},{7,8},{8,9},{9,10},{10,1... | collective-permute-start | bytes 3145736 | tf_op jit(solution)/shard_map/ppermute | solution.py:28
  103.5 10.4 %all-to-all-start.1 = ((bf16[128,16,256]{2,1,0:T(8,128)(2,1)}), bf16[128,16,256]{2,1,0:T(8,128)(2,1)S(1)}, u32[]{:S(2)}, u32[]{:S(2)}) async-start(bf16[128,16,256]{2,1,0:T(8,128)(2,1)} %bitcast.38), calls=%async_computation.1 | async-start | bytes 2097152 | tf_op jit(solution)/shard_map/all_to_all | solution.py:327
  113.9 2.0 %add_multiply_fusion.slope_ref = f32[2048,256]{1,0:T(8,128)} fusion(f32[2048,256]{1,0:T(8,128)S(1)} %fusion.2), kind=kLoop, calls=%fused_computation.3 | loop fusion | flops 3670016 | bytes 4194304 | tf_op jit(solution)/shard_map/mul | solution.py:278
  115.9 36.2 %all-to-all-done.1 = bf16[128,16,256]{2,1,0:T(8,128)(2,1)S(1)} async-done(((bf16[128,16,256]{2,1,0:T(8,128)(2,1)}), bf16[128,16,256]{2,1,0:T(8,128)(2,1)S(1)}, u32[]{:S(2)}, u32[]{:S(2)}) %all-to-all-start.1) | async-done | bytes 1048608 | tf_op jit(solution)/shard_map/all_to_all | solution.py:327
  152.1 5.5 %shard_map.143 = bf16[2048,256]{1,0:T(8,128)(2,1)} custom-call(f32[2048,256]{1,0:T(8,128)} %add_multiply_fusion.slope_ref, f32[2048,256]{1,0:T(8,128)} %bitcast.35, bf16[2048,256]{1,0:T(8,128)(2,1)} %collective-permute-done.4.a_ref, bf16[2048,256]{1,0:T(8,128)(2,1)} %collective-permute-done.5.b_ref, bf16[2048,256]{1,0:T(8,128)(2,1)} %collective-permute-done.6.c_ref, ...), custom_call_target="tpu_custom_call" | custom-call | flops 805306368 | bytes 11534336 | tf_op jit(solution)/shard_map/pallas_call | solution.py:258
  157.6 1.0 copy.18
  (18 shorter events, 0.0 us)
Async XLA Ops:
  0.6 28.5 %copy-start = (bf16[256,256]{1,0:T(8,128)(2,1)S(1)}, bf16[256,256]{1,0:T(8,128)(2,1)}, u32[]{:S(2)}) copy-start(bf16[256,256]{1,0:T(8,128)(2,1)} %param.24) | copy-start | bytes 393220
  0.6 12.0 %copy-start.3 = (bf16[256,256]{1,0:T(8,128)(2,1)S(1)}, bf16[256,256]{1,0:T(8,128)(2,1)}, u32[]{:S(2)}) copy-start(bf16[256,256]{1,0:T(8,128)(2,1)} %w1_ref.1) | copy-start | bytes 393220
  0.7 12.0 %copy-start.2 = (bf16[1,1,2048,256]{3,2,1,0:T(8,128)(2,1)S(1)}, bf16[1,1,2048,256]{3,2,1,0:T(8,128)(2,1)}, u32[]{:S(2)}) copy-start(bf16[1,1,2048,256]{3,2,1,0:T(8,128)(2,1)} %param.13) | copy-start | bytes 3145732
  0.7 30.4 %all-to-all-start = ((bf16[128,16,256]{2,1,0:T(8,128)(2,1)}), bf16[128,16,256]{2,1,0:T(8,128)(2,1)}, u32[]{:S(2)}, u32[]{:S(2)}) async-start(bf16[128,16,256]{2,1,0:T(8,128)(2,1)} %bitcast.37), calls=%async_computation | async-start | bytes 2097152 | tf_op jit(solution)/shard_map/all_to_all | solution.py:317
  12.6 0.9 copy-start.5
  13.6 14.1 %copy-start.6 = (s32[1,1,16,4]{2,3,1,0:T(4,128)S(1)}, s32[1,1,16,4]{2,3,1,0:T(4,128)}, u32[]{:S(2)}) copy-start(s32[1,1,16,4]{2,3,1,0:T(4,128)} %param.14) | copy-start | bytes 772
  13.6 14.8 %copy-start.7 = (s32[128,1]{0,1:T(1,128)S(1)}, s32[128,1]{0,1:T(1,128)}, u32[]{:S(2)}) copy-start(s32[128,1]{0,1:T(1,128)} %param.17) | copy-start | bytes 1540
  13.6 15.6 %copy-start.1 = (bf16[1,1,2048,256]{3,2,1,0:T(8,128)(2,1)S(1)}, bf16[1,1,2048,256]{3,2,1,0:T(8,128)(2,1)}, u32[]{:S(2)}) copy-start(bf16[1,1,2048,256]{3,2,1,0:T(8,128)(2,1)} %param.25) | copy-start | bytes 3145732
  15.2 32.4 %collective-permute-start.3 = (bf16[2048,256]{1,0:T(8,128)(2,1)}, bf16[2048,256]{1,0:T(8,128)(2,1)}, u32[]{:S(2)}, u32[]{:S(2)}) collective-permute-start(bf16[2048,256]{1,0:T(8,128)(2,1)} %convolution_convert_fusion.2), channel_id=1, source_target_pairs={{1,0},{2,1},{3,2},{4,3},{5,4},{6,5},{7,6},{8,7},{9,8},{10,9},{11,1... | collective-permute-start | bytes 3145736 | tf_op jit(solution)/shard_map/ppermute | solution.py:28
  16.5 31.1 %collective-permute-start.2 = (bf16[2048,256]{1,0:T(8,128)(2,1)}, bf16[2048,256]{1,0:T(8,128)(2,1)}, u32[]{:S(2)}, u32[]{:S(2)}) collective-permute-start(bf16[2048,256]{1,0:T(8,128)(2,1)} %convolution_convert_fusion.2), channel_id=1, source_target_pairs={{0,1},{1,2},{2,3},{3,4},{4,5},{5,6},{6,7},{7,8},{8,9},{9,10},{10,1... | collective-permute-start | bytes 3145736 | tf_op jit(solution)/shard_map/ppermute | solution.py:28
  21.5 26.1 %collective-permute-start.1 = (bf16[2048,256]{1,0:T(8,128)(2,1)}, bf16[2048,256]{1,0:T(8,128)(2,1)}, u32[]{:S(2)}, u32[]{:S(2)}) collective-permute-start(bf16[2048,256]{1,0:T(8,128)(2,1)} %convolution_convert_fusion.2), channel_id=1, source_target_pairs={{16,0},{32,16},{48,32},{64,48},{80,64},{96,80},{112,96},{17,1},{33... | collective-permute-start | bytes 3145736 | tf_op jit(solution)/shard_map/ppermute | solution.py:28
  25.1 22.5 %collective-permute-start = (bf16[2048,256]{1,0:T(8,128)(2,1)}, bf16[2048,256]{1,0:T(8,128)(2,1)}, u32[]{:S(2)}, u32[]{:S(2)}) collective-permute-start(bf16[2048,256]{1,0:T(8,128)(2,1)} %convolution_convert_fusion.2), channel_id=1, source_target_pairs={{0,16},{16,32},{32,48},{48,64},{64,80},{80,96},{96,112},{1,17},{17... | collective-permute-start | bytes 3145736 | tf_op jit(solution)/shard_map/ppermute | solution.py:28
  29.2 1.9 %copy-start.4 = (bf16[256,512]{1,0:T(8,128)(2,1)S(1)}, bf16[256,512]{1,0:T(8,128)(2,1)}, u32[]{:S(2)}) copy-start(bf16[256,512]{1,0:T(8,128)(2,1)} %wkv_ref.1) | copy-start | bytes 786436
  91.2 60.8 %collective-permute-start.4 = (bf16[2048,256]{1,0:T(8,128)(2,1)}, bf16[2048,256]{1,0:T(8,128)(2,1)}, u32[]{:S(2)}, u32[]{:S(2)}) collective-permute-start(bf16[2048,256]{1,0:T(8,128)(2,1)} %bitcast.43), channel_id=1, source_target_pairs={{16,0},{32,16},{48,32},{64,48},{80,64},{96,80},{112,96},{17,1},{33... | collective-permute-start | bytes 3145736 | tf_op jit(solution)/shard_map/ppermute | solution.py:28
  93.9 58.2 %collective-permute-start.5 = (bf16[2048,256]{1,0:T(8,128)(2,1)}, bf16[2048,256]{1,0:T(8,128)(2,1)}, u32[]{:S(2)}, u32[]{:S(2)}) collective-permute-start(bf16[2048,256]{1,0:T(8,128)(2,1)} %bitcast.42), channel_id=1, source_target_pairs={{0,16},{16,32},{32,48},{48,64},{64,80},{80,96},{96,112},{1,17},{17... | collective-permute-start | bytes 3145736 | tf_op jit(solution)/shard_map/ppermute | solution.py:28
  97.1 55.0 %collective-permute-start.6 = (bf16[2048,256]{1,0:T(8,128)(2,1)}, bf16[2048,256]{1,0:T(8,128)(2,1)}, u32[]{:S(2)}, u32[]{:S(2)}) collective-permute-start(bf16[2048,256]{1,0:T(8,128)(2,1)} %bitcast.41), channel_id=1, source_target_pairs={{1,0},{2,1},{3,2},{4,3},{5,4},{6,5},{7,6},{8,7},{9,8},{10,9},{11,1... | collective-permute-start | bytes 3145736 | tf_op jit(solution)/shard_map/ppermute | solution.py:28
  98.4 53.7 %collective-permute-start.7 = (bf16[2048,256]{1,0:T(8,128)(2,1)}, bf16[2048,256]{1,0:T(8,128)(2,1)}, u32[]{:S(2)}, u32[]{:S(2)}) collective-permute-start(bf16[2048,256]{1,0:T(8,128)(2,1)} %bitcast.40), channel_id=1, source_target_pairs={{0,1},{1,2},{2,3},{3,4},{4,5},{5,6},{6,7},{7,8},{8,9},{9,10},{10,1... | collective-permute-start | bytes 3145736 | tf_op jit(solution)/shard_map/ppermute | solution.py:28
  103.5 48.6 %all-to-all-start.1 = ((bf16[128,16,256]{2,1,0:T(8,128)(2,1)}), bf16[128,16,256]{2,1,0:T(8,128)(2,1)S(1)}, u32[]{:S(2)}, u32[]{:S(2)}) async-start(bf16[128,16,256]{2,1,0:T(8,128)(2,1)} %bitcast.38), calls=%async_computation.1 | async-start | bytes 2097152 | tf_op jit(solution)/shard_map/all_to_all | solution.py:327
